TPU v7x, 32 devices: a whole 2x2x4 slice. The times are simulated.
32 devices in a mesh: dp: 4 (over x, core), seq: 8 (over z, y).
Axes of the slice: x: 2, y: 2, z: 4, core: 2. Of those that a mesh axis runs over, the one named last changes fastest.
Arguments:
- inputs: bfloat16 [2, 4, 1024, 768], P(None, 'dp', 'seq'), may hold values from -6 to 6
- cotangent: bfloat16 [2, 4, 1024, 768], P(None, 'dp', 'seq'), may hold values from -6 to 6
- bounds: int32 [2, 4, 2, 2], P(None, 'dp'), may hold values from 0 to 1024, as said below
- ln1_gain: bfloat16 [768], P(('dp', 'seq')), may hold values from 0.5 to 1.5
- ln1_bias: bfloat16 [768], P(('dp', 'seq')), may hold values from -1 to 1
- w_qkv: bfloat16 [768, 2304], P(('dp', 'seq')), may hold values from -0.21875 to 0.21875
- b_query: bfloat16 [768], P(('dp', 'seq')), may hold values from -1.5 to 1.5
- b_value: bfloat16 [768], P(('dp', 'seq')), may hold values from -1.5 to 1.5
- w_out: bfloat16 [768, 768], P(('dp', 'seq')), may hold values from -1.25 to 1.25
- b_out: bfloat16 [768], P(('dp', 'seq')), may hold values from -1.5 to 1.5
- ln2_gain: bfloat16 [768], P(('dp', 'seq')), may hold values from 0.5 to 1.5
- ln2_bias: bfloat16 [768], P(('dp', 'seq')), may hold values from -1 to 1
- w_up: bfloat16 [768, 3072], P(('dp', 'seq')), may hold values from -0.21875 to 0.21875
- b_up: bfloat16 [3072], P(('dp', 'seq')), may hold values from -1.5 to 1.5
- w_down: bfloat16 [3072, 768], P(('dp', 'seq')), may hold values from -0.109375 to 0.109375
- b_down: bfloat16 [768], P(('dp', 'seq')), may hold values from -1.5 to 1.5
Outputs:
- outputs: bfloat16 [2, 4, 1024, 768], P(None, 'dp', 'seq')
- input_grad: bfloat16 [2, 4, 1024, 768], P(None, 'dp', 'seq')
- grad_ln1_gain: float32 [768], P(('dp', 'seq'))
- grad_ln1_bias: float32 [768], P(('dp', 'seq'))
- grad_w_qkv: float32 [768, 2304], P(('dp', 'seq'))
- grad_b_query: float32 [768], P(('dp', 'seq'))
- grad_b_value: float32 [768], P(('dp', 'seq'))
- grad_w_out: float32 [768, 768], P(('dp', 'seq'))
- grad_b_out: float32 [768], P(('dp', 'seq'))
- grad_ln2_gain: float32 [768], P(('dp', 'seq'))
- grad_ln2_bias: float32 [768], P(('dp', 'seq'))
- grad_w_up: float32 [768, 3072], P(('dp', 'seq'))
- grad_b_up: float32 [3072], P(('dp', 'seq'))
- grad_w_down: float32 [3072, 768], P(('dp', 'seq'))
- grad_b_down: float32 [768], P(('dp', 'seq'))
Inputs may be any that keep to these rules, and one draw needn't show every extreme that they name: `bounds`: for each sequence, 2 picture pieces [start, end) of exactly 256 rows each, in increasing order and not intersecting.
All inputs are finite; a program needn't handle non-finite values.
Results may differ from a plain program's by a relative error of at most 0.02.
Values may be sent and summed in bfloat16 or wider, within the bound.
No kernel may reach another device: no remote copies, remote signals or barrier semaphores. Data moves between devices by JAX's collectives and lax.ppermute only.
A program may use at most 256 MiB of HBM per device.

v0:
```python
from functools import partial

import jax
import jax.numpy as jnp
from jax import lax
from jax.sharding import PartitionSpec as P

HEADS = 12
HEAD = 64
EPSILON = 1e-05
ALL = ("dp", "seq")


def layer_norm(values, ln_gain, ln_shift):
    center = jnp.mean(values, axis=-1, keepdims=True)
    centered = values - center
    spread = jnp.mean(centered * centered, axis=-1, keepdims=True)
    return centered * lax.rsqrt(spread + EPSILON) * ln_gain + ln_shift


def piece_label(positions, bounds):
    inside = (positions[:, None] >= bounds[None, :, 0]) & (positions[:, None] < bounds[None, :, 1])
    labels = jnp.arange(1, bounds.shape[0] + 1, dtype=jnp.int32)
    return jnp.sum(jnp.where(inside, labels[None, :], 0), axis=1) - 1


def allowed_mask(query_pos, key_pos, bounds):
    query_label = piece_label(query_pos, bounds)
    key_label = piece_label(key_pos, bounds)
    causal = key_pos[None, :] <= query_pos[:, None]
    same_piece = (query_label[:, None] == key_label[None, :]) & (query_label[:, None] >= 0)
    return causal | same_piece


def outer_rows(left, right):
    return lax.dot_general(
        left, right, (((0,), (0,)), ((), ())), preferred_element_type=jnp.float32
    )


def times_transposed(left, right):
    return lax.dot_general(
        left, right, (((1,), (1,)), ((), ())), preferred_element_type=jnp.float32
    )


def route_orders(dp_size, seq_size):
    nbits = (dp_size * seq_size).bit_length() - 1
    if (dp_size, seq_size) == (4, 8):
        return [(3, 4, 0, 1, 2), (3, 0, 1, 4, 2), (3, 1, 4, 0, 2)]
    core = (seq_size.bit_length() - 1) if dp_size > 1 else None
    others = [b for b in range(nbits) if b != core]
    head = [core] if core is not None else []
    return [tuple(head + others[i:] + others[:i]) for i in range(3)]


def split_routes(arrays, routes, grain=128):
    sizes = [a.shape[0] * a.shape[1] for a in arrays]
    target = sum(sizes) / routes
    segs = [[] for _ in range(routes)]
    load = 0.0
    for i, a in enumerate(arrays):
        rows, width = a.shape
        c = 0
        while c < width:
            route = min(int(load // target), routes - 1)
            if route == routes - 1:
                take = width - c
            else:
                room = (route + 1) * target - load
                take = min(width - c, max(grain, int(room // rows) // grain * grain))
            segs[route].append((i, c, c + take))
            c += take
            load += take * rows
    return segs


def partner_pairs(count, bit):
    return [(i, i ^ (1 << bit)) for i in range(count)]


def tie(values, anchor):
    if anchor is None:
        return values
    values, _ = lax.optimization_barrier((values, anchor))
    return values


def gather_params(arrays, orders, count, me, anchors=None):
    nbits = count.bit_length() - 1
    segs = split_routes(arrays, len(orders))
    pieces = {}
    for route, order in zip(segs, orders):
        if not route:
            continue
        xs = [arrays[i][:, c0:c1] for i, c0, c1 in route]
        for step, b in enumerate(reversed(order)):
            if anchors is not None:
                xs = tie(xs, anchors[step])
            got = lax.ppermute(xs, ALL, partner_pairs(count, b))
            xs = [jnp.stack([x, g]) for x, g in zip(xs, got)]
        idx = jnp.arange(count, dtype=jnp.int32)
        rel = jnp.zeros((count,), jnp.int32)
        for j, b in enumerate(order):
            rel = rel + ((((idx >> b) & 1) ^ ((me >> b) & 1)) << (nbits - 1 - j))
        for (i, c0, c1), x in zip(route, xs):
            rows = arrays[i].shape[0]
            x = jnp.take(x.reshape(count, rows, c1 - c0), rel, axis=0)
            pieces[(i, c0)] = x.reshape(count * rows, c1 - c0)
    out = []
    for i in range(len(arrays)):
        parts = [pieces[k] for k in sorted(k for k in pieces if k[0] == i)]
        out.append(parts[0] if len(parts) == 1 else jnp.concatenate(parts, axis=1))
    return out


def reduce_params(arrays, orders, count, me, anchors=None):
    nbits = count.bit_length() - 1
    segs = split_routes(arrays, len(orders))
    pieces = {}
    for route, order in zip(segs, orders):
        if not route:
            continue
        xs = []
        for i, c0, c1 in route:
            rows = arrays[i].shape[0] // count
            xs.append(arrays[i][:, c0:c1].reshape([2] * nbits + [rows, c1 - c0]))
        remaining = list(range(nbits - 1, -1, -1))
        for step, b in enumerate(order):
            if anchors is not None:
                xs = tie(xs, anchors[step])
            axis = remaining.index(b)
            mine = (me >> b) & 1
            keep = [lax.dynamic_index_in_dim(x, mine, axis, keepdims=False) for x in xs]
            send = [
                lax.dynamic_index_in_dim(x, 1 - mine, axis, keepdims=False).astype(jnp.bfloat16)
                for x in xs
            ]
            got = lax.ppermute(send, ALL, partner_pairs(count, b))
            xs = [k + g.astype(jnp.float32) for k, g in zip(keep, got)]
            remaining.pop(axis)
        for (i, c0, c1), x in zip(route, xs):
            pieces[(i, c0)] = x.reshape(arrays[i].shape[0] // count, c1 - c0)
    out = []
    for i in range(len(arrays)):
        parts = [pieces[k] for k in sorted(k for k in pieces if k[0] == i)]
        out.append(parts[0] if len(parts) == 1 else jnp.concatenate(parts, axis=1))
    return out


def vector_block(vectors, rows, dtype):
    cols = [v.reshape(rows, -1).astype(dtype) for v in vectors]
    used = sum(c.shape[1] for c in cols)
    pad = -(-used // 128) * 128 - used
    if pad:
        cols.append(jnp.zeros((rows, pad), dtype))
    return jnp.concatenate(cols, axis=1)


def vector_unblock(block, sizes):
    out, at = [], 0
    rows = block.shape[0]
    for s in sizes:
        out.append(block[:, at : at + s].reshape(rows * s))
        at += s
    return out


def unit_bounds(bounds, unit_count, per_device):
    first = lax.axis_index("seq") * per_device
    micro = (first + jnp.arange(per_device, dtype=jnp.int32)) // HEADS
    return bounds[:, 0][micro]


def unit_masks(ubounds, length):
    pos = jnp.arange(length, dtype=jnp.int32)
    return jax.vmap(lambda b: allowed_mask(pos, pos, b))(ubounds)


def rows_to_units(x, seq_count, per_device, parts):
    micro, rows = x.shape[0], x.shape[1]
    x = jnp.transpose(x, (0, 3, 1, 2, 4)).reshape(seq_count, per_device, rows, parts, HEAD)
    x = lax.all_to_all(x, "seq", 0, 0, tiled=True)
    x = jnp.transpose(x, (1, 0, 2, 3, 4))
    return x.reshape(per_device, seq_count * rows, parts, HEAD)


def units_to_rows(x, seq_count, micro, parts):
    per_device, length = x.shape[0], x.shape[1]
    rows = length // seq_count
    x = x.reshape(per_device, seq_count, rows, parts, HEAD)
    x = jnp.transpose(x, (1, 0, 2, 3, 4))
    x = lax.all_to_all(x, "seq", 0, 0, tiled=True)
    x = x.reshape(micro, HEADS, rows, parts, HEAD)
    x = jnp.transpose(x, (0, 2, 3, 1, 4))
    return x.reshape(micro * rows, parts * HEADS * HEAD)


def unit_forward(q, k, v, allowed):
    factor = q.shape[-1] ** (-0.5)
    scores = jnp.einsum("uqd,ukd->uqk", q, k, preferred_element_type=jnp.float32) * factor
    weights = jnp.where(allowed, jnp.exp(scores), 0.0)
    totals = jnp.sum(weights, axis=-1)
    summed = jnp.einsum(
        "uqk,ukd->uqd", weights.astype(jnp.bfloat16), v, preferred_element_type=jnp.float32
    )
    return weights, totals, summed / totals[:, :, None]


def unit_backward(q, k, v, weights, totals, attended, attended_grad):
    factor = q.shape[-1] ** (-0.5)
    grad_f = attended_grad.astype(jnp.float32)
    delta = jnp.sum(grad_f * attended, axis=-1) / totals
    summed_grad = (grad_f / totals[:, :, None]).astype(jnp.bfloat16)
    products = jnp.einsum("uqd,ukd->uqk", summed_grad, v, preferred_element_type=jnp.float32)
    score_grad = (weights * (products - delta[:, :, None])).astype(jnp.bfloat16)
    q_grad = jnp.einsum("uqk,ukd->uqd", score_grad, k, preferred_element_type=jnp.float32) * factor
    k_grad = jnp.einsum("uqk,uqd->ukd", score_grad, q, preferred_element_type=jnp.float32) * factor
    v_grad = jnp.einsum(
        "uqk,uqd->ukd", weights.astype(jnp.bfloat16), summed_grad, preferred_element_type=jnp.float32
    )
    return jnp.stack([q_grad, k_grad, v_grad], axis=2).astype(jnp.bfloat16)


def fallback_attention(queries, keys, values, bounds, row_count):
    micro = bounds.shape[0]
    seq_count = lax.axis_size("seq")
    total_len = row_count * seq_count
    query_pos = lax.axis_index("seq") * row_count + jnp.arange(row_count, dtype=jnp.int32)
    key_pos = jnp.arange(total_len, dtype=jnp.int32)
    saved = []
    attended_all = []
    for m in range(micro):
        sl = slice(m * row_count, (m + 1) * row_count)
        qh = queries[sl].reshape(row_count, HEADS, HEAD)
        k_all = lax.all_gather(keys[sl], "seq", axis=0, tiled=True).reshape(total_len, HEADS, HEAD)
        v_all = lax.all_gather(values[sl], "seq", axis=0, tiled=True).reshape(total_len, HEADS, HEAD)
        allowed = allowed_mask(query_pos, key_pos, bounds[m, 0])
        scores = jnp.einsum("rhd,khd->hrk", qh, k_all, preferred_element_type=jnp.float32) * HEAD ** (-0.5)
        weights = jnp.where(allowed[None], jnp.exp(scores), 0.0)
        totals = jnp.sum(weights, axis=-1)
        summed = jnp.einsum(
            "hrk,khd->rhd", weights.astype(jnp.bfloat16), v_all, preferred_element_type=jnp.float32
        )
        attended = summed / totals.T[:, :, None]
        saved.append((qh, k_all, v_all, weights, totals, attended))
        attended_all.append(attended.reshape(row_count, HEADS * HEAD))
    return jnp.concatenate(attended_all, axis=0), saved


def fallback_attention_backward(saved, attended_grad, row_count):
    factor = HEAD ** (-0.5)
    proj = []
    for m, (qh, k_all, v_all, weights, totals, attended) in enumerate(saved):
        grad = attended_grad[m * row_count : (m + 1) * row_count].astype(jnp.float32)
        grad = grad.reshape(row_count, HEADS, HEAD)
        delta = jnp.sum(grad * attended, axis=-1).T / totals
        grad_heads = (grad / totals.T[:, :, None]).astype(jnp.bfloat16)
        products = jnp.einsum("rhd,khd->hrk", grad_heads, v_all, preferred_element_type=jnp.float32)
        score_grad = (weights * (products - delta[:, :, None])).astype(jnp.bfloat16)
        q_grad = jnp.einsum("hrk,khd->rhd", score_grad, k_all, preferred_element_type=jnp.float32) * factor
        k_rows = jnp.einsum("hrk,rhd->khd", score_grad, qh, preferred_element_type=jnp.float32) * factor
        v_rows = jnp.einsum(
            "hrk,rhd->khd", weights.astype(jnp.bfloat16), grad_heads, preferred_element_type=jnp.float32
        )
        width = HEADS * HEAD
        k_own = lax.psum_scatter(
            k_rows.reshape(-1, width).astype(jnp.bfloat16), "seq", scatter_dimension=0, tiled=True
        )
        v_own = lax.psum_scatter(
            v_rows.reshape(-1, width).astype(jnp.bfloat16), "seq", scatter_dimension=0, tiled=True
        )
        proj.append(
            jnp.concatenate(
                [q_grad.reshape(row_count, width).astype(jnp.bfloat16), k_own, v_own], axis=1
            )
        )
    return jnp.concatenate(proj, axis=0)


def body(inputs, cotangent, bounds, *shards):
    micro = inputs.shape[0]
    row_count = inputs.shape[2]
    width = inputs.shape[3]
    ff = shards[9].shape[1]
    rows = micro * row_count
    seq_count = lax.axis_size("seq")
    unit_count = micro * HEADS
    head_parallel = unit_count % seq_count == 0
    per_device = unit_count // seq_count
    dp_count = lax.axis_size("dp")
    count = dp_count * seq_count
    me = lax.axis_index("dp") * seq_count + lax.axis_index("seq")
    orders = route_orders(dp_count, seq_count)
    steps = len(orders[0])
    ln1_g, ln1_b, w_qkv, b_q, b_v, w_out, b_out, ln2_g, ln2_b, w_up, b_up, w_down, b_down = shards
    shard_rows = w_qkv.shape[0]
    ratio = ff // width
    vec_sizes = [1] * 8 + [ratio]
    vecs_local = vector_block(
        [ln1_g, ln1_b, b_q, b_v, b_out, ln2_g, ln2_b, b_down, b_up], shard_rows, jnp.bfloat16
    )
    proj_qkv, vecs_all = gather_params([w_qkv, vecs_local], orders, count, me)
    (
        gain_one,
        shift_one,
        bias_query,
        bias_value,
        bias_out,
        gain_two,
        shift_two,
        bias_down,
        bias_up,
    ) = vector_unblock(vecs_all, vec_sizes)

    seq_in = inputs[:, 0].reshape(rows, width).astype(jnp.float32)
    normed_f, norm_one_back = jax.vjp(
        layer_norm, seq_in, gain_one.astype(jnp.float32), shift_one.astype(jnp.float32)
    )
    normed = normed_f.astype(jnp.bfloat16)
    projected = jnp.dot(normed, proj_qkv, preferred_element_type=jnp.float32)
    queries = (projected[:, :width] + bias_query.astype(jnp.float32)).astype(jnp.bfloat16)
    keys_now = projected[:, width : 2 * width].astype(jnp.bfloat16)
    values_now = (projected[:, 2 * width :] + bias_value.astype(jnp.float32)).astype(jnp.bfloat16)

    if head_parallel:
        qkv_rows = jnp.concatenate([queries, keys_now, values_now], axis=1)
        qkv_units = rows_to_units(
            qkv_rows.reshape(micro, row_count, 3, HEADS, HEAD), seq_count, per_device, 3
        )
        uq, uk, uv = qkv_units[:, :, 0], qkv_units[:, :, 1], qkv_units[:, :, 2]
        allowed = unit_masks(unit_bounds(bounds, unit_count, per_device), seq_count * row_count)
        weights, totals, attended_u = unit_forward(uq, uk, uv, allowed)
        attended_b = units_to_rows(
            attended_u.astype(jnp.bfloat16)[:, :, None], seq_count, micro, 1
        )
        forward_anchors = [projected, qkv_units, weights, attended_u, attended_u]
    else:
        attended, saved = fallback_attention(queries, keys_now, values_now, bounds, row_count)
        attended_b = attended.astype(jnp.bfloat16)
        forward_anchors = [projected] + [attended] * (steps - 1)

    proj_out, proj_up, proj_down = gather_params(
        [w_out, w_up, w_down], orders, count, me, forward_anchors[:steps]
    )

    branch = jnp.dot(attended_b, proj_out, preferred_element_type=jnp.float32) + bias_out.astype(
        jnp.float32
    )
    middle = seq_in + branch
    normed_two_f, norm_two_back = jax.vjp(
        layer_norm, middle, gain_two.astype(jnp.float32), shift_two.astype(jnp.float32)
    )
    normed_two = normed_two_f.astype(jnp.bfloat16)
    hidden = jnp.dot(normed_two, proj_up, preferred_element_type=jnp.float32) + bias_up.astype(
        jnp.float32
    )
    activated_f, gelu_back = jax.vjp(partial(jax.nn.gelu, approximate=False), hidden)
    activated = activated_f.astype(jnp.bfloat16)
    mlp_out = jnp.dot(activated, proj_down, preferred_element_type=jnp.float32) + bias_down.astype(
        jnp.float32
    )
    outputs = (middle + mlp_out).astype(jnp.bfloat16)

    out_grad = cotangent[:, 0].reshape(rows, width)
    out_grad_f = out_grad.astype(jnp.float32)
    grad_down = outer_rows(activated, out_grad)
    grad_bias_down = jnp.sum(out_grad_f, axis=0)
    act_grad = times_transposed(out_grad, proj_down)
    (hidden_grad,) = gelu_back(act_grad)
    hidden_grad_b = hidden_grad.astype(jnp.bfloat16)
    grad_up = outer_rows(normed_two, hidden_grad_b)
    grad_bias_up = jnp.sum(hidden_grad_b.astype(jnp.float32), axis=0)
    normed_two_grad = times_transposed(hidden_grad_b, proj_up)
    middle_ln_grad, grad_gain_two, grad_shift_two = norm_two_back(normed_two_grad)
    middle_grad = out_grad_f + middle_ln_grad
    branch_grad = middle_grad.astype(jnp.bfloat16)
    grad_out = outer_rows(attended_b, branch_grad)
    grad_bias_out = jnp.sum(branch_grad.astype(jnp.float32), axis=0)
    attended_grad = times_transposed(branch_grad, proj_out).astype(jnp.bfloat16)

    if head_parallel:
        grad_units = rows_to_units(
            attended_grad.reshape(micro, row_count, 1, HEADS, HEAD), seq_count, per_device, 1
        )[:, :, 0]
        qkv_grad_u = unit_backward(uq, uk, uv, weights, totals, attended_u, grad_units)
        proj_grad = units_to_rows(qkv_grad_u, seq_count, micro, 3)
        backward_anchors = [None, grad_units, qkv_grad_u, proj_grad, proj_grad]
    else:
        proj_grad = fallback_attention_backward(saved, attended_grad, row_count)
        backward_anchors = [None] + [proj_grad] * (steps - 1)

    full_rows = count * shard_rows
    red_up, red_down, red_vec_one = reduce_params(
        [
            grad_up,
            grad_down,
            vector_block(
                [grad_bias_up, grad_bias_down, grad_gain_two, grad_shift_two], full_rows, jnp.float32
            ),
        ],
        orders,
        count,
        me,
        backward_anchors[:steps],
    )

    grad_qkv = outer_rows(normed, proj_grad)
    grad_bias_query = jnp.sum(proj_grad[:, :width].astype(jnp.float32), axis=0)
    grad_bias_value = jnp.sum(proj_grad[:, 2 * width :].astype(jnp.float32), axis=0)
    normed_grad = times_transposed(proj_grad, proj_qkv)
    input_ln_grad, grad_gain_one, grad_shift_one = norm_one_back(normed_grad)
    input_grads = (middle_grad + input_ln_grad).astype(jnp.bfloat16)

    red_qkv, red_out, red_vec_two = reduce_params(
        [
            grad_qkv,
            grad_out,
            vector_block(
                [grad_gain_one, grad_shift_one, grad_bias_query, grad_bias_value, grad_bias_out],
                full_rows,
                jnp.float32,
            ),
        ],
        orders,
        count,
        me,
    )
    r_bias_up, r_bias_down, r_gain_two, r_shift_two = vector_unblock(red_vec_one, [ratio, 1, 1, 1])
    r_gain_one, r_shift_one, r_bias_query, r_bias_value, r_bias_out = vector_unblock(
        red_vec_two, [1] * 5
    )
    reduced = (
        r_gain_one,
        r_shift_one,
        red_qkv,
        r_bias_query,
        r_bias_value,
        red_out,
        r_bias_out,
        r_gain_two,
        r_shift_two,
        red_up,
        r_bias_up,
        red_down,
        r_bias_down,
    )
    return (
        outputs.reshape(micro, 1, row_count, width),
        input_grads.reshape(micro, 1, row_count, width),
    ) + reduced


def solution(mesh):
    vec = P(ALL)
    mat = P(ALL, None)
    param_specs = (vec, vec, mat, vec, vec, mat, vec, vec, vec, mat, vec, mat, vec)
    return jax.shard_map(
        body,
        mesh=mesh,
        in_specs=(P(None, "dp", "seq", None), P(None, "dp", "seq", None), P(None, "dp", None, None))
        + param_specs,
        out_specs=(P(None, "dp", "seq", None), P(None, "dp", "seq", None)) + param_specs,
        check_vma=False,
    )
```

profile of v0, /device:TPU:0, one launch (start us, length us, event | category | flops | bytes accessed | tf_op | source)
XLA Modules:
  0.0 617.2 jit_solution(11727435702610400776)
XLA Ops:
  7.5 4.1 collective-permute-start
  64.3 5.2 collective-permute-done.18
  74.9 6.7 %collective-permute-done.8 = bf16[2,2,2,24,768]{4,3,2,1,0:T(8,128)(2,1)S(1)} collective-permute-done((bf16[2,2,2,24,768]{4,3,2,1,0:T(8,128)(2,1)S(1)}, bf16[2,2,2,24,768]{4,3,2,1,0:T(8,128)(2,1)S(1)}, u32[]{:S(2)}, u32[]{:S(2)}) %collective-permute-start.8) | collective-permute-done | bytes 294944 | tf_op jit(solution)/shard_map/ppermute | solution.py:100
  97.2 4.6 all-to-all-start
  112.5 24.8 %collective-permute-done.41 = bf16[96,128]{1,0:T(8,128)(2,1)S(1)} collective-permute-done((bf16[96,128]{1,0:T(8,128)(2,1)S(1)}, bf16[96,128]{1,0:T(8,128)(2,1)S(1)}, u32[]{:S(2)}, u32[]{:S(2)}) %collective-permute-start.41) | collective-permute-done | bytes 24608 | tf_op jit(solution)/shard_map/ppermute | solution.py:100
  137.3 6.6 %collective-permute-done.42 = bf16[96,128]{1,0:T(8,128)(2,1)S(1)} collective-permute-done((bf16[96,128]{1,0:T(8,128)(2,1)S(1)}, bf16[96,128]{1,0:T(8,128)(2,1)S(1)}, u32[]{:S(2)}, u32[]{:S(2)}) %collective-permute-start.42) | collective-permute-done | bytes 24608 | tf_op jit(solution)/shard_map/ppermute | solution.py:100
  150.3 6.2 fusion.187
  179.5 6.4 %collective-permute-done.47 = bf16[2,2,96,128]{3,2,1,0:T(8,128)(2,1)S(1)} collective-permute-done((bf16[2,2,96,128]{3,2,1,0:T(8,128)(2,1)S(1)}, bf16[2,2,96,128]{3,2,1,0:T(8,128)(2,1)S(1)}, u32[]{:S(2)}, u32[]{:S(2)}) %collective-permute-start.47) | collective-permute-done | bytes 98336 | tf_op jit(solution)/shard_map/ppermute | solution.py:100
  191.3 6.5 %collective-permute-done.57 = bf16[2,2,96,512]{3,2,1,0:T(8,128)(2,1)S(1)} collective-permute-done((bf16[2,2,96,512]{3,2,1,0:T(8,128)(2,1)S(1)}, bf16[2,2,96,512]{3,2,1,0:T(8,128)(2,1)S(1)}, u32[]{:S(2)}, u32[]{:S(2)}) %collective-permute-start.57) | collective-permute-done | bytes 393248 | tf_op jit(solution)/shard_map/ppermute | solution.py:100
  199.0 7.3 %collective-permute-done.50 = bf16[2,2,2,96,128]{4,3,2,1,0:T(8,128)(2,1)S(1)} collective-permute-done((bf16[2,2,2,96,128]{4,3,2,1,0:T(8,128)(2,1)S(1)}, bf16[2,2,2,96,128]{4,3,2,1,0:T(8,128)(2,1)S(1)}, u32[]{:S(2)}, u32[]{:S(2)}) %collective-permute-start.50) | collective-permute-done | bytes 196640 | tf_op jit(solution)/shard_map/ppermute | solution.py:100
  215.7 5.0 collective-permute-done.58
  247.2 11.1 %multiply_convert_fusion.1 = (bf16[256,3072]{1,0:T(8,128)(2,1)S(1)}, f32[256,3072]{1,0:T(8,128)}, f32[256,3072]{1,0:T(8,128)}) fusion(f32[3072]{0:T(1024)S(1)} %reshape.791, bf16[768,1536]{1,0:T(8,128)(2,1)S(1)} %bitcast.718, bf16[768,1536]{1,0:T(8,128)(2,1)S(1)} %bitcast.720, f32[256,768]{1,0:T(8,128)S(1)} %copy-done.14, f32[768]{0:T(1024)S(1)} %get-tuple-element.236, ...), kind=kOutput, calls=%fused_computation.28 | convolution fusion | flops 1270284288 | bytes 13389824 | tf_op jit(solution)/shard_map/dot_general | solution.py:355
  272.4 4.4 gather_fusion.1
  280.1 4.4 convert_reduce_fusion
  303.8 4.5 all-to-all-start.2
  333.7 6.8 %fusion.22 = bf16[3,1024,64]{1,2,0:T(8,128)(2,1)S(1)} fusion(f32[3,1024,1024]{1,2,0:T(8,128)} %copy-done.2, bf16[3,1024,64]{1,2,0:T(8,128)(2,1)S(1)} %squeeze_reshape.3, f32[3,1024]{1,0:T(4,128)S(1)} %get-tuple-element.336), kind=kOutput, calls=%fused_computation.76 | convolution fusion | flops 406585344 | bytes 13381632 | tf_op jit(solution)/shard_map/uqk,uqd->ukd/dot_general | solution.py:219
  340.8 6.4 %multiply_convert_fusion = bf16[3,1024,1024]{1,2,0:T(8,128)(2,1)S(1)} fusion(f32[3,1024,1024]{1,2,0:T(8,128)} %copy-done.2, f32[3,1024]{1,0:T(4,128)S(1)} %div.84, bf16[3,1024,3,64]{1,3,0,2:T(8,128)(2,1)S(1)} %copy-done.16, bf16[3,1024,64]{1,2,0:T(8,128)(2,1)S(1)} %squeeze_reshape.3, f32[3,1024]{1,0:T(4,128)S(1)} %get-tuple-element.336), kind=kOutput, calls=%fused_computation.13 | convolution fusion | flops 412680192 | bytes 19693568 | tf_op jit(solution)/shard_map/uqd,ukd->uqk/dot_general | solution.py:215
  352.0 4.8 all-to-all-start.3
  363.0 28.9 %collective-permute-done.98 = bf16[2,2,2,24,128]{4,3,2,1,0:T(8,128)(2,1)S(1)} collective-permute-done((bf16[2,2,2,24,128]{4,3,2,1,0:T(8,128)(2,1)S(1)}, bf16[2,2,2,24,128]{4,3,2,1,0:T(8,128)(2,1)S(1)}, u32[]{:S(2)}, u32[]{:S(2)}) %collective-permute-start.98) | collective-permute-done | bytes 49184 | tf_op jit(solution)/shard_map/ppermute | solution.py:139
  395.1 11.0 %collective-permute-done.119 = bf16[2,2,2,96,128]{4,3,1,0,2:T(8,128)(2,1)S(1)} collective-permute-done((bf16[2,2,2,96,128]{4,3,1,0,2:T(8,128)(2,1)S(1)}, bf16[2,2,2,96,128]{4,3,1,0,2:T(8,128)(2,1)S(1)}, u32[]{:S(2)}, u32[]{:S(2)}) %collective-permute-start.119) | collective-permute-done | bytes 196640 | tf_op jit(solution)/shard_map/ppermute | solution.py:139
  406.1 5.0 collective-permute-done.92
  434.1 5.1 collective-permute-done.100
  440.5 12.0 %collective-permute-done.107 = bf16[2,2,2,24,128]{4,3,0,1,2:T(8,128)(2,1)S(1)} collective-permute-done((bf16[2,2,2,24,128]{4,3,0,1,2:T(8,128)(2,1)S(1)}, bf16[2,2,2,24,128]{4,3,0,1,2:T(8,128)(2,1)S(1)}, u32[]{:S(2)}, u32[]{:S(2)}) %collective-permute-start.107) | collective-permute-done | bytes 49184 | tf_op jit(solution)/shard_map/ppermute | solution.py:139
  501.6 4.0 collective-permute-done.123
  (784 shorter events, 422.1 us)
Async XLA Ops:
  97.2 48.1 %all-to-all-start = ((bf16[8,3,128,3,64]{2,4,3,1,0:T(8,128)(2,1)}), bf16[8,3,128,3,64]{2,4,3,1,0:T(8,128)(2,1)S(1)}, u32[]{:S(2)}, u32[]{:S(2)}) async-start(bf16[8,3,128,3,64]{2,4,3,1,0:T(8,128)(2,1)} %bitcast.88), calls=%async_computation | async-start | bytes 2359296 | tf_op jit(solution)/shard_map/all_to_all | solution.py:183
  102.6 34.7 %collective-permute-start.41 = (bf16[96,128]{1,0:T(8,128)(2,1)S(1)}, bf16[96,128]{1,0:T(8,128)(2,1)S(1)}, u32[]{:S(2)}, u32[]{:S(2)}) collective-permute-start(bf16[96,128]{1,0:T(8,128)(2,1)S(1)} %get-tuple-element.89), channel_id=1, source_target_pairs={{0,4},{1,5},{2,6},{3,7},{4,0},{5,1},{6,2},{7,3},{8,12},{9,13},{10,... | collective-permute-start | bytes 73736 | tf_op jit(solution)/shard_map/ppermute | solution.py:100
  106.6 37.9 %collective-permute-start.30 = (bf16[24,768]{1,0:T(8,128)(2,1)S(1)}, bf16[24,768]{1,0:T(8,128)(2,1)S(1)}, u32[]{:S(2)}, u32[]{:S(2)}) collective-permute-start(bf16[24,768]{1,0:T(8,128)(2,1)S(1)} %copy-done.63), channel_id=1, source_target_pairs={{0,4},{1,5},{2,6},{3,7},{4,0},{5,1},{6,2},{7,3},{8,12},{9,13},{10,... | collective-permute-start | bytes 110600 | tf_op jit(solution)/shard_map/ppermute | solution.py:100
  106.6 37.9 %collective-permute-start.31 = (bf16[24,1536]{1,0:T(8,128)(2,1)S(1)}, bf16[24,1536]{1,0:T(8,128)(2,1)S(1)}, u32[]{:S(2)}, u32[]{:S(2)}) collective-permute-start(bf16[24,1536]{1,0:T(8,128)(2,1)S(1)} %get-tuple-element.79), channel_id=1, source_target_pairs={{0,4},{1,5},{2,6},{3,7},{4,0},{5,1},{6,2},{7,3},{8,12},{9,13},{10,... | collective-permute-start | bytes 221192 | tf_op jit(solution)/shard_map/ppermute | solution.py:100
  109.5 35.0 %collective-permute-start.40 = (bf16[24,1536]{1,0:T(8,128)(2,1)S(1)}, bf16[24,1536]{1,0:T(8,128)(2,1)S(1)}, u32[]{:S(2)}, u32[]{:S(2)}) collective-permute-start(bf16[24,1536]{1,0:T(8,128)(2,1)S(1)} %get-tuple-element.88), channel_id=1, source_target_pairs={{0,4},{1,5},{2,6},{3,7},{4,0},{5,1},{6,2},{7,3},{8,12},{9,13},{10,... | collective-permute-start | bytes 221192 | tf_op jit(solution)/shard_map/ppermute | solution.py:100
  109.6 34.3 %collective-permute-start.42 = (bf16[96,128]{1,0:T(8,128)(2,1)S(1)}, bf16[96,128]{1,0:T(8,128)(2,1)S(1)}, u32[]{:S(2)}, u32[]{:S(2)}) collective-permute-start(bf16[96,128]{1,0:T(8,128)(2,1)S(1)} %get-tuple-element.90), channel_id=1, source_target_pairs={{0,4},{1,5},{2,6},{3,7},{4,0},{5,1},{6,2},{7,3},{8,12},{9,13},{10,... | collective-permute-start | bytes 73736 | tf_op jit(solution)/shard_map/ppermute | solution.py:100
  162.2 52.3 %all-to-all-start.1 = ((bf16[8,3,128,1,64]{2,4,3,1,0:T(8,128)(2,1)}), bf16[8,3,128,1,64]{2,4,3,1,0:T(8,128)(2,1)S(1)}, u32[]{:S(2)}, u32[]{:S(2)}) async-start(bf16[8,3,128,1,64]{2,4,3,1,0:T(8,128)(2,1)} %bitcast.671), calls=%async_computation.1 | async-start | bytes 786432 | tf_op jit(solution)/shard_map/all_to_all | solution.py:193
  223.1 45.5 %collective-permute-start.59 = (bf16[2,2,2,2,96,512]{5,4,3,2,1,0:T(8,128)(2,1)}, bf16[2,2,2,2,96,512]{5,4,3,2,1,0:T(8,128)(2,1)}, u32[]{:S(2)}, u32[]{:S(2)}) collective-permute-start(bf16[2,2,2,2,96,512]{5,4,3,2,1,0:T(8,128)(2,1)} %pad_maximum_fusion.9), channel_id=1, source_target_pairs={{0,8},{1,9},{2,10},{3,11},{4,12},{5,13},{6,14},{7,15},{8,0},{9,1},... | collective-permute-start | bytes 4718600 | tf_op jit(solution)/shard_map/ppermute | solution.py:100
  266.2 57.6 %collective-permute-start.95 = (bf16[2,2,2,2,96,384]{5,4,1,3,0,2:T(8,128)(2,1)}, bf16[2,2,2,2,96,384]{5,4,1,3,0,2:T(8,128)(2,1)}, u32[]{:S(2)}, u32[]{:S(2)}) collective-permute-start(bf16[2,2,2,2,96,384]{5,4,1,3,0,2:T(8,128)(2,1)} %fusion.25), channel_id=1, source_target_pairs={{0,8},{1,9},{2,10},{3,11},{4,12},{5,13},{6,14},{7,15},{8,0},{9,1},... | collective-permute-start | bytes 3538952 | tf_op jit(solution)/shard_map/ppermute | solution.py:139
  267.1 52.3 %collective-permute-start.115 = (bf16[2,2,2,2,96,256]{5,4,1,0,2,3:T(8,128)(2,1)}, bf16[2,2,2,2,96,256]{5,4,1,0,2,3:T(8,128)(2,1)}, u32[]{:S(2)}, u32[]{:S(2)}) collective-permute-start(bf16[2,2,2,2,96,256]{5,4,1,0,2,3:T(8,128)(2,1)} %fusion.30), channel_id=1, source_target_pairs={{0,8},{1,9},{2,10},{3,11},{4,12},{5,13},{6,14},{7,15},{8,0},{9,1},... | collective-permute-start | bytes 2359304 | tf_op jit(solution)/shard_map/ppermute | solution.py:139
  316.0 43.1 %collective-permute-start.114 = (bf16[2,2,2,2,24,896]{5,4,1,0,2,3:T(8,128)(2,1)}, bf16[2,2,2,2,24,896]{5,4,1,0,2,3:T(8,128)(2,1)}, u32[]{:S(2)}, u32[]{:S(2)}) collective-permute-start(bf16[2,2,2,2,24,896]{5,4,1,0,2,3:T(8,128)(2,1)} %fusion.34), channel_id=1, source_target_pairs={{0,8},{1,9},{2,10},{3,11},{4,12},{5,13},{6,14},{7,15},{8,0},{9,1},... | collective-permute-start | bytes 2064392 | tf_op jit(solution)/shard_map/ppermute | solution.py:139
  319.5 112.1 %collective-permute-start.104 = (bf16[2,2,2,2,24,2048]{5,4,1,2,3,0:T(8,128)(2,1)}, bf16[2,2,2,2,24,2048]{5,4,1,2,3,0:T(8,128)(2,1)}, u32[]{:S(2)}, u32[]{:S(2)}) collective-permute-start(bf16[2,2,2,2,24,2048]{5,4,1,2,3,0:T(8,128)(2,1)} %fusion.12), channel_id=1, source_target_pairs={{0,8},{1,9},{2,10},{3,11},{4,12},{5,13},{6,14},{7,15},{8,0},{9,1},... | collective-permute-start | bytes 4718600 | tf_op jit(solution)/shard_map/ppermute | solution.py:139
  328.5 64.8 %collective-permute-start.91 = (bf16[2,2,2,24,768]{4,3,2,1,0:T(8,128)(2,1)}, bf16[2,2,2,24,768]{4,3,2,1,0:T(8,128)(2,1)}, u32[]{:S(2)}, u32[]{:S(2)}) collective-permute-start(bf16[2,2,2,24,768]{4,3,2,1,0:T(8,128)(2,1)} %fusion.46), channel_id=1, source_target_pairs={{0,2},{1,3},{2,0},{3,1},{4,6},{5,7},{6,4},{7,5},{8,10},{9,11},{10,... | collective-permute-start | bytes 884744 | tf_op jit(solution)/shard_map/ppermute | solution.py:139
  352.0 104.7 %all-to-all-start.3 = ((bf16[8,3,128,3,64]{2,4,3,1,0:T(8,128)(2,1)}), bf16[8,3,128,3,64]{2,4,3,1,0:T(8,128)(2,1)}, u32[]{:S(2)}, u32[]{:S(2)}) async-start(bf16[8,3,128,3,64]{2,4,3,1,0:T(8,128)(2,1)} %maximum_bitcast_fusion), calls=%async_computation.3 | async-start | bytes 2359296 | tf_op jit(solution)/shard_map/all_to_all | solution.py:193
  356.9 71.6 %collective-permute-start.97 = (bf16[2,2,2,96,384]{4,3,1,2,0:T(8,128)(2,1)S(1)}, bf16[2,2,2,96,384]{4,3,1,2,0:T(8,128)(2,1)S(1)}, u32[]{:S(2)}, u32[]{:S(2)}) collective-permute-start(bf16[2,2,2,96,384]{4,3,1,2,0:T(8,128)(2,1)S(1)} %fusion.36), channel_id=1, source_target_pairs={{0,2},{1,3},{2,0},{3,1},{4,6},{5,7},{6,4},{7,5},{8,10},{9,11},{10,... | collective-permute-start | bytes 1769480 | tf_op jit(solution)/shard_map/ppermute | solution.py:139
  359.0 32.9 %collective-permute-start.98 = (bf16[2,2,2,24,128]{4,3,2,1,0:T(8,128)(2,1)S(1)}, bf16[2,2,2,24,128]{4,3,2,1,0:T(8,128)(2,1)S(1)}, u32[]{:S(2)}, u32[]{:S(2)}) collective-permute-start(bf16[2,2,2,24,128]{4,3,2,1,0:T(8,128)(2,1)S(1)} %fusion.77), channel_id=1, source_target_pairs={{0,2},{1,3},{2,0},{3,1},{4,6},{5,7},{6,4},{7,5},{8,10},{9,11},{10,... | collective-permute-start | bytes 147464 | tf_op jit(solution)/shard_map/ppermute | solution.py:139
  360.8 52.1 %collective-permute-start.117 = (bf16[2,2,2,24,896]{4,3,1,0,2:T(8,128)(2,1)S(1)}, bf16[2,2,2,24,896]{4,3,1,0,2:T(8,128)(2,1)S(1)}, u32[]{:S(2)}, u32[]{:S(2)}) collective-permute-start(bf16[2,2,2,24,896]{4,3,1,0,2:T(8,128)(2,1)S(1)} %fusion.45), channel_id=1, source_target_pairs={{0,1},{1,0},{2,3},{3,2},{4,5},{5,4},{6,7},{7,6},{8,9},{9,8},{10,11... | collective-permute-start | bytes 1032200 | tf_op jit(solution)/shard_map/ppermute | solution.py:139
  454.2 34.9 %collective-permute-start.108 = (bf16[2,2,24,2048]{3,2,0,1:T(8,128)(2,1)}, bf16[2,2,24,2048]{3,2,0,1:T(8,128)(2,1)}, u32[]{:S(2)}, u32[]{:S(2)}) collective-permute-start(bf16[2,2,24,2048]{3,2,0,1:T(8,128)(2,1)} %fusion.39), channel_id=1, source_target_pairs={{0,1},{1,0},{2,3},{3,2},{4,5},{5,4},{6,7},{7,6},{8,9},{9,8},{10,11... | collective-permute-start | bytes 1179656 | tf_op jit(solution)/shard_map/ppermute | solution.py:139
  483.4 105.3 %collective-permute-start.65 = (bf16[2,2,2,2,24,1024]{5,4,1,2,3,0:T(8,128)(2,1)}, bf16[2,2,2,2,24,1024]{5,4,1,2,3,0:T(8,128)(2,1)}, u32[]{:S(2)}, u32[]{:S(2)}) collective-permute-start(bf16[2,2,2,2,24,1024]{5,4,1,2,3,0:T(8,128)(2,1)} %fusion.29), channel_id=1, source_target_pairs={{0,8},{1,9},{2,10},{3,11},{4,12},{5,13},{6,14},{7,15},{8,0},{9,1},... | collective-permute-start | bytes 2359304 | tf_op jit(solution)/shard_map/ppermute | solution.py:139
  487.2 99.2 %collective-permute-start.75 = (bf16[2,2,2,2,24,896]{5,4,1,0,2,3:T(8,128)(2,1)}, bf16[2,2,2,2,24,896]{5,4,1,0,2,3:T(8,128)(2,1)}, u32[]{:S(2)}, u32[]{:S(2)}) collective-permute-start(bf16[2,2,2,2,24,896]{5,4,1,0,2,3:T(8,128)(2,1)} %fusion.33), channel_id=1, source_target_pairs={{0,8},{1,9},{2,10},{3,11},{4,12},{5,13},{6,14},{7,15},{8,0},{9,1},... | collective-permute-start | bytes 2064392 | tf_op jit(solution)/shard_map/ppermute | solution.py:139
  507.8 62.8 %collective-permute-start.110 = (bf16[2,24,2048]{2,1,0:T(8,128)(2,1)}, bf16[2,24,2048]{2,1,0:T(8,128)(2,1)}, u32[]{:S(2)}, u32[]{:S(2)}) collective-permute-start(bf16[2,24,2048]{2,1,0:T(8,128)(2,1)} %fusion.49), channel_id=1, source_target_pairs={{0,2},{1,3},{2,0},{3,1},{4,6},{5,7},{6,4},{7,5},{8,10},{9,11},{10,... | collective-permute-start | bytes 589832 | tf_op jit(solution)/shard_map/ppermute | solution.py:139
  546.9 32.0 %collective-permute-start.129 = (bf16[96,384]{1,0:T(8,128)(2,1)}, bf16[96,384]{1,0:T(8,128)(2,1)S(1)}, u32[]{:S(2)}, u32[]{:S(2)}) collective-permute-start(bf16[96,384]{1,0:T(8,128)(2,1)} %fusion.71), channel_id=1, source_target_pairs={{0,4},{1,5},{2,6},{3,7},{4,0},{5,1},{6,2},{7,3},{8,12},{9,13},{10,... | collective-permute-start | bytes 221192 | tf_op jit(solution)/shard_map/ppermute | solution.py:139
  567.9 46.0 %collective-permute-start.74 = (bf16[24,128]{1,0:T(8,128)(2,1)S(1)}, bf16[24,128]{1,0:T(8,128)(2,1)S(1)}, u32[]{:S(2)}, u32[]{:S(2)}) collective-permute-start(bf16[24,128]{1,0:T(8,128)(2,1)S(1)} %fusion.138), channel_id=1, source_target_pairs={{0,4},{1,5},{2,6},{3,7},{4,0},{5,1},{6,2},{7,3},{8,12},{9,13},{10,... | collective-permute-start | bytes 18440 | tf_op jit(solution)/shard_map/ppermute | solution.py:139
  577.1 39.2 %collective-permute-start.84 = (bf16[24,128]{1,0:T(8,128)(2,1)S(1)}, bf16[24,128]{1,0:T(8,128)(2,1)S(1)}, u32[]{:S(2)}, u32[]{:S(2)}) collective-permute-start(bf16[24,128]{1,0:T(8,128)(2,1)S(1)} %fusion.137), channel_id=1, source_target_pairs={{0,4},{1,5},{2,6},{3,7},{4,0},{5,1},{6,2},{7,3},{8,12},{9,13},{10,... | collective-permute-start | bytes 18440 | tf_op jit(solution)/shard_map/ppermute | solution.py:139
  (198 other events, 2210.1 us)
where the time goes:
time: 627 us; the launch traced here: 617 us
  waiting for transfers between devices  209 us (33%)
  starting transfers between devices  154 us (25%)
  local copies, waits for them, and re-layouts  110 us (18%)
  other arithmetic  83.7 us (13%)
  matrix products  56.7 us (9%)
    ppermute x70, waiting for transfers between devices, reduce_params(): got = lax.ppermute(send, ALL, partner_pairs(count, b))  130 us
    ppermute x60, waiting for transfers between devices, gather_params(): got = lax.ppermute(xs, ALL, partner_pairs(count, b))  79.2 us
    ppermute x70, starting transfers between devices, reduce_params(): got = lax.ppermute(send, ALL, partner_pairs(count, b))  72 us
    ppermute x60, starting transfers between devices, gather_params(): got = lax.ppermute(xs, ALL, partner_pairs(count, b))  64.5 us
    add x65, other arithmetic, reduce_params(): xs = [k + g.astype(jnp.float32) for k, g in zip(keep, got)]  25.9 us
    another operation x60, other arithmetic, gather_params(): xs = [jnp.stack([x, g]) for x, g in zip(xs, got)]  23.9 us
    convert_element_type x70, local copies, waits for them, and re-layouts, reduce_params(): lax.dynamic_index_in_dim(x, 1 - mine, axis, keepdims=False)  23.3 us
    gather x12, local copies, waits for them, and re-layouts, gather_params(): x = jnp.take(x.reshape(count, rows, c1 - c0), rel, axis=0)  18.5 us
  transfers between devices with their start and end apart: 134, of which 57 were waited for; matrix products, arithmetic and copies ran while one was open for 36% of the time, Pallas kernels for 0%

commit v1 on v0

--- a/solution.py
+++ b/solution.py
@@ -54,27 +54,6 @@
     return [tuple(head + others[i:] + others[:i]) for i in range(3)]
 
 
-def split_routes(arrays, routes, grain=128):
-    sizes = [a.shape[0] * a.shape[1] for a in arrays]
-    target = sum(sizes) / routes
-    segs = [[] for _ in range(routes)]
-    load = 0.0
-    for i, a in enumerate(arrays):
-        rows, width = a.shape
-        c = 0
-        while c < width:
-            route = min(int(load // target), routes - 1)
-            if route == routes - 1:
-                take = width - c
-            else:
-                room = (route + 1) * target - load
-                take = min(width - c, max(grain, int(room // rows) // grain * grain))
-            segs[route].append((i, c, c + take))
-            c += take
-            load += take * rows
-    return segs
-
-
 def partner_pairs(count, bit):
     return [(i, i ^ (1 << bit)) for i in range(count)]
 
@@ -86,66 +65,58 @@
     return values
 
 
-def gather_params(arrays, orders, count, me, anchors=None):
+def gather_routes(routes, orders, count, me, anchors=None):
     nbits = count.bit_length() - 1
-    segs = split_routes(arrays, len(orders))
-    pieces = {}
-    for route, order in zip(segs, orders):
-        if not route:
-            continue
-        xs = [arrays[i][:, c0:c1] for i, c0, c1 in route]
+    idx = jnp.arange(count, dtype=jnp.int32)
+    out = []
+    for x, order in zip(routes, orders):
+        rows, cols = x.shape
         for step, b in enumerate(reversed(order)):
             if anchors is not None:
-                xs = tie(xs, anchors[step])
-            got = lax.ppermute(xs, ALL, partner_pairs(count, b))
-            xs = [jnp.stack([x, g]) for x, g in zip(xs, got)]
-        idx = jnp.arange(count, dtype=jnp.int32)
+                x = tie(x, anchors[step])
+            got = lax.ppermute(x, ALL, partner_pairs(count, b))
+            x = jnp.stack([x, got])
         rel = jnp.zeros((count,), jnp.int32)
         for j, b in enumerate(order):
             rel = rel + ((((idx >> b) & 1) ^ ((me >> b) & 1)) << (nbits - 1 - j))
-        for (i, c0, c1), x in zip(route, xs):
-            rows = arrays[i].shape[0]
-            x = jnp.take(x.reshape(count, rows, c1 - c0), rel, axis=0)
-            pieces[(i, c0)] = x.reshape(count * rows, c1 - c0)
+        x = jnp.take(x.reshape(count, rows, cols), rel, axis=0)
+        out.append(x.reshape(count * rows, cols))
+    return out
+
+
+def reduce_routes(routes, orders, count, me, anchors=None):
+    nbits = count.bit_length() - 1
     out = []
-    for i in range(len(arrays)):
-        parts = [pieces[k] for k in sorted(k for k in pieces if k[0] == i)]
-        out.append(parts[0] if len(parts) == 1 else jnp.concatenate(parts, axis=1))
-    return out
-
-
-def reduce_params(arrays, orders, count, me, anchors=None):
-    nbits = count.bit_length() - 1
-    segs = split_routes(arrays, len(orders))
-    pieces = {}
-    for route, order in zip(segs, orders):
-        if not route:
-            continue
-        xs = []
-        for i, c0, c1 in route:
-            rows = arrays[i].shape[0] // count
-            xs.append(arrays[i][:, c0:c1].reshape([2] * nbits + [rows, c1 - c0]))
+    for x, order in zip(routes, orders):
+        rows = x.shape[0] // count
+        cols = x.shape[1]
+        x = x.reshape([2] * nbits + [rows, cols])
         remaining = list(range(nbits - 1, -1, -1))
         for step, b in enumerate(order):
             if anchors is not None:
-                xs = tie(xs, anchors[step])
+                x = tie(x, anchors[step])
             axis = remaining.index(b)
             mine = (me >> b) & 1
-            keep = [lax.dynamic_index_in_dim(x, mine, axis, keepdims=False) for x in xs]
-            send = [
-                lax.dynamic_index_in_dim(x, 1 - mine, axis, keepdims=False).astype(jnp.bfloat16)
-                for x in xs
-            ]
+            keep = lax.dynamic_index_in_dim(x, mine, axis, keepdims=False)
+            send = lax.dynamic_index_in_dim(x, 1 - mine, axis, keepdims=False).astype(jnp.bfloat16)
             got = lax.ppermute(send, ALL, partner_pairs(count, b))
-            xs = [k + g.astype(jnp.float32) for k, g in zip(keep, got)]
+            x = keep + got.astype(jnp.float32)
             remaining.pop(axis)
-        for (i, c0, c1), x in zip(route, xs):
-            pieces[(i, c0)] = x.reshape(arrays[i].shape[0] // count, c1 - c0)
-    out = []
-    for i in range(len(arrays)):
-        parts = [pieces[k] for k in sorted(k for k in pieces if k[0] == i)]
-        out.append(parts[0] if len(parts) == 1 else jnp.concatenate(parts, axis=1))
+        out.append(x.reshape(rows, cols))
     return out
+
+
+def split_cols(x, widths):
+    out, at = [], 0
+    for w in widths:
+        out.append(x[:, at : at + w])
+        at += w
+    return out
+
+
+def thirds(width, grain=128):
+    first = -(-width // (3 * grain)) * grain
+    return [first, first, width - 2 * first]
 
 
 def vector_block(vectors, rows, dtype):
@@ -300,7 +271,16 @@
     vecs_local = vector_block(
         [ln1_g, ln1_b, b_q, b_v, b_out, ln2_g, ln2_b, b_down, b_up], shard_rows, jnp.bfloat16
     )
-    proj_qkv, vecs_all = gather_params([w_qkv, vecs_local], orders, count, me)
+    qkv_cols = thirds(w_qkv.shape[1])
+    qkv_parts = split_cols(w_qkv, qkv_cols)
+    gathered = gather_routes(
+        [qkv_parts[0], qkv_parts[1], jnp.concatenate([qkv_parts[2], vecs_local], axis=1)],
+        orders,
+        count,
+        me,
+    )
+    last_qkv, vecs_all = split_cols(gathered[2], [qkv_cols[2], vecs_local.shape[1]])
+    proj_qkv = jnp.concatenate([gathered[0], gathered[1], last_qkv], axis=1)
     (
         gain_one,
         shift_one,
@@ -340,8 +320,8 @@
         attended_b = attended.astype(jnp.bfloat16)
         forward_anchors = [projected] + [attended] * (steps - 1)
 
-    proj_out, proj_up, proj_down = gather_params(
-        [w_out, w_up, w_down], orders, count, me, forward_anchors[:steps]
+    proj_up, proj_down, proj_out = gather_routes(
+        [w_up, w_down, w_out], orders, count, me, forward_anchors[:steps]
     )
 
     branch = jnp.dot(attended_b, proj_out, preferred_element_type=jnp.float32) + bias_out.astype(
@@ -391,7 +371,7 @@
         backward_anchors = [None] + [proj_grad] * (steps - 1)
 
     full_rows = count * shard_rows
-    red_up, red_down, red_vec_one = reduce_params(
+    red_up, red_down, red_vec_one = reduce_routes(
         [
             grad_up,
             grad_down,
@@ -412,20 +392,17 @@
     input_ln_grad, grad_gain_one, grad_shift_one = norm_one_back(normed_grad)
     input_grads = (middle_grad + input_ln_grad).astype(jnp.bfloat16)
 
-    red_qkv, red_out, red_vec_two = reduce_params(
-        [
-            grad_qkv,
-            grad_out,
-            vector_block(
-                [grad_gain_one, grad_shift_one, grad_bias_query, grad_bias_value, grad_bias_out],
-                full_rows,
-                jnp.float32,
-            ),
-        ],
-        orders,
-        count,
-        me,
-    )
+    vec_two = vector_block(
+        [grad_gain_one, grad_shift_one, grad_bias_query, grad_bias_value, grad_bias_out],
+        full_rows,
+        jnp.float32,
+    )
+    gq = split_cols(grad_qkv, qkv_cols)
+    red = reduce_routes(
+        [gq[0], gq[1], jnp.concatenate([gq[2], grad_out, vec_two], axis=1)], orders, count, me
+    )
+    red_last, red_out, red_vec_two = split_cols(red[2], [qkv_cols[2], width, vec_two.shape[1]])
+    red_qkv = jnp.concatenate([red[0], red[1], red_last], axis=1)
     r_bias_up, r_bias_down, r_gain_two, r_shift_two = vector_unblock(red_vec_one, [ratio, 1, 1, 1])
     r_gain_one, r_shift_one, r_bias_query, r_bias_value, r_bias_out = vector_unblock(
         red_vec_two, [1] * 5

time: 627 us -> 480 us (0.77)
  starting transfers between devices: 154 us -> 92.6 us
  waiting for transfers between devices: 209 us -> 149 us
  local copies, waits for them, and re-layouts: 110 us -> 87.9 us
    ppermute x130 -> x60, waiting for transfers between devices: 209 us -> 144 us  [the longest x30 76.9 us: gather_routes(): got = lax.ppermute(x, ALL, partner_pairs(count, b))]
    ppermute x130 -> x60, starting transfers between devices: 136 us -> 73.1 us  [the longest x30 37.4 us: gather_routes(): got = lax.ppermute(x, ALL, partner_pairs(count, b))]
    slice x12 -> x3, local copies, waits for them, and re-layouts: 13.5 us -> 3.39 us  [split_cols(): out.append(x[:, at:at + w])]
    concatenate x1 -> x7, local copies, waits for them, and re-layouts: 0.16 us -> 9.87 us  [the longest x6 9.75 us: body(): jnp.concatenate([gq[2], grad_out, vec_two], axis=1)]
    concatenate x12 -> x5, local copies, waits for them, and re-layouts: 11.8 us -> 3.54 us  [vector_block(): return jnp.concatenate(cols, axis=1)]
    convert_element_type x0 -> x1, other arithmetic: none -> 7.48 us  [body(): activated = activated_f.astype(jnp.bfloat16)]
    convert_element_type x70 -> x31, local copies, waits for them, and re-layouts: 23.3 us -> 16 us  [the longest x30 14.2 us: reduce_routes(): lax.dynamic_index_in_dim(x, 1 - mine, axis, keepdims=False)]
    add x65 -> x30, other arithmetic: 25.9 us -> 18.7 us  [reduce_routes(): x = keep + got.astype(jnp.float32)]
  transfers between devices with their start and end apart: 134 -> 64, of which waited for: 57 -> 29; matrix products, arithmetic and copies ran while one was open for 36% -> 32% of each run, Pallas kernels for 0% -> 0%
where the time goes in v1:
time: 480 us; the launch traced here: 472 us
  waiting for transfers between devices  149 us (31%)
  starting transfers between devices  92.6 us (19%)
  local copies, waits for them, and re-layouts  87.9 us (18%)
  other arithmetic  82.2 us (17%)
  matrix products  57.4 us (12%)
    ppermute x30, waiting for transfers between devices, gather_routes(): got = lax.ppermute(x, ALL, partner_pairs(count, b))  76.9 us
    ppermute x30, waiting for transfers between devices, reduce_routes(): got = lax.ppermute(send, ALL, partner_pairs(count, b))  66.7 us
    ppermute x30, starting transfers between devices, gather_routes(): got = lax.ppermute(x, ALL, partner_pairs(count, b))  37.4 us
    ppermute x30, starting transfers between devices, reduce_routes(): got = lax.ppermute(send, ALL, partner_pairs(count, b))  35.7 us
    another operation x30, other arithmetic, gather_routes(): x = jnp.stack([x, got])  25.5 us
    add x30, other arithmetic, reduce_routes(): x = keep + got.astype(jnp.float32)  18.7 us
    gather x6, local copies, waits for them, and re-layouts, gather_routes(): x = jnp.take(x.reshape(count, rows, cols), rel, axis=0)  15 us
    select_n x10, other arithmetic, gather_routes(): x = jnp.take(x.reshape(count, rows, cols), rel, axis=0)  14.8 us
  transfers between devices with their start and end apart: 64, of which 29 were waited for; matrix products, arithmetic and copies ran while one was open for 32% of the time, Pallas kernels for 0%

profile of v1, /device:TPU:0, one launch (start us, length us, event | category | flops | bytes accessed | tf_op | source)
XLA Modules:
  0.0 471.9 jit_solution(16562315152634498633)
XLA Ops:
  8.3 4.1 collective-permute-start
  76.3 31.6 %collective-permute-done.25 = bf16[96,768]{1,0:T(8,128)(2,1)S(1)} collective-permute-done((bf16[96,768]{1,0:T(8,128)(2,1)S(1)}, bf16[96,768]{1,0:T(8,128)(2,1)S(1)}, u32[]{:S(2)}, u32[]{:S(2)}) %collective-permute-start.25) | collective-permute-done | bytes 147488 | tf_op jit(solution)/shard_map/ppermute | solution.py:77
  116.4 6.2 %fusion.117 = (f32[3,1024]{1,0:T(4,128)S(1)}, f32[3,1024,1024]{1,2,0:T(8,128)S(1)}) fusion(bf16[3,1024,3,64]{1,3,0,2:T(8,128)(2,1)S(1)} %reshape.721, pred[3,1024]{1,0:T(4,128)(4,1)S(1)} %broadcast_compare_fusion, s32[3,1024]{1,0:T(4,128)S(1)} %broadcast_add_fusion, pred[1024,1024]{0,1:T(8,128)(4,1)} %iota_compare_fusion), kind=kOutput, calls=%fused_computation.342 | convolution fusion | flops 421524480 | bytes 14467072 | tf_op jit(solution)/shard_map/uqd,ukd->uqk/dot_general | solution.py:172
  128.5 9.0 %collective-permute-done.27 = bf16[2,2,96,768]{3,2,1,0:T(8,128)(2,1)S(1)} collective-permute-done((bf16[2,2,96,768]{3,2,1,0:T(8,128)(2,1)S(1)}, bf16[2,2,96,768]{3,2,1,0:T(8,128)(2,1)S(1)}, u32[]{:S(2)}, u32[]{:S(2)}) %collective-permute-start.27) | collective-permute-done | bytes 589856 | tf_op jit(solution)/shard_map/ppermute | solution.py:77
  143.5 21.6 %collective-permute-done.16 = bf16[2,24,768]{2,1,0:T(8,128)(2,1)S(1)} collective-permute-done((bf16[2,24,768]{2,1,0:T(8,128)(2,1)S(1)}, bf16[2,24,768]{2,1,0:T(8,128)(2,1)S(1)}, u32[]{:S(2)}, u32[]{:S(2)}) %collective-permute-start.16) | collective-permute-done | bytes 73760 | tf_op jit(solution)/shard_map/ppermute | solution.py:77
  177.2 5.2 %all-to-all-start.1 = ((bf16[8,3,128,1,64]{2,4,3,1,0:T(8,128)(2,1)}), bf16[8,3,128,1,64]{2,4,3,1,0:T(8,128)(2,1)}, u32[]{:S(2)}, u32[]{:S(2)}) async-start(bf16[8,3,128,1,64]{2,4,3,1,0:T(8,128)(2,1)} %bitcast.506), calls=%async_computation.1 | async-start | bytes 786432 | tf_op jit(solution)/shard_map/all_to_all | solution.py:164
  189.2 5.3 %all-to-all-done.1 = bf16[8,3,128,1,64]{2,4,3,1,0:T(8,128)(2,1)} async-done(((bf16[8,3,128,1,64]{2,4,3,1,0:T(8,128)(2,1)}), bf16[8,3,128,1,64]{2,4,3,1,0:T(8,128)(2,1)}, u32[]{:S(2)}, u32[]{:S(2)}) %all-to-all-start.1) | async-done | bytes 393248 | tf_op jit(solution)/shard_map/all_to_all | solution.py:164
  201.1 4.9 %pad_maximum_fusion.1 = bf16[2,2,2,2,2,96,768]{6,5,4,3,2,1,0:T(8,128)(2,1)} fusion(bf16[1,2,2,2,2,96,768]{6,5,4,3,2,1,0:T(8,128)(2,1)} %bitcast.95, bf16[1,2,2,2,2,96,768]{6,5,4,3,2,1,0:T(8,128)(2,1)} %bitcast.94), kind=kLoop, calls=%fused_computation.12 | loop fusion | flops 2359296 | bytes 9437184 | tf_op jit(solution)/shard_map/stack | solution.py:78
  206.0 5.4 %gather_fusion.3 = bf16[32,96,768]{2,1,0:T(8,128)(2,1)} fusion(bf16[32,96,768]{2,1,0:T(8,128)(2,1)} %bitcast.464, s32[1024]{0:T(1024)S(1)} %pad_clamp_fusion), kind=kCustom, calls=%fused_computation.6 | custom fusion | bytes 9437312 | tf_op jit(solution)/shard_map/jit(_take)/gather | solution.py:82
  211.5 5.0 %broadcast_select_fusion = bf16[32,96,768]{2,1,0:T(8,128)(2,1)} fusion(bf16[32,96,768]{2,1,0:T(8,128)(2,1)} %gather_fusion.3, pred[32]{0:T(512)(128)(4,1)S(1)} %copy-done.48), kind=kLoop, calls=%fused_computation.19 | loop fusion | flops 2359296 | bytes 9437216 | tf_op jit(solution)/shard_map/jit(_take)/select_n | solution.py:82
  216.4 5.0 %pad_maximum_fusion = bf16[2,2,2,2,2,24,3072]{6,5,4,3,2,1,0:T(8,128)(2,1)} fusion(bf16[1,2,2,2,2,24,3072]{6,5,4,3,2,1,0:T(8,128)(2,1)} %bitcast.82, bf16[1,2,2,2,2,24,3072]{6,5,4,3,2,1,0:T(8,128)(2,1)} %bitcast.81), kind=kLoop, calls=%fused_computation.11 | loop fusion | flops 2359296 | bytes 9437184 | tf_op jit(solution)/shard_map/stack | solution.py:78
  221.4 5.4 %gather_fusion.2 = bf16[32,24,3072]{2,1,0:T(8,128)(2,1)} fusion(bf16[32,24,3072]{2,1,0:T(8,128)(2,1)} %bitcast.465, s32[1024]{0:T(1024)S(1)} %pad_clamp_fusion.1), kind=kCustom, calls=%fused_computation.5 | custom fusion | bytes 9437312 | tf_op jit(solution)/shard_map/jit(_take)/gather | solution.py:82
  229.7 8.0 %fusion = (f32[256,3072]{1,0:T(8,128)S(1)}, f32[256,3072]{1,0:T(8,128)S(1)}) fusion(f32[3072]{0:T(1024)S(1)} %reshape.754, bf16[768,3072]{1,0:T(8,128)(2,1)S(1)} %bitcast_select_fusion.1, f32[256,768]{1,0:T(8,128)S(1)} %get-tuple-element.240, f32[768]{0:T(1024)S(1)} %get-tuple-element.163, f32[768]{0:T(1024)S(1)} %get-tuple-element.164, ...), kind=kOutput, calls=%fused_computation.24 | convolution fusion | flops 1258487808 | bytes 11816960 | tf_op jit(solution)/shard_map/dot_general | solution.py:335
  241.6 5.2 %fusion.110 = f32[768,3072]{1,0:T(8,128)} fusion(bf16[256,3072]{1,0:T(8,128)(2,1)S(1)} %get-tuple-element.246, f32[256,768]{1,0:T(8,128)S(1)} %get-tuple-element.240, f32[768]{0:T(1024)S(1)} %get-tuple-element.163, f32[768]{0:T(1024)S(1)} %get-tuple-element.164, f32[256]{0:T(256)S(1)} %fusion.84, f32[256]{0:T(256)S(1)} %broadcast_multiply_fusion), kind=kOutput, calls=%fused_computation.336 | convolution fusion | flops 1208942592 | bytes 11804672 | tf_op jit(solution)/shard_map/dot_general | solution.py:36
  246.8 7.5 %fusion.3 = bf16[3072,256]{0,1:T(8,128)(2,1)} fusion(f32[256,3072]{1,0:T(8,128)S(1)} %get-tuple-element.242), kind=kLoop, calls=%fused_computation.27 | loop fusion | flops 51118080 | bytes 4718592 | tf_op jit(solution)/shard_map/convert_element_type | solution.py:339
  263.6 4.3 all-to-all-start.2
  289.7 6.4 %multiply_convert_fusion = bf16[3,1024,1024]{1,2,0:T(8,128)(2,1)S(1)} fusion(f32[3,1024,1024]{1,2,0:T(8,128)} %copy-done.2, f32[3,1024]{1,0:T(4,128)S(1)} %div.84, bf16[3,1024,3,64]{1,3,0,2:T(8,128)(2,1)S(1)} %copy-done.13, bf16[3,1024,64]{1,2,0:T(8,128)(2,1)S(1)} %squeeze_reshape.3, f32[3,1024]{1,0:T(4,128)S(1)} %get-tuple-element.235), kind=kOutput, calls=%fused_computation.7 | convolution fusion | flops 412680192 | bytes 19693568 | tf_op jit(solution)/shard_map/uqd,ukd->uqk/dot_general | solution.py:186
  296.1 6.6 %fusion.42 = bf16[3,1024,64]{1,2,0:T(8,128)(2,1)S(1)} fusion(f32[3,1024,1024]{1,2,0:T(8,128)} %copy-done.2, bf16[3,1024,64]{1,2,0:T(8,128)(2,1)S(1)} %squeeze_reshape.3, f32[3,1024]{1,0:T(4,128)S(1)} %get-tuple-element.235), kind=kOutput, calls=%fused_computation.94 | convolution fusion | flops 406585344 | bytes 13381632 | tf_op jit(solution)/shard_map/uqk,uqd->ukd/dot_general | solution.py:190
  307.7 6.2 %all-to-all-start.3 = ((bf16[8,3,128,3,64]{2,4,3,1,0:T(8,128)(2,1)}), bf16[8,3,128,3,64]{2,4,3,1,0:T(8,128)(2,1)S(1)}, u32[]{:S(2)}, u32[]{:S(2)}) async-start(bf16[8,3,128,3,64]{2,4,3,1,0:T(8,128)(2,1)} %maximum_bitcast_fusion), calls=%async_computation.3 | async-start | bytes 2359296 | tf_op jit(solution)/shard_map/all_to_all | solution.py:164
  316.1 18.9 %collective-permute-done.46 = bf16[2,2,2,24,128]{4,3,2,1,0:T(8,128)(2,1)S(1)} collective-permute-done((bf16[2,2,2,24,128]{4,3,2,1,0:T(8,128)(2,1)S(1)}, bf16[2,2,2,24,128]{4,3,2,1,0:T(8,128)(2,1)S(1)}, u32[]{:S(2)}, u32[]{:S(2)}) %collective-permute-start.46) | collective-permute-done | bytes 49184 | tf_op jit(solution)/shard_map/ppermute | solution.py:102
  367.1 6.1 %concatenate.51 = f32[2,2,2,2,2,24,1664]{6,5,4,3,2,1,0:T(8,128)} concatenate(f32[2,2,2,2,2,24,768]{6,5,4,3,2,1,0:T(8,128)S(1)} %bitcast.477, f32[2,2,2,2,2,24,768]{6,5,4,3,2,1,0:T(8,128)} %fusion.58, f32[2,2,2,2,2,24,1]{6,5,4,3,2,1,0:T(8,128)} %concatenate.58, f32[2,2,2,2,2,24,1]{6,5,4,3,2,1,0:T(8,128)} %concatenate.59, f32[2,2,2,2,2,24,1]{6,5,4,3,2,1,0:T(8,128)S(1)} %concatenate.60, ...), dimensions={6} | concatenate | bytes 10223616 | tf_op jit(solution)/shard_map/concatenate | solution.py:402
  380.8 4.4 collective-permute-start.49
  402.7 14.1 %collective-permute-done.42 = bf16[2,2,24,768]{3,2,1,0:T(8,128)(2,1)S(1)} collective-permute-done((bf16[2,2,24,768]{3,2,1,0:T(8,128)(2,1)S(1)}, bf16[2,2,24,768]{3,2,1,0:T(8,128)(2,1)S(1)}, u32[]{:S(2)}, u32[]{:S(2)}) %collective-permute-start.42) | collective-permute-done | bytes 147488 | tf_op jit(solution)/shard_map/ppermute | solution.py:102
  434.7 16.1 %collective-permute-done.53 = bf16[2,24,3072]{2,1,0:T(8,128)(2,1)S(1)} collective-permute-done((bf16[2,24,3072]{2,1,0:T(8,128)(2,1)S(1)}, bf16[2,24,3072]{2,1,0:T(8,128)(2,1)S(1)}, u32[]{:S(2)}, u32[]{:S(2)}) %collective-permute-start.53) | collective-permute-done | bytes 294944 | tf_op jit(solution)/shard_map/ppermute | solution.py:102
  (475 shorter events, 256.5 us)
Async XLA Ops:
  64.1 47.1 %all-to-all-start = ((bf16[8,3,128,3,64]{2,4,3,1,0:T(8,128)(2,1)}), bf16[8,3,128,3,64]{2,4,3,1,0:T(8,128)(2,1)S(1)}, u32[]{:S(2)}, u32[]{:S(2)}) async-start(bf16[8,3,128,3,64]{2,4,3,1,0:T(8,128)(2,1)} %bitcast.495), calls=%async_computation | async-start | bytes 2359296 | tf_op jit(solution)/shard_map/all_to_all | solution.py:154
  69.1 38.9 %collective-permute-start.25 = (bf16[96,768]{1,0:T(8,128)(2,1)S(1)}, bf16[96,768]{1,0:T(8,128)(2,1)S(1)}, u32[]{:S(2)}, u32[]{:S(2)}) collective-permute-start(bf16[96,768]{1,0:T(8,128)(2,1)S(1)} %copy-done.36), channel_id=1, source_target_pairs={{0,4},{1,5},{2,6},{3,7},{4,0},{5,1},{6,2},{7,3},{8,12},{9,13},{10,... | collective-permute-start | bytes 442376 | tf_op jit(solution)/shard_map/ppermute | solution.py:77
  73.3 37.8 %collective-permute-start.20 = (bf16[24,3072]{1,0:T(8,128)(2,1)S(1)}, bf16[24,3072]{1,0:T(8,128)(2,1)S(1)}, u32[]{:S(2)}, u32[]{:S(2)}) collective-permute-start(bf16[24,3072]{1,0:T(8,128)(2,1)S(1)} %copy-done.37), channel_id=1, source_target_pairs={{0,4},{1,5},{2,6},{3,7},{4,0},{5,1},{6,2},{7,3},{8,12},{9,13},{10,... | collective-permute-start | bytes 442376 | tf_op jit(solution)/shard_map/ppermute | solution.py:77
  73.4 67.9 %collective-permute-start.15 = (bf16[24,768]{1,0:T(8,128)(2,1)S(1)}, bf16[24,768]{1,0:T(8,128)(2,1)}, u32[]{:S(2)}, u32[]{:S(2)}) collective-permute-start(bf16[24,768]{1,0:T(8,128)(2,1)S(1)} %copy-done.38), channel_id=1, source_target_pairs={{0,4},{1,5},{2,6},{3,7},{4,0},{5,1},{6,2},{7,3},{8,12},{9,13},{10,... | collective-permute-start | bytes 110600 | tf_op jit(solution)/shard_map/ppermute | solution.py:77
  137.6 34.6 %collective-permute-start.28 = (bf16[2,2,2,96,768]{4,3,2,1,0:T(8,128)(2,1)S(1)}, bf16[2,2,2,96,768]{4,3,2,1,0:T(8,128)(2,1)S(1)}, u32[]{:S(2)}, u32[]{:S(2)}) collective-permute-start(bf16[2,2,2,96,768]{4,3,2,1,0:T(8,128)(2,1)S(1)} %pad_maximum_fusion.13), channel_id=1, source_target_pairs={{0,1},{1,0},{2,3},{3,2},{4,5},{5,4},{6,7},{7,6},{8,9},{9,8},{10,11... | collective-permute-start | bytes 3538952 | tf_op jit(solution)/shard_map/ppermute | solution.py:77
  139.3 45.2 %collective-permute-start.23 = (bf16[2,2,2,24,3072]{4,3,2,1,0:T(8,128)(2,1)S(1)}, bf16[2,2,2,24,3072]{4,3,2,1,0:T(8,128)(2,1)}, u32[]{:S(2)}, u32[]{:S(2)}) collective-permute-start(bf16[2,2,2,24,3072]{4,3,2,1,0:T(8,128)(2,1)S(1)} %pad_maximum_fusion.12), channel_id=1, source_target_pairs={{0,16},{1,17},{2,18},{3,19},{4,20},{5,21},{6,22},{7,23},{8,24},{9,... | collective-permute-start | bytes 3538952 | tf_op jit(solution)/shard_map/ppermute | solution.py:77
  142.1 23.0 %collective-permute-start.16 = (bf16[2,24,768]{2,1,0:T(8,128)(2,1)S(1)}, bf16[2,24,768]{2,1,0:T(8,128)(2,1)S(1)}, u32[]{:S(2)}, u32[]{:S(2)}) collective-permute-start(bf16[2,24,768]{2,1,0:T(8,128)(2,1)S(1)} %pad_maximum_fusion.35), channel_id=1, source_target_pairs={{0,1},{1,0},{2,3},{3,2},{4,5},{5,4},{6,7},{7,6},{8,9},{9,8},{10,11... | collective-permute-start | bytes 221192 | tf_op jit(solution)/shard_map/ppermute | solution.py:77
  173.8 27.3 %collective-permute-start.29 = (bf16[2,2,2,2,96,768]{5,4,3,2,1,0:T(8,128)(2,1)}, bf16[2,2,2,2,96,768]{5,4,3,2,1,0:T(8,128)(2,1)}, u32[]{:S(2)}, u32[]{:S(2)}) collective-permute-start(bf16[2,2,2,2,96,768]{5,4,3,2,1,0:T(8,128)(2,1)} %pad_maximum_fusion.4), channel_id=1, source_target_pairs={{0,8},{1,9},{2,10},{3,11},{4,12},{5,13},{6,14},{7,15},{8,0},{9,1},... | collective-permute-start | bytes 7077896 | tf_op jit(solution)/shard_map/ppermute | solution.py:77
  177.2 17.3 %all-to-all-start.1 = ((bf16[8,3,128,1,64]{2,4,3,1,0:T(8,128)(2,1)}), bf16[8,3,128,1,64]{2,4,3,1,0:T(8,128)(2,1)}, u32[]{:S(2)}, u32[]{:S(2)}) async-start(bf16[8,3,128,1,64]{2,4,3,1,0:T(8,128)(2,1)} %bitcast.506), calls=%async_computation.1 | async-start | bytes 786432 | tf_op jit(solution)/shard_map/all_to_all | solution.py:164
  187.5 28.9 %collective-permute-start.24 = (bf16[2,2,2,2,24,3072]{5,4,3,2,1,0:T(8,128)(2,1)}, bf16[2,2,2,2,24,3072]{5,4,3,2,1,0:T(8,128)(2,1)}, u32[]{:S(2)}, u32[]{:S(2)}) collective-permute-start(bf16[2,2,2,2,24,3072]{5,4,3,2,1,0:T(8,128)(2,1)} %pad_maximum_fusion.3), channel_id=1, source_target_pairs={{0,8},{1,9},{2,10},{3,11},{4,12},{5,13},{6,14},{7,15},{8,0},{9,1},... | collective-permute-start | bytes 7077896 | tf_op jit(solution)/shard_map/ppermute | solution.py:77
  263.6 23.2 %all-to-all-start.2 = ((bf16[8,3,128,1,64]{2,4,3,1,0:T(8,128)(2,1)}), bf16[8,3,128,1,64]{2,4,3,1,0:T(8,128)(2,1)}, u32[]{:S(2)}, u32[]{:S(2)}) async-start(bf16[8,3,128,1,64]{2,4,3,1,0:T(8,128)(2,1)} %bitcast.105), calls=%async_computation.2 | async-start | bytes 786432 | tf_op jit(solution)/shard_map/all_to_all | solution.py:154
  275.5 64.0 %collective-permute-start.50 = (bf16[2,2,2,2,24,3072]{5,4,1,2,3,0:T(8,128)(2,1)}, bf16[2,2,2,2,24,3072]{5,4,1,2,3,0:T(8,128)(2,1)}, u32[]{:S(2)}, u32[]{:S(2)}) collective-permute-start(bf16[2,2,2,2,24,3072]{5,4,1,2,3,0:T(8,128)(2,1)} %fusion.28), channel_id=1, source_target_pairs={{0,8},{1,9},{2,10},{3,11},{4,12},{5,13},{6,14},{7,15},{8,0},{9,1},... | collective-permute-start | bytes 7077896 | tf_op jit(solution)/shard_map/ppermute | solution.py:102
  282.1 63.7 %collective-permute-start.55 = (bf16[2,2,2,2,96,768]{5,4,3,2,1,0:T(8,128)(2,1)}, bf16[2,2,2,2,96,768]{5,4,3,2,1,0:T(8,128)(2,1)}, u32[]{:S(2)}, u32[]{:S(2)}) collective-permute-start(bf16[2,2,2,2,96,768]{5,4,3,2,1,0:T(8,128)(2,1)} %fusion.27), channel_id=1, source_target_pairs={{0,8},{1,9},{2,10},{3,11},{4,12},{5,13},{6,14},{7,15},{8,0},{9,1},... | collective-permute-start | bytes 7077896 | tf_op jit(solution)/shard_map/ppermute | solution.py:102
  307.7 45.3 %all-to-all-start.3 = ((bf16[8,3,128,3,64]{2,4,3,1,0:T(8,128)(2,1)}), bf16[8,3,128,3,64]{2,4,3,1,0:T(8,128)(2,1)S(1)}, u32[]{:S(2)}, u32[]{:S(2)}) async-start(bf16[8,3,128,3,64]{2,4,3,1,0:T(8,128)(2,1)} %maximum_bitcast_fusion), calls=%async_computation.3 | async-start | bytes 2359296 | tf_op jit(solution)/shard_map/all_to_all | solution.py:164
  314.0 21.0 %collective-permute-start.46 = (bf16[2,2,2,24,128]{4,3,2,1,0:T(8,128)(2,1)S(1)}, bf16[2,2,2,24,128]{4,3,2,1,0:T(8,128)(2,1)S(1)}, u32[]{:S(2)}, u32[]{:S(2)}) collective-permute-start(bf16[2,2,2,24,128]{4,3,2,1,0:T(8,128)(2,1)S(1)} %fusion.74), channel_id=1, source_target_pairs={{0,2},{1,3},{2,0},{3,1},{4,6},{5,7},{6,4},{7,5},{8,10},{9,11},{10,... | collective-permute-start | bytes 147464 | tf_op jit(solution)/shard_map/ppermute | solution.py:102
  344.6 48.2 %collective-permute-start.51 = (bf16[2,2,2,24,3072]{4,3,0,1,2:T(8,128)(2,1)}, bf16[2,2,2,24,3072]{4,3,0,1,2:T(8,128)(2,1)}, u32[]{:S(2)}, u32[]{:S(2)}) collective-permute-start(bf16[2,2,2,24,3072]{4,3,0,1,2:T(8,128)(2,1)} %fusion.46), channel_id=1, source_target_pairs={{0,16},{1,17},{2,18},{3,19},{4,20},{5,21},{6,22},{7,23},{8,24},{9,... | collective-permute-start | bytes 3538952 | tf_op jit(solution)/shard_map/ppermute | solution.py:102
  351.9 44.8 %collective-permute-start.56 = (bf16[2,2,2,96,768]{4,3,2,1,0:T(8,128)(2,1)}, bf16[2,2,2,96,768]{4,3,2,1,0:T(8,128)(2,1)}, u32[]{:S(2)}, u32[]{:S(2)}) collective-permute-start(bf16[2,2,2,96,768]{4,3,2,1,0:T(8,128)(2,1)} %fusion.47), channel_id=1, source_target_pairs={{0,1},{1,0},{2,3},{3,2},{4,5},{5,4},{6,7},{7,6},{8,9},{9,8},{10,11... | collective-permute-start | bytes 3538952 | tf_op jit(solution)/shard_map/ppermute | solution.py:102
  376.3 53.0 %collective-permute-start.30 = (bf16[2,2,2,2,24,1664]{5,4,3,2,1,0:T(8,128)(2,1)}, bf16[2,2,2,2,24,1664]{5,4,3,2,1,0:T(8,128)(2,1)}, u32[]{:S(2)}, u32[]{:S(2)}) collective-permute-start(bf16[2,2,2,2,24,1664]{5,4,3,2,1,0:T(8,128)(2,1)} %fusion.34), channel_id=1, source_target_pairs={{0,8},{1,9},{2,10},{3,11},{4,12},{5,13},{6,14},{7,15},{8,0},{9,1},... | collective-permute-start | bytes 3833864 | tf_op jit(solution)/shard_map/ppermute | solution.py:102
  395.2 36.1 %collective-permute-start.52 = (bf16[2,2,24,3072]{3,2,0,1:T(8,128)(2,1)S(1)}, bf16[2,2,24,3072]{3,2,0,1:T(8,128)(2,1)S(1)}, u32[]{:S(2)}, u32[]{:S(2)}) collective-permute-start(bf16[2,2,24,3072]{3,2,0,1:T(8,128)(2,1)S(1)} %fusion.53), channel_id=1, source_target_pairs={{0,1},{1,0},{2,3},{3,2},{4,5},{5,4},{6,7},{7,6},{8,9},{9,8},{10,11... | collective-permute-start | bytes 1769480 | tf_op jit(solution)/shard_map/ppermute | solution.py:102
  398.6 34.8 %collective-permute-start.57 = (bf16[2,2,96,768]{3,2,1,0:T(8,128)(2,1)S(1)}, bf16[2,2,96,768]{3,2,1,0:T(8,128)(2,1)S(1)}, u32[]{:S(2)}, u32[]{:S(2)}) collective-permute-start(bf16[2,2,96,768]{3,2,1,0:T(8,128)(2,1)S(1)} %fusion.54), channel_id=1, source_target_pairs={{0,2},{1,3},{2,0},{3,1},{4,6},{5,7},{6,4},{7,5},{8,10},{9,11},{10,... | collective-permute-start | bytes 1769480 | tf_op jit(solution)/shard_map/ppermute | solution.py:102
  400.0 16.7 %collective-permute-start.42 = (bf16[2,2,24,768]{3,2,1,0:T(8,128)(2,1)S(1)}, bf16[2,2,24,768]{3,2,1,0:T(8,128)(2,1)S(1)}, u32[]{:S(2)}, u32[]{:S(2)}) collective-permute-start(bf16[2,2,24,768]{3,2,1,0:T(8,128)(2,1)S(1)} %fusion.67), channel_id=1, source_target_pairs={{0,2},{1,3},{2,0},{3,1},{4,6},{5,7},{6,4},{7,5},{8,10},{9,11},{10,... | collective-permute-start | bytes 442376 | tf_op jit(solution)/shard_map/ppermute | solution.py:102
  431.0 20.1 %collective-permute-start.31 = (bf16[2,2,2,24,1664]{4,3,2,1,0:T(8,128)(2,1)S(1)}, bf16[2,2,2,24,1664]{4,3,2,1,0:T(8,128)(2,1)S(1)}, u32[]{:S(2)}, u32[]{:S(2)}) collective-permute-start(bf16[2,2,2,24,1664]{4,3,2,1,0:T(8,128)(2,1)S(1)} %fusion.52), channel_id=1, source_target_pairs={{0,2},{1,3},{2,0},{3,1},{4,6},{5,7},{6,4},{7,5},{8,10},{9,11},{10,... | collective-permute-start | bytes 1916936 | tf_op jit(solution)/shard_map/ppermute | solution.py:102
  431.4 19.3 %collective-permute-start.53 = (bf16[2,24,3072]{2,1,0:T(8,128)(2,1)S(1)}, bf16[2,24,3072]{2,1,0:T(8,128)(2,1)S(1)}, u32[]{:S(2)}, u32[]{:S(2)}) collective-permute-start(bf16[2,24,3072]{2,1,0:T(8,128)(2,1)S(1)} %fusion.63), channel_id=1, source_target_pairs={{0,2},{1,3},{2,0},{3,1},{4,6},{5,7},{6,4},{7,5},{8,10},{9,11},{10,... | collective-permute-start | bytes 884744 | tf_op jit(solution)/shard_map/ppermute | solution.py:102
  433.5 18.8 %collective-permute-start.58 = (bf16[2,96,768]{2,1,0:T(8,128)(2,1)S(1)}, bf16[2,96,768]{2,1,0:T(8,128)(2,1)S(1)}, u32[]{:S(2)}, u32[]{:S(2)}) collective-permute-start(bf16[2,96,768]{2,1,0:T(8,128)(2,1)S(1)} %fusion.64), channel_id=1, source_target_pairs={{0,16},{1,17},{2,18},{3,19},{4,20},{5,21},{6,22},{7,23},{8,24},{9,... | collective-permute-start | bytes 884744 | tf_op jit(solution)/shard_map/ppermute | solution.py:102
  (105 other events, 972.4 us)

commit v2 on v1

--- a/solution.py
+++ b/solution.py
@@ -280,7 +280,7 @@
         me,
     )
     last_qkv, vecs_all = split_cols(gathered[2], [qkv_cols[2], vecs_local.shape[1]])
-    proj_qkv = jnp.concatenate([gathered[0], gathered[1], last_qkv], axis=1)
+    qkv_weights = [gathered[0], gathered[1], last_qkv]
     (
         gain_one,
         shift_one,
@@ -298,10 +298,18 @@
         layer_norm, seq_in, gain_one.astype(jnp.float32), shift_one.astype(jnp.float32)
     )
     normed = normed_f.astype(jnp.bfloat16)
-    projected = jnp.dot(normed, proj_qkv, preferred_element_type=jnp.float32)
-    queries = (projected[:, :width] + bias_query.astype(jnp.float32)).astype(jnp.bfloat16)
-    keys_now = projected[:, width : 2 * width].astype(jnp.bfloat16)
-    values_now = (projected[:, 2 * width :] + bias_value.astype(jnp.float32)).astype(jnp.bfloat16)
+    if qkv_cols == [width] * 3:
+        proj_q, proj_k, proj_v = [
+            jnp.dot(normed, w, preferred_element_type=jnp.float32) for w in qkv_weights
+        ]
+    else:
+        projected = jnp.dot(
+            normed, jnp.concatenate(qkv_weights, axis=1), preferred_element_type=jnp.float32
+        )
+        proj_q, proj_k, proj_v = split_cols(projected, [width] * 3)
+    queries = (proj_q + bias_query.astype(jnp.float32)).astype(jnp.bfloat16)
+    keys_now = proj_k.astype(jnp.bfloat16)
+    values_now = (proj_v + bias_value.astype(jnp.float32)).astype(jnp.bfloat16)
 
     if head_parallel:
         qkv_rows = jnp.concatenate([queries, keys_now, values_now], axis=1)
@@ -314,11 +322,11 @@
         attended_b = units_to_rows(
             attended_u.astype(jnp.bfloat16)[:, :, None], seq_count, micro, 1
         )
-        forward_anchors = [projected, qkv_units, weights, attended_u, attended_u]
+        forward_anchors = [queries, qkv_units, weights, attended_u, attended_u]
     else:
         attended, saved = fallback_attention(queries, keys_now, values_now, bounds, row_count)
         attended_b = attended.astype(jnp.bfloat16)
-        forward_anchors = [projected] + [attended] * (steps - 1)
+        forward_anchors = [queries] + [attended] * (steps - 1)
 
     proj_up, proj_down, proj_out = gather_routes(
         [w_up, w_down, w_out], orders, count, me, forward_anchors[:steps]
@@ -371,24 +379,25 @@
         backward_anchors = [None] + [proj_grad] * (steps - 1)
 
     full_rows = count * shard_rows
-    red_up, red_down, red_vec_one = reduce_routes(
-        [
-            grad_up,
-            grad_down,
-            vector_block(
-                [grad_bias_up, grad_bias_down, grad_gain_two, grad_shift_two], full_rows, jnp.float32
-            ),
-        ],
+    vec_one = vector_block(
+        [grad_bias_up, grad_bias_down, grad_gain_two, grad_shift_two], full_rows, jnp.float32
+    )
+    red_up, red_down, red_mixed = reduce_routes(
+        [grad_up, grad_down, jnp.concatenate([grad_out, vec_one], axis=1)],
         orders,
         count,
         me,
         backward_anchors[:steps],
     )
-
-    grad_qkv = outer_rows(normed, proj_grad)
+    red_out, red_vec_one = split_cols(red_mixed, [width, vec_one.shape[1]])
+
     grad_bias_query = jnp.sum(proj_grad[:, :width].astype(jnp.float32), axis=0)
     grad_bias_value = jnp.sum(proj_grad[:, 2 * width :].astype(jnp.float32), axis=0)
-    normed_grad = times_transposed(proj_grad, proj_qkv)
+    grad_parts = split_cols(proj_grad, qkv_cols)
+    grad_qkv = [outer_rows(normed, g) for g in grad_parts]
+    normed_grad = times_transposed(grad_parts[0], qkv_weights[0])
+    for g, w in zip(grad_parts[1:], qkv_weights[1:]):
+        normed_grad = normed_grad + times_transposed(g, w)
     input_ln_grad, grad_gain_one, grad_shift_one = norm_one_back(normed_grad)
     input_grads = (middle_grad + input_ln_grad).astype(jnp.bfloat16)
 
@@ -397,11 +406,13 @@
         full_rows,
         jnp.float32,
     )
-    gq = split_cols(grad_qkv, qkv_cols)
     red = reduce_routes(
-        [gq[0], gq[1], jnp.concatenate([gq[2], grad_out, vec_two], axis=1)], orders, count, me
-    )
-    red_last, red_out, red_vec_two = split_cols(red[2], [qkv_cols[2], width, vec_two.shape[1]])
+        [grad_qkv[0], grad_qkv[1], jnp.concatenate([grad_qkv[2], vec_two], axis=1)],
+        orders,
+        count,
+        me,
+    )
+    red_last, red_vec_two = split_cols(red[2], [qkv_cols[2], vec_two.shape[1]])
     red_qkv = jnp.concatenate([red[0], red[1], red_last], axis=1)
     r_bias_up, r_bias_down, r_gain_two, r_shift_two = vector_unblock(red_vec_one, [ratio, 1, 1, 1])
     r_gain_one, r_shift_one, r_bias_query, r_bias_value, r_bias_out = vector_unblock(

time: 480 us -> 471 us (0.981)
  waiting for transfers between devices: 149 us -> 129 us
  starting transfers between devices: 92.6 us -> 78.4 us
  local copies, waits for them, and re-layouts: 87.9 us -> 102 us
  other arithmetic: 82.2 us -> 89.3 us
    ppermute x30, waiting for transfers between devices: 66.7 us -> 47.5 us  [reduce_routes(): got = lax.ppermute(send, ALL, partner_pairs(count, b))]
    ppermute x30, starting transfers between devices: 35.7 us -> 26.3 us  [reduce_routes(): got = lax.ppermute(send, ALL, partner_pairs(count, b))]
    unnamed x136 -> x167, local copies, waits for them, and re-layouts: 8.47 us -> 16 us
    convert_element_type x30, local copies, waits for them, and re-layouts: 14.2 us -> 19.1 us  [reduce_routes(): lax.dynamic_index_in_dim(x, 1 - mine, axis, keepdims=False)]
    dot_general x4 -> x6, matrix products: 10.7 us -> 12.4 us  [outer_rows(): lax.dot_general(left, right, (((0,), (0,)), ((), ())), preferred_element_...]
  transfers between devices with their start and end apart: 64 -> 64, of which waited for: 29 -> 29; matrix products, arithmetic and copies ran while one was open for 32% -> 39% of each run, Pallas kernels for 0% -> 0%
where the time goes in v2:
time: 471 us; the launch traced here: 463 us
  waiting for transfers between devices  129 us (27%)
  local copies, waits for them, and re-layouts  102 us (22%)
  other arithmetic  89.3 us (19%)
  starting transfers between devices  78.4 us (17%)
  matrix products  61.6 us (13%)
    ppermute x30, waiting for transfers between devices, gather_routes(): got = lax.ppermute(x, ALL, partner_pairs(count, b))  77 us
    ppermute x30, waiting for transfers between devices, reduce_routes(): got = lax.ppermute(send, ALL, partner_pairs(count, b))  47.5 us
    ppermute x30, starting transfers between devices, gather_routes(): got = lax.ppermute(x, ALL, partner_pairs(count, b))  33.9 us
    ppermute x30, starting transfers between devices, reduce_routes(): got = lax.ppermute(send, ALL, partner_pairs(count, b))  26.3 us
    another operation x30, other arithmetic, gather_routes(): x = jnp.stack([x, got])  25.3 us
    add x30, other arithmetic, reduce_routes(): x = keep + got.astype(jnp.float32)  20 us
    convert_element_type x30, local copies, waits for them, and re-layouts, reduce_routes(): lax.dynamic_index_in_dim(x, 1 - mine, axis, keepdims=False)  19.1 us
    gather x6, local copies, waits for them, and re-layouts, gather_routes(): x = jnp.take(x.reshape(count, rows, cols), rel, axis=0)  18.7 us
  transfers between devices with their start and end apart: 64, of which 29 were waited for; matrix products, arithmetic and copies ran while one was open for 39% of the time, Pallas kernels for 0%

profile of v2, /device:TPU:0, one launch (start us, length us, event | category | flops | bytes accessed | tf_op | source)
XLA Modules:
  0.0 462.9 jit_solution(3330587618858311744)
XLA Ops:
  8.3 4.1 collective-permute-start
  71.9 33.8 %collective-permute-done.25 = bf16[96,768]{1,0:T(8,128)(2,1)S(1)} collective-permute-done((bf16[96,768]{1,0:T(8,128)(2,1)S(1)}, bf16[96,768]{1,0:T(8,128)(2,1)S(1)}, u32[]{:S(2)}, u32[]{:S(2)}) %collective-permute-start.25) | collective-permute-done | bytes 147488 | tf_op jit(solution)/shard_map/ppermute | solution.py:77
  110.9 6.2 %fusion.123 = (f32[3,1024]{1,0:T(4,128)S(1)}, f32[3,1024,1024]{1,2,0:T(8,128)S(1)}) fusion(bf16[3,1024,3,64]{1,3,0,2:T(8,128)(2,1)S(1)} %reshape.745, pred[3,1024]{1,0:T(4,128)(4,1)S(1)} %broadcast_compare_fusion, s32[3,1024]{1,0:T(4,128)S(1)} %broadcast_add_fusion, pred[1024,1024]{0,1:T(8,128)(4,1)} %iota_compare_fusion), kind=kOutput, calls=%fused_computation.349 | convolution fusion | flops 421524480 | bytes 14467072 | tf_op jit(solution)/shard_map/uqd,ukd->uqk/dot_general | solution.py:172
  123.2 9.5 %collective-permute-done.27 = bf16[2,2,96,768]{3,2,1,0:T(8,128)(2,1)S(1)} collective-permute-done((bf16[2,2,96,768]{3,2,1,0:T(8,128)(2,1)S(1)}, bf16[2,2,96,768]{3,2,1,0:T(8,128)(2,1)S(1)}, u32[]{:S(2)}, u32[]{:S(2)}) %collective-permute-start.27) | collective-permute-done | bytes 589856 | tf_op jit(solution)/shard_map/ppermute | solution.py:77
  139.9 20.4 %collective-permute-done.16 = bf16[2,24,768]{2,1,0:T(8,128)(2,1)S(1)} collective-permute-done((bf16[2,24,768]{2,1,0:T(8,128)(2,1)S(1)}, bf16[2,24,768]{2,1,0:T(8,128)(2,1)S(1)}, u32[]{:S(2)}, u32[]{:S(2)}) %collective-permute-start.16) | collective-permute-done | bytes 73760 | tf_op jit(solution)/shard_map/ppermute | solution.py:77
  173.6 4.5 all-to-all-start.1
  201.9 4.2 pad_maximum_fusion.1
  206.1 5.5 %gather_fusion.3 = bf16[32,96,768]{2,1,0:T(8,128)(2,1)} fusion(bf16[32,96,768]{2,1,0:T(8,128)(2,1)} %bitcast.482, s32[1024]{0:T(1024)} %pad_clamp_fusion), kind=kCustom, calls=%fused_computation.6 | custom fusion | bytes 9437312 | tf_op jit(solution)/shard_map/jit(_take)/gather | solution.py:82
  211.6 5.0 %broadcast_select_fusion = bf16[32,96,768]{2,1,0:T(8,128)(2,1)} fusion(bf16[32,96,768]{2,1,0:T(8,128)(2,1)} %gather_fusion.3, pred[32]{0:T(512)(128)(4,1)S(1)} %copy-done.60), kind=kLoop, calls=%fused_computation.19 | loop fusion | flops 2359296 | bytes 9437216 | tf_op jit(solution)/shard_map/jit(_take)/select_n | solution.py:82
  216.6 5.0 %pad_maximum_fusion = bf16[2,2,2,2,2,24,3072]{6,5,4,3,2,1,0:T(8,128)(2,1)} fusion(bf16[1,2,2,2,2,24,3072]{6,5,4,3,2,1,0:T(8,128)(2,1)} %bitcast.83, bf16[1,2,2,2,2,24,3072]{6,5,4,3,2,1,0:T(8,128)(2,1)} %bitcast.82), kind=kLoop, calls=%fused_computation.11 | loop fusion | flops 2359296 | bytes 9437184 | tf_op jit(solution)/shard_map/stack | solution.py:78
  221.6 5.5 %gather_fusion.2 = bf16[32,24,3072]{2,1,0:T(8,128)(2,1)} fusion(bf16[32,24,3072]{2,1,0:T(8,128)(2,1)} %bitcast.483, s32[1024]{0:T(1024)} %pad_clamp_fusion.1), kind=kCustom, calls=%fused_computation.5 | custom fusion | bytes 9437312 | tf_op jit(solution)/shard_map/jit(_take)/gather | solution.py:82
  230.1 8.0 %fusion = (f32[256,3072]{1,0:T(8,128)S(1)}, f32[256,3072]{1,0:T(8,128)S(1)}) fusion(f32[3072]{0:T(1024)S(1)} %copy-done.53, bf16[768,3072]{1,0:T(8,128)(2,1)S(1)} %bitcast_select_fusion.1, f32[256,768]{1,0:T(8,128)S(1)} %get-tuple-element.203, f32[768]{0:T(1024)S(1)} %get-tuple-element.133, f32[768]{0:T(1024)S(1)} %get-tuple-element.134, ...), kind=kOutput, calls=%fused_computation.23 | convolution fusion | flops 1258487808 | bytes 11816960 | tf_op jit(solution)/shard_map/dot_general | solution.py:343
  243.1 5.2 %fusion.117 = f32[768,3072]{1,0:T(8,128)} fusion(bf16[256,3072]{1,0:T(8,128)(2,1)S(1)} %get-tuple-element.209, f32[256,768]{1,0:T(8,128)S(1)} %get-tuple-element.203, f32[768]{0:T(1024)S(1)} %get-tuple-element.133, f32[768]{0:T(1024)S(1)} %get-tuple-element.134, f32[256]{0:T(256)S(1)} %copy-done.51, f32[256]{0:T(256)S(1)} %broadcast_multiply_fusion), kind=kOutput, calls=%fused_computation.344 | convolution fusion | flops 1208942592 | bytes 11804672 | tf_op jit(solution)/shard_map/dot_general | solution.py:36
  248.2 7.5 %fusion.3 = bf16[3072,256]{0,1:T(8,128)(2,1)} fusion(f32[256,3072]{1,0:T(8,128)S(1)} %get-tuple-element.205), kind=kLoop, calls=%fused_computation.26 | loop fusion | flops 51118080 | bytes 4718592 | tf_op jit(solution)/shard_map/convert_element_type | solution.py:347
  258.8 5.1 %all-to-all-start.2 = ((bf16[8,3,128,1,64]{2,4,3,1,0:T(8,128)(2,1)}), bf16[8,3,128,1,64]{2,4,3,1,0:T(8,128)(2,1)}, u32[]{:S(2)}, u32[]{:S(2)}) async-start(bf16[8,3,128,1,64]{2,4,3,1,0:T(8,128)(2,1)} %bitcast.106), calls=%async_computation.2 | async-start | bytes 786432 | tf_op jit(solution)/shard_map/all_to_all | solution.py:154
  270.0 4.2 concatenate.50
  294.0 6.8 %fusion.41 = bf16[3,1024,64]{1,2,0:T(8,128)(2,1)S(1)} fusion(f32[3,1024,1024]{1,2,0:T(8,128)} %copy-done.2, bf16[3,1024,64]{1,2,0:T(8,128)(2,1)S(1)} %squeeze_reshape.3, f32[3,1024]{1,0:T(4,128)S(1)} %copy-done.39), kind=kOutput, calls=%fused_computation.96 | convolution fusion | flops 406585344 | bytes 13381632 | tf_op jit(solution)/shard_map/uqk,uqd->ukd/dot_general | solution.py:190
  300.9 6.6 %multiply_convert_fusion = bf16[3,1024,1024]{1,2,0:T(8,128)(2,1)S(1)} fusion(f32[3,1024,1024]{1,2,0:T(8,128)} %copy-done.2, f32[3,1024]{1,0:T(4,128)S(1)} %div.84, bf16[3,1024,3,64]{1,3,0,2:T(8,128)(2,1)S(1)} %copy-done.20, bf16[3,1024,64]{1,2,0:T(8,128)(2,1)S(1)} %squeeze_reshape.3, f32[3,1024]{1,0:T(4,128)S(1)} %copy-done.39), kind=kOutput, calls=%fused_computation.7 | convolution fusion | flops 412680192 | bytes 19693568 | tf_op jit(solution)/shard_map/uqd,ukd->uqk/dot_general | solution.py:186
  315.5 5.0 %all-to-all-start.3 = ((bf16[8,3,128,3,64]{2,4,3,1,0:T(8,128)(2,1)}), bf16[8,3,128,3,64]{2,4,3,1,0:T(8,128)(2,1)}, u32[]{:S(2)}, u32[]{:S(2)}) async-start(bf16[8,3,128,3,64]{2,4,3,1,0:T(8,128)(2,1)} %maximum_bitcast_fusion), calls=%async_computation.3 | async-start | bytes 2359296 | tf_op jit(solution)/shard_map/all_to_all | solution.py:164
  324.3 5.8 %fusion.44 = bf16[256,768]{1,0:T(8,128)(2,1)} fusion(f32[256,768]{1,0:T(8,128)} %copy-done.9, bf16[3072,768]{1,0:T(8,128)(2,1)} %bitcast_select_fusion, f32[256,3072]{1,0:T(8,128)} %copy-done.31, f32[256,3072]{1,0:T(8,128)S(1)} %copy-done.8, f32[768]{0:T(1024)S(1)} %copy-done.48), kind=kOutput, calls=%fused_computation.99 | convolution fusion | flops 1210908672 | bytes 12192768 | tf_op jit(solution)/shard_map/dot_general | solution.py:348
  370.3 4.5 concatenate.44
  409.3 13.6 %collective-permute-done.42 = bf16[2,2,24,768]{3,2,1,0:T(8,128)(2,1)S(1)} collective-permute-done((bf16[2,2,24,768]{3,2,1,0:T(8,128)(2,1)S(1)}, bf16[2,2,24,768]{3,2,1,0:T(8,128)(2,1)S(1)}, u32[]{:S(2)}, u32[]{:S(2)}) %collective-permute-start.42) | collective-permute-done | bytes 147488 | tf_op jit(solution)/shard_map/ppermute | solution.py:102
  443.5 7.2 %collective-permute-done.53 = bf16[2,24,3072]{2,1,0:T(8,128)(2,1)S(1)} collective-permute-done((bf16[2,24,3072]{2,1,0:T(8,128)(2,1)S(1)}, bf16[2,24,3072]{2,1,0:T(8,128)(2,1)S(1)}, u32[]{:S(2)}, u32[]{:S(2)}) %collective-permute-start.53) | collective-permute-done | bytes 294944 | tf_op jit(solution)/shard_map/ppermute | solution.py:102
  454.0 6.1 %collective-permute-done.54 = bf16[24,3072]{1,0:T(8,128)(2,1)S(1)} collective-permute-done((bf16[24,3072]{1,0:T(8,128)(2,1)S(1)}, bf16[24,3072]{1,0:T(8,128)(2,1)S(1)}, u32[]{:S(2)}, u32[]{:S(2)}) %collective-permute-start.54) | collective-permute-done | bytes 147488 | tf_op jit(solution)/shard_map/ppermute | solution.py:102
  (511 shorter events, 270.9 us)
Async XLA Ops:
  8.3 15.0 %collective-permute-start = (bf16[24,896]{1,0:T(8,128)(2,1)S(1)}, bf16[24,896]{1,0:T(8,128)(2,1)S(1)}, u32[]{:S(2)}, u32[]{:S(2)}) collective-permute-start(bf16[24,896]{1,0:T(8,128)(2,1)S(1)} %concatenate.37), channel_id=1, source_target_pairs={{0,4},{1,5},{2,6},{3,7},{4,0},{5,1},{6,2},{7,3},{8,12},{9,13},{10,... | collective-permute-start | bytes 129032 | tf_op jit(solution)/shard_map/ppermute | solution.py:77
  62.6 45.9 %all-to-all-start = ((bf16[8,3,128,3,64]{2,4,3,1,0:T(8,128)(2,1)}), bf16[8,3,128,3,64]{2,4,3,1,0:T(8,128)(2,1)S(1)}, u32[]{:S(2)}, u32[]{:S(2)}) async-start(bf16[8,3,128,3,64]{2,4,3,1,0:T(8,128)(2,1)} %bitcast.54), calls=%async_computation | async-start | bytes 2359296 | tf_op jit(solution)/shard_map/all_to_all | solution.py:154
  67.6 38.1 %collective-permute-start.25 = (bf16[96,768]{1,0:T(8,128)(2,1)S(1)}, bf16[96,768]{1,0:T(8,128)(2,1)S(1)}, u32[]{:S(2)}, u32[]{:S(2)}) collective-permute-start(bf16[96,768]{1,0:T(8,128)(2,1)S(1)} %copy-done.40), channel_id=1, source_target_pairs={{0,4},{1,5},{2,6},{3,7},{4,0},{5,1},{6,2},{7,3},{8,12},{9,13},{10,... | collective-permute-start | bytes 442376 | tf_op jit(solution)/shard_map/ppermute | solution.py:77
  70.5 37.9 %collective-permute-start.20 = (bf16[24,3072]{1,0:T(8,128)(2,1)S(1)}, bf16[24,3072]{1,0:T(8,128)(2,1)S(1)}, u32[]{:S(2)}, u32[]{:S(2)}) collective-permute-start(bf16[24,3072]{1,0:T(8,128)(2,1)S(1)} %copy-done.41), channel_id=1, source_target_pairs={{0,4},{1,5},{2,6},{3,7},{4,0},{5,1},{6,2},{7,3},{8,12},{9,13},{10,... | collective-permute-start | bytes 442376 | tf_op jit(solution)/shard_map/ppermute | solution.py:77
  119.3 16.3 %collective-permute-start.22 = (bf16[2,2,24,3072]{3,2,1,0:T(8,128)(2,1)S(1)}, bf16[2,2,24,3072]{3,2,1,0:T(8,128)(2,1)S(1)}, u32[]{:S(2)}, u32[]{:S(2)}) collective-permute-start(bf16[2,2,24,3072]{3,2,1,0:T(8,128)(2,1)S(1)} %pad_maximum_fusion.16), channel_id=1, source_target_pairs={{0,1},{1,0},{2,3},{3,2},{4,5},{5,4},{6,7},{7,6},{8,9},{9,8},{10,11... | collective-permute-start | bytes 1769480 | tf_op jit(solution)/shard_map/ppermute | solution.py:77
  132.8 35.3 %collective-permute-start.28 = (bf16[2,2,2,96,768]{4,3,2,1,0:T(8,128)(2,1)S(1)}, bf16[2,2,2,96,768]{4,3,2,1,0:T(8,128)(2,1)S(1)}, u32[]{:S(2)}, u32[]{:S(2)}) collective-permute-start(bf16[2,2,2,96,768]{4,3,2,1,0:T(8,128)(2,1)S(1)} %pad_maximum_fusion.10), channel_id=1, source_target_pairs={{0,1},{1,0},{2,3},{3,2},{4,5},{5,4},{6,7},{7,6},{8,9},{9,8},{10,11... | collective-permute-start | bytes 3538952 | tf_op jit(solution)/shard_map/ppermute | solution.py:77
  136.8 43.0 %collective-permute-start.23 = (bf16[2,2,2,24,3072]{4,3,2,1,0:T(8,128)(2,1)}, bf16[2,2,2,24,3072]{4,3,2,1,0:T(8,128)(2,1)}, u32[]{:S(2)}, u32[]{:S(2)}) collective-permute-start(bf16[2,2,2,24,3072]{4,3,2,1,0:T(8,128)(2,1)} %pad_maximum_fusion.9), channel_id=1, source_target_pairs={{0,16},{1,17},{2,18},{3,19},{4,20},{5,21},{6,22},{7,23},{8,24},{9,... | collective-permute-start | bytes 3538952 | tf_op jit(solution)/shard_map/ppermute | solution.py:77
  139.2 21.1 %collective-permute-start.16 = (bf16[2,24,768]{2,1,0:T(8,128)(2,1)S(1)}, bf16[2,24,768]{2,1,0:T(8,128)(2,1)S(1)}, u32[]{:S(2)}, u32[]{:S(2)}) collective-permute-start(bf16[2,24,768]{2,1,0:T(8,128)(2,1)S(1)} %pad_maximum_fusion.32), channel_id=1, source_target_pairs={{0,1},{1,0},{2,3},{3,2},{4,5},{5,4},{6,7},{7,6},{8,9},{9,8},{10,11... | collective-permute-start | bytes 221192 | tf_op jit(solution)/shard_map/ppermute | solution.py:77
  171.0 30.9 %collective-permute-start.29 = (bf16[2,2,2,2,96,768]{5,4,3,2,1,0:T(8,128)(2,1)S(1)}, bf16[2,2,2,2,96,768]{5,4,3,2,1,0:T(8,128)(2,1)}, u32[]{:S(2)}, u32[]{:S(2)}) collective-permute-start(bf16[2,2,2,2,96,768]{5,4,3,2,1,0:T(8,128)(2,1)S(1)} %pad_maximum_fusion.3), channel_id=1, source_target_pairs={{0,8},{1,9},{2,10},{3,11},{4,12},{5,13},{6,14},{7,15},{8,0},{9,1},... | collective-permute-start | bytes 7077896 | tf_op jit(solution)/shard_map/ppermute | solution.py:77
  173.6 16.7 %all-to-all-start.1 = ((bf16[8,3,128,1,64]{2,4,3,1,0:T(8,128)(2,1)}), bf16[8,3,128,1,64]{2,4,3,1,0:T(8,128)(2,1)}, u32[]{:S(2)}, u32[]{:S(2)}) async-start(bf16[8,3,128,1,64]{2,4,3,1,0:T(8,128)(2,1)} %bitcast.476), calls=%async_computation.1 | async-start | bytes 786432 | tf_op jit(solution)/shard_map/all_to_all | solution.py:164
  183.1 33.5 %collective-permute-start.24 = (bf16[2,2,2,2,24,3072]{5,4,3,2,1,0:T(8,128)(2,1)}, bf16[2,2,2,2,24,3072]{5,4,3,2,1,0:T(8,128)(2,1)}, u32[]{:S(2)}, u32[]{:S(2)}) collective-permute-start(bf16[2,2,2,2,24,3072]{5,4,3,2,1,0:T(8,128)(2,1)} %pad_maximum_fusion.2), channel_id=1, source_target_pairs={{0,8},{1,9},{2,10},{3,11},{4,12},{5,13},{6,14},{7,15},{8,0},{9,1},... | collective-permute-start | bytes 7077896 | tf_op jit(solution)/shard_map/ppermute | solution.py:77
  258.8 33.7 %all-to-all-start.2 = ((bf16[8,3,128,1,64]{2,4,3,1,0:T(8,128)(2,1)}), bf16[8,3,128,1,64]{2,4,3,1,0:T(8,128)(2,1)}, u32[]{:S(2)}, u32[]{:S(2)}) async-start(bf16[8,3,128,1,64]{2,4,3,1,0:T(8,128)(2,1)} %bitcast.106), calls=%async_computation.2 | async-start | bytes 786432 | tf_op jit(solution)/shard_map/all_to_all | solution.py:154
  276.4 31.1 %collective-permute-start.45 = (bf16[2,2,2,2,24,896]{5,4,3,2,1,0:T(8,128)(2,1)}, bf16[2,2,2,2,24,896]{5,4,3,2,1,0:T(8,128)(2,1)S(1)}, u32[]{:S(2)}, u32[]{:S(2)}) collective-permute-start(bf16[2,2,2,2,24,896]{5,4,3,2,1,0:T(8,128)(2,1)} %fusion.52), channel_id=1, source_target_pairs={{0,8},{1,9},{2,10},{3,11},{4,12},{5,13},{6,14},{7,15},{8,0},{9,1},... | collective-permute-start | bytes 2064392 | tf_op jit(solution)/shard_map/ppermute | solution.py:102
  280.5 51.8 %collective-permute-start.50 = (bf16[2,2,2,2,24,3072]{5,4,1,2,3,0:T(8,128)(2,1)}, bf16[2,2,2,2,24,3072]{5,4,1,2,3,0:T(8,128)(2,1)}, u32[]{:S(2)}, u32[]{:S(2)}) collective-permute-start(bf16[2,2,2,2,24,3072]{5,4,1,2,3,0:T(8,128)(2,1)} %fusion.28), channel_id=1, source_target_pairs={{0,8},{1,9},{2,10},{3,11},{4,12},{5,13},{6,14},{7,15},{8,0},{9,1},... | collective-permute-start | bytes 7077896 | tf_op jit(solution)/shard_map/ppermute | solution.py:102
  289.5 48.8 %collective-permute-start.55 = (bf16[2,2,2,2,96,768]{5,4,3,2,1,0:T(8,128)(2,1)}, bf16[2,2,2,2,96,768]{5,4,3,2,1,0:T(8,128)(2,1)}, u32[]{:S(2)}, u32[]{:S(2)}) collective-permute-start(bf16[2,2,2,2,96,768]{5,4,3,2,1,0:T(8,128)(2,1)} %fusion.27), channel_id=1, source_target_pairs={{0,8},{1,9},{2,10},{3,11},{4,12},{5,13},{6,14},{7,15},{8,0},{9,1},... | collective-permute-start | bytes 7077896 | tf_op jit(solution)/shard_map/ppermute | solution.py:102
  315.5 34.0 %all-to-all-start.3 = ((bf16[8,3,128,3,64]{2,4,3,1,0:T(8,128)(2,1)}), bf16[8,3,128,3,64]{2,4,3,1,0:T(8,128)(2,1)}, u32[]{:S(2)}, u32[]{:S(2)}) async-start(bf16[8,3,128,3,64]{2,4,3,1,0:T(8,128)(2,1)} %maximum_bitcast_fusion), calls=%async_computation.3 | async-start | bytes 2359296 | tf_op jit(solution)/shard_map/all_to_all | solution.py:164
  337.3 59.9 %collective-permute-start.51 = (bf16[2,2,2,24,3072]{4,3,0,1,2:T(8,128)(2,1)}, bf16[2,2,2,24,3072]{4,3,0,1,2:T(8,128)(2,1)}, u32[]{:S(2)}, u32[]{:S(2)}) collective-permute-start(bf16[2,2,2,24,3072]{4,3,0,1,2:T(8,128)(2,1)} %fusion.45), channel_id=1, source_target_pairs={{0,16},{1,17},{2,18},{3,19},{4,20},{5,21},{6,22},{7,23},{8,24},{9,... | collective-permute-start | bytes 3538952 | tf_op jit(solution)/shard_map/ppermute | solution.py:102
  344.5 55.3 %collective-permute-start.56 = (bf16[2,2,2,96,768]{4,3,2,1,0:T(8,128)(2,1)}, bf16[2,2,2,96,768]{4,3,2,1,0:T(8,128)(2,1)}, u32[]{:S(2)}, u32[]{:S(2)}) collective-permute-start(bf16[2,2,2,96,768]{4,3,2,1,0:T(8,128)(2,1)} %fusion.46), channel_id=1, source_target_pairs={{0,1},{1,0},{2,3},{3,2},{4,5},{5,4},{6,7},{7,6},{8,9},{9,8},{10,11... | collective-permute-start | bytes 3538952 | tf_op jit(solution)/shard_map/ppermute | solution.py:102
  377.3 19.7 %collective-permute-start.30 = (bf16[2,2,2,2,24,896]{5,4,3,2,1,0:T(8,128)(2,1)}, bf16[2,2,2,2,24,896]{5,4,3,2,1,0:T(8,128)(2,1)S(1)}, u32[]{:S(2)}, u32[]{:S(2)}) collective-permute-start(bf16[2,2,2,2,24,896]{5,4,3,2,1,0:T(8,128)(2,1)} %fusion.51), channel_id=1, source_target_pairs={{0,8},{1,9},{2,10},{3,11},{4,12},{5,13},{6,14},{7,15},{8,0},{9,1},... | collective-permute-start | bytes 2064392 | tf_op jit(solution)/shard_map/ppermute | solution.py:102
  399.0 42.9 %collective-permute-start.52 = (bf16[2,2,24,3072]{3,2,0,1:T(8,128)(2,1)S(1)}, bf16[2,2,24,3072]{3,2,0,1:T(8,128)(2,1)S(1)}, u32[]{:S(2)}, u32[]{:S(2)}) collective-permute-start(bf16[2,2,24,3072]{3,2,0,1:T(8,128)(2,1)S(1)} %fusion.53), channel_id=1, source_target_pairs={{0,1},{1,0},{2,3},{3,2},{4,5},{5,4},{6,7},{7,6},{8,9},{9,8},{10,11... | collective-permute-start | bytes 1769480 | tf_op jit(solution)/shard_map/ppermute | solution.py:102
  401.4 40.9 %collective-permute-start.57 = (bf16[2,2,96,768]{3,2,1,0:T(8,128)(2,1)S(1)}, bf16[2,2,96,768]{3,2,1,0:T(8,128)(2,1)S(1)}, u32[]{:S(2)}, u32[]{:S(2)}) collective-permute-start(bf16[2,2,96,768]{3,2,1,0:T(8,128)(2,1)S(1)} %fusion.54), channel_id=1, source_target_pairs={{0,2},{1,3},{2,0},{3,1},{4,6},{5,7},{6,4},{7,5},{8,10},{9,11},{10,... | collective-permute-start | bytes 1769480 | tf_op jit(solution)/shard_map/ppermute | solution.py:102
  403.6 19.4 %collective-permute-start.42 = (bf16[2,2,24,768]{3,2,1,0:T(8,128)(2,1)S(1)}, bf16[2,2,24,768]{3,2,1,0:T(8,128)(2,1)S(1)}, u32[]{:S(2)}, u32[]{:S(2)}) collective-permute-start(bf16[2,2,24,768]{3,2,1,0:T(8,128)(2,1)S(1)} %fusion.77), channel_id=1, source_target_pairs={{0,2},{1,3},{2,0},{3,1},{4,6},{5,7},{6,4},{7,5},{8,10},{9,11},{10,... | collective-permute-start | bytes 442376 | tf_op jit(solution)/shard_map/ppermute | solution.py:102
  405.2 18.9 %collective-permute-start.37 = (bf16[2,2,24,768]{3,2,0,1:T(8,128)(2,1)S(1)}, bf16[2,2,24,768]{3,2,0,1:T(8,128)(2,1)S(1)}, u32[]{:S(2)}, u32[]{:S(2)}) collective-permute-start(bf16[2,2,24,768]{3,2,0,1:T(8,128)(2,1)S(1)} %fusion.76), channel_id=1, source_target_pairs={{0,1},{1,0},{2,3},{3,2},{4,5},{5,4},{6,7},{7,6},{8,9},{9,8},{10,11... | collective-permute-start | bytes 442376 | tf_op jit(solution)/shard_map/ppermute | solution.py:102
  408.3 22.3 %collective-permute-start.32 = (bf16[2,2,24,896]{3,2,1,0:T(8,128)(2,1)S(1)}, bf16[2,2,24,896]{3,2,1,0:T(8,128)(2,1)S(1)}, u32[]{:S(2)}, u32[]{:S(2)}) collective-permute-start(bf16[2,2,24,896]{3,2,1,0:T(8,128)(2,1)S(1)} %fusion.74), channel_id=1, source_target_pairs={{0,16},{1,17},{2,18},{3,19},{4,20},{5,21},{6,22},{7,23},{8,24},{9,... | collective-permute-start | bytes 516104 | tf_op jit(solution)/shard_map/ppermute | solution.py:102
  (119 other events, 1050.1 us)

commit v3 on v2

--- a/solution.py
+++ b/solution.py
@@ -322,7 +322,7 @@
         attended_b = units_to_rows(
             attended_u.astype(jnp.bfloat16)[:, :, None], seq_count, micro, 1
         )
-        forward_anchors = [queries, qkv_units, weights, attended_u, attended_u]
+        forward_anchors = [normed, qkv_units, weights, attended_u, attended_u]
     else:
         attended, saved = fallback_attention(queries, keys_now, values_now, bounds, row_count)
         attended_b = attended.astype(jnp.bfloat16)

time: 471 us -> 468 us (level)
  other arithmetic: 89.3 us -> 84 us
    unnamed x167 -> x153, local copies, waits for them, and re-layouts: 16 us -> 16.7 us
  transfers between devices with their start and end apart: 64 -> 64, of which waited for: 29 -> 30; matrix products, arithmetic and copies ran while one was open for 39% -> 38% of each run, Pallas kernels for 0% -> 0%
where the time goes in v3:
time: 468 us; the launch traced here: 460 us
  waiting for transfers between devices  130 us (28%)
  local copies, waits for them, and re-layouts  102 us (22%)
  other arithmetic  84 us (18%)
  starting transfers between devices  79.9 us (17%)
  matrix products  61.6 us (13%)
    ppermute x30, waiting for transfers between devices, gather_routes(): got = lax.ppermute(x, ALL, partner_pairs(count, b))  78.8 us
    ppermute x30, waiting for transfers between devices, reduce_routes(): got = lax.ppermute(send, ALL, partner_pairs(count, b))  47.1 us
    ppermute x30, starting transfers between devices, gather_routes(): got = lax.ppermute(x, ALL, partner_pairs(count, b))  34.5 us
    ppermute x30, starting transfers between devices, reduce_routes(): got = lax.ppermute(send, ALL, partner_pairs(count, b))  26.5 us
    another operation x30, other arithmetic, gather_routes(): x = jnp.stack([x, got])  24.8 us
    add x30, other arithmetic, reduce_routes(): x = keep + got.astype(jnp.float32)  20 us
    convert_element_type x30, local copies, waits for them, and re-layouts, reduce_routes(): lax.dynamic_index_in_dim(x, 1 - mine, axis, keepdims=False)  19.2 us
    gather x6, local copies, waits for them, and re-layouts, gather_routes(): x = jnp.take(x.reshape(count, rows, cols), rel, axis=0)  18.1 us
  transfers between devices with their start and end apart: 64, of which 30 were waited for; matrix products, arithmetic and copies ran while one was open for 38% of the time, Pallas kernels for 0%

profile of v3, /device:TPU:0, one launch (start us, length us, event | category | flops | bytes accessed | tf_op | source)
XLA Modules:
  0.0 459.9 jit_solution(2267852209842991335)
XLA Ops:
  59.5 4.3 all-to-all-start
  69.4 33.8 %collective-permute-done.25 = bf16[96,768]{1,0:T(8,128)(2,1)S(1)} collective-permute-done((bf16[96,768]{1,0:T(8,128)(2,1)S(1)}, bf16[96,768]{1,0:T(8,128)(2,1)S(1)}, u32[]{:S(2)}, u32[]{:S(2)}) %collective-permute-start.25) | collective-permute-done | bytes 147488 | tf_op jit(solution)/shard_map/ppermute | solution.py:77
  107.8 6.2 %fusion.123 = (f32[3,1024]{1,0:T(4,128)S(1)}, f32[3,1024,1024]{1,2,0:T(8,128)S(1)}) fusion(bf16[3,1024,3,64]{1,3,0,2:T(8,128)(2,1)S(1)} %reshape.745, pred[3,1024]{1,0:T(4,128)(4,1)S(1)} %broadcast_compare_fusion, s32[3,1024]{1,0:T(4,128)S(1)} %broadcast_add_fusion, pred[1024,1024]{0,1:T(8,128)(4,1)} %iota_compare_fusion), kind=kOutput, calls=%fused_computation.349 | convolution fusion | flops 421524480 | bytes 14467072 | tf_op jit(solution)/shard_map/uqd,ukd->uqk/dot_general | solution.py:172
  120.0 9.3 %collective-permute-done.27 = bf16[2,2,96,768]{3,2,1,0:T(8,128)(2,1)S(1)} collective-permute-done((bf16[2,2,96,768]{3,2,1,0:T(8,128)(2,1)S(1)}, bf16[2,2,96,768]{3,2,1,0:T(8,128)(2,1)S(1)}, u32[]{:S(2)}, u32[]{:S(2)}) %collective-permute-start.27) | collective-permute-done | bytes 589856 | tf_op jit(solution)/shard_map/ppermute | solution.py:77
  136.6 20.3 %collective-permute-done.16 = bf16[2,24,768]{2,1,0:T(8,128)(2,1)S(1)} collective-permute-done((bf16[2,24,768]{2,1,0:T(8,128)(2,1)S(1)}, bf16[2,24,768]{2,1,0:T(8,128)(2,1)S(1)}, u32[]{:S(2)}, u32[]{:S(2)}) %collective-permute-start.16) | collective-permute-done | bytes 73760 | tf_op jit(solution)/shard_map/ppermute | solution.py:77
  170.7 4.5 all-to-all-start.1
  199.1 4.2 pad_maximum_fusion.1
  203.3 5.5 %gather_fusion.3 = bf16[32,96,768]{2,1,0:T(8,128)(2,1)} fusion(bf16[32,96,768]{2,1,0:T(8,128)(2,1)} %bitcast.482, s32[1024]{0:T(1024)} %pad_clamp_fusion), kind=kCustom, calls=%fused_computation.6 | custom fusion | bytes 9437312 | tf_op jit(solution)/shard_map/jit(_take)/gather | solution.py:82
  208.8 5.0 %broadcast_select_fusion = bf16[32,96,768]{2,1,0:T(8,128)(2,1)} fusion(bf16[32,96,768]{2,1,0:T(8,128)(2,1)} %gather_fusion.3, pred[32]{0:T(512)(128)(4,1)S(1)} %copy-done.58), kind=kLoop, calls=%fused_computation.19 | loop fusion | flops 2359296 | bytes 9437216 | tf_op jit(solution)/shard_map/jit(_take)/select_n | solution.py:82
  213.7 5.0 %pad_maximum_fusion = bf16[2,2,2,2,2,24,3072]{6,5,4,3,2,1,0:T(8,128)(2,1)} fusion(bf16[1,2,2,2,2,24,3072]{6,5,4,3,2,1,0:T(8,128)(2,1)} %bitcast.83, bf16[1,2,2,2,2,24,3072]{6,5,4,3,2,1,0:T(8,128)(2,1)} %bitcast.82), kind=kLoop, calls=%fused_computation.11 | loop fusion | flops 2359296 | bytes 9437184 | tf_op jit(solution)/shard_map/stack | solution.py:78
  218.7 5.5 %gather_fusion.2 = bf16[32,24,3072]{2,1,0:T(8,128)(2,1)} fusion(bf16[32,24,3072]{2,1,0:T(8,128)(2,1)} %bitcast.483, s32[1024]{0:T(1024)} %pad_clamp_fusion.1), kind=kCustom, calls=%fused_computation.5 | custom fusion | bytes 9437312 | tf_op jit(solution)/shard_map/jit(_take)/gather | solution.py:82
  227.2 8.0 %fusion = (f32[256,3072]{1,0:T(8,128)S(1)}, f32[256,3072]{1,0:T(8,128)S(1)}) fusion(f32[3072]{0:T(1024)S(1)} %copy-done.54, bf16[768,3072]{1,0:T(8,128)(2,1)S(1)} %bitcast_select_fusion.1, f32[256,768]{1,0:T(8,128)S(1)} %get-tuple-element.203, f32[768]{0:T(1024)S(1)} %get-tuple-element.133, f32[768]{0:T(1024)S(1)} %get-tuple-element.134, ...), kind=kOutput, calls=%fused_computation.23 | convolution fusion | flops 1258487808 | bytes 11816960 | tf_op jit(solution)/shard_map/dot_general | solution.py:343
  240.2 5.2 %fusion.117 = f32[768,3072]{1,0:T(8,128)} fusion(bf16[256,3072]{1,0:T(8,128)(2,1)S(1)} %get-tuple-element.209, f32[256,768]{1,0:T(8,128)S(1)} %get-tuple-element.203, f32[768]{0:T(1024)S(1)} %get-tuple-element.133, f32[768]{0:T(1024)S(1)} %get-tuple-element.134, f32[256]{0:T(256)S(1)} %copy-done.52, f32[256]{0:T(256)S(1)} %broadcast_multiply_fusion), kind=kOutput, calls=%fused_computation.344 | convolution fusion | flops 1208942592 | bytes 11804672 | tf_op jit(solution)/shard_map/dot_general | solution.py:36
  245.4 7.5 %fusion.3 = bf16[3072,256]{0,1:T(8,128)(2,1)} fusion(f32[256,3072]{1,0:T(8,128)S(1)} %get-tuple-element.205), kind=kLoop, calls=%fused_computation.26 | loop fusion | flops 51118080 | bytes 4718592 | tf_op jit(solution)/shard_map/convert_element_type | solution.py:347
  256.0 5.1 %all-to-all-start.2 = ((bf16[8,3,128,1,64]{2,4,3,1,0:T(8,128)(2,1)}), bf16[8,3,128,1,64]{2,4,3,1,0:T(8,128)(2,1)}, u32[]{:S(2)}, u32[]{:S(2)}) async-start(bf16[8,3,128,1,64]{2,4,3,1,0:T(8,128)(2,1)} %bitcast.106), calls=%async_computation.2 | async-start | bytes 786432 | tf_op jit(solution)/shard_map/all_to_all | solution.py:154
  267.2 4.2 concatenate.50
  291.2 6.8 %fusion.41 = bf16[3,1024,64]{1,2,0:T(8,128)(2,1)S(1)} fusion(f32[3,1024,1024]{1,2,0:T(8,128)} %copy-done.2, bf16[3,1024,64]{1,2,0:T(8,128)(2,1)S(1)} %squeeze_reshape.3, f32[3,1024]{1,0:T(4,128)S(1)} %copy-done.40), kind=kOutput, calls=%fused_computation.96 | convolution fusion | flops 406585344 | bytes 13381632 | tf_op jit(solution)/shard_map/uqk,uqd->ukd/dot_general | solution.py:190
  298.2 6.6 %multiply_convert_fusion = bf16[3,1024,1024]{1,2,0:T(8,128)(2,1)S(1)} fusion(f32[3,1024,1024]{1,2,0:T(8,128)} %copy-done.2, f32[3,1024]{1,0:T(4,128)S(1)} %div.84, bf16[3,1024,3,64]{1,3,0,2:T(8,128)(2,1)S(1)} %copy-done.20, bf16[3,1024,64]{1,2,0:T(8,128)(2,1)S(1)} %squeeze_reshape.3, f32[3,1024]{1,0:T(4,128)S(1)} %copy-done.40), kind=kOutput, calls=%fused_computation.7 | convolution fusion | flops 412680192 | bytes 19693568 | tf_op jit(solution)/shard_map/uqd,ukd->uqk/dot_general | solution.py:186
  312.7 5.0 %all-to-all-start.3 = ((bf16[8,3,128,3,64]{2,4,3,1,0:T(8,128)(2,1)}), bf16[8,3,128,3,64]{2,4,3,1,0:T(8,128)(2,1)}, u32[]{:S(2)}, u32[]{:S(2)}) async-start(bf16[8,3,128,3,64]{2,4,3,1,0:T(8,128)(2,1)} %maximum_bitcast_fusion), calls=%async_computation.3 | async-start | bytes 2359296 | tf_op jit(solution)/shard_map/all_to_all | solution.py:164
  321.4 5.8 %fusion.44 = bf16[256,768]{1,0:T(8,128)(2,1)} fusion(f32[256,768]{1,0:T(8,128)} %copy-done.9, bf16[3072,768]{1,0:T(8,128)(2,1)} %bitcast_select_fusion, f32[256,3072]{1,0:T(8,128)} %copy-done.32, f32[256,3072]{1,0:T(8,128)S(1)} %copy-done.8, f32[768]{0:T(1024)S(1)} %copy-done.49), kind=kOutput, calls=%fused_computation.99 | convolution fusion | flops 1210908672 | bytes 12192768 | tf_op jit(solution)/shard_map/dot_general | solution.py:348
  367.5 4.4 concatenate.44
  406.5 13.4 %collective-permute-done.42 = bf16[2,2,24,768]{3,2,1,0:T(8,128)(2,1)S(1)} collective-permute-done((bf16[2,2,24,768]{3,2,1,0:T(8,128)(2,1)S(1)}, bf16[2,2,24,768]{3,2,1,0:T(8,128)(2,1)S(1)}, u32[]{:S(2)}, u32[]{:S(2)}) %collective-permute-start.42) | collective-permute-done | bytes 147488 | tf_op jit(solution)/shard_map/ppermute | solution.py:102
  440.7 7.1 %collective-permute-done.53 = bf16[2,24,3072]{2,1,0:T(8,128)(2,1)S(1)} collective-permute-done((bf16[2,24,3072]{2,1,0:T(8,128)(2,1)S(1)}, bf16[2,24,3072]{2,1,0:T(8,128)(2,1)S(1)}, u32[]{:S(2)}, u32[]{:S(2)}) %collective-permute-start.53) | collective-permute-done | bytes 294944 | tf_op jit(solution)/shard_map/ppermute | solution.py:102
  451.0 6.0 %collective-permute-done.54 = bf16[24,3072]{1,0:T(8,128)(2,1)S(1)} collective-permute-done((bf16[24,3072]{1,0:T(8,128)(2,1)S(1)}, bf16[24,3072]{1,0:T(8,128)(2,1)S(1)}, u32[]{:S(2)}, u32[]{:S(2)}) %collective-permute-start.54) | collective-permute-done | bytes 147488 | tf_op jit(solution)/shard_map/ppermute | solution.py:102
  (497 shorter events, 268.3 us)
Async XLA Ops:
  59.5 46.2 %all-to-all-start = ((bf16[8,3,128,3,64]{2,4,3,1,0:T(8,128)(2,1)}), bf16[8,3,128,3,64]{2,4,3,1,0:T(8,128)(2,1)S(1)}, u32[]{:S(2)}, u32[]{:S(2)}) async-start(bf16[8,3,128,3,64]{2,4,3,1,0:T(8,128)(2,1)} %bitcast.54), calls=%async_computation | async-start | bytes 2359296 | tf_op jit(solution)/shard_map/all_to_all | solution.py:154
  65.1 38.2 %collective-permute-start.25 = (bf16[96,768]{1,0:T(8,128)(2,1)S(1)}, bf16[96,768]{1,0:T(8,128)(2,1)S(1)}, u32[]{:S(2)}, u32[]{:S(2)}) collective-permute-start(bf16[96,768]{1,0:T(8,128)(2,1)S(1)} %copy-done.41), channel_id=1, source_target_pairs={{0,4},{1,5},{2,6},{3,7},{4,0},{5,1},{6,2},{7,3},{8,12},{9,13},{10,... | collective-permute-start | bytes 442376 | tf_op jit(solution)/shard_map/ppermute | solution.py:77
  68.1 37.6 %collective-permute-start.20 = (bf16[24,3072]{1,0:T(8,128)(2,1)S(1)}, bf16[24,3072]{1,0:T(8,128)(2,1)S(1)}, u32[]{:S(2)}, u32[]{:S(2)}) collective-permute-start(bf16[24,3072]{1,0:T(8,128)(2,1)S(1)} %copy-done.42), channel_id=1, source_target_pairs={{0,4},{1,5},{2,6},{3,7},{4,0},{5,1},{6,2},{7,3},{8,12},{9,13},{10,... | collective-permute-start | bytes 442376 | tf_op jit(solution)/shard_map/ppermute | solution.py:77
  115.5 13.8 %collective-permute-start.27 = (bf16[2,2,96,768]{3,2,1,0:T(8,128)(2,1)S(1)}, bf16[2,2,96,768]{3,2,1,0:T(8,128)(2,1)S(1)}, u32[]{:S(2)}, u32[]{:S(2)}) collective-permute-start(bf16[2,2,96,768]{3,2,1,0:T(8,128)(2,1)S(1)} %pad_maximum_fusion.17), channel_id=1, source_target_pairs={{0,2},{1,3},{2,0},{3,1},{4,6},{5,7},{6,4},{7,5},{8,10},{9,11},{10,... | collective-permute-start | bytes 1769480 | tf_op jit(solution)/shard_map/ppermute | solution.py:77
  116.2 16.4 %collective-permute-start.22 = (bf16[2,2,24,3072]{3,2,1,0:T(8,128)(2,1)S(1)}, bf16[2,2,24,3072]{3,2,1,0:T(8,128)(2,1)S(1)}, u32[]{:S(2)}, u32[]{:S(2)}) collective-permute-start(bf16[2,2,24,3072]{3,2,1,0:T(8,128)(2,1)S(1)} %pad_maximum_fusion.16), channel_id=1, source_target_pairs={{0,1},{1,0},{2,3},{3,2},{4,5},{5,4},{6,7},{7,6},{8,9},{9,8},{10,11... | collective-permute-start | bytes 1769480 | tf_op jit(solution)/shard_map/ppermute | solution.py:77
  129.4 35.8 %collective-permute-start.28 = (bf16[2,2,2,96,768]{4,3,2,1,0:T(8,128)(2,1)S(1)}, bf16[2,2,2,96,768]{4,3,2,1,0:T(8,128)(2,1)S(1)}, u32[]{:S(2)}, u32[]{:S(2)}) collective-permute-start(bf16[2,2,2,96,768]{4,3,2,1,0:T(8,128)(2,1)S(1)} %pad_maximum_fusion.10), channel_id=1, source_target_pairs={{0,1},{1,0},{2,3},{3,2},{4,5},{5,4},{6,7},{7,6},{8,9},{9,8},{10,11... | collective-permute-start | bytes 3538952 | tf_op jit(solution)/shard_map/ppermute | solution.py:77
  133.8 43.2 %collective-permute-start.23 = (bf16[2,2,2,24,3072]{4,3,2,1,0:T(8,128)(2,1)}, bf16[2,2,2,24,3072]{4,3,2,1,0:T(8,128)(2,1)}, u32[]{:S(2)}, u32[]{:S(2)}) collective-permute-start(bf16[2,2,2,24,3072]{4,3,2,1,0:T(8,128)(2,1)} %pad_maximum_fusion.9), channel_id=1, source_target_pairs={{0,16},{1,17},{2,18},{3,19},{4,20},{5,21},{6,22},{7,23},{8,24},{9,... | collective-permute-start | bytes 3538952 | tf_op jit(solution)/shard_map/ppermute | solution.py:77
  135.8 21.1 %collective-permute-start.16 = (bf16[2,24,768]{2,1,0:T(8,128)(2,1)S(1)}, bf16[2,24,768]{2,1,0:T(8,128)(2,1)S(1)}, u32[]{:S(2)}, u32[]{:S(2)}) collective-permute-start(bf16[2,24,768]{2,1,0:T(8,128)(2,1)S(1)} %pad_maximum_fusion.32), channel_id=1, source_target_pairs={{0,1},{1,0},{2,3},{3,2},{4,5},{5,4},{6,7},{7,6},{8,9},{9,8},{10,11... | collective-permute-start | bytes 221192 | tf_op jit(solution)/shard_map/ppermute | solution.py:77
  168.1 30.9 %collective-permute-start.29 = (bf16[2,2,2,2,96,768]{5,4,3,2,1,0:T(8,128)(2,1)S(1)}, bf16[2,2,2,2,96,768]{5,4,3,2,1,0:T(8,128)(2,1)}, u32[]{:S(2)}, u32[]{:S(2)}) collective-permute-start(bf16[2,2,2,2,96,768]{5,4,3,2,1,0:T(8,128)(2,1)S(1)} %pad_maximum_fusion.3), channel_id=1, source_target_pairs={{0,8},{1,9},{2,10},{3,11},{4,12},{5,13},{6,14},{7,15},{8,0},{9,1},... | collective-permute-start | bytes 7077896 | tf_op jit(solution)/shard_map/ppermute | solution.py:77
  170.7 16.7 %all-to-all-start.1 = ((bf16[8,3,128,1,64]{2,4,3,1,0:T(8,128)(2,1)}), bf16[8,3,128,1,64]{2,4,3,1,0:T(8,128)(2,1)}, u32[]{:S(2)}, u32[]{:S(2)}) async-start(bf16[8,3,128,1,64]{2,4,3,1,0:T(8,128)(2,1)} %bitcast.476), calls=%async_computation.1 | async-start | bytes 786432 | tf_op jit(solution)/shard_map/all_to_all | solution.py:164
  180.2 33.5 %collective-permute-start.24 = (bf16[2,2,2,2,24,3072]{5,4,3,2,1,0:T(8,128)(2,1)}, bf16[2,2,2,2,24,3072]{5,4,3,2,1,0:T(8,128)(2,1)}, u32[]{:S(2)}, u32[]{:S(2)}) collective-permute-start(bf16[2,2,2,2,24,3072]{5,4,3,2,1,0:T(8,128)(2,1)} %pad_maximum_fusion.2), channel_id=1, source_target_pairs={{0,8},{1,9},{2,10},{3,11},{4,12},{5,13},{6,14},{7,15},{8,0},{9,1},... | collective-permute-start | bytes 7077896 | tf_op jit(solution)/shard_map/ppermute | solution.py:77
  256.0 33.8 %all-to-all-start.2 = ((bf16[8,3,128,1,64]{2,4,3,1,0:T(8,128)(2,1)}), bf16[8,3,128,1,64]{2,4,3,1,0:T(8,128)(2,1)}, u32[]{:S(2)}, u32[]{:S(2)}) async-start(bf16[8,3,128,1,64]{2,4,3,1,0:T(8,128)(2,1)} %bitcast.106), calls=%async_computation.2 | async-start | bytes 786432 | tf_op jit(solution)/shard_map/all_to_all | solution.py:154
  273.6 31.1 %collective-permute-start.45 = (bf16[2,2,2,2,24,896]{5,4,3,2,1,0:T(8,128)(2,1)}, bf16[2,2,2,2,24,896]{5,4,3,2,1,0:T(8,128)(2,1)S(1)}, u32[]{:S(2)}, u32[]{:S(2)}) collective-permute-start(bf16[2,2,2,2,24,896]{5,4,3,2,1,0:T(8,128)(2,1)} %fusion.52), channel_id=1, source_target_pairs={{0,8},{1,9},{2,10},{3,11},{4,12},{5,13},{6,14},{7,15},{8,0},{9,1},... | collective-permute-start | bytes 2064392 | tf_op jit(solution)/shard_map/ppermute | solution.py:102
  277.7 51.6 %collective-permute-start.50 = (bf16[2,2,2,2,24,3072]{5,4,1,2,3,0:T(8,128)(2,1)}, bf16[2,2,2,2,24,3072]{5,4,1,2,3,0:T(8,128)(2,1)}, u32[]{:S(2)}, u32[]{:S(2)}) collective-permute-start(bf16[2,2,2,2,24,3072]{5,4,1,2,3,0:T(8,128)(2,1)} %fusion.28), channel_id=1, source_target_pairs={{0,8},{1,9},{2,10},{3,11},{4,12},{5,13},{6,14},{7,15},{8,0},{9,1},... | collective-permute-start | bytes 7077896 | tf_op jit(solution)/shard_map/ppermute | solution.py:102
  286.7 48.9 %collective-permute-start.55 = (bf16[2,2,2,2,96,768]{5,4,3,2,1,0:T(8,128)(2,1)}, bf16[2,2,2,2,96,768]{5,4,3,2,1,0:T(8,128)(2,1)}, u32[]{:S(2)}, u32[]{:S(2)}) collective-permute-start(bf16[2,2,2,2,96,768]{5,4,3,2,1,0:T(8,128)(2,1)} %fusion.27), channel_id=1, source_target_pairs={{0,8},{1,9},{2,10},{3,11},{4,12},{5,13},{6,14},{7,15},{8,0},{9,1},... | collective-permute-start | bytes 7077896 | tf_op jit(solution)/shard_map/ppermute | solution.py:102
  312.7 34.0 %all-to-all-start.3 = ((bf16[8,3,128,3,64]{2,4,3,1,0:T(8,128)(2,1)}), bf16[8,3,128,3,64]{2,4,3,1,0:T(8,128)(2,1)}, u32[]{:S(2)}, u32[]{:S(2)}) async-start(bf16[8,3,128,3,64]{2,4,3,1,0:T(8,128)(2,1)} %maximum_bitcast_fusion), calls=%async_computation.3 | async-start | bytes 2359296 | tf_op jit(solution)/shard_map/all_to_all | solution.py:164
  334.4 59.8 %collective-permute-start.51 = (bf16[2,2,2,24,3072]{4,3,0,1,2:T(8,128)(2,1)}, bf16[2,2,2,24,3072]{4,3,0,1,2:T(8,128)(2,1)}, u32[]{:S(2)}, u32[]{:S(2)}) collective-permute-start(bf16[2,2,2,24,3072]{4,3,0,1,2:T(8,128)(2,1)} %fusion.45), channel_id=1, source_target_pairs={{0,16},{1,17},{2,18},{3,19},{4,20},{5,21},{6,22},{7,23},{8,24},{9,... | collective-permute-start | bytes 3538952 | tf_op jit(solution)/shard_map/ppermute | solution.py:102
  341.7 55.0 %collective-permute-start.56 = (bf16[2,2,2,96,768]{4,3,2,1,0:T(8,128)(2,1)}, bf16[2,2,2,96,768]{4,3,2,1,0:T(8,128)(2,1)}, u32[]{:S(2)}, u32[]{:S(2)}) collective-permute-start(bf16[2,2,2,96,768]{4,3,2,1,0:T(8,128)(2,1)} %fusion.46), channel_id=1, source_target_pairs={{0,1},{1,0},{2,3},{3,2},{4,5},{5,4},{6,7},{7,6},{8,9},{9,8},{10,11... | collective-permute-start | bytes 3538952 | tf_op jit(solution)/shard_map/ppermute | solution.py:102
  374.4 19.5 %collective-permute-start.30 = (bf16[2,2,2,2,24,896]{5,4,3,2,1,0:T(8,128)(2,1)}, bf16[2,2,2,2,24,896]{5,4,3,2,1,0:T(8,128)(2,1)S(1)}, u32[]{:S(2)}, u32[]{:S(2)}) collective-permute-start(bf16[2,2,2,2,24,896]{5,4,3,2,1,0:T(8,128)(2,1)} %fusion.51), channel_id=1, source_target_pairs={{0,8},{1,9},{2,10},{3,11},{4,12},{5,13},{6,14},{7,15},{8,0},{9,1},... | collective-permute-start | bytes 2064392 | tf_op jit(solution)/shard_map/ppermute | solution.py:102
  396.0 43.0 %collective-permute-start.52 = (bf16[2,2,24,3072]{3,2,0,1:T(8,128)(2,1)S(1)}, bf16[2,2,24,3072]{3,2,0,1:T(8,128)(2,1)S(1)}, u32[]{:S(2)}, u32[]{:S(2)}) collective-permute-start(bf16[2,2,24,3072]{3,2,0,1:T(8,128)(2,1)S(1)} %fusion.53), channel_id=1, source_target_pairs={{0,1},{1,0},{2,3},{3,2},{4,5},{5,4},{6,7},{7,6},{8,9},{9,8},{10,11... | collective-permute-start | bytes 1769480 | tf_op jit(solution)/shard_map/ppermute | solution.py:102
  398.4 40.9 %collective-permute-start.57 = (bf16[2,2,96,768]{3,2,1,0:T(8,128)(2,1)S(1)}, bf16[2,2,96,768]{3,2,1,0:T(8,128)(2,1)S(1)}, u32[]{:S(2)}, u32[]{:S(2)}) collective-permute-start(bf16[2,2,96,768]{3,2,1,0:T(8,128)(2,1)S(1)} %fusion.54), channel_id=1, source_target_pairs={{0,2},{1,3},{2,0},{3,1},{4,6},{5,7},{6,4},{7,5},{8,10},{9,11},{10,... | collective-permute-start | bytes 1769480 | tf_op jit(solution)/shard_map/ppermute | solution.py:102
  400.5 19.4 %collective-permute-start.42 = (bf16[2,2,24,768]{3,2,1,0:T(8,128)(2,1)S(1)}, bf16[2,2,24,768]{3,2,1,0:T(8,128)(2,1)S(1)}, u32[]{:S(2)}, u32[]{:S(2)}) collective-permute-start(bf16[2,2,24,768]{3,2,1,0:T(8,128)(2,1)S(1)} %fusion.77), channel_id=1, source_target_pairs={{0,2},{1,3},{2,0},{3,1},{4,6},{5,7},{6,4},{7,5},{8,10},{9,11},{10,... | collective-permute-start | bytes 442376 | tf_op jit(solution)/shard_map/ppermute | solution.py:102
  402.3 18.9 %collective-permute-start.37 = (bf16[2,2,24,768]{3,2,0,1:T(8,128)(2,1)S(1)}, bf16[2,2,24,768]{3,2,0,1:T(8,128)(2,1)S(1)}, u32[]{:S(2)}, u32[]{:S(2)}) collective-permute-start(bf16[2,2,24,768]{3,2,0,1:T(8,128)(2,1)S(1)} %fusion.76), channel_id=1, source_target_pairs={{0,1},{1,0},{2,3},{3,2},{4,5},{5,4},{6,7},{7,6},{8,9},{9,8},{10,11... | collective-permute-start | bytes 442376 | tf_op jit(solution)/shard_map/ppermute | solution.py:102
  405.2 22.3 %collective-permute-start.32 = (bf16[2,2,24,896]{3,2,1,0:T(8,128)(2,1)S(1)}, bf16[2,2,24,896]{3,2,1,0:T(8,128)(2,1)S(1)}, u32[]{:S(2)}, u32[]{:S(2)}) collective-permute-start(bf16[2,2,24,896]{3,2,1,0:T(8,128)(2,1)S(1)} %fusion.74), channel_id=1, source_target_pairs={{0,16},{1,17},{2,18},{3,19},{4,20},{5,21},{6,22},{7,23},{8,24},{9,... | collective-permute-start | bytes 516104 | tf_op jit(solution)/shard_map/ppermute | solution.py:102
  (112 other events, 1086.6 us)

commit v4 on v3

--- a/solution.py
+++ b/solution.py
@@ -373,7 +373,7 @@
         )[:, :, 0]
         qkv_grad_u = unit_backward(uq, uk, uv, weights, totals, attended_u, grad_units)
         proj_grad = units_to_rows(qkv_grad_u, seq_count, micro, 3)
-        backward_anchors = [None, grad_units, qkv_grad_u, proj_grad, proj_grad]
+        backward_anchors = [None, None, grad_units, qkv_grad_u, qkv_grad_u]
     else:
         proj_grad = fallback_attention_backward(saved, attended_grad, row_count)
         backward_anchors = [None] + [proj_grad] * (steps - 1)

time: 468 us -> 475 us (1.015)
  waiting for transfers between devices: 130 us -> 144 us
  local copies, waits for them, and re-layouts: 102 us -> 92.1 us
    all_to_all x2, waiting for transfers between devices: 4.04 us -> 14 us  [units_to_rows(): x = lax.all_to_all(x, 'seq', 0, 0, tiled=True)]
    unnamed x153 -> x165, local copies, waits for them, and re-layouts: 16.7 us -> 10.8 us
    ppermute x30, waiting for transfers between devices: 47.1 us -> 52.3 us  [reduce_routes(): got = lax.ppermute(send, ALL, partner_pairs(count, b))]
  transfers between devices with their start and end apart: 64 -> 64, of which waited for: 30 -> 30; matrix products, arithmetic and copies ran while one was open for 38% -> 35% of each run, Pallas kernels for 0% -> 0%
where the time goes in v4:
time: 475 us; the launch traced here: 467 us
  waiting for transfers between devices  144 us (30%)
  local copies, waits for them, and re-layouts  92.1 us (19%)
  other arithmetic  82.4 us (17%)
  starting transfers between devices  79.8 us (17%)
  matrix products  65.5 us (14%)
    ppermute x30, waiting for transfers between devices, gather_routes(): got = lax.ppermute(x, ALL, partner_pairs(count, b))  78.1 us
    ppermute x30, waiting for transfers between devices, reduce_routes(): got = lax.ppermute(send, ALL, partner_pairs(count, b))  52.3 us
    ppermute x30, starting transfers between devices, gather_routes(): got = lax.ppermute(x, ALL, partner_pairs(count, b))  34.5 us
    ppermute x30, starting transfers between devices, reduce_routes(): got = lax.ppermute(send, ALL, partner_pairs(count, b))  28.5 us
    another operation x30, other arithmetic, gather_routes(): x = jnp.stack([x, got])  27.8 us
    add x30, other arithmetic, reduce_routes(): x = keep + got.astype(jnp.float32)  18.1 us
    dot_general x6, matrix products, outer_rows(): lax.dot_general(left, right, (((0,), (0,)), ((), ())), preferred_element_...  16.4 us
    convert_element_type x30, local copies, waits for them, and re-layouts, reduce_routes(): lax.dynamic_index_in_dim(x, 1 - mine, axis, keepdims=False)  16.4 us
  transfers between devices with their start and end apart: 64, of which 30 were waited for; matrix products, arithmetic and copies ran while one was open for 35% of the time, Pallas kernels for 0%

profile of v4, /device:TPU:0, one launch (start us, length us, event | category | flops | bytes accessed | tf_op | source)
XLA Modules:
  0.0 467.2 jit_solution(1219653960471942100)
XLA Ops:
  8.3 4.1 collective-permute-start
  62.7 4.3 all-to-all-start
  73.1 33.3 %collective-permute-done.25 = bf16[96,768]{1,0:T(8,128)(2,1)S(1)} collective-permute-done((bf16[96,768]{1,0:T(8,128)(2,1)S(1)}, bf16[96,768]{1,0:T(8,128)(2,1)S(1)}, u32[]{:S(2)}, u32[]{:S(2)}) %collective-permute-start.25) | collective-permute-done | bytes 147488 | tf_op jit(solution)/shard_map/ppermute | solution.py:77
  115.2 6.2 %fusion.123 = (f32[3,1024]{1,0:T(4,128)S(1)}, f32[3,1024,1024]{1,2,0:T(8,128)S(1)}) fusion(bf16[3,1024,3,64]{1,3,0,2:T(8,128)(2,1)S(1)} %reshape.745, pred[3,1024]{1,0:T(4,128)(4,1)S(1)} %broadcast_compare_fusion, s32[3,1024]{1,0:T(4,128)} %broadcast_add_fusion, pred[1024,1024]{0,1:T(8,128)(4,1)} %iota_compare_fusion), kind=kOutput, calls=%fused_computation.349 | convolution fusion | flops 421524480 | bytes 14467072 | tf_op jit(solution)/shard_map/uqd,ukd->uqk/dot_general | solution.py:172
  127.3 8.9 %collective-permute-done.27 = bf16[2,2,96,768]{3,2,1,0:T(8,128)(2,1)S(1)} collective-permute-done((bf16[2,2,96,768]{3,2,1,0:T(8,128)(2,1)S(1)}, bf16[2,2,96,768]{3,2,1,0:T(8,128)(2,1)S(1)}, u32[]{:S(2)}, u32[]{:S(2)}) %collective-permute-start.27) | collective-permute-done | bytes 589856 | tf_op jit(solution)/shard_map/ppermute | solution.py:77
  144.4 20.2 %collective-permute-done.16 = bf16[2,24,768]{2,1,0:T(8,128)(2,1)S(1)} collective-permute-done((bf16[2,24,768]{2,1,0:T(8,128)(2,1)S(1)}, bf16[2,24,768]{2,1,0:T(8,128)(2,1)S(1)}, u32[]{:S(2)}, u32[]{:S(2)}) %collective-permute-start.16) | collective-permute-done | bytes 73760 | tf_op jit(solution)/shard_map/ppermute | solution.py:77
  178.3 4.6 all-to-all-start.1
  200.4 4.9 %pad_maximum_fusion.1 = bf16[2,2,2,2,2,96,768]{6,5,4,3,2,1,0:T(8,128)(2,1)} fusion(bf16[1,2,2,2,2,96,768]{6,5,4,3,2,1,0:T(8,128)(2,1)} %bitcast.96, bf16[1,2,2,2,2,96,768]{6,5,4,3,2,1,0:T(8,128)(2,1)} %bitcast.95), kind=kLoop, calls=%fused_computation.12 | loop fusion | flops 2359296 | bytes 9437184 | tf_op jit(solution)/shard_map/stack | solution.py:78
  205.3 5.5 %gather_fusion.3 = bf16[32,96,768]{2,1,0:T(8,128)(2,1)} fusion(bf16[32,96,768]{2,1,0:T(8,128)(2,1)} %bitcast.482, s32[1024]{0:T(1024)} %pad_clamp_fusion), kind=kCustom, calls=%fused_computation.6 | custom fusion | bytes 9437312 | tf_op jit(solution)/shard_map/jit(_take)/gather | solution.py:82
  210.8 5.0 %broadcast_select_fusion = bf16[32,96,768]{2,1,0:T(8,128)(2,1)} fusion(bf16[32,96,768]{2,1,0:T(8,128)(2,1)} %gather_fusion.3, pred[32]{0:T(512)(128)(4,1)S(1)} %copy-done.58), kind=kLoop, calls=%fused_computation.19 | loop fusion | flops 2359296 | bytes 9437216 | tf_op jit(solution)/shard_map/jit(_take)/select_n | solution.py:82
  215.8 5.0 %pad_maximum_fusion = bf16[2,2,2,2,2,24,3072]{6,5,4,3,2,1,0:T(8,128)(2,1)} fusion(bf16[1,2,2,2,2,24,3072]{6,5,4,3,2,1,0:T(8,128)(2,1)} %bitcast.83, bf16[1,2,2,2,2,24,3072]{6,5,4,3,2,1,0:T(8,128)(2,1)} %bitcast.82), kind=kLoop, calls=%fused_computation.11 | loop fusion | flops 2359296 | bytes 9437184 | tf_op jit(solution)/shard_map/stack | solution.py:78
  220.8 5.5 %gather_fusion.2 = bf16[32,24,3072]{2,1,0:T(8,128)(2,1)} fusion(bf16[32,24,3072]{2,1,0:T(8,128)(2,1)} %bitcast.483, s32[1024]{0:T(1024)} %pad_clamp_fusion.1), kind=kCustom, calls=%fused_computation.5 | custom fusion | bytes 9437312 | tf_op jit(solution)/shard_map/jit(_take)/gather | solution.py:82
  229.2 8.0 %fusion = (f32[256,3072]{1,0:T(8,128)S(1)}, f32[256,3072]{1,0:T(8,128)S(1)}) fusion(f32[3072]{0:T(1024)S(1)} %copy-done.52, bf16[768,3072]{1,0:T(8,128)(2,1)S(1)} %bitcast_select_fusion.1, f32[256,768]{1,0:T(8,128)S(1)} %get-tuple-element.197, f32[768]{0:T(1024)S(1)} %get-tuple-element.127, f32[768]{0:T(1024)S(1)} %get-tuple-element.128, ...), kind=kOutput, calls=%fused_computation.23 | convolution fusion | flops 1258487808 | bytes 11816960 | tf_op jit(solution)/shard_map/dot_general | solution.py:343
  242.2 5.2 %fusion.117 = f32[768,3072]{1,0:T(8,128)} fusion(bf16[256,3072]{1,0:T(8,128)(2,1)S(1)} %get-tuple-element.203, f32[256,768]{1,0:T(8,128)S(1)} %get-tuple-element.197, f32[768]{0:T(1024)S(1)} %get-tuple-element.127, f32[768]{0:T(1024)S(1)} %get-tuple-element.128, f32[256]{0:T(256)S(1)} %fusion.89, f32[256]{0:T(256)S(1)} %broadcast_multiply_fusion), kind=kOutput, calls=%fused_computation.344 | convolution fusion | flops 1208942592 | bytes 11804672 | tf_op jit(solution)/shard_map/dot_general | solution.py:36
  247.4 7.5 %fusion.3 = bf16[3072,256]{0,1:T(8,128)(2,1)} fusion(f32[256,3072]{1,0:T(8,128)S(1)} %get-tuple-element.199), kind=kLoop, calls=%fused_computation.26 | loop fusion | flops 51118080 | bytes 4718592 | tf_op jit(solution)/shard_map/convert_element_type | solution.py:347
  259.6 4.1 all-to-all-start.2
  268.5 4.3 concatenate.50
  293.9 7.5 %fusion.41 = bf16[3,1024,64]{1,2,0:T(8,128)(2,1)} fusion(f32[3,1024,1024]{1,2,0:T(8,128)} %copy-done.2, bf16[3,1024,64]{1,2,0:T(8,128)(2,1)S(1)} %squeeze_reshape.3, f32[3,1024]{1,0:T(4,128)} %copy-done.38), kind=kOutput, calls=%fused_computation.96 | convolution fusion | flops 406585344 | bytes 13381632 | tf_op jit(solution)/shard_map/uqk,uqd->ukd/dot_general | solution.py:190
  301.6 6.6 %multiply_convert_fusion = bf16[3,1024,1024]{1,2,0:T(8,128)(2,1)S(1)} fusion(f32[3,1024,1024]{1,2,0:T(8,128)} %copy-done.2, f32[3,1024]{1,0:T(4,128)S(1)} %div.84, bf16[3,1024,3,64]{1,3,0,2:T(8,128)(2,1)S(1)} %copy-done.16, bf16[3,1024,64]{1,2,0:T(8,128)(2,1)S(1)} %squeeze_reshape.3, f32[3,1024]{1,0:T(4,128)S(1)} %copy-done.39), kind=kOutput, calls=%fused_computation.7 | convolution fusion | flops 412680192 | bytes 19693568 | tf_op jit(solution)/shard_map/uqd,ukd->uqk/dot_general | solution.py:186
  313.5 6.7 %collective-permute-done.46 = bf16[2,2,2,24,896]{4,3,2,1,0:T(8,128)(2,1)S(1)} collective-permute-done((bf16[2,2,2,24,896]{4,3,2,1,0:T(8,128)(2,1)S(1)}, bf16[2,2,2,24,896]{4,3,2,1,0:T(8,128)(2,1)S(1)}, u32[]{:S(2)}, u32[]{:S(2)}) %collective-permute-start.46) | collective-permute-done | bytes 344096 | tf_op jit(solution)/shard_map/ppermute | solution.py:102
  357.0 11.3 %all-to-all-done.3 = bf16[8,3,128,3,64]{2,4,3,1,0:T(8,128)(2,1)S(1)} async-done(((bf16[8,3,128,3,64]{2,4,3,1,0:T(8,128)(2,1)}), bf16[8,3,128,3,64]{2,4,3,1,0:T(8,128)(2,1)S(1)}, u32[]{:S(2)}, u32[]{:S(2)}) %all-to-all-start.3) | async-done | bytes 1179680 | tf_op jit(solution)/shard_map/all_to_all | solution.py:164
  413.8 13.5 %collective-permute-done.42 = bf16[2,2,24,768]{3,2,1,0:T(8,128)(2,1)S(1)} collective-permute-done((bf16[2,2,24,768]{3,2,1,0:T(8,128)(2,1)S(1)}, bf16[2,2,24,768]{3,2,1,0:T(8,128)(2,1)S(1)}, u32[]{:S(2)}, u32[]{:S(2)}) %collective-permute-start.42) | collective-permute-done | bytes 147488 | tf_op jit(solution)/shard_map/ppermute | solution.py:102
  448.0 7.1 %collective-permute-done.53 = bf16[2,24,3072]{2,1,0:T(8,128)(2,1)S(1)} collective-permute-done((bf16[2,24,3072]{2,1,0:T(8,128)(2,1)S(1)}, bf16[2,24,3072]{2,1,0:T(8,128)(2,1)S(1)}, u32[]{:S(2)}, u32[]{:S(2)}) %collective-permute-start.53) | collective-permute-done | bytes 294944 | tf_op jit(solution)/shard_map/ppermute | solution.py:102
  458.3 6.0 %collective-permute-done.54 = bf16[24,3072]{1,0:T(8,128)(2,1)S(1)} collective-permute-done((bf16[24,3072]{1,0:T(8,128)(2,1)S(1)}, bf16[24,3072]{1,0:T(8,128)(2,1)S(1)}, u32[]{:S(2)}, u32[]{:S(2)}) %collective-permute-start.54) | collective-permute-done | bytes 147488 | tf_op jit(solution)/shard_map/ppermute | solution.py:102
  (510 shorter events, 268.9 us)
Async XLA Ops:
  8.3 12.8 %collective-permute-start = (bf16[24,896]{1,0:T(8,128)(2,1)S(1)}, bf16[24,896]{1,0:T(8,128)(2,1)S(1)}, u32[]{:S(2)}, u32[]{:S(2)}) collective-permute-start(bf16[24,896]{1,0:T(8,128)(2,1)S(1)} %concatenate.37), channel_id=1, source_target_pairs={{0,4},{1,5},{2,6},{3,7},{4,0},{5,1},{6,2},{7,3},{8,12},{9,13},{10,... | collective-permute-start | bytes 129032 | tf_op jit(solution)/shard_map/ppermute | solution.py:77
  62.7 47.1 %all-to-all-start = ((bf16[8,3,128,3,64]{2,4,3,1,0:T(8,128)(2,1)}), bf16[8,3,128,3,64]{2,4,3,1,0:T(8,128)(2,1)S(1)}, u32[]{:S(2)}, u32[]{:S(2)}) async-start(bf16[8,3,128,3,64]{2,4,3,1,0:T(8,128)(2,1)} %bitcast.518), calls=%async_computation | async-start | bytes 2359296 | tf_op jit(solution)/shard_map/all_to_all | solution.py:154
  68.9 37.6 %collective-permute-start.25 = (bf16[96,768]{1,0:T(8,128)(2,1)S(1)}, bf16[96,768]{1,0:T(8,128)(2,1)S(1)}, u32[]{:S(2)}, u32[]{:S(2)}) collective-permute-start(bf16[96,768]{1,0:T(8,128)(2,1)S(1)} %copy-done.40), channel_id=1, source_target_pairs={{0,4},{1,5},{2,6},{3,7},{4,0},{5,1},{6,2},{7,3},{8,12},{9,13},{10,... | collective-permute-start | bytes 442376 | tf_op jit(solution)/shard_map/ppermute | solution.py:77
  71.8 37.1 %collective-permute-start.20 = (bf16[24,3072]{1,0:T(8,128)(2,1)}, bf16[24,3072]{1,0:T(8,128)(2,1)S(1)}, u32[]{:S(2)}, u32[]{:S(2)}) collective-permute-start(bf16[24,3072]{1,0:T(8,128)(2,1)} %param.30), channel_id=1, source_target_pairs={{0,4},{1,5},{2,6},{3,7},{4,0},{5,1},{6,2},{7,3},{8,12},{9,13},{10,... | collective-permute-start | bytes 442376 | tf_op jit(solution)/shard_map/ppermute | solution.py:77
  122.4 13.8 %collective-permute-start.27 = (bf16[2,2,96,768]{3,2,1,0:T(8,128)(2,1)S(1)}, bf16[2,2,96,768]{3,2,1,0:T(8,128)(2,1)S(1)}, u32[]{:S(2)}, u32[]{:S(2)}) collective-permute-start(bf16[2,2,96,768]{3,2,1,0:T(8,128)(2,1)S(1)} %pad_maximum_fusion.17), channel_id=1, source_target_pairs={{0,2},{1,3},{2,0},{3,1},{4,6},{5,7},{6,4},{7,5},{8,10},{9,11},{10,... | collective-permute-start | bytes 1769480 | tf_op jit(solution)/shard_map/ppermute | solution.py:77
  123.6 17.2 %collective-permute-start.22 = (bf16[2,2,24,3072]{3,2,1,0:T(8,128)(2,1)S(1)}, bf16[2,2,24,3072]{3,2,1,0:T(8,128)(2,1)S(1)}, u32[]{:S(2)}, u32[]{:S(2)}) collective-permute-start(bf16[2,2,24,3072]{3,2,1,0:T(8,128)(2,1)S(1)} %pad_maximum_fusion.16), channel_id=1, source_target_pairs={{0,1},{1,0},{2,3},{3,2},{4,5},{5,4},{6,7},{7,6},{8,9},{9,8},{10,11... | collective-permute-start | bytes 1769480 | tf_op jit(solution)/shard_map/ppermute | solution.py:77
  137.3 35.7 %collective-permute-start.28 = (bf16[2,2,2,96,768]{4,3,2,1,0:T(8,128)(2,1)}, bf16[2,2,2,96,768]{4,3,2,1,0:T(8,128)(2,1)}, u32[]{:S(2)}, u32[]{:S(2)}) collective-permute-start(bf16[2,2,2,96,768]{4,3,2,1,0:T(8,128)(2,1)} %pad_maximum_fusion.10), channel_id=1, source_target_pairs={{0,1},{1,0},{2,3},{3,2},{4,5},{5,4},{6,7},{7,6},{8,9},{9,8},{10,11... | collective-permute-start | bytes 3538952 | tf_op jit(solution)/shard_map/ppermute | solution.py:77
  142.0 42.4 %collective-permute-start.23 = (bf16[2,2,2,24,3072]{4,3,2,1,0:T(8,128)(2,1)}, bf16[2,2,2,24,3072]{4,3,2,1,0:T(8,128)(2,1)}, u32[]{:S(2)}, u32[]{:S(2)}) collective-permute-start(bf16[2,2,2,24,3072]{4,3,2,1,0:T(8,128)(2,1)} %pad_maximum_fusion.9), channel_id=1, source_target_pairs={{0,16},{1,17},{2,18},{3,19},{4,20},{5,21},{6,22},{7,23},{8,24},{9,... | collective-permute-start | bytes 3538952 | tf_op jit(solution)/shard_map/ppermute | solution.py:77
  143.6 21.0 %collective-permute-start.16 = (bf16[2,24,768]{2,1,0:T(8,128)(2,1)S(1)}, bf16[2,24,768]{2,1,0:T(8,128)(2,1)S(1)}, u32[]{:S(2)}, u32[]{:S(2)}) collective-permute-start(bf16[2,24,768]{2,1,0:T(8,128)(2,1)S(1)} %pad_maximum_fusion.32), channel_id=1, source_target_pairs={{0,1},{1,0},{2,3},{3,2},{4,5},{5,4},{6,7},{7,6},{8,9},{9,8},{10,11... | collective-permute-start | bytes 221192 | tf_op jit(solution)/shard_map/ppermute | solution.py:77
  176.3 24.1 %collective-permute-start.29 = (bf16[2,2,2,2,96,768]{5,4,3,2,1,0:T(8,128)(2,1)}, bf16[2,2,2,2,96,768]{5,4,3,2,1,0:T(8,128)(2,1)}, u32[]{:S(2)}, u32[]{:S(2)}) collective-permute-start(bf16[2,2,2,2,96,768]{5,4,3,2,1,0:T(8,128)(2,1)} %pad_maximum_fusion.3), channel_id=1, source_target_pairs={{0,8},{1,9},{2,10},{3,11},{4,12},{5,13},{6,14},{7,15},{8,0},{9,1},... | collective-permute-start | bytes 7077896 | tf_op jit(solution)/shard_map/ppermute | solution.py:77
  178.3 16.5 %all-to-all-start.1 = ((bf16[8,3,128,1,64]{2,4,3,1,0:T(8,128)(2,1)}), bf16[8,3,128,1,64]{2,4,3,1,0:T(8,128)(2,1)S(1)}, u32[]{:S(2)}, u32[]{:S(2)}) async-start(bf16[8,3,128,1,64]{2,4,3,1,0:T(8,128)(2,1)} %bitcast.476), calls=%async_computation.1 | async-start | bytes 786432 | tf_op jit(solution)/shard_map/all_to_all | solution.py:164
  187.6 28.1 %collective-permute-start.24 = (bf16[2,2,2,2,24,3072]{5,4,3,2,1,0:T(8,128)(2,1)}, bf16[2,2,2,2,24,3072]{5,4,3,2,1,0:T(8,128)(2,1)}, u32[]{:S(2)}, u32[]{:S(2)}) collective-permute-start(bf16[2,2,2,2,24,3072]{5,4,3,2,1,0:T(8,128)(2,1)} %pad_maximum_fusion.2), channel_id=1, source_target_pairs={{0,8},{1,9},{2,10},{3,11},{4,12},{5,13},{6,14},{7,15},{8,0},{9,1},... | collective-permute-start | bytes 7077896 | tf_op jit(solution)/shard_map/ppermute | solution.py:77
  259.6 32.8 %all-to-all-start.2 = ((bf16[8,3,128,1,64]{2,4,3,1,0:T(8,128)(2,1)}), bf16[8,3,128,1,64]{2,4,3,1,0:T(8,128)(2,1)}, u32[]{:S(2)}, u32[]{:S(2)}) async-start(bf16[8,3,128,1,64]{2,4,3,1,0:T(8,128)(2,1)} %bitcast.106), calls=%async_computation.2 | async-start | bytes 786432 | tf_op jit(solution)/shard_map/all_to_all | solution.py:154
  275.0 33.2 %collective-permute-start.45 = (bf16[2,2,2,2,24,896]{5,4,3,2,1,0:T(8,128)(2,1)}, bf16[2,2,2,2,24,896]{5,4,3,2,1,0:T(8,128)(2,1)}, u32[]{:S(2)}, u32[]{:S(2)}) collective-permute-start(bf16[2,2,2,2,24,896]{5,4,3,2,1,0:T(8,128)(2,1)} %fusion.52), channel_id=1, source_target_pairs={{0,8},{1,9},{2,10},{3,11},{4,12},{5,13},{6,14},{7,15},{8,0},{9,1},... | collective-permute-start | bytes 2064392 | tf_op jit(solution)/shard_map/ppermute | solution.py:102
  279.1 64.0 %collective-permute-start.50 = (bf16[2,2,2,2,24,3072]{5,4,1,2,3,0:T(8,128)(2,1)}, bf16[2,2,2,2,24,3072]{5,4,1,2,3,0:T(8,128)(2,1)}, u32[]{:S(2)}, u32[]{:S(2)}) collective-permute-start(bf16[2,2,2,2,24,3072]{5,4,1,2,3,0:T(8,128)(2,1)} %fusion.28), channel_id=1, source_target_pairs={{0,8},{1,9},{2,10},{3,11},{4,12},{5,13},{6,14},{7,15},{8,0},{9,1},... | collective-permute-start | bytes 7077896 | tf_op jit(solution)/shard_map/ppermute | solution.py:102
  289.2 59.8 %collective-permute-start.55 = (bf16[2,2,2,2,96,768]{5,4,3,2,1,0:T(8,128)(2,1)}, bf16[2,2,2,2,96,768]{5,4,3,2,1,0:T(8,128)(2,1)}, u32[]{:S(2)}, u32[]{:S(2)}) collective-permute-start(bf16[2,2,2,2,96,768]{5,4,3,2,1,0:T(8,128)(2,1)} %fusion.27), channel_id=1, source_target_pairs={{0,8},{1,9},{2,10},{3,11},{4,12},{5,13},{6,14},{7,15},{8,0},{9,1},... | collective-permute-start | bytes 7077896 | tf_op jit(solution)/shard_map/ppermute | solution.py:102
  337.2 31.1 %all-to-all-start.3 = ((bf16[8,3,128,3,64]{2,4,3,1,0:T(8,128)(2,1)}), bf16[8,3,128,3,64]{2,4,3,1,0:T(8,128)(2,1)S(1)}, u32[]{:S(2)}, u32[]{:S(2)}) async-start(bf16[8,3,128,3,64]{2,4,3,1,0:T(8,128)(2,1)} %maximum_bitcast_fusion), calls=%async_computation.3 | async-start | bytes 2359296 | tf_op jit(solution)/shard_map/all_to_all | solution.py:164
  348.0 53.6 %collective-permute-start.51 = (bf16[2,2,2,24,3072]{4,3,0,1,2:T(8,128)(2,1)}, bf16[2,2,2,24,3072]{4,3,0,1,2:T(8,128)(2,1)}, u32[]{:S(2)}, u32[]{:S(2)}) collective-permute-start(bf16[2,2,2,24,3072]{4,3,0,1,2:T(8,128)(2,1)} %fusion.45), channel_id=1, source_target_pairs={{0,16},{1,17},{2,18},{3,19},{4,20},{5,21},{6,22},{7,23},{8,24},{9,... | collective-permute-start | bytes 3538952 | tf_op jit(solution)/shard_map/ppermute | solution.py:102
  355.1 49.1 %collective-permute-start.56 = (bf16[2,2,2,96,768]{4,3,2,1,0:T(8,128)(2,1)}, bf16[2,2,2,96,768]{4,3,2,1,0:T(8,128)(2,1)}, u32[]{:S(2)}, u32[]{:S(2)}) collective-permute-start(bf16[2,2,2,96,768]{4,3,2,1,0:T(8,128)(2,1)} %fusion.46), channel_id=1, source_target_pairs={{0,1},{1,0},{2,3},{3,2},{4,5},{5,4},{6,7},{7,6},{8,9},{9,8},{10,11... | collective-permute-start | bytes 3538952 | tf_op jit(solution)/shard_map/ppermute | solution.py:102
  403.4 42.9 %collective-permute-start.52 = (bf16[2,2,24,3072]{3,2,0,1:T(8,128)(2,1)S(1)}, bf16[2,2,24,3072]{3,2,0,1:T(8,128)(2,1)S(1)}, u32[]{:S(2)}, u32[]{:S(2)}) collective-permute-start(bf16[2,2,24,3072]{3,2,0,1:T(8,128)(2,1)S(1)} %fusion.53), channel_id=1, source_target_pairs={{0,1},{1,0},{2,3},{3,2},{4,5},{5,4},{6,7},{7,6},{8,9},{9,8},{10,11... | collective-permute-start | bytes 1769480 | tf_op jit(solution)/shard_map/ppermute | solution.py:102
  405.8 40.8 %collective-permute-start.57 = (bf16[2,2,96,768]{3,2,1,0:T(8,128)(2,1)S(1)}, bf16[2,2,96,768]{3,2,1,0:T(8,128)(2,1)S(1)}, u32[]{:S(2)}, u32[]{:S(2)}) collective-permute-start(bf16[2,2,96,768]{3,2,1,0:T(8,128)(2,1)S(1)} %fusion.54), channel_id=1, source_target_pairs={{0,2},{1,3},{2,0},{3,1},{4,6},{5,7},{6,4},{7,5},{8,10},{9,11},{10,... | collective-permute-start | bytes 1769480 | tf_op jit(solution)/shard_map/ppermute | solution.py:102
  408.0 19.3 %collective-permute-start.42 = (bf16[2,2,24,768]{3,2,1,0:T(8,128)(2,1)S(1)}, bf16[2,2,24,768]{3,2,1,0:T(8,128)(2,1)S(1)}, u32[]{:S(2)}, u32[]{:S(2)}) collective-permute-start(bf16[2,2,24,768]{3,2,1,0:T(8,128)(2,1)S(1)} %fusion.77), channel_id=1, source_target_pairs={{0,2},{1,3},{2,0},{3,1},{4,6},{5,7},{6,4},{7,5},{8,10},{9,11},{10,... | collective-permute-start | bytes 442376 | tf_op jit(solution)/shard_map/ppermute | solution.py:102
  409.6 18.9 %collective-permute-start.37 = (bf16[2,2,24,768]{3,2,0,1:T(8,128)(2,1)S(1)}, bf16[2,2,24,768]{3,2,0,1:T(8,128)(2,1)S(1)}, u32[]{:S(2)}, u32[]{:S(2)}) collective-permute-start(bf16[2,2,24,768]{3,2,0,1:T(8,128)(2,1)S(1)} %fusion.76), channel_id=1, source_target_pairs={{0,1},{1,0},{2,3},{3,2},{4,5},{5,4},{6,7},{7,6},{8,9},{9,8},{10,11... | collective-permute-start | bytes 442376 | tf_op jit(solution)/shard_map/ppermute | solution.py:102
  412.6 22.3 %collective-permute-start.32 = (bf16[2,2,24,896]{3,2,1,0:T(8,128)(2,1)S(1)}, bf16[2,2,24,896]{3,2,1,0:T(8,128)(2,1)S(1)}, u32[]{:S(2)}, u32[]{:S(2)}) collective-permute-start(bf16[2,2,24,896]{3,2,1,0:T(8,128)(2,1)S(1)} %fusion.74), channel_id=1, source_target_pairs={{0,16},{1,17},{2,18},{3,19},{4,20},{5,21},{6,22},{7,23},{8,24},{9,... | collective-permute-start | bytes 516104 | tf_op jit(solution)/shard_map/ppermute | solution.py:102
  (118 other events, 1212.1 us)

commit v5 on v3

--- a/solution.py
+++ b/solution.py
@@ -271,6 +271,7 @@
     vecs_local = vector_block(
         [ln1_g, ln1_b, b_q, b_v, b_out, ln2_g, ln2_b, b_down, b_up], shard_rows, jnp.bfloat16
     )
+    mlp_pack = jnp.concatenate([w_out, w_up, w_down.reshape(shard_rows, ratio * width)], axis=1)
     qkv_cols = thirds(w_qkv.shape[1])
     qkv_parts = split_cols(w_qkv, qkv_cols)
     gathered = gather_routes(
@@ -328,9 +329,10 @@
         attended_b = attended.astype(jnp.bfloat16)
         forward_anchors = [queries] + [attended] * (steps - 1)
 
-    proj_up, proj_down, proj_out = gather_routes(
-        [w_up, w_down, w_out], orders, count, me, forward_anchors[:steps]
-    )
+    proj_out, proj_up, down_view = split_cols(
+        lax.all_gather(mlp_pack, ALL, axis=0, tiled=True), [width, ff, ff]
+    )
+    proj_down = down_view.reshape(count * shard_rows * ratio, width)
 
     branch = jnp.dot(attended_b, proj_out, preferred_element_type=jnp.float32) + bias_out.astype(
         jnp.float32

time: 468 us -> 424 us (0.906)
  other arithmetic: 84 us -> 50.6 us
  starting transfers between devices: 79.9 us -> 62.7 us
  between operations: 2.92 us -> 15.8 us
  waiting for transfers between devices: 130 us -> 121 us
    ppermute x30 -> x15, waiting for transfers between devices: 78.8 us -> 21.9 us  [gather_routes(): got = lax.ppermute(x, ALL, partner_pairs(count, b))]
    all_to_all x2, waiting for transfers between devices: 0.01 us -> 38.8 us  [rows_to_units(): x = lax.all_to_all(x, 'seq', 0, 0, tiled=True)]
    another operation x30 -> x15, other arithmetic: 24.8 us -> 4.94 us  [gather_routes(): x = jnp.stack([x, got])]
    ppermute x30 -> x15, starting transfers between devices: 34.5 us -> 17.2 us  [gather_routes(): got = lax.ppermute(x, ALL, partner_pairs(count, b))]
    gather x6 -> x3, local copies, waits for them, and re-layouts: 18.1 us -> 4.08 us  [gather_routes(): x = jnp.take(x.reshape(count, rows, cols), rel, axis=0)]
    select_n x10 -> x4, other arithmetic: 15.8 us -> 2.95 us  [gather_routes(): x = jnp.take(x.reshape(count, rows, cols), rel, axis=0)]
    reshape x0 -> x2, local copies, waits for them, and re-layouts: none -> 9.48 us  [the longest x1 8.47 us: body(): proj_down = down_view.reshape(count * shard_rows * ratio, width)]
    all_to_all x2, waiting for transfers between devices: 4.04 us -> 11.7 us  [units_to_rows(): x = lax.all_to_all(x, 'seq', 0, 0, tiled=True)]
  transfers between devices with their start and end apart: 64 -> 50, of which waited for: 30 -> 24; matrix products, arithmetic and copies ran while one was open for 38% -> 38% of each run, Pallas kernels for 0% -> 0%
where the time goes in v5:
time: 424 us; the launch traced here: 416 us
  waiting for transfers between devices  121 us (29%)
  local copies, waits for them, and re-layouts  103 us (24%)
  matrix products  63.5 us (15%)
  starting transfers between devices  62.7 us (15%)
  other arithmetic  50.6 us (12%)
  between operations  15.8 us (4%)
    ppermute x30, waiting for transfers between devices, reduce_routes(): got = lax.ppermute(send, ALL, partner_pairs(count, b))  48.4 us
    all_to_all x2, waiting for transfers between devices, rows_to_units(): x = lax.all_to_all(x, 'seq', 0, 0, tiled=True)  38.8 us
    ppermute x30, starting transfers between devices, reduce_routes(): got = lax.ppermute(send, ALL, partner_pairs(count, b))  25.9 us
    ppermute x15, waiting for transfers between devices, gather_routes(): got = lax.ppermute(x, ALL, partner_pairs(count, b))  21.9 us
    add x30, other arithmetic, reduce_routes(): x = keep + got.astype(jnp.float32)  20.1 us
    convert_element_type x30, local copies, waits for them, and re-layouts, reduce_routes(): lax.dynamic_index_in_dim(x, 1 - mine, axis, keepdims=False)  19 us
    ppermute x15, starting transfers between devices, gather_routes(): got = lax.ppermute(x, ALL, partner_pairs(count, b))  17.2 us
    unnamed x107, local copies, waits for them, and re-layouts  16.4 us
  transfers between devices with their start and end apart: 50, of which 24 were waited for; matrix products, arithmetic and copies ran while one was open for 38% of the time, Pallas kernels for 0%

profile of v5, /device:TPU:0, one launch (start us, length us, event | category | flops | bytes accessed | tf_op | source)
XLA Modules:
  0.0 416.4 jit_solution(13179467457359775343)
XLA Ops:
  17.7 4.1 collective-permute-start
  48.4 5.7 %collective-permute-done.13 = bf16[2,2,2,24,768]{4,3,2,1,0:T(8,128)(2,1)S(1)} collective-permute-done((bf16[2,2,2,24,768]{4,3,2,1,0:T(8,128)(2,1)S(1)}, bf16[2,2,2,24,768]{4,3,2,1,0:T(8,128)(2,1)S(1)}, u32[]{:S(2)}, u32[]{:S(2)}) %collective-permute-start.13) | collective-permute-done | bytes 294944 | tf_op jit(solution)/shard_map/ppermute | solution.py:77
  54.3 4.7 %collective-permute-done.8 = bf16[2,2,2,24,768]{4,3,2,1,0:T(8,128)(2,1)S(1)} collective-permute-done((bf16[2,2,2,24,768]{4,3,2,1,0:T(8,128)(2,1)S(1)}, bf16[2,2,2,24,768]{4,3,2,1,0:T(8,128)(2,1)S(1)}, u32[]{:S(2)}, u32[]{:S(2)}) %collective-permute-start.8) | collective-permute-done | bytes 294944 | tf_op jit(solution)/shard_map/ppermute | solution.py:77
  82.1 6.2 %all-to-all-start = ((bf16[8,3,128,3,64]{2,4,3,1,0:T(8,128)(2,1)}), bf16[8,3,128,3,64]{2,4,3,1,0:T(8,128)(2,1)S(1)}, u32[]{:S(2)}, u32[]{:S(2)}) async-start(bf16[8,3,128,3,64]{2,4,3,1,0:T(8,128)(2,1)} %bitcast.461), calls=%async_computation | async-start | bytes 2359296 | tf_op jit(solution)/shard_map/all_to_all | solution.py:154
  90.9 38.8 %all-to-all-done = bf16[8,3,128,3,64]{2,4,3,1,0:T(8,128)(2,1)S(1)} async-done(((bf16[8,3,128,3,64]{2,4,3,1,0:T(8,128)(2,1)}), bf16[8,3,128,3,64]{2,4,3,1,0:T(8,128)(2,1)S(1)}, u32[]{:S(2)}, u32[]{:S(2)}) %all-to-all-start) | async-done | bytes 1179680 | tf_op jit(solution)/shard_map/all_to_all | solution.py:154
  133.9 6.6 %fusion.130 = (f32[3,1024]{1,0:T(4,128)S(1)}, f32[3,1024,1024]{1,2,0:T(8,128)S(1)}) fusion(bf16[3,1024,3,64]{1,3,0,2:T(8,128)(2,1)S(1)} %reshape.631, pred[3,1024]{1,0:T(4,128)(4,1)S(1)} %broadcast_compare_fusion, s32[3,1024]{1,0:T(4,128)S(1)} %broadcast_add_fusion, pred[1024,1024]{0,1:T(8,128)(4,1)} %iota_compare_fusion), kind=kOutput, calls=%fused_computation.322 | convolution fusion | flops 421524480 | bytes 14467072 | tf_op jit(solution)/shard_map/uqd,ukd->uqk/dot_general | solution.py:172
  152.4 9.4 %all-to-all-done.1 = bf16[8,3,128,1,64]{2,4,3,1,0:T(8,128)(2,1)S(1)} async-done(((bf16[8,3,128,1,64]{2,4,3,1,0:T(8,128)(2,1)}), bf16[8,3,128,1,64]{2,4,3,1,0:T(8,128)(2,1)S(1)}, u32[]{:S(2)}, u32[]{:S(2)}) %all-to-all-start.1) | async-done | bytes 393248 | tf_op jit(solution)/shard_map/all_to_all | solution.py:164
  163.0 4.9 %slice.189 = bf16[768,3072]{1,0:T(8,128)(2,1)} slice(bf16[768,6912]{1,0:T(8,128)(2,1)} %all-gather.2.cloned.1.call-done), slice={[0:768], [3840:6912]} | slice | bytes 9437184 | tf_op jit(solution)/shard_map/slice | solution.py:112
  167.9 8.5 %reshape.635 = bf16[3072,768]{1,0:T(8,128)(2,1)} reshape(bf16[768,3072]{1,0:T(8,128)(2,1)} %slice.189) | data formatting | bytes 9437184 | tf_op jit(solution)/shard_map/reshape | solution.py:335
  178.6 9.5 %fusion.7 = (f32[256,3072]{1,0:T(8,128)S(1)}, f32[256,3072]{1,0:T(8,128)S(1)}) fusion(f32[3072]{0:T(1024)S(1)} %reshape.660, bf16[768,6912]{1,0:T(8,128)(2,1)} %all-gather.2.cloned.1.call-done, f32[256,768]{1,0:T(8,128)S(1)} %get-tuple-element.171, f32[768]{0:T(1024)S(1)} %get-tuple-element.103, f32[768]{0:T(1024)S(1)} %get-tuple-element.104, ...), kind=kOutput, calls=%fused_computation.19 | convolution fusion | flops 1258487808 | bytes 11816960 | tf_op jit(solution)/shard_map/dot_general | solution.py:345
  188.2 7.7 %fusion.10 = bf16[3072,256]{0,1:T(8,128)(2,1)} fusion(f32[256,3072]{1,0:T(8,128)S(1)} %get-tuple-element.173), kind=kLoop, calls=%fused_computation.22 | loop fusion | flops 51118080 | bytes 4718592 | tf_op jit(solution)/shard_map/convert_element_type | solution.py:349
  198.1 5.1 %fusion.124 = f32[768,3072]{1,0:T(8,128)} fusion(bf16[256,3072]{1,0:T(8,128)(2,1)S(1)} %get-tuple-element.177, f32[256,768]{1,0:T(8,128)S(1)} %get-tuple-element.171, f32[768]{0:T(1024)S(1)} %get-tuple-element.103, f32[768]{0:T(1024)S(1)} %get-tuple-element.104, f32[256]{0:T(256)S(1)} %fusion.98, f32[256]{0:T(256)S(1)} %broadcast_multiply_fusion), kind=kOutput, calls=%fused_computation.317 | convolution fusion | flops 1208942592 | bytes 11804672 | tf_op jit(solution)/shard_map/dot_general | solution.py:36
  208.5 4.3 %all-to-all-start.2 = ((bf16[8,3,128,1,64]{2,4,3,1,0:T(8,128)(2,1)}), bf16[8,3,128,1,64]{2,4,3,1,0:T(8,128)(2,1)}, u32[]{:S(2)}, u32[]{:S(2)}) async-start(bf16[8,3,128,1,64]{2,4,3,1,0:T(8,128)(2,1)} %bitcast.67), calls=%async_computation.2 | async-start | bytes 786432 | tf_op jit(solution)/shard_map/all_to_all | solution.py:154
  218.5 4.2 %concatenate.54 = f32[2,2,2,2,2,24,896]{6,5,4,3,2,1,0:T(8,128)} concatenate(f32[2,2,2,2,2,24,768]{6,5,4,3,2,1,0:T(8,128)S(1)} %fusion.73, f32[2,2,2,2,2,24,4]{6,5,4,3,2,1,0:T(8,128)} %concatenate.50, f32[2,2,2,2,2,24,1]{6,5,4,3,2,1,0:T(8,128)} %concatenate.60, f32[2,2,2,2,2,24,1]{6,5,4,3,2,1,0:T(8,128)} %concatenate.61, f32[2,2,2,2,2,24,1]{6,5,4,3,2,1,0:T(8,128)} %concatenate.62, ...), dimensions={6} | concatenate | bytes 5505024 | tf_op jit(solution)/shard_map/concatenate | solution.py:388
  225.0 4.1 fusion.35
  239.4 6.8 %fusion.48 = bf16[3,1024,64]{1,2,0:T(8,128)(2,1)S(1)} fusion(f32[3,1024,1024]{1,2,0:T(8,128)} %copy-done.2, bf16[3,1024,64]{1,2,0:T(8,128)(2,1)S(1)} %squeeze_reshape.3, f32[3,1024]{1,0:T(4,128)S(1)} %get-tuple-element.166), kind=kOutput, calls=%fused_computation.90 | convolution fusion | flops 406585344 | bytes 13381632 | tf_op jit(solution)/shard_map/uqk,uqd->ukd/dot_general | solution.py:190
  246.3 6.6 %multiply_convert_fusion = bf16[3,1024,1024]{1,2,0:T(8,128)(2,1)S(1)} fusion(f32[3,1024,1024]{1,2,0:T(8,128)} %copy-done.2, f32[3,1024]{1,0:T(4,128)S(1)} %div.84, bf16[3,1024,3,64]{1,3,0,2:T(8,128)(2,1)S(1)} %copy-done.20, bf16[3,1024,64]{1,2,0:T(8,128)(2,1)S(1)} %squeeze_reshape.3, f32[3,1024]{1,0:T(4,128)S(1)} %get-tuple-element.166), kind=kOutput, calls=%fused_computation.4 | convolution fusion | flops 412680192 | bytes 19693568 | tf_op jit(solution)/shard_map/uqd,ukd->uqk/dot_general | solution.py:186
  260.8 5.2 %all-to-all-start.3 = ((bf16[8,3,128,3,64]{2,4,3,1,0:T(8,128)(2,1)}), bf16[8,3,128,3,64]{2,4,3,1,0:T(8,128)(2,1)}, u32[]{:S(2)}, u32[]{:S(2)}) async-start(bf16[8,3,128,3,64]{2,4,3,1,0:T(8,128)(2,1)} %maximum_bitcast_fusion), calls=%async_computation.3 | async-start | bytes 2359296 | tf_op jit(solution)/shard_map/all_to_all | solution.py:164
  270.4 5.8 %fusion.51 = bf16[256,768]{1,0:T(8,128)(2,1)} fusion(f32[256,768]{1,0:T(8,128)} %copy-done.9, bf16[3072,768]{1,0:T(8,128)(2,1)} %reshape.635, f32[256,3072]{1,0:T(8,128)} %copy-done.28, f32[256,3072]{1,0:T(8,128)S(1)} %copy-done.8, f32[768]{0:T(1024)S(1)} %copy-done.35), kind=kOutput, calls=%fused_computation.93 | convolution fusion | flops 1210908672 | bytes 12192768 | tf_op jit(solution)/shard_map/dot_general | solution.py:350
  317.0 4.3 %concatenate.48 = f32[2,2,2,2,2,24,896]{6,5,4,3,2,1,0:T(8,128)} concatenate(f32[2,2,2,2,2,24,768]{6,5,4,3,2,1,0:T(8,128)S(1)} %fusion.71, f32[2,2,2,2,2,24,1]{6,5,4,3,2,1,0:T(8,128)S(1)} %concatenate.55, f32[2,2,2,2,2,24,1]{6,5,4,3,2,1,0:T(8,128)S(1)} %concatenate.56, f32[2,2,2,2,2,24,1]{6,5,4,3,2,1,0:T(8,128)} %concatenate.57, f32[2,2,2,2,2,24,1]{6,5,4,3,2,1,0:T(8,128)} %concatenate.58, ...), dimensions={6} | concatenate | bytes 5505024 | tf_op jit(solution)/shard_map/concatenate | solution.py:412
  355.8 14.1 %collective-permute-done.27 = bf16[2,2,24,768]{3,2,1,0:T(8,128)(2,1)S(1)} collective-permute-done((bf16[2,2,24,768]{3,2,1,0:T(8,128)(2,1)S(1)}, bf16[2,2,24,768]{3,2,1,0:T(8,128)(2,1)S(1)}, u32[]{:S(2)}, u32[]{:S(2)}) %collective-permute-start.27) | collective-permute-done | bytes 147488 | tf_op jit(solution)/shard_map/ppermute | solution.py:102
  382.8 4.6 %collective-permute-done.19 = bf16[24,896]{1,0:T(8,128)(2,1)S(1)} collective-permute-done((bf16[24,896]{1,0:T(8,128)(2,1)S(1)}, bf16[24,896]{1,0:T(8,128)(2,1)S(1)}, u32[]{:S(2)}, u32[]{:S(2)}) %collective-permute-start.19) | collective-permute-done | bytes 43040 | tf_op jit(solution)/shard_map/ppermute | solution.py:102
  390.5 7.2 %collective-permute-done.38 = bf16[2,24,3072]{2,1,0:T(8,128)(2,1)S(1)} collective-permute-done((bf16[2,24,3072]{2,1,0:T(8,128)(2,1)S(1)}, bf16[2,24,3072]{2,1,0:T(8,128)(2,1)S(1)}, u32[]{:S(2)}, u32[]{:S(2)}) %collective-permute-start.38) | collective-permute-done | bytes 294944 | tf_op jit(solution)/shard_map/ppermute | solution.py:102
  400.9 6.1 %collective-permute-done.39 = bf16[24,3072]{1,0:T(8,128)(2,1)S(1)} collective-permute-done((bf16[24,3072]{1,0:T(8,128)(2,1)S(1)}, bf16[24,3072]{1,0:T(8,128)(2,1)S(1)}, u32[]{:S(2)}, u32[]{:S(2)}) %collective-permute-start.39) | collective-permute-done | bytes 147488 | tf_op jit(solution)/shard_map/ppermute | solution.py:102
  (397 shorter events, 216.2 us)
Async XLA Ops:
  7.2 155.8 %all-gather.2.cloned.1.call-start = ((), (), s32[]{:S(2)}) async-start(), calls=%async_computation.4 | async-start | bytes 10948608 | tf_op jit(solution)/shard_map/all_gather | solution.py:333
  17.7 14.9 %collective-permute-start = (bf16[24,896]{1,0:T(8,128)(2,1)S(1)}, bf16[24,896]{1,0:T(8,128)(2,1)S(1)}, u32[]{:S(2)}, u32[]{:S(2)}) collective-permute-start(bf16[24,896]{1,0:T(8,128)(2,1)S(1)} %concatenate.40), channel_id=1, source_target_pairs={{0,4},{1,5},{2,6},{3,7},{4,0},{5,1},{6,2},{7,3},{8,12},{9,13},{10,... | collective-permute-start | bytes 129032 | tf_op jit(solution)/shard_map/ppermute | solution.py:77
  41.1 13.0 %collective-permute-start.13 = (bf16[2,2,2,24,768]{4,3,2,1,0:T(8,128)(2,1)S(1)}, bf16[2,2,2,24,768]{4,3,2,1,0:T(8,128)(2,1)S(1)}, u32[]{:S(2)}, u32[]{:S(2)}) collective-permute-start(bf16[2,2,2,24,768]{4,3,2,1,0:T(8,128)(2,1)S(1)} %get-tuple-element.144), channel_id=1, source_target_pairs={{0,1},{1,0},{2,3},{3,2},{4,5},{5,4},{6,7},{7,6},{8,9},{9,8},{10,11... | collective-permute-start | bytes 884744 | tf_op jit(solution)/shard_map/ppermute | solution.py:77
  43.8 15.2 %collective-permute-start.8 = (bf16[2,2,2,24,768]{4,3,2,1,0:T(8,128)(2,1)S(1)}, bf16[2,2,2,24,768]{4,3,2,1,0:T(8,128)(2,1)S(1)}, u32[]{:S(2)}, u32[]{:S(2)}) collective-permute-start(bf16[2,2,2,24,768]{4,3,2,1,0:T(8,128)(2,1)S(1)} %get-tuple-element.142), channel_id=1, source_target_pairs={{0,16},{1,17},{2,18},{3,19},{4,20},{5,21},{6,22},{7,23},{8,24},{9,... | collective-permute-start | bytes 884744 | tf_op jit(solution)/shard_map/ppermute | solution.py:77
  48.3 12.4 %collective-permute-start.3 = (bf16[2,2,2,24,896]{4,3,2,1,0:T(8,128)(2,1)S(1)}, bf16[2,2,2,24,896]{4,3,2,1,0:T(8,128)(2,1)S(1)}, u32[]{:S(2)}, u32[]{:S(2)}) collective-permute-start(bf16[2,2,2,24,896]{4,3,2,1,0:T(8,128)(2,1)S(1)} %get-tuple-element.140), channel_id=1, source_target_pairs={{0,2},{1,3},{2,0},{3,1},{4,6},{5,7},{6,4},{7,5},{8,10},{9,11},{10,... | collective-permute-start | bytes 1032200 | tf_op jit(solution)/shard_map/ppermute | solution.py:77
  82.1 47.6 %all-to-all-start = ((bf16[8,3,128,3,64]{2,4,3,1,0:T(8,128)(2,1)}), bf16[8,3,128,3,64]{2,4,3,1,0:T(8,128)(2,1)S(1)}, u32[]{:S(2)}, u32[]{:S(2)}) async-start(bf16[8,3,128,3,64]{2,4,3,1,0:T(8,128)(2,1)} %bitcast.461), calls=%async_computation | async-start | bytes 2359296 | tf_op jit(solution)/shard_map/all_to_all | solution.py:154
  146.1 15.6 %all-to-all-start.1 = ((bf16[8,3,128,1,64]{2,4,3,1,0:T(8,128)(2,1)}), bf16[8,3,128,1,64]{2,4,3,1,0:T(8,128)(2,1)S(1)}, u32[]{:S(2)}, u32[]{:S(2)}) async-start(bf16[8,3,128,1,64]{2,4,3,1,0:T(8,128)(2,1)} %bitcast.429), calls=%async_computation.1 | async-start | bytes 786432 | tf_op jit(solution)/shard_map/all_to_all | solution.py:164
  208.5 29.4 %all-to-all-start.2 = ((bf16[8,3,128,1,64]{2,4,3,1,0:T(8,128)(2,1)}), bf16[8,3,128,1,64]{2,4,3,1,0:T(8,128)(2,1)}, u32[]{:S(2)}, u32[]{:S(2)}) async-start(bf16[8,3,128,1,64]{2,4,3,1,0:T(8,128)(2,1)} %bitcast.67), calls=%async_computation.2 | async-start | bytes 786432 | tf_op jit(solution)/shard_map/all_to_all | solution.py:154
  225.0 27.9 %collective-permute-start.30 = (bf16[2,2,2,2,24,896]{5,4,3,2,1,0:T(8,128)(2,1)}, bf16[2,2,2,2,24,896]{5,4,3,2,1,0:T(8,128)(2,1)S(1)}, u32[]{:S(2)}, u32[]{:S(2)}) collective-permute-start(bf16[2,2,2,2,24,896]{5,4,3,2,1,0:T(8,128)(2,1)} %fusion.61), channel_id=1, source_target_pairs={{0,8},{1,9},{2,10},{3,11},{4,12},{5,13},{6,14},{7,15},{8,0},{9,1},... | collective-permute-start | bytes 2064392 | tf_op jit(solution)/shard_map/ppermute | solution.py:102
  229.0 50.0 %collective-permute-start.35 = (bf16[2,2,2,2,24,3072]{5,4,1,2,3,0:T(8,128)(2,1)}, bf16[2,2,2,2,24,3072]{5,4,1,2,3,0:T(8,128)(2,1)}, u32[]{:S(2)}, u32[]{:S(2)}) collective-permute-start(bf16[2,2,2,2,24,3072]{5,4,1,2,3,0:T(8,128)(2,1)} %fusion.35), channel_id=1, source_target_pairs={{0,8},{1,9},{2,10},{3,11},{4,12},{5,13},{6,14},{7,15},{8,0},{9,1},... | collective-permute-start | bytes 7077896 | tf_op jit(solution)/shard_map/ppermute | solution.py:102
  237.9 46.6 %collective-permute-start.40 = (bf16[2,2,2,2,96,768]{5,4,3,2,1,0:T(8,128)(2,1)}, bf16[2,2,2,2,96,768]{5,4,3,2,1,0:T(8,128)(2,1)}, u32[]{:S(2)}, u32[]{:S(2)}) collective-permute-start(bf16[2,2,2,2,96,768]{5,4,3,2,1,0:T(8,128)(2,1)} %fusion.34), channel_id=1, source_target_pairs={{0,8},{1,9},{2,10},{3,11},{4,12},{5,13},{6,14},{7,15},{8,0},{9,1},... | collective-permute-start | bytes 7077896 | tf_op jit(solution)/shard_map/ppermute | solution.py:102
  253.9 12.1 %collective-permute-start.31 = (bf16[2,2,2,24,896]{4,3,2,1,0:T(8,128)(2,1)}, bf16[2,2,2,24,896]{4,3,2,1,0:T(8,128)(2,1)}, u32[]{:S(2)}, u32[]{:S(2)}) collective-permute-start(bf16[2,2,2,24,896]{4,3,2,1,0:T(8,128)(2,1)} %fusion.78), channel_id=1, source_target_pairs={{0,2},{1,3},{2,0},{3,1},{4,6},{5,7},{6,4},{7,5},{8,10},{9,11},{10,... | collective-permute-start | bytes 1032200 | tf_op jit(solution)/shard_map/ppermute | solution.py:102
  260.8 34.2 %all-to-all-start.3 = ((bf16[8,3,128,3,64]{2,4,3,1,0:T(8,128)(2,1)}), bf16[8,3,128,3,64]{2,4,3,1,0:T(8,128)(2,1)}, u32[]{:S(2)}, u32[]{:S(2)}) async-start(bf16[8,3,128,3,64]{2,4,3,1,0:T(8,128)(2,1)} %maximum_bitcast_fusion), calls=%async_computation.3 | async-start | bytes 2359296 | tf_op jit(solution)/shard_map/all_to_all | solution.py:164
  284.0 60.1 %collective-permute-start.36 = (bf16[2,2,2,24,3072]{4,3,0,1,2:T(8,128)(2,1)}, bf16[2,2,2,24,3072]{4,3,0,1,2:T(8,128)(2,1)}, u32[]{:S(2)}, u32[]{:S(2)}) collective-permute-start(bf16[2,2,2,24,3072]{4,3,0,1,2:T(8,128)(2,1)} %fusion.52), channel_id=1, source_target_pairs={{0,16},{1,17},{2,18},{3,19},{4,20},{5,21},{6,22},{7,23},{8,24},{9,... | collective-permute-start | bytes 3538952 | tf_op jit(solution)/shard_map/ppermute | solution.py:102
  290.8 55.9 %collective-permute-start.41 = (bf16[2,2,2,96,768]{4,3,2,1,0:T(8,128)(2,1)}, bf16[2,2,2,96,768]{4,3,2,1,0:T(8,128)(2,1)}, u32[]{:S(2)}, u32[]{:S(2)}) collective-permute-start(bf16[2,2,2,96,768]{4,3,2,1,0:T(8,128)(2,1)} %fusion.53), channel_id=1, source_target_pairs={{0,1},{1,0},{2,3},{3,2},{4,5},{5,4},{6,7},{7,6},{8,9},{9,8},{10,11... | collective-permute-start | bytes 3538952 | tf_op jit(solution)/shard_map/ppermute | solution.py:102
  323.7 20.2 %collective-permute-start.15 = (bf16[2,2,2,2,24,896]{5,4,3,2,1,0:T(8,128)(2,1)}, bf16[2,2,2,2,24,896]{5,4,3,2,1,0:T(8,128)(2,1)S(1)}, u32[]{:S(2)}, u32[]{:S(2)}) collective-permute-start(bf16[2,2,2,2,24,896]{5,4,3,2,1,0:T(8,128)(2,1)} %fusion.60), channel_id=1, source_target_pairs={{0,8},{1,9},{2,10},{3,11},{4,12},{5,13},{6,14},{7,15},{8,0},{9,1},... | collective-permute-start | bytes 2064392 | tf_op jit(solution)/shard_map/ppermute | solution.py:102
  339.4 11.0 %collective-permute-start.26 = (bf16[2,2,2,24,768]{4,3,1,0,2:T(8,128)(2,1)S(1)}, bf16[2,2,2,24,768]{4,3,1,0,2:T(8,128)(2,1)S(1)}, u32[]{:S(2)}, u32[]{:S(2)}) collective-permute-start(bf16[2,2,2,24,768]{4,3,1,0,2:T(8,128)(2,1)S(1)} %fusion.80), channel_id=1, source_target_pairs={{0,1},{1,0},{2,3},{3,2},{4,5},{5,4},{6,7},{7,6},{8,9},{9,8},{10,11... | collective-permute-start | bytes 884744 | tf_op jit(solution)/shard_map/ppermute | solution.py:102
  344.1 11.0 %collective-permute-start.16 = (bf16[2,2,2,24,896]{4,3,2,1,0:T(8,128)(2,1)S(1)}, bf16[2,2,2,24,896]{4,3,2,1,0:T(8,128)(2,1)S(1)}, u32[]{:S(2)}, u32[]{:S(2)}) collective-permute-start(bf16[2,2,2,24,896]{4,3,2,1,0:T(8,128)(2,1)S(1)} %fusion.77), channel_id=1, source_target_pairs={{0,2},{1,3},{2,0},{3,1},{4,6},{5,7},{6,4},{7,5},{8,10},{9,11},{10,... | collective-permute-start | bytes 1032200 | tf_op jit(solution)/shard_map/ppermute | solution.py:102
  345.9 42.9 %collective-permute-start.37 = (bf16[2,2,24,3072]{3,2,0,1:T(8,128)(2,1)S(1)}, bf16[2,2,24,3072]{3,2,0,1:T(8,128)(2,1)S(1)}, u32[]{:S(2)}, u32[]{:S(2)}) collective-permute-start(bf16[2,2,24,3072]{3,2,0,1:T(8,128)(2,1)S(1)} %fusion.62), channel_id=1, source_target_pairs={{0,1},{1,0},{2,3},{3,2},{4,5},{5,4},{6,7},{7,6},{8,9},{9,8},{10,11... | collective-permute-start | bytes 1769480 | tf_op jit(solution)/shard_map/ppermute | solution.py:102
  348.3 40.9 %collective-permute-start.42 = (bf16[2,2,96,768]{3,2,1,0:T(8,128)(2,1)S(1)}, bf16[2,2,96,768]{3,2,1,0:T(8,128)(2,1)S(1)}, u32[]{:S(2)}, u32[]{:S(2)}) collective-permute-start(bf16[2,2,96,768]{3,2,1,0:T(8,128)(2,1)S(1)} %fusion.63), channel_id=1, source_target_pairs={{0,2},{1,3},{2,0},{3,1},{4,6},{5,7},{6,4},{7,5},{8,10},{9,11},{10,... | collective-permute-start | bytes 1769480 | tf_op jit(solution)/shard_map/ppermute | solution.py:102
  350.5 19.4 %collective-permute-start.27 = (bf16[2,2,24,768]{3,2,1,0:T(8,128)(2,1)S(1)}, bf16[2,2,24,768]{3,2,1,0:T(8,128)(2,1)S(1)}, u32[]{:S(2)}, u32[]{:S(2)}) collective-permute-start(bf16[2,2,24,768]{3,2,1,0:T(8,128)(2,1)S(1)} %fusion.86), channel_id=1, source_target_pairs={{0,2},{1,3},{2,0},{3,1},{4,6},{5,7},{6,4},{7,5},{8,10},{9,11},{10,... | collective-permute-start | bytes 442376 | tf_op jit(solution)/shard_map/ppermute | solution.py:102
  351.6 18.9 %collective-permute-start.22 = (bf16[2,2,24,768]{3,2,0,1:T(8,128)(2,1)S(1)}, bf16[2,2,24,768]{3,2,0,1:T(8,128)(2,1)S(1)}, u32[]{:S(2)}, u32[]{:S(2)}) collective-permute-start(bf16[2,2,24,768]{3,2,0,1:T(8,128)(2,1)S(1)} %fusion.85), channel_id=1, source_target_pairs={{0,1},{1,0},{2,3},{3,2},{4,5},{5,4},{6,7},{7,6},{8,9},{9,8},{10,11... | collective-permute-start | bytes 442376 | tf_op jit(solution)/shard_map/ppermute | solution.py:102
  355.2 22.3 %collective-permute-start.17 = (bf16[2,2,24,896]{3,2,1,0:T(8,128)(2,1)S(1)}, bf16[2,2,24,896]{3,2,1,0:T(8,128)(2,1)S(1)}, u32[]{:S(2)}, u32[]{:S(2)}) collective-permute-start(bf16[2,2,24,896]{3,2,1,0:T(8,128)(2,1)S(1)} %fusion.83), channel_id=1, source_target_pairs={{0,16},{1,17},{2,18},{3,19},{4,20},{5,21},{6,22},{7,23},{8,24},{9,... | collective-permute-start | bytes 516104 | tf_op jit(solution)/shard_map/ppermute | solution.py:102
  398.7 9.9 %collective-permute-start.44 = (bf16[96,768]{1,0:T(8,128)(2,1)S(1)}, bf16[96,768]{1,0:T(8,128)(2,1)S(1)}, u32[]{:S(2)}, u32[]{:S(2)}) collective-permute-start(bf16[96,768]{1,0:T(8,128)(2,1)S(1)} %fusion.88), channel_id=1, source_target_pairs={{0,4},{1,5},{2,6},{3,7},{4,0},{5,1},{6,2},{7,3},{8,12},{9,13},{10,... | collective-permute-start | bytes 442376 | tf_op jit(solution)/shard_map/ppermute | solution.py:102
  (75 other events, 676.7 us)
Sparse Core Ops, SparseCore 0:
  10.9 117.9 all-gather.1

commit v6 on v5

--- a/solution.py
+++ b/solution.py
@@ -384,13 +384,19 @@
     vec_one = vector_block(
         [grad_bias_up, grad_bias_down, grad_gain_two, grad_shift_two], full_rows, jnp.float32
     )
-    red_up, red_down, red_mixed = reduce_routes(
-        [grad_up, grad_down, jnp.concatenate([grad_out, vec_one], axis=1)],
+    red_down = lax.psum_scatter(
+        grad_down.astype(jnp.bfloat16), ALL, scatter_dimension=0, tiled=True
+    ).astype(jnp.float32)
+    up_cols = [ff // 2, ff - ff // 2]
+    up_parts = split_cols(grad_up, up_cols)
+    red_up_a, red_up_b, red_mixed = reduce_routes(
+        [up_parts[0], up_parts[1], jnp.concatenate([grad_out, vec_one], axis=1)],
         orders,
         count,
         me,
         backward_anchors[:steps],
     )
+    red_up = jnp.concatenate([red_up_a, red_up_b], axis=1)
     red_out, red_vec_one = split_cols(red_mixed, [width, vec_one.shape[1]])
 
     grad_bias_query = jnp.sum(proj_grad[:, :width].astype(jnp.float32), axis=0)

time: 424 us -> 447 us (1.054)
  matrix products: 63.5 us -> 76.7 us
  local copies, waits for them, and re-layouts: 103 us -> 112 us
  other arithmetic: 50.6 us -> 42.7 us
  waiting for transfers between devices: 121 us -> 126 us
    ppermute x30, waiting for transfers between devices: 48.4 us -> 62.4 us  [reduce_routes(): got = lax.ppermute(send, ALL, partner_pairs(count, b))]
    dot_general x6, matrix products: 12.4 us -> 20.7 us  [outer_rows(): lax.dot_general(left, right, (((0,), (0,)), ((), ())), preferred_element_...]
    unnamed x107 -> x89, local copies, waits for them, and re-layouts: 16.4 us -> 8.39 us
    convert_element_type x1, other arithmetic: 7.69 us -> 1.64 us  [body(): red_down = lax.psum_scatter(grad_down.astype(jnp.bfloat16), ALL, scatter_...]
    dot_general x6, matrix products: 6.44 us -> 11.5 us  [times_transposed(): lax.dot_general(left, right, (((1,), (1,)), ((), ())), preferred_element_...]
    slice x3 -> x4, local copies, waits for them, and re-layouts: 5.52 us -> 10.3 us  [split_cols(): out.append(x[:, at:at + w])]
    all_to_all x2, waiting for transfers between devices: 11.7 us -> 6.93 us  [units_to_rows(): x = lax.all_to_all(x, 'seq', 0, 0, tiled=True)]
  transfers between devices with their start and end apart: 50 -> 51, of which waited for: 24 -> 26; matrix products, arithmetic and copies ran while one was open for 38% -> 38% of each run, Pallas kernels for 0% -> 0%
where the time goes in v6:
time: 447 us; the launch traced here: 439 us
  waiting for transfers between devices  126 us (28%)
  local copies, waits for them, and re-layouts  112 us (25%)
  matrix products  76.7 us (17%)
  starting transfers between devices  65.5 us (15%)
  other arithmetic  42.7 us (10%)
  between operations  15.8 us (4%)
    ppermute x30, waiting for transfers between devices, reduce_routes(): got = lax.ppermute(send, ALL, partner_pairs(count, b))  62.4 us
    all_to_all x2, waiting for transfers between devices, rows_to_units(): x = lax.all_to_all(x, 'seq', 0, 0, tiled=True)  34.8 us
    ppermute x30, starting transfers between devices, reduce_routes(): got = lax.ppermute(send, ALL, partner_pairs(count, b))  28.6 us
    ppermute x15, waiting for transfers between devices, gather_routes(): got = lax.ppermute(x, ALL, partner_pairs(count, b))  22.3 us
    dot_general x6, matrix products, outer_rows(): lax.dot_general(left, right, (((0,), (0,)), ((), ())), preferred_element_...  20.7 us
    ppermute x15, starting transfers between devices, gather_routes(): got = lax.ppermute(x, ALL, partner_pairs(count, b))  17.4 us
    add x30, other arithmetic, reduce_routes(): x = keep + got.astype(jnp.float32)  16.2 us
    convert_element_type x30, local copies, waits for them, and re-layouts, reduce_routes(): lax.dynamic_index_in_dim(x, 1 - mine, axis, keepdims=False)  15.7 us
  transfers between devices with their start and end apart: 51, of which 26 were waited for; matrix products, arithmetic and copies ran while one was open for 38% of the time, Pallas kernels for 0%

profile of v6, /device:TPU:0, one launch (start us, length us, event | category | flops | bytes accessed | tf_op | source)
XLA Modules:
  0.0 439.0 jit_solution(10655204080536846396)
XLA Ops:
  10.8 4.1 collective-permute-start.10
  43.3 8.1 %collective-permute-done.13 = bf16[2,2,2,24,768]{4,3,2,1,0:T(8,128)(2,1)S(1)} collective-permute-done((bf16[2,2,2,24,768]{4,3,2,1,0:T(8,128)(2,1)S(1)}, bf16[2,2,2,24,768]{4,3,2,1,0:T(8,128)(2,1)S(1)}, u32[]{:S(2)}, u32[]{:S(2)}) %collective-permute-start.13) | collective-permute-done | bytes 294944 | tf_op jit(solution)/shard_map/ppermute | solution.py:77
  56.2 4.4 %collective-permute-done.3 = bf16[2,2,2,24,896]{4,3,2,1,0:T(8,128)(2,1)S(1)} collective-permute-done((bf16[2,2,2,24,896]{4,3,2,1,0:T(8,128)(2,1)S(1)}, bf16[2,2,2,24,896]{4,3,2,1,0:T(8,128)(2,1)S(1)}, u32[]{:S(2)}, u32[]{:S(2)}) %collective-permute-start.3) | collective-permute-done | bytes 344096 | tf_op jit(solution)/shard_map/ppermute | solution.py:77
  85.7 5.7 %all-to-all-start = ((bf16[8,3,128,3,64]{2,4,3,1,0:T(8,128)(2,1)}), bf16[8,3,128,3,64]{2,4,3,1,0:T(8,128)(2,1)}, u32[]{:S(2)}, u32[]{:S(2)}) async-start(bf16[8,3,128,3,64]{2,4,3,1,0:T(8,128)(2,1)} %bitcast.399), calls=%async_computation | async-start | bytes 2359296 | tf_op jit(solution)/shard_map/all_to_all | solution.py:154
  93.9 34.8 %all-to-all-done = bf16[8,3,128,3,64]{2,4,3,1,0:T(8,128)(2,1)} async-done(((bf16[8,3,128,3,64]{2,4,3,1,0:T(8,128)(2,1)}), bf16[8,3,128,3,64]{2,4,3,1,0:T(8,128)(2,1)}, u32[]{:S(2)}, u32[]{:S(2)}) %all-to-all-start) | async-done | bytes 1179680 | tf_op jit(solution)/shard_map/all_to_all | solution.py:154
  134.9 6.4 %fusion.111 = (f32[3,1024]{1,0:T(4,128)S(1)}, f32[3,1024,1024]{1,2,0:T(8,128)S(1)}) fusion(bf16[3,1024,3,64]{1,3,0,2:T(8,128)(2,1)} %reshape.632, pred[3,1024]{1,0:T(4,128)(4,1)S(1)} %broadcast_compare_fusion, s32[3,1024]{1,0:T(4,128)S(1)} %broadcast_add_fusion, pred[1024,1024]{0,1:T(8,128)(4,1)} %iota_compare_fusion), kind=kOutput, calls=%fused_computation.302 | convolution fusion | flops 421524480 | bytes 14467072 | tf_op jit(solution)/shard_map/uqd,ukd->uqk/dot_general | solution.py:172
  141.4 4.1 fusion.112
  147.0 4.7 %all-to-all-start.1 = ((bf16[8,3,128,1,64]{2,4,3,1,0:T(8,128)(2,1)}), bf16[8,3,128,1,64]{2,4,3,1,0:T(8,128)(2,1)}, u32[]{:S(2)}, u32[]{:S(2)}) async-start(bf16[8,3,128,1,64]{2,4,3,1,0:T(8,128)(2,1)} %bitcast.405), calls=%async_computation.1 | async-start | bytes 786432 | tf_op jit(solution)/shard_map/all_to_all | solution.py:164
  156.9 6.9 %all-to-all-done.1 = bf16[8,3,128,1,64]{2,4,3,1,0:T(8,128)(2,1)} async-done(((bf16[8,3,128,1,64]{2,4,3,1,0:T(8,128)(2,1)}), bf16[8,3,128,1,64]{2,4,3,1,0:T(8,128)(2,1)}, u32[]{:S(2)}, u32[]{:S(2)}) %all-to-all-start.1) | async-done | bytes 393248 | tf_op jit(solution)/shard_map/all_to_all | solution.py:164
  166.8 4.9 %slice.197 = bf16[768,3072]{1,0:T(8,128)(2,1)} slice(bf16[768,6912]{1,0:T(8,128)(2,1)} %all-gather.2.cloned.1.call-done), slice={[0:768], [3840:6912]} | slice | bytes 9437184 | tf_op jit(solution)/shard_map/slice | solution.py:112
  171.7 8.5 %reshape.636 = bf16[3072,768]{1,0:T(8,128)(2,1)} reshape(bf16[768,3072]{1,0:T(8,128)(2,1)} %slice.197) | data formatting | bytes 9437184 | tf_op jit(solution)/shard_map/reshape | solution.py:335
  182.5 10.8 %multiply_convert_fusion.1 = (bf16[256,3072]{1,0:T(8,128)(2,1)}, f32[256,3072]{1,0:T(8,128)S(1)}, f32[256,3072]{1,0:T(8,128)S(1)}) fusion(f32[3072]{0:T(1024)S(1)} %reshape.662, bf16[768,6912]{1,0:T(8,128)(2,1)} %all-gather.2.cloned.1.call-done, f32[256,768]{1,0:T(8,128)S(1)} %get-tuple-element.175, f32[768]{0:T(1024)S(1)} %get-tuple-element.103, ...), kind=kOutput, calls=%fused_computation.18 | convolution fusion | flops 1260847104 | bytes 13389824 | tf_op jit(solution)/shard_map/dot_general | solution.py:345
  197.9 6.9 %fusion.103 = f32[768,3072]{1,0:T(8,128)} fusion(bf16[256,3072]{1,0:T(8,128)(2,1)} %get-tuple-element.180, f32[256,768]{1,0:T(8,128)} %copy-done.12, f32[768]{0:T(1024)S(1)} %get-tuple-element.103, f32[768]{0:T(1024)S(1)} %get-tuple-element.104, f32[256]{0:T(256)S(1)} %fusion.78, f32[256]{0:T(256)S(1)} %broadcast_multiply_fusion), kind=kOutput, calls=%fused_computation.296 | convolution fusion | flops 1208942592 | bytes 11804672 | tf_op jit(solution)/shard_map/dot_general | solution.py:36
  231.2 4.8 %concatenate.57 = f32[2,2,2,2,2,24,896]{6,5,4,3,2,1,0:T(8,128)} concatenate(f32[2,2,2,2,2,24,768]{6,5,4,3,2,1,0:T(8,128)} %fusion.51, f32[2,2,2,2,2,24,4]{6,5,4,3,2,1,0:T(8,128)} %concatenate.53, f32[2,2,2,2,2,24,1]{6,5,4,3,2,1,0:T(8,128)} %concatenate.64, f32[2,2,2,2,2,24,1]{6,5,4,3,2,1,0:T(8,128)} %concatenate.65, f32[2,2,2,2,2,24,1]{6,5,4,3,2,1,0:T(8,128)} %concatenate.66, ...), dimensions={6} | concatenate | bytes 5505024 | tf_op jit(solution)/shard_map/concatenate | solution.py:393
  238.3 5.0 %convolution_convert_fusion = bf16[3072,768]{1,0:T(8,128)(2,1)} fusion(bf16[256,3072]{1,0:T(8,128)(2,1)} %get-tuple-element.127, bf16[256,768]{1,0:T(8,128)(2,1)S(1)} %bitcast.386), kind=kOutput, calls=%fused_computation.6 | convolution fusion | flops 1210318848 | bytes 6684672 | tf_op jit(solution)/shard_map/dot_general | solution.py:36
  243.3 4.8 %fusion.108 = (f32[768,1536]{1,0:T(8,128)S(1)}, f32[768,1536]{1,0:T(8,128)S(1)}) fusion(f32[768,3072]{1,0:T(8,128)} %fusion.103), kind=kLoop, calls=%fused_computation.299 | loop fusion | bytes 18874368 | tf_op jit(solution)/shard_map/slice | solution.py:112
  259.6 7.0 %multiply_convert_fusion = bf16[3,1024,1024]{1,2,0:T(8,128)(2,1)S(1)} fusion(f32[3,1024,1024]{1,2,0:T(8,128)} %copy-done.2, f32[3,1024]{1,0:T(4,128)S(1)} %div.84, bf16[3,1024,3,64]{1,3,0,2:T(8,128)(2,1)} %reshape.632, bf16[3,1024,64]{1,2,0:T(8,128)(2,1)S(1)} %squeeze_reshape.3, f32[3,1024]{1,0:T(4,128)S(1)} %get-tuple-element.170), kind=kOutput, calls=%fused_computation.4 | convolution fusion | flops 412680192 | bytes 19685376 | tf_op jit(solution)/shard_map/uqd,ukd->uqk/dot_general | solution.py:186
  268.6 7.1 %fusion.27 = bf16[3,1024,64]{1,2,0:T(8,128)(2,1)S(1)} fusion(f32[3,1024,1024]{1,2,0:T(8,128)} %copy-done.2, bf16[3,1024,64]{1,2,0:T(8,128)(2,1)S(1)} %squeeze_reshape.3, f32[3,1024]{1,0:T(4,128)S(1)} %get-tuple-element.170), kind=kOutput, calls=%fused_computation.62 | convolution fusion | flops 406585344 | bytes 13381632 | tf_op jit(solution)/shard_map/uqk,uqd->ukd/dot_general | solution.py:190
  282.6 4.9 %all-to-all-start.3 = ((bf16[8,3,128,3,64]{2,4,3,1,0:T(8,128)(2,1)}), bf16[8,3,128,3,64]{2,4,3,1,0:T(8,128)(2,1)}, u32[]{:S(2)}, u32[]{:S(2)}) async-start(bf16[8,3,128,3,64]{2,4,3,1,0:T(8,128)(2,1)} %maximum_bitcast_fusion), calls=%async_computation.3 | async-start | bytes 2359296 | tf_op jit(solution)/shard_map/all_to_all | solution.py:164
  299.6 17.7 %collective-permute-done.36 = bf16[2,2,2,24,1536]{4,3,0,1,2:T(8,128)(2,1)S(1)} collective-permute-done((bf16[2,2,2,24,1536]{4,3,0,1,2:T(8,128)(2,1)S(1)}, bf16[2,2,2,24,1536]{4,3,0,1,2:T(8,128)(2,1)S(1)}, u32[]{:S(2)}, u32[]{:S(2)}) %collective-permute-start.36) | collective-permute-done | bytes 589856 | tf_op jit(solution)/shard_map/ppermute | solution.py:102
  319.4 5.3 %collective-permute-done.41 = bf16[2,2,2,24,1536]{4,3,1,0,2:T(8,128)(2,1)S(1)} collective-permute-done((bf16[2,2,2,24,1536]{4,3,1,0,2:T(8,128)(2,1)S(1)}, bf16[2,2,2,24,1536]{4,3,1,0,2:T(8,128)(2,1)S(1)}, u32[]{:S(2)}, u32[]{:S(2)}) %collective-permute-start.41) | collective-permute-done | bytes 589856 | tf_op jit(solution)/shard_map/ppermute | solution.py:102
  325.7 5.0 %collective-permute-done.37 = bf16[2,2,24,1536]{3,2,0,1:T(8,128)(2,1)S(1)} collective-permute-done((bf16[2,2,24,1536]{3,2,0,1:T(8,128)(2,1)S(1)}, bf16[2,2,24,1536]{3,2,0,1:T(8,128)(2,1)S(1)}, u32[]{:S(2)}, u32[]{:S(2)}) %collective-permute-start.37) | collective-permute-done | bytes 294944 | tf_op jit(solution)/shard_map/ppermute | solution.py:102
  362.1 4.7 %concatenate.51 = f32[2,2,2,2,2,24,896]{6,5,4,3,2,1,0:T(8,128)} concatenate(f32[2,2,2,2,2,24,768]{6,5,4,3,2,1,0:T(8,128)S(1)} %copy-done.6, f32[2,2,2,2,2,24,1]{6,5,4,3,2,1,0:T(8,128)} %concatenate.59, f32[2,2,2,2,2,24,1]{6,5,4,3,2,1,0:T(8,128)} %concatenate.60, f32[2,2,2,2,2,24,1]{6,5,4,3,2,1,0:T(8,128)} %concatenate.61, f32[2,2,2,2,2,24,1]{6,5,4,3,2,1,0:T(8,128)} %concatenate.62, ...), dimensions={6} | concatenate | bytes 5505024 | tf_op jit(solution)/shard_map/concatenate | solution.py:418
  424.1 4.4 collective-permute-done.19
  (382 shorter events, 242.2 us)
Async XLA Ops:
  7.2 159.6 %all-gather.2.cloned.1.call-start = ((), (), s32[]{:S(2)}) async-start(), calls=%async_computation.5 | async-start | bytes 10948608 | tf_op jit(solution)/shard_map/all_gather | solution.py:333
  10.8 15.5 %collective-permute-start.10 = (bf16[24,768]{1,0:T(8,128)(2,1)S(1)}, bf16[24,768]{1,0:T(8,128)(2,1)S(1)}, u32[]{:S(2)}, u32[]{:S(2)}) collective-permute-start(bf16[24,768]{1,0:T(8,128)(2,1)S(1)} %get-tuple-element.158), channel_id=1, source_target_pairs={{0,4},{1,5},{2,6},{3,7},{4,0},{5,1},{6,2},{7,3},{8,12},{9,13},{10,... | collective-permute-start | bytes 110600 | tf_op jit(solution)/shard_map/ppermute | solution.py:77
  14.9 12.9 %collective-permute-start.5 = (bf16[24,768]{1,0:T(8,128)(2,1)S(1)}, bf16[24,768]{1,0:T(8,128)(2,1)S(1)}, u32[]{:S(2)}, u32[]{:S(2)}) collective-permute-start(bf16[24,768]{1,0:T(8,128)(2,1)S(1)} %get-tuple-element.159), channel_id=1, source_target_pairs={{0,4},{1,5},{2,6},{3,7},{4,0},{5,1},{6,2},{7,3},{8,12},{9,13},{10,... | collective-permute-start | bytes 110600 | tf_op jit(solution)/shard_map/ppermute | solution.py:77
  39.0 12.5 %collective-permute-start.13 = (bf16[2,2,2,24,768]{4,3,2,1,0:T(8,128)(2,1)S(1)}, bf16[2,2,2,24,768]{4,3,2,1,0:T(8,128)(2,1)S(1)}, u32[]{:S(2)}, u32[]{:S(2)}) collective-permute-start(bf16[2,2,2,24,768]{4,3,2,1,0:T(8,128)(2,1)S(1)} %get-tuple-element.148), channel_id=1, source_target_pairs={{0,1},{1,0},{2,3},{3,2},{4,5},{5,4},{6,7},{7,6},{8,9},{9,8},{10,11... | collective-permute-start | bytes 884744 | tf_op jit(solution)/shard_map/ppermute | solution.py:77
  41.0 14.0 %collective-permute-start.8 = (bf16[2,2,2,24,768]{4,3,2,1,0:T(8,128)(2,1)S(1)}, bf16[2,2,2,24,768]{4,3,2,1,0:T(8,128)(2,1)S(1)}, u32[]{:S(2)}, u32[]{:S(2)}) collective-permute-start(bf16[2,2,2,24,768]{4,3,2,1,0:T(8,128)(2,1)S(1)} %get-tuple-element.146), channel_id=1, source_target_pairs={{0,16},{1,17},{2,18},{3,19},{4,20},{5,21},{6,22},{7,23},{8,24},{9,... | collective-permute-start | bytes 884744 | tf_op jit(solution)/shard_map/ppermute | solution.py:77
  43.0 17.6 %collective-permute-start.3 = (bf16[2,2,2,24,896]{4,3,2,1,0:T(8,128)(2,1)S(1)}, bf16[2,2,2,24,896]{4,3,2,1,0:T(8,128)(2,1)S(1)}, u32[]{:S(2)}, u32[]{:S(2)}) collective-permute-start(bf16[2,2,2,24,896]{4,3,2,1,0:T(8,128)(2,1)S(1)} %get-tuple-element.144), channel_id=1, source_target_pairs={{0,2},{1,3},{2,0},{3,1},{4,6},{5,7},{6,4},{7,5},{8,10},{9,11},{10,... | collective-permute-start | bytes 1032200 | tf_op jit(solution)/shard_map/ppermute | solution.py:77
  85.7 43.1 %all-to-all-start = ((bf16[8,3,128,3,64]{2,4,3,1,0:T(8,128)(2,1)}), bf16[8,3,128,3,64]{2,4,3,1,0:T(8,128)(2,1)}, u32[]{:S(2)}, u32[]{:S(2)}) async-start(bf16[8,3,128,3,64]{2,4,3,1,0:T(8,128)(2,1)} %bitcast.399), calls=%async_computation | async-start | bytes 2359296 | tf_op jit(solution)/shard_map/all_to_all | solution.py:154
  147.0 16.7 %all-to-all-start.1 = ((bf16[8,3,128,1,64]{2,4,3,1,0:T(8,128)(2,1)}), bf16[8,3,128,1,64]{2,4,3,1,0:T(8,128)(2,1)}, u32[]{:S(2)}, u32[]{:S(2)}) async-start(bf16[8,3,128,1,64]{2,4,3,1,0:T(8,128)(2,1)} %bitcast.405), calls=%async_computation.1 | async-start | bytes 786432 | tf_op jit(solution)/shard_map/all_to_all | solution.py:164
  222.3 32.8 %all-to-all-start.2 = ((bf16[8,3,128,1,64]{2,4,3,1,0:T(8,128)(2,1)}), bf16[8,3,128,1,64]{2,4,3,1,0:T(8,128)(2,1)}, u32[]{:S(2)}, u32[]{:S(2)}) async-start(bf16[8,3,128,1,64]{2,4,3,1,0:T(8,128)(2,1)} %bitcast.407), calls=%async_computation.2 | async-start | bytes 786432 | tf_op jit(solution)/shard_map/all_to_all | solution.py:154
  226.4 203.7 %reduce-scatter.2.cloned.1.call-start = ((), (), s32[]{:S(2)}) async-start(), calls=%async_computation.6 | async-start | bytes 4866048 | tf_op jit(solution)/shard_map/reduce_scatter | solution.py:387
  238.3 37.3 %collective-permute-start.30 = (bf16[2,2,2,2,24,896]{5,4,3,2,1,0:T(8,128)(2,1)}, bf16[2,2,2,2,24,896]{5,4,3,2,1,0:T(8,128)(2,1)}, u32[]{:S(2)}, u32[]{:S(2)}) collective-permute-start(bf16[2,2,2,2,24,896]{5,4,3,2,1,0:T(8,128)(2,1)} %fusion.39), channel_id=1, source_target_pairs={{0,8},{1,9},{2,10},{3,11},{4,12},{5,13},{6,14},{7,15},{8,0},{9,1},... | collective-permute-start | bytes 2064392 | tf_op jit(solution)/shard_map/ppermute | solution.py:102
  249.3 42.1 %collective-permute-start.35 = (bf16[2,2,2,2,24,1536]{5,4,1,2,3,0:T(8,128)(2,1)}, bf16[2,2,2,2,24,1536]{5,4,1,2,3,0:T(8,128)(2,1)}, u32[]{:S(2)}, u32[]{:S(2)}) collective-permute-start(bf16[2,2,2,2,24,1536]{5,4,1,2,3,0:T(8,128)(2,1)} %fusion.30), channel_id=1, source_target_pairs={{0,8},{1,9},{2,10},{3,11},{4,12},{5,13},{6,14},{7,15},{8,0},{9,1},... | collective-permute-start | bytes 3538952 | tf_op jit(solution)/shard_map/ppermute | solution.py:102
  251.3 43.3 %collective-permute-start.40 = (bf16[2,2,2,2,24,1536]{5,4,1,0,2,3:T(8,128)(2,1)}, bf16[2,2,2,2,24,1536]{5,4,1,0,2,3:T(8,128)(2,1)}, u32[]{:S(2)}, u32[]{:S(2)}) collective-permute-start(bf16[2,2,2,2,24,1536]{5,4,1,0,2,3:T(8,128)(2,1)} %fusion.31), channel_id=1, source_target_pairs={{0,8},{1,9},{2,10},{3,11},{4,12},{5,13},{6,14},{7,15},{8,0},{9,1},... | collective-permute-start | bytes 3538952 | tf_op jit(solution)/shard_map/ppermute | solution.py:102
  277.8 10.9 %collective-permute-start.31 = (bf16[2,2,2,24,896]{4,3,2,1,0:T(8,128)(2,1)}, bf16[2,2,2,24,896]{4,3,2,1,0:T(8,128)(2,1)}, u32[]{:S(2)}, u32[]{:S(2)}) collective-permute-start(bf16[2,2,2,24,896]{4,3,2,1,0:T(8,128)(2,1)} %fusion.56), channel_id=1, source_target_pairs={{0,2},{1,3},{2,0},{3,1},{4,6},{5,7},{6,4},{7,5},{8,10},{9,11},{10,... | collective-permute-start | bytes 1032200 | tf_op jit(solution)/shard_map/ppermute | solution.py:102
  282.6 53.1 %all-to-all-start.3 = ((bf16[8,3,128,3,64]{2,4,3,1,0:T(8,128)(2,1)}), bf16[8,3,128,3,64]{2,4,3,1,0:T(8,128)(2,1)}, u32[]{:S(2)}, u32[]{:S(2)}) async-start(bf16[8,3,128,3,64]{2,4,3,1,0:T(8,128)(2,1)} %maximum_bitcast_fusion), calls=%async_computation.3 | async-start | bytes 2359296 | tf_op jit(solution)/shard_map/all_to_all | solution.py:164
  293.9 23.5 %collective-permute-start.36 = (bf16[2,2,2,24,1536]{4,3,0,1,2:T(8,128)(2,1)S(1)}, bf16[2,2,2,24,1536]{4,3,0,1,2:T(8,128)(2,1)S(1)}, u32[]{:S(2)}, u32[]{:S(2)}) collective-permute-start(bf16[2,2,2,24,1536]{4,3,0,1,2:T(8,128)(2,1)S(1)} %fusion.40), channel_id=1, source_target_pairs={{0,16},{1,17},{2,18},{3,19},{4,20},{5,21},{6,22},{7,23},{8,24},{9,... | collective-permute-start | bytes 1769480 | tf_op jit(solution)/shard_map/ppermute | solution.py:102
  296.3 28.3 %collective-permute-start.41 = (bf16[2,2,2,24,1536]{4,3,1,0,2:T(8,128)(2,1)S(1)}, bf16[2,2,2,24,1536]{4,3,1,0,2:T(8,128)(2,1)S(1)}, u32[]{:S(2)}, u32[]{:S(2)}) collective-permute-start(bf16[2,2,2,24,1536]{4,3,1,0,2:T(8,128)(2,1)S(1)} %fusion.41), channel_id=1, source_target_pairs={{0,1},{1,0},{2,3},{3,2},{4,5},{5,4},{6,7},{7,6},{8,9},{9,8},{10,11... | collective-permute-start | bytes 1769480 | tf_op jit(solution)/shard_map/ppermute | solution.py:102
  317.5 13.1 %collective-permute-start.37 = (bf16[2,2,24,1536]{3,2,0,1:T(8,128)(2,1)S(1)}, bf16[2,2,24,1536]{3,2,0,1:T(8,128)(2,1)S(1)}, u32[]{:S(2)}, u32[]{:S(2)}) collective-permute-start(bf16[2,2,24,1536]{3,2,0,1:T(8,128)(2,1)S(1)} %fusion.59), channel_id=1, source_target_pairs={{0,1},{1,0},{2,3},{3,2},{4,5},{5,4},{6,7},{7,6},{8,9},{9,8},{10,11... | collective-permute-start | bytes 884744 | tf_op jit(solution)/shard_map/ppermute | solution.py:102
  355.0 14.9 %collective-permute-start.33 = (bf16[2,24,896]{2,1,0:T(8,128)(2,1)}, bf16[2,24,896]{2,1,0:T(8,128)(2,1)}, u32[]{:S(2)}, u32[]{:S(2)}) collective-permute-start(bf16[2,24,896]{2,1,0:T(8,128)(2,1)} %fusion.68), channel_id=1, source_target_pairs={{0,1},{1,0},{2,3},{3,2},{4,5},{5,4},{6,7},{7,6},{8,9},{9,8},{10,11... | collective-permute-start | bytes 258056 | tf_op jit(solution)/shard_map/ppermute | solution.py:102
  358.7 33.9 %collective-permute-start.20 = (bf16[2,2,2,2,24,768]{5,4,1,2,3,0:T(8,128)(2,1)}, bf16[2,2,2,2,24,768]{5,4,1,2,3,0:T(8,128)(2,1)}, u32[]{:S(2)}, u32[]{:S(2)}) collective-permute-start(bf16[2,2,2,2,24,768]{5,4,1,2,3,0:T(8,128)(2,1)} %fusion.42), channel_id=1, source_target_pairs={{0,8},{1,9},{2,10},{3,11},{4,12},{5,13},{6,14},{7,15},{8,0},{9,1},... | collective-permute-start | bytes 1769480 | tf_op jit(solution)/shard_map/ppermute | solution.py:102
  360.8 33.7 %collective-permute-start.25 = (bf16[2,2,2,2,24,768]{5,4,1,0,2,3:T(8,128)(2,1)}, bf16[2,2,2,2,24,768]{5,4,1,0,2,3:T(8,128)(2,1)}, u32[]{:S(2)}, u32[]{:S(2)}) collective-permute-start(bf16[2,2,2,2,24,768]{5,4,1,0,2,3:T(8,128)(2,1)} %fusion.43), channel_id=1, source_target_pairs={{0,8},{1,9},{2,10},{3,11},{4,12},{5,13},{6,14},{7,15},{8,0},{9,1},... | collective-permute-start | bytes 1769480 | tf_op jit(solution)/shard_map/ppermute | solution.py:102
  369.2 28.2 %collective-permute-start.15 = (bf16[2,2,2,2,24,896]{5,4,3,2,1,0:T(8,128)(2,1)}, bf16[2,2,2,2,24,896]{5,4,3,2,1,0:T(8,128)(2,1)}, u32[]{:S(2)}, u32[]{:S(2)}) collective-permute-start(bf16[2,2,2,2,24,896]{5,4,3,2,1,0:T(8,128)(2,1)} %fusion.38), channel_id=1, source_target_pairs={{0,8},{1,9},{2,10},{3,11},{4,12},{5,13},{6,14},{7,15},{8,0},{9,1},... | collective-permute-start | bytes 2064392 | tf_op jit(solution)/shard_map/ppermute | solution.py:102
  369.9 10.9 %collective-permute-start.38 = (bf16[2,24,1536]{2,1,0:T(8,128)(2,1)}, bf16[2,24,1536]{2,1,0:T(8,128)(2,1)}, u32[]{:S(2)}, u32[]{:S(2)}) collective-permute-start(bf16[2,24,1536]{2,1,0:T(8,128)(2,1)} %fusion.65), channel_id=1, source_target_pairs={{0,2},{1,3},{2,0},{3,1},{4,6},{5,7},{6,4},{7,5},{8,10},{9,11},{10,... | collective-permute-start | bytes 442376 | tf_op jit(solution)/shard_map/ppermute | solution.py:102
  398.7 14.4 %collective-permute-start.16 = (bf16[2,2,2,24,896]{4,3,2,1,0:T(8,128)(2,1)S(1)}, bf16[2,2,2,24,896]{4,3,2,1,0:T(8,128)(2,1)S(1)}, u32[]{:S(2)}, u32[]{:S(2)}) collective-permute-start(bf16[2,2,2,24,896]{4,3,2,1,0:T(8,128)(2,1)S(1)} %fusion.55), channel_id=1, source_target_pairs={{0,2},{1,3},{2,0},{3,1},{4,6},{5,7},{6,4},{7,5},{8,10},{9,11},{10,... | collective-permute-start | bytes 1032200 | tf_op jit(solution)/shard_map/ppermute | solution.py:102
  (67 other events, 530.4 us)
Sparse Core Ops, SparseCore 0:
  10.9 102.3 all-gather.1
  243.4 124.9 reduce-scatter.1

commit v7 on v5

--- a/solution.py
+++ b/solution.py
@@ -332,7 +332,7 @@
     proj_out, proj_up, down_view = split_cols(
         lax.all_gather(mlp_pack, ALL, axis=0, tiled=True), [width, ff, ff]
     )
-    proj_down = down_view.reshape(count * shard_rows * ratio, width)
+    down_parts = split_cols(down_view, [width] * ratio)
 
     branch = jnp.dot(attended_b, proj_out, preferred_element_type=jnp.float32) + bias_out.astype(
         jnp.float32
@@ -347,16 +347,19 @@
     )
     activated_f, gelu_back = jax.vjp(partial(jax.nn.gelu, approximate=False), hidden)
     activated = activated_f.astype(jnp.bfloat16)
-    mlp_out = jnp.dot(activated, proj_down, preferred_element_type=jnp.float32) + bias_down.astype(
-        jnp.float32
-    )
+    mlp_sum = None
+    for c, part in enumerate(down_parts):
+        term = jnp.dot(activated[:, c::ratio], part, preferred_element_type=jnp.float32)
+        mlp_sum = term if mlp_sum is None else mlp_sum + term
+    mlp_out = mlp_sum + bias_down.astype(jnp.float32)
     outputs = (middle + mlp_out).astype(jnp.bfloat16)
 
     out_grad = cotangent[:, 0].reshape(rows, width)
     out_grad_f = out_grad.astype(jnp.float32)
     grad_down = outer_rows(activated, out_grad)
     grad_bias_down = jnp.sum(out_grad_f, axis=0)
-    act_grad = times_transposed(out_grad, proj_down)
+    act_grad = jnp.stack([times_transposed(out_grad, part) for part in down_parts], axis=-1)
+    act_grad = act_grad.reshape(rows, ratio * width)
     (hidden_grad,) = gelu_back(act_grad)
     hidden_grad_b = hidden_grad.astype(jnp.bfloat16)
     grad_up = outer_rows(normed_two, hidden_grad_b)

time: 424 us -> 510 us (1.20)
  local copies, waits for them, and re-layouts: 103 us -> 168 us
  matrix products: 63.5 us -> 77.5 us
    slice x0 -> x4, local copies, waits for them, and re-layouts: none -> 65.4 us  [body(): activated[:, c::ratio]]
    dot_general x6 -> x9, matrix products: 6.44 us -> 15.9 us  [times_transposed(): lax.dot_general(left, right, (((1,), (1,)), ((), ())), preferred_element_...]
    unnamed x107 -> x141, local copies, waits for them, and re-layouts: 16.4 us -> 19.2 us
  transfers between devices with their start and end apart: 50 -> 50, of which waited for: 24 -> 25; matrix products, arithmetic and copies ran while one was open for 38% -> 36% of each run, Pallas kernels for 0% -> 0%
where the time goes in v7:
time: 510 us; the launch traced here: 502 us
  local copies, waits for them, and re-layouts  168 us (33%)
  waiting for transfers between devices  122 us (24%)
  matrix products  77.5 us (15%)
  starting transfers between devices  63.2 us (12%)
  other arithmetic  55.3 us (11%)
  between operations  15.9 us (3%)
    slice x4, local copies, waits for them, and re-layouts, body(): activated[:, c::ratio]  65.4 us
    ppermute x30, waiting for transfers between devices, reduce_routes(): got = lax.ppermute(send, ALL, partner_pairs(count, b))  49.7 us
    all_to_all x2, waiting for transfers between devices, rows_to_units(): x = lax.all_to_all(x, 'seq', 0, 0, tiled=True)  39 us
    ppermute x30, starting transfers between devices, reduce_routes(): got = lax.ppermute(send, ALL, partner_pairs(count, b))  26.5 us
    ppermute x15, waiting for transfers between devices, gather_routes(): got = lax.ppermute(x, ALL, partner_pairs(count, b))  21.8 us
    add x30, other arithmetic, reduce_routes(): x = keep + got.astype(jnp.float32)  21.6 us
    unnamed x141, local copies, waits for them, and re-layouts  19.2 us
    convert_element_type x30, local copies, waits for them, and re-layouts, reduce_routes(): lax.dynamic_index_in_dim(x, 1 - mine, axis, keepdims=False)  19.1 us
  transfers between devices with their start and end apart: 50, of which 25 were waited for; matrix products, arithmetic and copies ran while one was open for 36% of the time, Pallas kernels for 0%

profile of v7, /device:TPU:0, one launch (start us, length us, event | category | flops | bytes accessed | tf_op | source)
XLA Modules:
  0.0 501.8 jit_solution(3167593830160694344)
XLA Ops:
  48.4 5.7 %collective-permute-done.13 = bf16[2,2,2,24,768]{4,3,2,1,0:T(8,128)(2,1)S(1)} collective-permute-done((bf16[2,2,2,24,768]{4,3,2,1,0:T(8,128)(2,1)S(1)}, bf16[2,2,2,24,768]{4,3,2,1,0:T(8,128)(2,1)S(1)}, u32[]{:S(2)}, u32[]{:S(2)}) %collective-permute-start.13) | collective-permute-done | bytes 294944 | tf_op jit(solution)/shard_map/ppermute | solution.py:77
  54.3 4.7 collective-permute-done.8
  82.2 6.0 %all-to-all-start = ((bf16[8,3,128,3,64]{2,4,3,1,0:T(8,128)(2,1)}), bf16[8,3,128,3,64]{2,4,3,1,0:T(8,128)(2,1)S(1)}, u32[]{:S(2)}, u32[]{:S(2)}) async-start(bf16[8,3,128,3,64]{2,4,3,1,0:T(8,128)(2,1)} %bitcast.484), calls=%async_computation | async-start | bytes 2359296 | tf_op jit(solution)/shard_map/all_to_all | solution.py:154
  90.7 39.0 %all-to-all-done = bf16[8,3,128,3,64]{2,4,3,1,0:T(8,128)(2,1)S(1)} async-done(((bf16[8,3,128,3,64]{2,4,3,1,0:T(8,128)(2,1)}), bf16[8,3,128,3,64]{2,4,3,1,0:T(8,128)(2,1)S(1)}, u32[]{:S(2)}, u32[]{:S(2)}) %all-to-all-start) | async-done | bytes 1179680 | tf_op jit(solution)/shard_map/all_to_all | solution.py:154
  133.9 6.6 %fusion.137 = (f32[3,1024]{1,0:T(4,128)S(1)}, f32[3,1024,1024]{1,2,0:T(8,128)S(1)}) fusion(bf16[3,1024,3,64]{1,3,0,2:T(8,128)(2,1)S(1)} %reshape.631, pred[3,1024]{1,0:T(4,128)(4,1)S(1)} %broadcast_compare_fusion, s32[3,1024]{1,0:T(4,128)S(1)} %broadcast_add_fusion, pred[1024,1024]{0,1:T(8,128)(4,1)} %iota_compare_fusion), kind=kOutput, calls=%fused_computation.335 | convolution fusion | flops 421524480 | bytes 14467072 | tf_op jit(solution)/shard_map/uqd,ukd->uqk/dot_general | solution.py:172
  146.4 4.1 all-to-all-start.1
  153.6 8.8 %all-to-all-done.1 = bf16[8,3,128,1,64]{2,4,3,1,0:T(8,128)(2,1)S(1)} async-done(((bf16[8,3,128,1,64]{2,4,3,1,0:T(8,128)(2,1)}), bf16[8,3,128,1,64]{2,4,3,1,0:T(8,128)(2,1)S(1)}, u32[]{:S(2)}, u32[]{:S(2)}) %all-to-all-start.1) | async-done | bytes 393248 | tf_op jit(solution)/shard_map/all_to_all | solution.py:164
  182.4 11.9 %convert_reduce_fusion = (f32[3072]{0:T(1024)}, bf16[256,3072]{1,0:T(8,128)(2,1)}, f32[256,3072]{1,0:T(8,128)S(1)}, f32[256,3072]{1,0:T(8,128)S(1)}) fusion(f32[256,3072]{1,0:T(8,128)S(1)} %copy-done.29, f32[3072]{0:T(1024)S(1)} %copy-done.53, bf16[768,6912]{1,0:T(8,128)(2,1)} %all-gather.2.cloned.1.call-done, f32[256,768]{1,0:T(8,128)S(1)} %get-tuple-element.174, ...), kind=kOutput, calls=%fused_computation.40 | convolution fusion | flops 1267921920 | bytes 16547840 | tf_op jit(solution)/shard_map/dot_general | solution.py:345
  196.1 16.5 %slice.175 = bf16[256,768]{1,0:T(8,128)(2,1)} slice(bf16[256,3072]{1,0:T(8,128)(2,1)} %multiply_convert_fusion.1), slice={[0:256:1], [0:3072:4]} | slice | bytes 786432 | tf_op jit(solution)/shard_map/slice | solution.py:352
  212.6 16.3 %slice.179 = bf16[256,768]{1,0:T(8,128)(2,1)} slice(bf16[256,3072]{1,0:T(8,128)(2,1)} %multiply_convert_fusion.1), slice={[0:256:1], [2:3072:4]} | slice | bytes 786432 | tf_op jit(solution)/shard_map/slice | solution.py:352
  228.9 16.3 %slice.181 = bf16[256,768]{1,0:T(8,128)(2,1)} slice(bf16[256,3072]{1,0:T(8,128)(2,1)} %multiply_convert_fusion.1), slice={[0:256:1], [3:3072:4]} | slice | bytes 786432 | tf_op jit(solution)/shard_map/slice | solution.py:352
  245.3 7.6 %fusion.10 = bf16[3072,256]{0,1:T(8,128)(2,1)} fusion(f32[256,3072]{1,0:T(8,128)S(1)} %get-tuple-element.175), kind=kLoop, calls=%fused_computation.21 | loop fusion | flops 51118080 | bytes 4718592 | tf_op jit(solution)/shard_map/convert_element_type | solution.py:349
  252.9 5.9 %fusion.130 = f32[768,3072]{1,0:T(8,128)} fusion(bf16[256,3072]{1,0:T(8,128)(2,1)S(1)} %copy-done.41, f32[256,768]{1,0:T(8,128)S(1)} %copy-done.9, f32[768]{0:T(1024)S(1)} %get-tuple-element.103, f32[768]{0:T(1024)S(1)} %get-tuple-element.104, f32[256]{0:T(256)} %copy-done.51, f32[256]{0:T(256)S(1)} %broadcast_multiply_fusion), kind=kOutput, calls=%fused_computation.330 | convolution fusion | flops 1208942592 | bytes 11804672 | tf_op jit(solution)/shard_map/dot_general | solution.py:36
  258.8 4.6 multiply_reduce_fusion
  278.2 4.2 concatenate.54
  284.7 4.2 fusion.35
  299.5 16.3 %slice.177 = bf16[256,768]{1,0:T(8,128)(2,1)S(1)} slice(bf16[256,3072]{1,0:T(8,128)(2,1)} %multiply_convert_fusion.1), slice={[0:256:1], [1:3072:4]} | slice | bytes 786432 | tf_op jit(solution)/shard_map/slice | solution.py:352
  323.8 6.6 %multiply_convert_fusion = bf16[3,1024,1024]{1,2,0:T(8,128)(2,1)S(1)} fusion(f32[3,1024,1024]{1,2,0:T(8,128)} %copy-done.2, f32[3,1024]{1,0:T(4,128)S(1)} %div.84, bf16[3,1024,3,64]{1,3,0,2:T(8,128)(2,1)S(1)} %copy-done.19, bf16[3,1024,64]{1,2,0:T(8,128)(2,1)S(1)} %squeeze_reshape.3, f32[3,1024]{1,0:T(4,128)} %copy-done.42), kind=kOutput, calls=%fused_computation.4 | convolution fusion | flops 412680192 | bytes 19689472 | tf_op jit(solution)/shard_map/uqd,ukd->uqk/dot_general | solution.py:186
  347.5 5.2 %all-to-all-start.3 = ((bf16[8,3,128,3,64]{2,4,3,1,0:T(8,128)(2,1)}), bf16[8,3,128,3,64]{2,4,3,1,0:T(8,128)(2,1)S(1)}, u32[]{:S(2)}, u32[]{:S(2)}) async-start(bf16[8,3,128,3,64]{2,4,3,1,0:T(8,128)(2,1)} %maximum_bitcast_fusion), calls=%async_computation.3 | async-start | bytes 2359296 | tf_op jit(solution)/shard_map/all_to_all | solution.py:164
  402.3 4.3 concatenate.48
  441.1 14.2 %collective-permute-done.27 = bf16[2,2,24,768]{3,2,1,0:T(8,128)(2,1)S(1)} collective-permute-done((bf16[2,2,24,768]{3,2,1,0:T(8,128)(2,1)S(1)}, bf16[2,2,24,768]{3,2,1,0:T(8,128)(2,1)S(1)}, u32[]{:S(2)}, u32[]{:S(2)}) %collective-permute-start.27) | collective-permute-done | bytes 147488 | tf_op jit(solution)/shard_map/ppermute | solution.py:102
  468.1 4.7 collective-permute-done.19
  476.0 7.1 %collective-permute-done.38 = bf16[2,24,3072]{2,1,0:T(8,128)(2,1)S(1)} collective-permute-done((bf16[2,24,3072]{2,1,0:T(8,128)(2,1)S(1)}, bf16[2,24,3072]{2,1,0:T(8,128)(2,1)S(1)}, u32[]{:S(2)}, u32[]{:S(2)}) %collective-permute-start.38) | collective-permute-done | bytes 294944 | tf_op jit(solution)/shard_map/ppermute | solution.py:102
  486.4 6.1 %collective-permute-done.39 = bf16[24,3072]{1,0:T(8,128)(2,1)S(1)} collective-permute-done((bf16[24,3072]{1,0:T(8,128)(2,1)S(1)}, bf16[24,3072]{1,0:T(8,128)(2,1)S(1)}, u32[]{:S(2)}, u32[]{:S(2)}) %collective-permute-start.39) | collective-permute-done | bytes 147488 | tf_op jit(solution)/shard_map/ppermute | solution.py:102
  (443 shorter events, 259.1 us)
Async XLA Ops:
  7.2 156.4 %all-gather.2.cloned.1.call-start = ((), (), s32[]{:S(2)}) async-start(), calls=%async_computation.4 | async-start | bytes 10948608 | tf_op jit(solution)/shard_map/all_gather | solution.py:333
  17.7 14.9 %collective-permute-start = (bf16[24,896]{1,0:T(8,128)(2,1)S(1)}, bf16[24,896]{1,0:T(8,128)(2,1)S(1)}, u32[]{:S(2)}, u32[]{:S(2)}) collective-permute-start(bf16[24,896]{1,0:T(8,128)(2,1)S(1)} %concatenate.40), channel_id=1, source_target_pairs={{0,4},{1,5},{2,6},{3,7},{4,0},{5,1},{6,2},{7,3},{8,12},{9,13},{10,... | collective-permute-start | bytes 129032 | tf_op jit(solution)/shard_map/ppermute | solution.py:77
  41.1 13.0 %collective-permute-start.13 = (bf16[2,2,2,24,768]{4,3,2,1,0:T(8,128)(2,1)S(1)}, bf16[2,2,2,24,768]{4,3,2,1,0:T(8,128)(2,1)S(1)}, u32[]{:S(2)}, u32[]{:S(2)}) collective-permute-start(bf16[2,2,2,24,768]{4,3,2,1,0:T(8,128)(2,1)S(1)} %get-tuple-element.147), channel_id=1, source_target_pairs={{0,1},{1,0},{2,3},{3,2},{4,5},{5,4},{6,7},{7,6},{8,9},{9,8},{10,11... | collective-permute-start | bytes 884744 | tf_op jit(solution)/shard_map/ppermute | solution.py:77
  43.8 15.2 %collective-permute-start.8 = (bf16[2,2,2,24,768]{4,3,2,1,0:T(8,128)(2,1)S(1)}, bf16[2,2,2,24,768]{4,3,2,1,0:T(8,128)(2,1)S(1)}, u32[]{:S(2)}, u32[]{:S(2)}) collective-permute-start(bf16[2,2,2,24,768]{4,3,2,1,0:T(8,128)(2,1)S(1)} %get-tuple-element.145), channel_id=1, source_target_pairs={{0,16},{1,17},{2,18},{3,19},{4,20},{5,21},{6,22},{7,23},{8,24},{9,... | collective-permute-start | bytes 884744 | tf_op jit(solution)/shard_map/ppermute | solution.py:77
  48.3 12.4 %collective-permute-start.3 = (bf16[2,2,2,24,896]{4,3,2,1,0:T(8,128)(2,1)S(1)}, bf16[2,2,2,24,896]{4,3,2,1,0:T(8,128)(2,1)S(1)}, u32[]{:S(2)}, u32[]{:S(2)}) collective-permute-start(bf16[2,2,2,24,896]{4,3,2,1,0:T(8,128)(2,1)S(1)} %get-tuple-element.143), channel_id=1, source_target_pairs={{0,2},{1,3},{2,0},{3,1},{4,6},{5,7},{6,4},{7,5},{8,10},{9,11},{10,... | collective-permute-start | bytes 1032200 | tf_op jit(solution)/shard_map/ppermute | solution.py:77
  82.2 47.5 %all-to-all-start = ((bf16[8,3,128,3,64]{2,4,3,1,0:T(8,128)(2,1)}), bf16[8,3,128,3,64]{2,4,3,1,0:T(8,128)(2,1)S(1)}, u32[]{:S(2)}, u32[]{:S(2)}) async-start(bf16[8,3,128,3,64]{2,4,3,1,0:T(8,128)(2,1)} %bitcast.484), calls=%async_computation | async-start | bytes 2359296 | tf_op jit(solution)/shard_map/all_to_all | solution.py:154
  146.4 15.9 %all-to-all-start.1 = ((bf16[8,3,128,1,64]{2,4,3,1,0:T(8,128)(2,1)}), bf16[8,3,128,1,64]{2,4,3,1,0:T(8,128)(2,1)S(1)}, u32[]{:S(2)}, u32[]{:S(2)}) async-start(bf16[8,3,128,1,64]{2,4,3,1,0:T(8,128)(2,1)} %bitcast.448), calls=%async_computation.1 | async-start | bytes 786432 | tf_op jit(solution)/shard_map/all_to_all | solution.py:164
  267.1 53.3 %all-to-all-start.2 = ((bf16[8,3,128,1,64]{2,4,3,1,0:T(8,128)(2,1)}), bf16[8,3,128,1,64]{2,4,3,1,0:T(8,128)(2,1)}, u32[]{:S(2)}, u32[]{:S(2)}) async-start(bf16[8,3,128,1,64]{2,4,3,1,0:T(8,128)(2,1)} %bitcast.74), calls=%async_computation.2 | async-start | bytes 786432 | tf_op jit(solution)/shard_map/all_to_all | solution.py:154
  284.7 49.0 %collective-permute-start.30 = (bf16[2,2,2,2,24,896]{5,4,3,2,1,0:T(8,128)(2,1)}, bf16[2,2,2,2,24,896]{5,4,3,2,1,0:T(8,128)(2,1)}, u32[]{:S(2)}, u32[]{:S(2)}) collective-permute-start(bf16[2,2,2,2,24,896]{5,4,3,2,1,0:T(8,128)(2,1)} %fusion.68), channel_id=1, source_target_pairs={{0,8},{1,9},{2,10},{3,11},{4,12},{5,13},{6,14},{7,15},{8,0},{9,1},... | collective-permute-start | bytes 2064392 | tf_op jit(solution)/shard_map/ppermute | solution.py:102
  288.8 75.1 %collective-permute-start.35 = (bf16[2,2,2,2,24,3072]{5,4,1,2,3,0:T(8,128)(2,1)}, bf16[2,2,2,2,24,3072]{5,4,1,2,3,0:T(8,128)(2,1)}, u32[]{:S(2)}, u32[]{:S(2)}) collective-permute-start(bf16[2,2,2,2,24,3072]{5,4,1,2,3,0:T(8,128)(2,1)} %fusion.35), channel_id=1, source_target_pairs={{0,8},{1,9},{2,10},{3,11},{4,12},{5,13},{6,14},{7,15},{8,0},{9,1},... | collective-permute-start | bytes 7077896 | tf_op jit(solution)/shard_map/ppermute | solution.py:102
  297.7 72.8 %collective-permute-start.40 = (bf16[2,2,2,2,96,768]{5,4,3,2,1,0:T(8,128)(2,1)}, bf16[2,2,2,2,96,768]{5,4,3,2,1,0:T(8,128)(2,1)}, u32[]{:S(2)}, u32[]{:S(2)}) collective-permute-start(bf16[2,2,2,2,96,768]{5,4,3,2,1,0:T(8,128)(2,1)} %fusion.34), channel_id=1, source_target_pairs={{0,8},{1,9},{2,10},{3,11},{4,12},{5,13},{6,14},{7,15},{8,0},{9,1},... | collective-permute-start | bytes 7077896 | tf_op jit(solution)/shard_map/ppermute | solution.py:102
  337.8 14.9 %collective-permute-start.31 = (bf16[2,2,2,24,896]{4,3,2,1,0:T(8,128)(2,1)}, bf16[2,2,2,24,896]{4,3,2,1,0:T(8,128)(2,1)}, u32[]{:S(2)}, u32[]{:S(2)}) collective-permute-start(bf16[2,2,2,24,896]{4,3,2,1,0:T(8,128)(2,1)} %fusion.85), channel_id=1, source_target_pairs={{0,2},{1,3},{2,0},{3,1},{4,6},{5,7},{6,4},{7,5},{8,10},{9,11},{10,... | collective-permute-start | bytes 1032200 | tf_op jit(solution)/shard_map/ppermute | solution.py:102
  347.5 34.1 %all-to-all-start.3 = ((bf16[8,3,128,3,64]{2,4,3,1,0:T(8,128)(2,1)}), bf16[8,3,128,3,64]{2,4,3,1,0:T(8,128)(2,1)S(1)}, u32[]{:S(2)}, u32[]{:S(2)}) async-start(bf16[8,3,128,3,64]{2,4,3,1,0:T(8,128)(2,1)} %maximum_bitcast_fusion), calls=%async_computation.3 | async-start | bytes 2359296 | tf_op jit(solution)/shard_map/all_to_all | solution.py:164
  369.0 60.7 %collective-permute-start.36 = (bf16[2,2,2,24,3072]{4,3,0,1,2:T(8,128)(2,1)}, bf16[2,2,2,24,3072]{4,3,0,1,2:T(8,128)(2,1)}, u32[]{:S(2)}, u32[]{:S(2)}) collective-permute-start(bf16[2,2,2,24,3072]{4,3,0,1,2:T(8,128)(2,1)} %fusion.50), channel_id=1, source_target_pairs={{0,16},{1,17},{2,18},{3,19},{4,20},{5,21},{6,22},{7,23},{8,24},{9,... | collective-permute-start | bytes 3538952 | tf_op jit(solution)/shard_map/ppermute | solution.py:102
  376.7 55.5 %collective-permute-start.41 = (bf16[2,2,2,96,768]{4,3,2,1,0:T(8,128)(2,1)}, bf16[2,2,2,96,768]{4,3,2,1,0:T(8,128)(2,1)}, u32[]{:S(2)}, u32[]{:S(2)}) collective-permute-start(bf16[2,2,2,96,768]{4,3,2,1,0:T(8,128)(2,1)} %fusion.51), channel_id=1, source_target_pairs={{0,1},{1,0},{2,3},{3,2},{4,5},{5,4},{6,7},{7,6},{8,9},{9,8},{10,11... | collective-permute-start | bytes 3538952 | tf_op jit(solution)/shard_map/ppermute | solution.py:102
  409.1 20.2 %collective-permute-start.15 = (bf16[2,2,2,2,24,896]{5,4,3,2,1,0:T(8,128)(2,1)}, bf16[2,2,2,2,24,896]{5,4,3,2,1,0:T(8,128)(2,1)S(1)}, u32[]{:S(2)}, u32[]{:S(2)}) collective-permute-start(bf16[2,2,2,2,24,896]{5,4,3,2,1,0:T(8,128)(2,1)} %fusion.67), channel_id=1, source_target_pairs={{0,8},{1,9},{2,10},{3,11},{4,12},{5,13},{6,14},{7,15},{8,0},{9,1},... | collective-permute-start | bytes 2064392 | tf_op jit(solution)/shard_map/ppermute | solution.py:102
  424.8 11.1 %collective-permute-start.26 = (bf16[2,2,2,24,768]{4,3,1,0,2:T(8,128)(2,1)S(1)}, bf16[2,2,2,24,768]{4,3,1,0,2:T(8,128)(2,1)S(1)}, u32[]{:S(2)}, u32[]{:S(2)}) collective-permute-start(bf16[2,2,2,24,768]{4,3,1,0,2:T(8,128)(2,1)S(1)} %fusion.87), channel_id=1, source_target_pairs={{0,1},{1,0},{2,3},{3,2},{4,5},{5,4},{6,7},{7,6},{8,9},{9,8},{10,11... | collective-permute-start | bytes 884744 | tf_op jit(solution)/shard_map/ppermute | solution.py:102
  429.5 11.0 %collective-permute-start.16 = (bf16[2,2,2,24,896]{4,3,2,1,0:T(8,128)(2,1)S(1)}, bf16[2,2,2,24,896]{4,3,2,1,0:T(8,128)(2,1)S(1)}, u32[]{:S(2)}, u32[]{:S(2)}) collective-permute-start(bf16[2,2,2,24,896]{4,3,2,1,0:T(8,128)(2,1)S(1)} %fusion.84), channel_id=1, source_target_pairs={{0,2},{1,3},{2,0},{3,1},{4,6},{5,7},{6,4},{7,5},{8,10},{9,11},{10,... | collective-permute-start | bytes 1032200 | tf_op jit(solution)/shard_map/ppermute | solution.py:102
  431.4 42.9 %collective-permute-start.37 = (bf16[2,2,24,3072]{3,2,0,1:T(8,128)(2,1)S(1)}, bf16[2,2,24,3072]{3,2,0,1:T(8,128)(2,1)S(1)}, u32[]{:S(2)}, u32[]{:S(2)}) collective-permute-start(bf16[2,2,24,3072]{3,2,0,1:T(8,128)(2,1)S(1)} %fusion.69), channel_id=1, source_target_pairs={{0,1},{1,0},{2,3},{3,2},{4,5},{5,4},{6,7},{7,6},{8,9},{9,8},{10,11... | collective-permute-start | bytes 1769480 | tf_op jit(solution)/shard_map/ppermute | solution.py:102
  433.8 40.9 %collective-permute-start.42 = (bf16[2,2,96,768]{3,2,1,0:T(8,128)(2,1)S(1)}, bf16[2,2,96,768]{3,2,1,0:T(8,128)(2,1)S(1)}, u32[]{:S(2)}, u32[]{:S(2)}) collective-permute-start(bf16[2,2,96,768]{3,2,1,0:T(8,128)(2,1)S(1)} %fusion.70), channel_id=1, source_target_pairs={{0,2},{1,3},{2,0},{3,1},{4,6},{5,7},{6,4},{7,5},{8,10},{9,11},{10,... | collective-permute-start | bytes 1769480 | tf_op jit(solution)/shard_map/ppermute | solution.py:102
  435.9 19.4 %collective-permute-start.27 = (bf16[2,2,24,768]{3,2,1,0:T(8,128)(2,1)S(1)}, bf16[2,2,24,768]{3,2,1,0:T(8,128)(2,1)S(1)}, u32[]{:S(2)}, u32[]{:S(2)}) collective-permute-start(bf16[2,2,24,768]{3,2,1,0:T(8,128)(2,1)S(1)} %fusion.93), channel_id=1, source_target_pairs={{0,2},{1,3},{2,0},{3,1},{4,6},{5,7},{6,4},{7,5},{8,10},{9,11},{10,... | collective-permute-start | bytes 442376 | tf_op jit(solution)/shard_map/ppermute | solution.py:102
  437.0 18.9 %collective-permute-start.22 = (bf16[2,2,24,768]{3,2,0,1:T(8,128)(2,1)S(1)}, bf16[2,2,24,768]{3,2,0,1:T(8,128)(2,1)S(1)}, u32[]{:S(2)}, u32[]{:S(2)}) collective-permute-start(bf16[2,2,24,768]{3,2,0,1:T(8,128)(2,1)S(1)} %fusion.92), channel_id=1, source_target_pairs={{0,1},{1,0},{2,3},{3,2},{4,5},{5,4},{6,7},{7,6},{8,9},{9,8},{10,11... | collective-permute-start | bytes 442376 | tf_op jit(solution)/shard_map/ppermute | solution.py:102
  440.6 22.3 %collective-permute-start.17 = (bf16[2,2,24,896]{3,2,1,0:T(8,128)(2,1)S(1)}, bf16[2,2,24,896]{3,2,1,0:T(8,128)(2,1)S(1)}, u32[]{:S(2)}, u32[]{:S(2)}) collective-permute-start(bf16[2,2,24,896]{3,2,1,0:T(8,128)(2,1)S(1)} %fusion.90), channel_id=1, source_target_pairs={{0,16},{1,17},{2,18},{3,19},{4,20},{5,21},{6,22},{7,23},{8,24},{9,... | collective-permute-start | bytes 516104 | tf_op jit(solution)/shard_map/ppermute | solution.py:102
  484.0 10.1 %collective-permute-start.44 = (bf16[96,768]{1,0:T(8,128)(2,1)S(1)}, bf16[96,768]{1,0:T(8,128)(2,1)S(1)}, u32[]{:S(2)}, u32[]{:S(2)}) collective-permute-start(bf16[96,768]{1,0:T(8,128)(2,1)S(1)} %fusion.95), channel_id=1, source_target_pairs={{0,4},{1,5},{2,6},{3,7},{4,0},{5,1},{6,2},{7,3},{8,12},{9,13},{10,... | collective-permute-start | bytes 442376 | tf_op jit(solution)/shard_map/ppermute | solution.py:102
  (92 other events, 829.1 us)
Sparse Core Ops, SparseCore 0:
  10.9 118.1 all-gather.1

commit v8 on v7

--- a/solution.py
+++ b/solution.py
@@ -88,21 +88,22 @@
     nbits = count.bit_length() - 1
     out = []
     for x, order in zip(routes, orders):
-        rows = x.shape[0] // count
-        cols = x.shape[1]
-        x = x.reshape([2] * nbits + [rows, cols])
+        lead = list(x.shape[:-2])
+        rows = x.shape[-2] // count
+        cols = x.shape[-1]
+        x = x.reshape(lead + [2] * nbits + [rows, cols])
         remaining = list(range(nbits - 1, -1, -1))
         for step, b in enumerate(order):
             if anchors is not None:
                 x = tie(x, anchors[step])
-            axis = remaining.index(b)
+            axis = len(lead) + remaining.index(b)
             mine = (me >> b) & 1
             keep = lax.dynamic_index_in_dim(x, mine, axis, keepdims=False)
             send = lax.dynamic_index_in_dim(x, 1 - mine, axis, keepdims=False).astype(jnp.bfloat16)
             got = lax.ppermute(send, ALL, partner_pairs(count, b))
             x = keep + got.astype(jnp.float32)
-            remaining.pop(axis)
-        out.append(x.reshape(rows, cols))
+            remaining.pop(axis - len(lead))
+        out.append(x.reshape(lead + [rows, cols]))
     return out
 
 
@@ -271,7 +272,10 @@
     vecs_local = vector_block(
         [ln1_g, ln1_b, b_q, b_v, b_out, ln2_g, ln2_b, b_down, b_up], shard_rows, jnp.bfloat16
     )
-    mlp_pack = jnp.concatenate([w_out, w_up, w_down.reshape(shard_rows, ratio * width)], axis=1)
+    w_up_p = jnp.transpose(w_up.reshape(shard_rows, ff // ratio, ratio), (0, 2, 1)).reshape(
+        shard_rows, ff
+    )
+    mlp_pack = jnp.concatenate([w_out, w_up_p, w_down.reshape(shard_rows, ratio * width)], axis=1)
     qkv_cols = thirds(w_qkv.shape[1])
     qkv_parts = split_cols(w_qkv, qkv_cols)
     gathered = gather_routes(
@@ -333,6 +337,7 @@
         lax.all_gather(mlp_pack, ALL, axis=0, tiled=True), [width, ff, ff]
     )
     down_parts = split_cols(down_view, [width] * ratio)
+    bias_up_p = jnp.transpose(bias_up.reshape(ff // ratio, ratio)).reshape(ff)
 
     branch = jnp.dot(attended_b, proj_out, preferred_element_type=jnp.float32) + bias_out.astype(
         jnp.float32
@@ -342,28 +347,29 @@
         layer_norm, middle, gain_two.astype(jnp.float32), shift_two.astype(jnp.float32)
     )
     normed_two = normed_two_f.astype(jnp.bfloat16)
-    hidden = jnp.dot(normed_two, proj_up, preferred_element_type=jnp.float32) + bias_up.astype(
+    hidden = jnp.dot(normed_two, proj_up, preferred_element_type=jnp.float32) + bias_up_p.astype(
         jnp.float32
     )
     activated_f, gelu_back = jax.vjp(partial(jax.nn.gelu, approximate=False), hidden)
     activated = activated_f.astype(jnp.bfloat16)
-    mlp_sum = None
-    for c, part in enumerate(down_parts):
-        term = jnp.dot(activated[:, c::ratio], part, preferred_element_type=jnp.float32)
-        mlp_sum = term if mlp_sum is None else mlp_sum + term
+    act_parts = split_cols(activated, [width] * ratio)
+    mlp_sum = jnp.dot(act_parts[0], down_parts[0], preferred_element_type=jnp.float32)
+    for a, w in zip(act_parts[1:], down_parts[1:]):
+        mlp_sum = mlp_sum + jnp.dot(a, w, preferred_element_type=jnp.float32)
     mlp_out = mlp_sum + bias_down.astype(jnp.float32)
     outputs = (middle + mlp_out).astype(jnp.bfloat16)
 
     out_grad = cotangent[:, 0].reshape(rows, width)
     out_grad_f = out_grad.astype(jnp.float32)
-    grad_down = outer_rows(activated, out_grad)
+    grad_down = outer_rows(activated, out_grad).reshape(ratio, ff // ratio, width)
     grad_bias_down = jnp.sum(out_grad_f, axis=0)
-    act_grad = jnp.stack([times_transposed(out_grad, part) for part in down_parts], axis=-1)
-    act_grad = act_grad.reshape(rows, ratio * width)
+    act_grad = jnp.concatenate([times_transposed(out_grad, w) for w in down_parts], axis=1)
     (hidden_grad,) = gelu_back(act_grad)
     hidden_grad_b = hidden_grad.astype(jnp.bfloat16)
     grad_up = outer_rows(normed_two, hidden_grad_b)
-    grad_bias_up = jnp.sum(hidden_grad_b.astype(jnp.float32), axis=0)
+    grad_bias_up = jnp.transpose(
+        jnp.sum(hidden_grad_b.astype(jnp.float32), axis=0).reshape(ratio, ff // ratio)
+    ).reshape(ff)
     normed_two_grad = times_transposed(hidden_grad_b, proj_up)
     middle_ln_grad, grad_gain_two, grad_shift_two = norm_two_back(normed_two_grad)
     middle_grad = out_grad_f + middle_ln_grad
@@ -395,6 +401,10 @@
         backward_anchors[:steps],
     )
     red_out, red_vec_one = split_cols(red_mixed, [width, vec_one.shape[1]])
+    red_up = jnp.transpose(red_up.reshape(shard_rows, ratio, ff // ratio), (0, 2, 1)).reshape(
+        shard_rows, ff
+    )
+    red_down = jnp.transpose(red_down, (1, 0, 2)).reshape(shard_rows * ratio, width)
 
     grad_bias_query = jnp.sum(proj_grad[:, :width].astype(jnp.float32), axis=0)
     grad_bias_value = jnp.sum(proj_grad[:, 2 * width :].astype(jnp.float32), axis=0)

time: 510 us -> 443 us (0.87)
  local copies, waits for them, and re-layouts: 168 us -> 98.4 us
  waiting for transfers between devices: 122 us -> 109 us
  starting transfers between devices: 63.2 us -> 75.5 us
    slice x4 -> x0, local copies, waits for them, and re-layouts: 65.4 us -> none  [body(): activated[:, c::ratio]]
    all_to_all x2, starting transfers between devices: 10.1 us -> 21.1 us  [rows_to_units(): x = lax.all_to_all(x, 'seq', 0, 0, tiled=True)]
    ppermute x15, waiting for transfers between devices: 21.8 us -> 13 us  [gather_routes(): got = lax.ppermute(x, ALL, partner_pairs(count, b))]
    reshape x9, local copies, waits for them, and re-layouts: 6.74 us -> 0.89 us  [vector_block(): cols = [v.reshape(rows, -1).astype(dtype) for v in vectors]]
    add x30 -> x29, other arithmetic: 21.6 us -> 20.2 us  [reduce_routes(): x = keep + got.astype(jnp.float32)]
    unnamed x141 -> x144, local copies, waits for them, and re-layouts: 19.2 us -> 18.7 us
  transfers between devices with their start and end apart: 50 -> 50, of which waited for: 25 -> 23; matrix products, arithmetic and copies ran while one was open for 36% -> 40% of each run, Pallas kernels for 0% -> 0%
where the time goes in v8:
time: 443 us; the launch traced here: 434 us
  waiting for transfers between devices  109 us (25%)
  local copies, waits for them, and re-layouts  98.4 us (22%)
  matrix products  78.8 us (18%)
  starting transfers between devices  75.5 us (17%)
  other arithmetic  55.9 us (13%)
  between operations  16.1 us (4%)
    ppermute x30, waiting for transfers between devices, reduce_routes(): got = lax.ppermute(send, ALL, partner_pairs(count, b))  47.7 us
    all_to_all x2, waiting for transfers between devices, rows_to_units(): x = lax.all_to_all(x, 'seq', 0, 0, tiled=True)  34.9 us
    ppermute x30, starting transfers between devices, reduce_routes(): got = lax.ppermute(send, ALL, partner_pairs(count, b))  25.4 us
    all_to_all x2, starting transfers between devices, rows_to_units(): x = lax.all_to_all(x, 'seq', 0, 0, tiled=True)  21.1 us
    add x29, other arithmetic, reduce_routes(): x = keep + got.astype(jnp.float32)  20.2 us
    ppermute x15, starting transfers between devices, gather_routes(): got = lax.ppermute(x, ALL, partner_pairs(count, b))  20.1 us
    unnamed x144, local copies, waits for them, and re-layouts  18.7 us
    convert_element_type x30, local copies, waits for them, and re-layouts, reduce_routes(): lax.dynamic_index_in_dim(x, 1 - mine, axis, keepdims=False)  18.6 us
  transfers between devices with their start and end apart: 50, of which 23 were waited for; matrix products, arithmetic and copies ran while one was open for 40% of the time, Pallas kernels for 0%

profile of v8, /device:TPU:0, one launch (start us, length us, event | category | flops | bytes accessed | tf_op | source)
XLA Modules:
  0.0 434.0 jit_solution(4713896395529022530)
XLA Ops:
  13.0 4.1 collective-permute-start
  45.8 4.5 %collective-permute-done.3 = bf16[2,2,2,24,896]{4,3,2,1,0:T(8,128)(2,1)S(1)} collective-permute-done((bf16[2,2,2,24,896]{4,3,2,1,0:T(8,128)(2,1)S(1)}, bf16[2,2,2,24,896]{4,3,2,1,0:T(8,128)(2,1)S(1)}, u32[]{:S(2)}, u32[]{:S(2)}) %collective-permute-start.3) | collective-permute-done | bytes 344096 | tf_op jit(solution)/shard_map/ppermute | solution.py:77
  73.3 16.9 %all-to-all-start = ((bf16[8,3,128,3,64]{2,4,3,1,0:T(8,128)(2,1)}), bf16[8,3,128,3,64]{2,4,3,1,0:T(8,128)(2,1)S(1)}, u32[]{:S(2)}, u32[]{:S(2)}) async-start(bf16[8,3,128,3,64]{2,4,3,1,0:T(8,128)(2,1)} %bitcast.485), calls=%async_computation | async-start | bytes 2359296 | tf_op jit(solution)/shard_map/all_to_all | solution.py:155
  92.8 34.9 %all-to-all-done = bf16[8,3,128,3,64]{2,4,3,1,0:T(8,128)(2,1)S(1)} async-done(((bf16[8,3,128,3,64]{2,4,3,1,0:T(8,128)(2,1)}), bf16[8,3,128,3,64]{2,4,3,1,0:T(8,128)(2,1)S(1)}, u32[]{:S(2)}, u32[]{:S(2)}) %all-to-all-start) | async-done | bytes 1179680 | tf_op jit(solution)/shard_map/all_to_all | solution.py:155
  131.8 6.6 %fusion.142 = (f32[3,1024]{1,0:T(4,128)S(1)}, f32[3,1024,1024]{1,2,0:T(8,128)S(1)}) fusion(bf16[3,1024,3,64]{1,3,0,2:T(8,128)(2,1)S(1)} %reshape.643, pred[3,1024]{1,0:T(4,128)(4,1)S(1)} %broadcast_compare_fusion, s32[3,1024]{1,0:T(4,128)S(1)} %broadcast_add_fusion, pred[1024,1024]{0,1:T(8,128)(4,1)} %iota_compare_fusion), kind=kOutput, calls=%fused_computation.340 | convolution fusion | flops 421524480 | bytes 14467072 | tf_op jit(solution)/shard_map/uqd,ukd->uqk/dot_general | solution.py:173
  144.3 4.1 all-to-all-start.1
  151.7 8.6 %all-to-all-done.1 = bf16[8,3,128,1,64]{2,4,3,1,0:T(8,128)(2,1)S(1)} async-done(((bf16[8,3,128,1,64]{2,4,3,1,0:T(8,128)(2,1)}), bf16[8,3,128,1,64]{2,4,3,1,0:T(8,128)(2,1)S(1)}, u32[]{:S(2)}, u32[]{:S(2)}) %all-to-all-start.1) | async-done | bytes 393248 | tf_op jit(solution)/shard_map/all_to_all | solution.py:165
  170.2 9.1 %convert_reduce_fusion = (f32[3072]{0:T(1024)}, bf16[256,3072]{1,0:T(8,128)(2,1)S(1)}, f32[256,3072]{1,0:T(8,128)S(1)}, f32[256,3072]{1,0:T(8,128)S(1)}) fusion(f32[256,768]{1,0:T(8,128)S(1)} %convolution_bitcast_fusion, f32[256,768]{1,0:T(8,128)S(1)} %convolution_bitcast_fusion.1, f32[256,768]{1,0:T(8,128)S(1)} %convolution_bitcast_fusion.2, ...), kind=kOutput, calls=%fused_computation.40 | convolution fusion | flops 1270281216 | bytes 16549888 | tf_op jit(solution)/shard_map/dot_general | solution.py:350
  179.3 7.6 %fusion.10 = bf16[3072,256]{0,1:T(8,128)(2,1)} fusion(f32[256,3072]{1,0:T(8,128)S(1)} %get-tuple-element.175), kind=kLoop, calls=%fused_computation.21 | loop fusion | flops 51118080 | bytes 4718592 | tf_op jit(solution)/shard_map/convert_element_type | solution.py:354
  188.7 5.1 %fusion.135 = f32[768,3072]{1,0:T(8,128)} fusion(bf16[256,3072]{1,0:T(8,128)(2,1)S(1)} %get-tuple-element.124, f32[256,768]{1,0:T(8,128)S(1)} %get-tuple-element.174, f32[768]{0:T(1024)S(1)} %get-tuple-element.103, f32[768]{0:T(1024)S(1)} %get-tuple-element.104, f32[256]{0:T(256)S(1)} %fusion.110, f32[256]{0:T(256)S(1)} %broadcast_multiply_fusion), kind=kOutput, calls=%fused_computation.335 | convolution fusion | flops 1208942592 | bytes 11804672 | tf_op jit(solution)/shard_map/dot_general | solution.py:36
  204.1 4.2 all-to-all-start.2
  217.2 4.5 %concatenate.58 = f32[2,2,2,2,2,24,896]{6,5,4,3,2,1,0:T(8,128)} concatenate(f32[2,2,2,2,2,24,768]{6,5,4,3,2,1,0:T(8,128)} %fusion.84, f32[2,2,2,2,2,24,4]{6,5,4,3,2,1,0:T(8,128)} %bitcast.499, f32[2,2,2,2,2,24,1]{6,5,4,3,2,1,0:T(8,128)} %concatenate.64, f32[2,2,2,2,2,24,1]{6,5,4,3,2,1,0:T(8,128)} %concatenate.65, f32[2,2,2,2,2,24,1]{6,5,4,3,2,1,0:T(8,128)} %concatenate.66, ...), dimensions={6} | concatenate | bytes 5505024 | tf_op jit(solution)/shard_map/concatenate | solution.py:397
  224.0 4.1 fusion.35
  250.8 6.7 %multiply_convert_fusion = bf16[3,1024,1024]{1,2,0:T(8,128)(2,1)S(1)} fusion(f32[3,1024,1024]{1,2,0:T(8,128)} %copy-done.2, f32[3,1024]{1,0:T(4,128)S(1)} %div.84, bf16[3,1024,3,64]{1,3,0,2:T(8,128)(2,1)} %copy-done.14, bf16[3,1024,64]{1,2,0:T(8,128)(2,1)S(1)} %squeeze_reshape.3, f32[3,1024]{1,0:T(4,128)} %copy-done.32), kind=kOutput, calls=%fused_computation.4 | convolution fusion | flops 412680192 | bytes 19689472 | tf_op jit(solution)/shard_map/uqd,ukd->uqk/dot_general | solution.py:187
  257.5 4.2 fusion.45
  269.9 4.2 fusion.46
  275.7 4.8 %all-to-all-start.3 = ((bf16[8,3,128,3,64]{2,4,3,1,0:T(8,128)(2,1)}), bf16[8,3,128,3,64]{2,4,3,1,0:T(8,128)(2,1)}, u32[]{:S(2)}, u32[]{:S(2)}) async-start(bf16[8,3,128,3,64]{2,4,3,1,0:T(8,128)(2,1)} %maximum_bitcast_fusion), calls=%async_computation.3 | async-start | bytes 2359296 | tf_op jit(solution)/shard_map/all_to_all | solution.py:165
  304.2 5.1 %all-to-all-done.3 = bf16[8,3,128,3,64]{2,4,3,1,0:T(8,128)(2,1)} async-done(((bf16[8,3,128,3,64]{2,4,3,1,0:T(8,128)(2,1)}), bf16[8,3,128,3,64]{2,4,3,1,0:T(8,128)(2,1)}, u32[]{:S(2)}, u32[]{:S(2)}) %all-to-all-start.3) | async-done | bytes 1179680 | tf_op jit(solution)/shard_map/all_to_all | solution.py:165
  334.0 4.4 %concatenate.52 = f32[2,2,2,2,2,24,896]{6,5,4,3,2,1,0:T(8,128)} concatenate(f32[2,2,2,2,2,24,768]{6,5,4,3,2,1,0:T(8,128)S(1)} %copy-done.8, f32[2,2,2,2,2,24,1]{6,5,4,3,2,1,0:T(8,128)S(1)} %concatenate.59, f32[2,2,2,2,2,24,1]{6,5,4,3,2,1,0:T(8,128)S(1)} %concatenate.60, f32[2,2,2,2,2,24,1]{6,5,4,3,2,1,0:T(8,128)} %concatenate.61, f32[2,2,2,2,2,24,1]{6,5,4,3,2,1,0:T(8,128)} %concatenate.62, ...), dimensions={6} | concatenate | bytes 5505024 | tf_op jit(solution)/shard_map/concatenate | solution.py:425
  348.7 4.0 collective-permute-done.34
  372.9 13.2 %collective-permute-done.27 = bf16[2,2,24,768]{3,2,1,0:T(8,128)(2,1)S(1)} collective-permute-done((bf16[2,2,24,768]{3,2,1,0:T(8,128)(2,1)S(1)}, bf16[2,2,24,768]{3,2,1,0:T(8,128)(2,1)S(1)}, u32[]{:S(2)}, u32[]{:S(2)}) %collective-permute-start.27) | collective-permute-done | bytes 147488 | tf_op jit(solution)/shard_map/ppermute | solution.py:103
  399.9 3.9 collective-permute-done.19
  407.1 7.9 %collective-permute-done.38 = bf16[2,24,3072]{2,1,0:T(8,128)(2,1)S(1)} collective-permute-done((bf16[2,24,3072]{2,1,0:T(8,128)(2,1)S(1)}, bf16[2,24,3072]{2,1,0:T(8,128)(2,1)S(1)}, u32[]{:S(2)}, u32[]{:S(2)}) %collective-permute-start.38) | collective-permute-done | bytes 294944 | tf_op jit(solution)/shard_map/ppermute | solution.py:103
  418.2 5.5 %collective-permute-done.39 = bf16[24,3072]{1,0:T(8,128)(2,1)S(1)} collective-permute-done((bf16[24,3072]{1,0:T(8,128)(2,1)S(1)}, bf16[24,3072]{1,0:T(8,128)(2,1)S(1)}, u32[]{:S(2)}, u32[]{:S(2)}) %collective-permute-start.39) | collective-permute-done | bytes 147488 | tf_op jit(solution)/shard_map/ppermute | solution.py:103
  (445 shorter events, 239.7 us)
Async XLA Ops:
  7.3 154.2 %all-gather.2.cloned.1.call-start = ((), (), s32[]{:S(2)}) async-start(), calls=%async_computation.4 | async-start | bytes 10948608 | tf_op jit(solution)/shard_map/all_gather | solution.py:337
  13.0 12.4 %collective-permute-start = (bf16[24,896]{1,0:T(8,128)(2,1)S(1)}, bf16[24,896]{1,0:T(8,128)(2,1)S(1)}, u32[]{:S(2)}, u32[]{:S(2)}) collective-permute-start(bf16[24,896]{1,0:T(8,128)(2,1)S(1)} %concatenate.43), channel_id=1, source_target_pairs={{0,4},{1,5},{2,6},{3,7},{4,0},{5,1},{6,2},{7,3},{8,12},{9,13},{10,... | collective-permute-start | bytes 129032 | tf_op jit(solution)/shard_map/ppermute | solution.py:77
  39.5 10.7 %collective-permute-start.3 = (bf16[2,2,2,24,896]{4,3,2,1,0:T(8,128)(2,1)S(1)}, bf16[2,2,2,24,896]{4,3,2,1,0:T(8,128)(2,1)S(1)}, u32[]{:S(2)}, u32[]{:S(2)}) collective-permute-start(bf16[2,2,2,24,896]{4,3,2,1,0:T(8,128)(2,1)S(1)} %get-tuple-element.143), channel_id=1, source_target_pairs={{0,2},{1,3},{2,0},{3,1},{4,6},{5,7},{6,4},{7,5},{8,10},{9,11},{10,... | collective-permute-start | bytes 1032200 | tf_op jit(solution)/shard_map/ppermute | solution.py:77
  73.3 54.3 %all-to-all-start = ((bf16[8,3,128,3,64]{2,4,3,1,0:T(8,128)(2,1)}), bf16[8,3,128,3,64]{2,4,3,1,0:T(8,128)(2,1)S(1)}, u32[]{:S(2)}, u32[]{:S(2)}) async-start(bf16[8,3,128,3,64]{2,4,3,1,0:T(8,128)(2,1)} %bitcast.485), calls=%async_computation | async-start | bytes 2359296 | tf_op jit(solution)/shard_map/all_to_all | solution.py:155
  144.3 15.9 %all-to-all-start.1 = ((bf16[8,3,128,1,64]{2,4,3,1,0:T(8,128)(2,1)}), bf16[8,3,128,1,64]{2,4,3,1,0:T(8,128)(2,1)S(1)}, u32[]{:S(2)}, u32[]{:S(2)}) async-start(bf16[8,3,128,1,64]{2,4,3,1,0:T(8,128)(2,1)} %bitcast.449), calls=%async_computation.1 | async-start | bytes 786432 | tf_op jit(solution)/shard_map/all_to_all | solution.py:165
  204.1 41.4 %all-to-all-start.2 = ((bf16[8,3,128,1,64]{2,4,3,1,0:T(8,128)(2,1)}), bf16[8,3,128,1,64]{2,4,3,1,0:T(8,128)(2,1)}, u32[]{:S(2)}, u32[]{:S(2)}) async-start(bf16[8,3,128,1,64]{2,4,3,1,0:T(8,128)(2,1)} %bitcast.494), calls=%async_computation.2 | async-start | bytes 786432 | tf_op jit(solution)/shard_map/all_to_all | solution.py:155
  224.0 37.7 %collective-permute-start.30 = (bf16[2,2,2,2,24,896]{5,4,3,2,1,0:T(8,128)(2,1)}, bf16[2,2,2,2,24,896]{5,4,3,2,1,0:T(8,128)(2,1)}, u32[]{:S(2)}, u32[]{:S(2)}) collective-permute-start(bf16[2,2,2,2,24,896]{5,4,3,2,1,0:T(8,128)(2,1)} %fusion.68), channel_id=1, source_target_pairs={{0,8},{1,9},{2,10},{3,11},{4,12},{5,13},{6,14},{7,15},{8,0},{9,1},... | collective-permute-start | bytes 2064392 | tf_op jit(solution)/shard_map/ppermute | solution.py:103
  228.1 62.7 %collective-permute-start.35 = (bf16[2,2,2,2,24,3072]{5,4,1,2,3,0:T(8,128)(2,1)}, bf16[2,2,2,2,24,3072]{5,4,1,2,3,0:T(8,128)(2,1)}, u32[]{:S(2)}, u32[]{:S(2)}) collective-permute-start(bf16[2,2,2,2,24,3072]{5,4,1,2,3,0:T(8,128)(2,1)} %fusion.35), channel_id=1, source_target_pairs={{0,8},{1,9},{2,10},{3,11},{4,12},{5,13},{6,14},{7,15},{8,0},{9,1},... | collective-permute-start | bytes 7077896 | tf_op jit(solution)/shard_map/ppermute | solution.py:103
  239.4 57.1 %collective-permute-start.40 = (bf16[4,2,2,2,2,24,768]{6,5,4,3,2,1,0:T(8,128)(2,1)}, bf16[4,2,2,2,2,24,768]{6,5,4,3,2,1,0:T(8,128)(2,1)}, u32[]{:S(2)}, u32[]{:S(2)}) collective-permute-start(bf16[4,2,2,2,2,24,768]{6,5,4,3,2,1,0:T(8,128)(2,1)} %fusion.34), channel_id=1, source_target_pairs={{0,8},{1,9},{2,10},{3,11},{4,12},{5,13},{6,14},{7,15},{8,0},{9,1},... | collective-permute-start | bytes 7077896 | tf_op jit(solution)/shard_map/ppermute | solution.py:103
  265.2 15.4 %collective-permute-start.31 = (bf16[2,2,2,24,896]{4,3,2,1,0:T(8,128)(2,1)}, bf16[2,2,2,24,896]{4,3,2,1,0:T(8,128)(2,1)}, u32[]{:S(2)}, u32[]{:S(2)}) collective-permute-start(bf16[2,2,2,24,896]{4,3,2,1,0:T(8,128)(2,1)} %fusion.89), channel_id=1, source_target_pairs={{0,2},{1,3},{2,0},{3,1},{4,6},{5,7},{6,4},{7,5},{8,10},{9,11},{10,... | collective-permute-start | bytes 1032200 | tf_op jit(solution)/shard_map/ppermute | solution.py:103
  275.7 33.6 %all-to-all-start.3 = ((bf16[8,3,128,3,64]{2,4,3,1,0:T(8,128)(2,1)}), bf16[8,3,128,3,64]{2,4,3,1,0:T(8,128)(2,1)}, u32[]{:S(2)}, u32[]{:S(2)}) async-start(bf16[8,3,128,3,64]{2,4,3,1,0:T(8,128)(2,1)} %maximum_bitcast_fusion), calls=%async_computation.3 | async-start | bytes 2359296 | tf_op jit(solution)/shard_map/all_to_all | solution.py:165
  295.8 64.6 %collective-permute-start.36 = (bf16[2,2,2,24,3072]{4,3,0,1,2:T(8,128)(2,1)}, bf16[2,2,2,24,3072]{4,3,0,1,2:T(8,128)(2,1)}, u32[]{:S(2)}, u32[]{:S(2)}) collective-permute-start(bf16[2,2,2,24,3072]{4,3,0,1,2:T(8,128)(2,1)} %fusion.50), channel_id=1, source_target_pairs={{0,16},{1,17},{2,18},{3,19},{4,20},{5,21},{6,22},{7,23},{8,24},{9,... | collective-permute-start | bytes 3538952 | tf_op jit(solution)/shard_map/ppermute | solution.py:103
  302.8 60.2 %collective-permute-start.41 = (bf16[4,2,2,2,24,768]{5,4,3,2,1,0:T(8,128)(2,1)}, bf16[4,2,2,2,24,768]{5,4,3,2,1,0:T(8,128)(2,1)}, u32[]{:S(2)}, u32[]{:S(2)}) collective-permute-start(bf16[4,2,2,2,24,768]{5,4,3,2,1,0:T(8,128)(2,1)} %fusion.51), channel_id=1, source_target_pairs={{0,1},{1,0},{2,3},{3,2},{4,5},{5,4},{6,7},{7,6},{8,9},{9,8},{10,11... | collective-permute-start | bytes 3538952 | tf_op jit(solution)/shard_map/ppermute | solution.py:103
  340.8 19.3 %collective-permute-start.15 = (bf16[2,2,2,2,24,896]{5,4,3,2,1,0:T(8,128)(2,1)}, bf16[2,2,2,2,24,896]{5,4,3,2,1,0:T(8,128)(2,1)S(1)}, u32[]{:S(2)}, u32[]{:S(2)}) collective-permute-start(bf16[2,2,2,2,24,896]{5,4,3,2,1,0:T(8,128)(2,1)} %fusion.67), channel_id=1, source_target_pairs={{0,8},{1,9},{2,10},{3,11},{4,12},{5,13},{6,14},{7,15},{8,0},{9,1},... | collective-permute-start | bytes 2064392 | tf_op jit(solution)/shard_map/ppermute | solution.py:103
  356.5 10.2 %collective-permute-start.26 = (bf16[2,2,2,24,768]{4,3,1,0,2:T(8,128)(2,1)S(1)}, bf16[2,2,2,24,768]{4,3,1,0,2:T(8,128)(2,1)S(1)}, u32[]{:S(2)}, u32[]{:S(2)}) collective-permute-start(bf16[2,2,2,24,768]{4,3,1,0,2:T(8,128)(2,1)S(1)} %fusion.91), channel_id=1, source_target_pairs={{0,1},{1,0},{2,3},{3,2},{4,5},{5,4},{6,7},{7,6},{8,9},{9,8},{10,11... | collective-permute-start | bytes 884744 | tf_op jit(solution)/shard_map/ppermute | solution.py:103
  360.3 11.0 %collective-permute-start.16 = (bf16[2,2,2,24,896]{4,3,2,1,0:T(8,128)(2,1)S(1)}, bf16[2,2,2,24,896]{4,3,2,1,0:T(8,128)(2,1)S(1)}, u32[]{:S(2)}, u32[]{:S(2)}) collective-permute-start(bf16[2,2,2,24,896]{4,3,2,1,0:T(8,128)(2,1)S(1)} %fusion.88), channel_id=1, source_target_pairs={{0,2},{1,3},{2,0},{3,1},{4,6},{5,7},{6,4},{7,5},{8,10},{9,11},{10,... | collective-permute-start | bytes 1032200 | tf_op jit(solution)/shard_map/ppermute | solution.py:103
  362.2 43.2 %collective-permute-start.37 = (bf16[2,2,24,3072]{3,2,0,1:T(8,128)(2,1)S(1)}, bf16[2,2,24,3072]{3,2,0,1:T(8,128)(2,1)S(1)}, u32[]{:S(2)}, u32[]{:S(2)}) collective-permute-start(bf16[2,2,24,3072]{3,2,0,1:T(8,128)(2,1)S(1)} %fusion.69), channel_id=1, source_target_pairs={{0,1},{1,0},{2,3},{3,2},{4,5},{5,4},{6,7},{7,6},{8,9},{9,8},{10,11... | collective-permute-start | bytes 1769480 | tf_op jit(solution)/shard_map/ppermute | solution.py:103
  364.7 41.2 %collective-permute-start.42 = (bf16[4,2,2,24,768]{4,3,2,1,0:T(8,128)(2,1)S(1)}, bf16[4,2,2,24,768]{4,3,2,1,0:T(8,128)(2,1)S(1)}, u32[]{:S(2)}, u32[]{:S(2)}) collective-permute-start(bf16[4,2,2,24,768]{4,3,2,1,0:T(8,128)(2,1)S(1)} %fusion.70), channel_id=1, source_target_pairs={{0,2},{1,3},{2,0},{3,1},{4,6},{5,7},{6,4},{7,5},{8,10},{9,11},{10,... | collective-permute-start | bytes 1769480 | tf_op jit(solution)/shard_map/ppermute | solution.py:103
  366.8 19.3 %collective-permute-start.27 = (bf16[2,2,24,768]{3,2,1,0:T(8,128)(2,1)S(1)}, bf16[2,2,24,768]{3,2,1,0:T(8,128)(2,1)S(1)}, u32[]{:S(2)}, u32[]{:S(2)}) collective-permute-start(bf16[2,2,24,768]{3,2,1,0:T(8,128)(2,1)S(1)} %fusion.98), channel_id=1, source_target_pairs={{0,2},{1,3},{2,0},{3,1},{4,6},{5,7},{6,4},{7,5},{8,10},{9,11},{10,... | collective-permute-start | bytes 442376 | tf_op jit(solution)/shard_map/ppermute | solution.py:103
  368.7 18.9 %collective-permute-start.22 = (bf16[2,2,24,768]{3,2,0,1:T(8,128)(2,1)S(1)}, bf16[2,2,24,768]{3,2,0,1:T(8,128)(2,1)S(1)}, u32[]{:S(2)}, u32[]{:S(2)}) collective-permute-start(bf16[2,2,24,768]{3,2,0,1:T(8,128)(2,1)S(1)} %fusion.97), channel_id=1, source_target_pairs={{0,1},{1,0},{2,3},{3,2},{4,5},{5,4},{6,7},{7,6},{8,9},{9,8},{10,11... | collective-permute-start | bytes 442376 | tf_op jit(solution)/shard_map/ppermute | solution.py:103
  371.4 22.3 %collective-permute-start.17 = (bf16[2,2,24,896]{3,2,1,0:T(8,128)(2,1)S(1)}, bf16[2,2,24,896]{3,2,1,0:T(8,128)(2,1)S(1)}, u32[]{:S(2)}, u32[]{:S(2)}) collective-permute-start(bf16[2,2,24,896]{3,2,1,0:T(8,128)(2,1)S(1)} %fusion.95), channel_id=1, source_target_pairs={{0,16},{1,17},{2,18},{3,19},{4,20},{5,21},{6,22},{7,23},{8,24},{9,... | collective-permute-start | bytes 516104 | tf_op jit(solution)/shard_map/ppermute | solution.py:103
  405.5 9.4 %collective-permute-start.38 = (bf16[2,24,3072]{2,1,0:T(8,128)(2,1)S(1)}, bf16[2,24,3072]{2,1,0:T(8,128)(2,1)S(1)}, u32[]{:S(2)}, u32[]{:S(2)}) collective-permute-start(bf16[2,24,3072]{2,1,0:T(8,128)(2,1)S(1)} %fusion.92), channel_id=1, source_target_pairs={{0,2},{1,3},{2,0},{3,1},{4,6},{5,7},{6,4},{7,5},{8,10},{9,11},{10,... | collective-permute-start | bytes 884744 | tf_op jit(solution)/shard_map/ppermute | solution.py:103
  406.1 10.0 %collective-permute-start.43 = (bf16[4,2,24,768]{3,2,1,0:T(8,128)(2,1)S(1)}, bf16[4,2,24,768]{3,2,1,0:T(8,128)(2,1)S(1)}, u32[]{:S(2)}, u32[]{:S(2)}) collective-permute-start(bf16[4,2,24,768]{3,2,1,0:T(8,128)(2,1)S(1)} %fusion.93), channel_id=1, source_target_pairs={{0,16},{1,17},{2,18},{3,19},{4,20},{5,21},{6,22},{7,23},{8,24},{9,... | collective-permute-start | bytes 884744 | tf_op jit(solution)/shard_map/ppermute | solution.py:103
  416.1 9.6 %collective-permute-start.44 = (bf16[4,24,768]{2,1,0:T(8,128)(2,1)S(1)}, bf16[4,24,768]{2,1,0:T(8,128)(2,1)S(1)}, u32[]{:S(2)}, u32[]{:S(2)}) collective-permute-start(bf16[4,24,768]{2,1,0:T(8,128)(2,1)S(1)} %fusion.100), channel_id=1, source_target_pairs={{0,4},{1,5},{2,6},{3,7},{4,0},{5,1},{6,2},{7,3},{8,12},{9,13},{10,... | collective-permute-start | bytes 442376 | tf_op jit(solution)/shard_map/ppermute | solution.py:103
  (92 other events, 633.2 us)
Sparse Core Ops, SparseCore 0:
  12.0 100.0 all-gather.1

commit v9 on v3

--- a/solution.py
+++ b/solution.py
@@ -271,6 +271,14 @@
     vecs_local = vector_block(
         [ln1_g, ln1_b, b_q, b_v, b_out, ln2_g, ln2_b, b_down, b_up], shard_rows, jnp.bfloat16
     )
+    mlp_pack = jnp.concatenate(
+        [
+            w_out.reshape(shard_rows * ratio, width // ratio),
+            w_up.reshape(shard_rows * ratio, ff // ratio),
+            w_down,
+        ],
+        axis=1,
+    )
     qkv_cols = thirds(w_qkv.shape[1])
     qkv_parts = split_cols(w_qkv, qkv_cols)
     gathered = gather_routes(
@@ -328,21 +336,24 @@
         attended_b = attended.astype(jnp.bfloat16)
         forward_anchors = [queries] + [attended] * (steps - 1)
 
-    proj_up, proj_down, proj_out = gather_routes(
-        [w_up, w_down, w_out], orders, count, me, forward_anchors[:steps]
-    )
-
-    branch = jnp.dot(attended_b, proj_out, preferred_element_type=jnp.float32) + bias_out.astype(
-        jnp.float32
-    )
+    out_view, up_view, proj_down = split_cols(
+        lax.all_gather(mlp_pack, ALL, axis=0, tiled=True), [width // ratio, ff // ratio, width]
+    )
+    full_rows = count * shard_rows
+    out3 = out_view.reshape(full_rows, ratio, width // ratio)
+    up3 = up_view.reshape(full_rows, ratio, ff // ratio)
+
+    branch = jnp.einsum(
+        "nr,rck->nck", attended_b, out3, preferred_element_type=jnp.float32
+    ).reshape(rows, width) + bias_out.astype(jnp.float32)
     middle = seq_in + branch
     normed_two_f, norm_two_back = jax.vjp(
         layer_norm, middle, gain_two.astype(jnp.float32), shift_two.astype(jnp.float32)
     )
     normed_two = normed_two_f.astype(jnp.bfloat16)
-    hidden = jnp.dot(normed_two, proj_up, preferred_element_type=jnp.float32) + bias_up.astype(
-        jnp.float32
-    )
+    hidden = jnp.einsum(
+        "nr,rck->nck", normed_two, up3, preferred_element_type=jnp.float32
+    ).reshape(rows, ff) + bias_up.astype(jnp.float32)
     activated_f, gelu_back = jax.vjp(partial(jax.nn.gelu, approximate=False), hidden)
     activated = activated_f.astype(jnp.bfloat16)
     mlp_out = jnp.dot(activated, proj_down, preferred_element_type=jnp.float32) + bias_down.astype(
@@ -359,13 +370,19 @@
     hidden_grad_b = hidden_grad.astype(jnp.bfloat16)
     grad_up = outer_rows(normed_two, hidden_grad_b)
     grad_bias_up = jnp.sum(hidden_grad_b.astype(jnp.float32), axis=0)
-    normed_two_grad = times_transposed(hidden_grad_b, proj_up)
+    normed_two_grad = jnp.einsum(
+        "nck,rck->nr", hidden_grad_b.reshape(rows, ratio, ff // ratio), up3,
+        preferred_element_type=jnp.float32,
+    )
     middle_ln_grad, grad_gain_two, grad_shift_two = norm_two_back(normed_two_grad)
     middle_grad = out_grad_f + middle_ln_grad
     branch_grad = middle_grad.astype(jnp.bfloat16)
     grad_out = outer_rows(attended_b, branch_grad)
     grad_bias_out = jnp.sum(branch_grad.astype(jnp.float32), axis=0)
-    attended_grad = times_transposed(branch_grad, proj_out).astype(jnp.bfloat16)
+    attended_grad = jnp.einsum(
+        "nck,rck->nr", branch_grad.reshape(rows, ratio, width // ratio), out3,
+        preferred_element_type=jnp.float32,
+    ).astype(jnp.bfloat16)
 
     if head_parallel:
         grad_units = rows_to_units(
@@ -378,7 +395,6 @@
         proj_grad = fallback_attention_backward(saved, attended_grad, row_count)
         backward_anchors = [None] + [proj_grad] * (steps - 1)
 
-    full_rows = count * shard_rows
     vec_one = vector_block(
         [grad_bias_up, grad_bias_down, grad_gain_two, grad_shift_two], full_rows, jnp.float32
     )

time: 468 us -> 450 us (0.962)
  other arithmetic: 84 us -> 49.2 us
  local copies, waits for them, and re-layouts: 102 us -> 125 us
  starting transfers between devices: 79.9 us -> 63.6 us
  between operations: 2.92 us -> 16 us
  waiting for transfers between devices: 130 us -> 121 us
  matrix products: 61.6 us -> 66.6 us
    ppermute x30 -> x15, waiting for transfers between devices: 78.8 us -> 21.6 us  [gather_routes(): got = lax.ppermute(x, ALL, partner_pairs(count, b))]
    all_to_all x2, waiting for transfers between devices: 0.01 us -> 40 us  [rows_to_units(): x = lax.all_to_all(x, 'seq', 0, 0, tiled=True)]
    another operation x30 -> x15, other arithmetic: 24.8 us -> 4.94 us  [gather_routes(): x = jnp.stack([x, got])]
    ppermute x30 -> x15, starting transfers between devices: 34.5 us -> 17.9 us  [gather_routes(): got = lax.ppermute(x, ALL, partner_pairs(count, b))]
    gather x6 -> x3, local copies, waits for them, and re-layouts: 18.1 us -> 4.12 us  [gather_routes(): x = jnp.take(x.reshape(count, rows, cols), rel, axis=0)]
    select_n x10 -> x4, other arithmetic: 15.8 us -> 2.96 us  [gather_routes(): x = jnp.take(x.reshape(count, rows, cols), rel, axis=0)]
    reshape x0 -> x4, local copies, waits for them, and re-layouts: none -> 12.8 us  [the longest x1 8.93 us: body(): up3 = up_view.reshape(full_rows, ratio, ff // ratio)]
    dot_general x0 -> x2, local copies, waits for them, and re-layouts: none -> 11.2 us  [the longest x1 8.52 us: body(): jnp.einsum('nr,rck->nck', normed_two, up3, preferred_element_type=jnp.flo...]
  transfers between devices with their start and end apart: 64 -> 50, of which waited for: 30 -> 24; matrix products, arithmetic and copies ran while one was open for 38% -> 36% of each run, Pallas kernels for 0% -> 0%
where the time goes in v9:
time: 450 us; the launch traced here: 441 us
  local copies, waits for them, and re-layouts  125 us (28%)
  waiting for transfers between devices  121 us (27%)
  matrix products  66.6 us (15%)
  starting transfers between devices  63.6 us (14%)
  other arithmetic  49.2 us (11%)
  between operations  16 us (4%)
    ppermute x30, waiting for transfers between devices, reduce_routes(): got = lax.ppermute(send, ALL, partner_pairs(count, b))  48.1 us
    all_to_all x2, waiting for transfers between devices, rows_to_units(): x = lax.all_to_all(x, 'seq', 0, 0, tiled=True)  40 us
    ppermute x30, starting transfers between devices, reduce_routes(): got = lax.ppermute(send, ALL, partner_pairs(count, b))  26.1 us
    ppermute x15, waiting for transfers between devices, gather_routes(): got = lax.ppermute(x, ALL, partner_pairs(count, b))  21.6 us
    add x30, other arithmetic, reduce_routes(): x = keep + got.astype(jnp.float32)  21 us
    convert_element_type x30, local copies, waits for them, and re-layouts, reduce_routes(): lax.dynamic_index_in_dim(x, 1 - mine, axis, keepdims=False)  18.6 us
    ppermute x15, starting transfers between devices, gather_routes(): got = lax.ppermute(x, ALL, partner_pairs(count, b))  17.9 us
    unnamed x113, local copies, waits for them, and re-layouts  16.7 us
  transfers between devices with their start and end apart: 50, of which 24 were waited for; matrix products, arithmetic and copies ran while one was open for 36% of the time, Pallas kernels for 0%

profile of v9, /device:TPU:0, one launch (start us, length us, event | category | flops | bytes accessed | tf_op | source)
XLA Modules:
  0.0 441.5 jit_solution(16950438827011892693)
XLA Ops:
  18.8 4.1 collective-permute-start
  50.2 5.4 %collective-permute-done.13 = bf16[2,2,2,24,768]{4,3,2,1,0:T(8,128)(2,1)S(1)} collective-permute-done((bf16[2,2,2,24,768]{4,3,2,1,0:T(8,128)(2,1)S(1)}, bf16[2,2,2,24,768]{4,3,2,1,0:T(8,128)(2,1)S(1)}, u32[]{:S(2)}, u32[]{:S(2)}) %collective-permute-start.13) | collective-permute-done | bytes 294944 | tf_op jit(solution)/shard_map/ppermute | solution.py:77
  55.8 4.9 %collective-permute-done.8 = bf16[2,2,2,24,768]{4,3,2,1,0:T(8,128)(2,1)S(1)} collective-permute-done((bf16[2,2,2,24,768]{4,3,2,1,0:T(8,128)(2,1)S(1)}, bf16[2,2,2,24,768]{4,3,2,1,0:T(8,128)(2,1)S(1)}, u32[]{:S(2)}, u32[]{:S(2)}) %collective-permute-start.8) | collective-permute-done | bytes 294944 | tf_op jit(solution)/shard_map/ppermute | solution.py:77
  83.4 6.5 %all-to-all-start = ((bf16[8,3,128,3,64]{2,4,3,1,0:T(8,128)(2,1)}), bf16[8,3,128,3,64]{2,4,3,1,0:T(8,128)(2,1)S(1)}, u32[]{:S(2)}, u32[]{:S(2)}) async-start(bf16[8,3,128,3,64]{2,4,3,1,0:T(8,128)(2,1)} %bitcast.485), calls=%async_computation | async-start | bytes 2359296 | tf_op jit(solution)/shard_map/all_to_all | solution.py:154
  92.5 40.0 %all-to-all-done = bf16[8,3,128,3,64]{2,4,3,1,0:T(8,128)(2,1)S(1)} async-done(((bf16[8,3,128,3,64]{2,4,3,1,0:T(8,128)(2,1)}), bf16[8,3,128,3,64]{2,4,3,1,0:T(8,128)(2,1)S(1)}, u32[]{:S(2)}, u32[]{:S(2)}) %all-to-all-start) | async-done | bytes 1179680 | tf_op jit(solution)/shard_map/all_to_all | solution.py:154
  136.7 6.6 %fusion.152 = (f32[3,1024]{1,0:T(4,128)S(1)}, f32[3,1024,1024]{1,2,0:T(8,128)S(1)}) fusion(bf16[3,1024,3,64]{1,3,0,2:T(8,128)(2,1)S(1)} %reshape.647, pred[3,1024]{1,0:T(4,128)(4,1)S(1)} %broadcast_compare_fusion, s32[3,1024]{1,0:T(4,128)S(1)} %broadcast_add_fusion, pred[1024,1024]{0,1:T(8,128)(4,1)} %iota_compare_fusion), kind=kOutput, calls=%fused_computation.326 | convolution fusion | flops 421524480 | bytes 14467072 | tf_op jit(solution)/shard_map/uqd,ukd->uqk/dot_general | solution.py:172
  155.7 9.5 %all-to-all-done.1 = bf16[8,3,128,1,64]{2,4,3,1,0:T(8,128)(2,1)S(1)} async-done(((bf16[8,3,128,1,64]{2,4,3,1,0:T(8,128)(2,1)}), bf16[8,3,128,1,64]{2,4,3,1,0:T(8,128)(2,1)S(1)}, u32[]{:S(2)}, u32[]{:S(2)}) %all-to-all-start.1) | async-done | bytes 393248 | tf_op jit(solution)/shard_map/all_to_all | solution.py:164
  172.6 7.4 %slice.187 = bf16[3072,768]{1,0:T(8,128)(2,1)} slice(bf16[3072,1728]{1,0:T(8,128)(2,1)} %all-gather.2.cloned.1.call-done), slice={[0:3072], [192:960]} | slice | bytes 9437184 | tf_op jit(solution)/shard_map/slice | solution.py:112
  180.0 8.9 %reshape.653 = bf16[768,4,768]{2,1,0:T(4,128)(2,1)} reshape(bf16[3072,768]{1,0:T(8,128)(2,1)} %slice.187) | data formatting | bytes 9437184 | tf_op jit(solution)/shard_map/reshape | solution.py:344
  188.9 8.5 %copy.196 = bf16[4,768,768]{2,1,0:T(8,128)(2,1)} copy(bf16[4,768,768]{1,0,2:T(4,128)(2,1)} %bitcast.452) | data formatting | bytes 9437184 | tf_op jit(solution)/shard_map/nr,rck->nck/dot_general | solution.py:354
  198.3 9.9 %fusion.9 = (f32[256,3072]{1,0:T(8,128)S(1)}, f32[256,3072]{1,0:T(8,128)S(1)}) fusion(f32[3072]{0:T(1024)S(1)} %reshape.680, bf16[3072,768]{1,0:T(8,128)(2,1)} %bitcast.482, f32[256,768]{1,0:T(8,128)S(1)} %get-tuple-element.171, f32[768]{0:T(1024)S(1)} %get-tuple-element.103, f32[768]{0:T(1024)S(1)} %get-tuple-element.104, f32[256]{0:T(256)S(1)} %fusion.120, ...), kind=kOutput, calls=%fused_computation.21 | convolution fusion | flops 1258487808 | bytes 11816960 | tf_op jit(solution)/shard_map/nr,rck->nck/dot_general | solution.py:354
  208.2 7.5 %fusion.12 = bf16[3072,256]{0,1:T(8,128)(2,1)} fusion(f32[256,3072]{1,0:T(8,128)S(1)} %get-tuple-element.173), kind=kLoop, calls=%fused_computation.24 | loop fusion | flops 51118080 | bytes 4718592 | tf_op jit(solution)/shard_map/convert_element_type | solution.py:358
  219.7 5.1 %fusion.146 = f32[768,3072]{1,0:T(8,128)} fusion(bf16[256,3072]{1,0:T(8,128)(2,1)S(1)} %get-tuple-element.177, f32[256,768]{1,0:T(8,128)S(1)} %get-tuple-element.171, f32[768]{0:T(1024)S(1)} %get-tuple-element.103, f32[768]{0:T(1024)S(1)} %get-tuple-element.104, f32[256]{0:T(256)S(1)} %fusion.120, f32[256]{0:T(256)S(1)} %broadcast_multiply_fusion), kind=kOutput, calls=%fused_computation.321 | convolution fusion | flops 1208942592 | bytes 11804672 | tf_op jit(solution)/shard_map/dot_general | solution.py:36
  243.9 4.3 concatenate.54
  250.5 4.2 fusion.39
  265.0 6.8 %fusion.70 = bf16[3,1024,64]{1,2,0:T(8,128)(2,1)S(1)} fusion(f32[3,1024,1024]{1,2,0:T(8,128)} %copy-done.2, bf16[3,1024,64]{1,2,0:T(8,128)(2,1)S(1)} %squeeze_reshape.3, f32[3,1024]{1,0:T(4,128)S(1)} %copy-done.36), kind=kOutput, calls=%fused_computation.98 | convolution fusion | flops 406585344 | bytes 13381632 | tf_op jit(solution)/shard_map/uqk,uqd->ukd/dot_general | solution.py:190
  272.0 6.6 %multiply_convert_fusion = bf16[3,1024,1024]{1,2,0:T(8,128)(2,1)S(1)} fusion(f32[3,1024,1024]{1,2,0:T(8,128)} %copy-done.2, f32[3,1024]{1,0:T(4,128)S(1)} %div.84, bf16[3,1024,3,64]{1,3,0,2:T(8,128)(2,1)S(1)} %copy-done.18, bf16[3,1024,64]{1,2,0:T(8,128)(2,1)S(1)} %squeeze_reshape.3, f32[3,1024]{1,0:T(4,128)S(1)} %copy-done.36), kind=kOutput, calls=%fused_computation.4 | convolution fusion | flops 412680192 | bytes 19693568 | tf_op jit(solution)/shard_map/uqd,ukd->uqk/dot_general | solution.py:186
  287.4 4.8 %all-to-all-start.3 = ((bf16[8,3,128,3,64]{2,4,3,1,0:T(8,128)(2,1)}), bf16[8,3,128,3,64]{2,4,3,1,0:T(8,128)(2,1)S(1)}, u32[]{:S(2)}, u32[]{:S(2)}) async-start(bf16[8,3,128,3,64]{2,4,3,1,0:T(8,128)(2,1)} %maximum_bitcast_fusion), calls=%async_computation.3 | async-start | bytes 2359296 | tf_op jit(solution)/shard_map/all_to_all | solution.py:164
  295.8 7.3 %fusion.73 = bf16[256,768]{1,0:T(8,128)(2,1)} fusion(f32[256,768]{1,0:T(8,128)S(1)} %get-tuple-element.171, bf16[3072,1728]{1,0:T(8,128)(2,1)} %all-gather.2.cloned.1.call-done, f32[256,3072]{1,0:T(8,128)} %copy-done.29, f32[256,3072]{1,0:T(8,128)} %copy-done.7, f32[768]{0:T(1024)S(1)} %get-tuple-element.102), kind=kOutput, calls=%fused_computation.100 | convolution fusion | flops 1210908672 | bytes 12192768 | tf_op jit(solution)/shard_map/dot_general | solution.py:359
  341.8 4.4 concatenate.48
  380.7 14.0 %collective-permute-done.27 = bf16[2,2,24,768]{3,2,1,0:T(8,128)(2,1)S(1)} collective-permute-done((bf16[2,2,24,768]{3,2,1,0:T(8,128)(2,1)S(1)}, bf16[2,2,24,768]{3,2,1,0:T(8,128)(2,1)S(1)}, u32[]{:S(2)}, u32[]{:S(2)}) %collective-permute-start.27) | collective-permute-done | bytes 147488 | tf_op jit(solution)/shard_map/ppermute | solution.py:102
  407.7 4.5 %collective-permute-done.19 = bf16[24,896]{1,0:T(8,128)(2,1)S(1)} collective-permute-done((bf16[24,896]{1,0:T(8,128)(2,1)S(1)}, bf16[24,896]{1,0:T(8,128)(2,1)S(1)}, u32[]{:S(2)}, u32[]{:S(2)}) %collective-permute-start.19) | collective-permute-done | bytes 43040 | tf_op jit(solution)/shard_map/ppermute | solution.py:102
  415.3 7.2 %collective-permute-done.38 = bf16[2,24,3072]{2,1,0:T(8,128)(2,1)S(1)} collective-permute-done((bf16[2,24,3072]{2,1,0:T(8,128)(2,1)S(1)}, bf16[2,24,3072]{2,1,0:T(8,128)(2,1)S(1)}, u32[]{:S(2)}, u32[]{:S(2)}) %collective-permute-start.38) | collective-permute-done | bytes 294944 | tf_op jit(solution)/shard_map/ppermute | solution.py:102
  425.8 6.1 %collective-permute-done.39 = bf16[24,3072]{1,0:T(8,128)(2,1)S(1)} collective-permute-done((bf16[24,3072]{1,0:T(8,128)(2,1)S(1)}, bf16[24,3072]{1,0:T(8,128)(2,1)S(1)}, u32[]{:S(2)}, u32[]{:S(2)}) %collective-permute-start.39) | collective-permute-done | bytes 147488 | tf_op jit(solution)/shard_map/ppermute | solution.py:102
  (410 shorter events, 230.9 us)
Async XLA Ops:
  7.2 159.3 %all-gather.2.cloned.1.call-start = ((), (), s32[]{:S(2)}) async-start(), calls=%async_computation.4 | async-start | bytes 11354112 | tf_op jit(solution)/shard_map/all_gather | solution.py:340
  18.8 15.2 %collective-permute-start = (bf16[24,896]{1,0:T(8,128)(2,1)S(1)}, bf16[24,896]{1,0:T(8,128)(2,1)S(1)}, u32[]{:S(2)}, u32[]{:S(2)}) collective-permute-start(bf16[24,896]{1,0:T(8,128)(2,1)S(1)} %concatenate.40), channel_id=1, source_target_pairs={{0,4},{1,5},{2,6},{3,7},{4,0},{5,1},{6,2},{7,3},{8,12},{9,13},{10,... | collective-permute-start | bytes 129032 | tf_op jit(solution)/shard_map/ppermute | solution.py:77
  23.0 10.1 %collective-permute-start.5 = (bf16[24,768]{1,0:T(8,128)(2,1)S(1)}, bf16[24,768]{1,0:T(8,128)(2,1)S(1)}, u32[]{:S(2)}, u32[]{:S(2)}) collective-permute-start(bf16[24,768]{1,0:T(8,128)(2,1)S(1)} %get-tuple-element.155), channel_id=1, source_target_pairs={{0,4},{1,5},{2,6},{3,7},{4,0},{5,1},{6,2},{7,3},{8,12},{9,13},{10,... | collective-permute-start | bytes 110600 | tf_op jit(solution)/shard_map/ppermute | solution.py:77
  42.5 13.1 %collective-permute-start.13 = (bf16[2,2,2,24,768]{4,3,2,1,0:T(8,128)(2,1)S(1)}, bf16[2,2,2,24,768]{4,3,2,1,0:T(8,128)(2,1)S(1)}, u32[]{:S(2)}, u32[]{:S(2)}) collective-permute-start(bf16[2,2,2,24,768]{4,3,2,1,0:T(8,128)(2,1)S(1)} %get-tuple-element.144), channel_id=1, source_target_pairs={{0,1},{1,0},{2,3},{3,2},{4,5},{5,4},{6,7},{7,6},{8,9},{9,8},{10,11... | collective-permute-start | bytes 884744 | tf_op jit(solution)/shard_map/ppermute | solution.py:77
  45.9 14.8 %collective-permute-start.8 = (bf16[2,2,2,24,768]{4,3,2,1,0:T(8,128)(2,1)S(1)}, bf16[2,2,2,24,768]{4,3,2,1,0:T(8,128)(2,1)S(1)}, u32[]{:S(2)}, u32[]{:S(2)}) collective-permute-start(bf16[2,2,2,24,768]{4,3,2,1,0:T(8,128)(2,1)S(1)} %get-tuple-element.142), channel_id=1, source_target_pairs={{0,16},{1,17},{2,18},{3,19},{4,20},{5,21},{6,22},{7,23},{8,24},{9,... | collective-permute-start | bytes 884744 | tf_op jit(solution)/shard_map/ppermute | solution.py:77
  50.1 12.1 %collective-permute-start.3 = (bf16[2,2,2,24,896]{4,3,2,1,0:T(8,128)(2,1)S(1)}, bf16[2,2,2,24,896]{4,3,2,1,0:T(8,128)(2,1)S(1)}, u32[]{:S(2)}, u32[]{:S(2)}) collective-permute-start(bf16[2,2,2,24,896]{4,3,2,1,0:T(8,128)(2,1)S(1)} %get-tuple-element.140), channel_id=1, source_target_pairs={{0,2},{1,3},{2,0},{3,1},{4,6},{5,7},{6,4},{7,5},{8,10},{9,11},{10,... | collective-permute-start | bytes 1032200 | tf_op jit(solution)/shard_map/ppermute | solution.py:77
  83.4 49.1 %all-to-all-start = ((bf16[8,3,128,3,64]{2,4,3,1,0:T(8,128)(2,1)}), bf16[8,3,128,3,64]{2,4,3,1,0:T(8,128)(2,1)S(1)}, u32[]{:S(2)}, u32[]{:S(2)}) async-start(bf16[8,3,128,3,64]{2,4,3,1,0:T(8,128)(2,1)} %bitcast.485), calls=%async_computation | async-start | bytes 2359296 | tf_op jit(solution)/shard_map/all_to_all | solution.py:154
  149.2 16.0 %all-to-all-start.1 = ((bf16[8,3,128,1,64]{2,4,3,1,0:T(8,128)(2,1)}), bf16[8,3,128,1,64]{2,4,3,1,0:T(8,128)(2,1)S(1)}, u32[]{:S(2)}, u32[]{:S(2)}) async-start(bf16[8,3,128,1,64]{2,4,3,1,0:T(8,128)(2,1)} %bitcast.447), calls=%async_computation.1 | async-start | bytes 786432 | tf_op jit(solution)/shard_map/all_to_all | solution.py:164
  232.1 31.4 %all-to-all-start.2 = ((bf16[8,3,128,1,64]{2,4,3,1,0:T(8,128)(2,1)}), bf16[8,3,128,1,64]{2,4,3,1,0:T(8,128)(2,1)}, u32[]{:S(2)}, u32[]{:S(2)}) async-start(bf16[8,3,128,1,64]{2,4,3,1,0:T(8,128)(2,1)} %bitcast.74), calls=%async_computation.2 | async-start | bytes 786432 | tf_op jit(solution)/shard_map/all_to_all | solution.py:154
  250.5 28.0 %collective-permute-start.30 = (bf16[2,2,2,2,24,896]{5,4,3,2,1,0:T(8,128)(2,1)}, bf16[2,2,2,2,24,896]{5,4,3,2,1,0:T(8,128)(2,1)}, u32[]{:S(2)}, u32[]{:S(2)}) collective-permute-start(bf16[2,2,2,2,24,896]{5,4,3,2,1,0:T(8,128)(2,1)} %fusion.83), channel_id=1, source_target_pairs={{0,8},{1,9},{2,10},{3,11},{4,12},{5,13},{6,14},{7,15},{8,0},{9,1},... | collective-permute-start | bytes 2064392 | tf_op jit(solution)/shard_map/ppermute | solution.py:102
  254.7 50.6 %collective-permute-start.35 = (bf16[2,2,2,2,24,3072]{5,4,1,2,3,0:T(8,128)(2,1)}, bf16[2,2,2,2,24,3072]{5,4,1,2,3,0:T(8,128)(2,1)}, u32[]{:S(2)}, u32[]{:S(2)}) collective-permute-start(bf16[2,2,2,2,24,3072]{5,4,1,2,3,0:T(8,128)(2,1)} %fusion.39), channel_id=1, source_target_pairs={{0,8},{1,9},{2,10},{3,11},{4,12},{5,13},{6,14},{7,15},{8,0},{9,1},... | collective-permute-start | bytes 7077896 | tf_op jit(solution)/shard_map/ppermute | solution.py:102
  263.6 47.4 %collective-permute-start.40 = (bf16[2,2,2,2,96,768]{5,4,3,2,1,0:T(8,128)(2,1)}, bf16[2,2,2,2,96,768]{5,4,3,2,1,0:T(8,128)(2,1)}, u32[]{:S(2)}, u32[]{:S(2)}) collective-permute-start(bf16[2,2,2,2,96,768]{5,4,3,2,1,0:T(8,128)(2,1)} %fusion.38), channel_id=1, source_target_pairs={{0,8},{1,9},{2,10},{3,11},{4,12},{5,13},{6,14},{7,15},{8,0},{9,1},... | collective-permute-start | bytes 7077896 | tf_op jit(solution)/shard_map/ppermute | solution.py:102
  280.7 11.6 %collective-permute-start.31 = (bf16[2,2,2,24,896]{4,3,2,1,0:T(8,128)(2,1)}, bf16[2,2,2,24,896]{4,3,2,1,0:T(8,128)(2,1)S(1)}, u32[]{:S(2)}, u32[]{:S(2)}) collective-permute-start(bf16[2,2,2,24,896]{4,3,2,1,0:T(8,128)(2,1)} %fusion.100), channel_id=1, source_target_pairs={{0,2},{1,3},{2,0},{3,1},{4,6},{5,7},{6,4},{7,5},{8,10},{9,11},{10,... | collective-permute-start | bytes 1032200 | tf_op jit(solution)/shard_map/ppermute | solution.py:102
  287.4 33.7 %all-to-all-start.3 = ((bf16[8,3,128,3,64]{2,4,3,1,0:T(8,128)(2,1)}), bf16[8,3,128,3,64]{2,4,3,1,0:T(8,128)(2,1)S(1)}, u32[]{:S(2)}, u32[]{:S(2)}) async-start(bf16[8,3,128,3,64]{2,4,3,1,0:T(8,128)(2,1)} %maximum_bitcast_fusion), calls=%async_computation.3 | async-start | bytes 2359296 | tf_op jit(solution)/shard_map/all_to_all | solution.py:164
  310.4 58.7 %collective-permute-start.36 = (bf16[2,2,2,24,3072]{4,3,0,1,2:T(8,128)(2,1)}, bf16[2,2,2,24,3072]{4,3,0,1,2:T(8,128)(2,1)}, u32[]{:S(2)}, u32[]{:S(2)}) collective-permute-start(bf16[2,2,2,24,3072]{4,3,0,1,2:T(8,128)(2,1)} %fusion.76), channel_id=1, source_target_pairs={{0,16},{1,17},{2,18},{3,19},{4,20},{5,21},{6,22},{7,23},{8,24},{9,... | collective-permute-start | bytes 3538952 | tf_op jit(solution)/shard_map/ppermute | solution.py:102
  317.1 54.5 %collective-permute-start.41 = (bf16[2,2,2,96,768]{4,3,2,1,0:T(8,128)(2,1)}, bf16[2,2,2,96,768]{4,3,2,1,0:T(8,128)(2,1)}, u32[]{:S(2)}, u32[]{:S(2)}) collective-permute-start(bf16[2,2,2,96,768]{4,3,2,1,0:T(8,128)(2,1)} %fusion.77), channel_id=1, source_target_pairs={{0,1},{1,0},{2,3},{3,2},{4,5},{5,4},{6,7},{7,6},{8,9},{9,8},{10,11... | collective-permute-start | bytes 3538952 | tf_op jit(solution)/shard_map/ppermute | solution.py:102
  348.6 20.1 %collective-permute-start.15 = (bf16[2,2,2,2,24,896]{5,4,3,2,1,0:T(8,128)(2,1)}, bf16[2,2,2,2,24,896]{5,4,3,2,1,0:T(8,128)(2,1)S(1)}, u32[]{:S(2)}, u32[]{:S(2)}) collective-permute-start(bf16[2,2,2,2,24,896]{5,4,3,2,1,0:T(8,128)(2,1)} %fusion.82), channel_id=1, source_target_pairs={{0,8},{1,9},{2,10},{3,11},{4,12},{5,13},{6,14},{7,15},{8,0},{9,1},... | collective-permute-start | bytes 2064392 | tf_op jit(solution)/shard_map/ppermute | solution.py:102
  364.3 10.9 %collective-permute-start.26 = (bf16[2,2,2,24,768]{4,3,1,0,2:T(8,128)(2,1)S(1)}, bf16[2,2,2,24,768]{4,3,1,0,2:T(8,128)(2,1)S(1)}, u32[]{:S(2)}, u32[]{:S(2)}) collective-permute-start(bf16[2,2,2,24,768]{4,3,1,0,2:T(8,128)(2,1)S(1)} %fusion.102), channel_id=1, source_target_pairs={{0,1},{1,0},{2,3},{3,2},{4,5},{5,4},{6,7},{7,6},{8,9},{9,8},{10,11... | collective-permute-start | bytes 884744 | tf_op jit(solution)/shard_map/ppermute | solution.py:102
  368.9 11.0 %collective-permute-start.16 = (bf16[2,2,2,24,896]{4,3,2,1,0:T(8,128)(2,1)S(1)}, bf16[2,2,2,24,896]{4,3,2,1,0:T(8,128)(2,1)S(1)}, u32[]{:S(2)}, u32[]{:S(2)}) collective-permute-start(bf16[2,2,2,24,896]{4,3,2,1,0:T(8,128)(2,1)S(1)} %fusion.99), channel_id=1, source_target_pairs={{0,2},{1,3},{2,0},{3,1},{4,6},{5,7},{6,4},{7,5},{8,10},{9,11},{10,... | collective-permute-start | bytes 1032200 | tf_op jit(solution)/shard_map/ppermute | solution.py:102
  370.8 42.9 %collective-permute-start.37 = (bf16[2,2,24,3072]{3,2,0,1:T(8,128)(2,1)S(1)}, bf16[2,2,24,3072]{3,2,0,1:T(8,128)(2,1)S(1)}, u32[]{:S(2)}, u32[]{:S(2)}) collective-permute-start(bf16[2,2,24,3072]{3,2,0,1:T(8,128)(2,1)S(1)} %fusion.84), channel_id=1, source_target_pairs={{0,1},{1,0},{2,3},{3,2},{4,5},{5,4},{6,7},{7,6},{8,9},{9,8},{10,11... | collective-permute-start | bytes 1769480 | tf_op jit(solution)/shard_map/ppermute | solution.py:102
  373.2 40.9 %collective-permute-start.42 = (bf16[2,2,96,768]{3,2,1,0:T(8,128)(2,1)S(1)}, bf16[2,2,96,768]{3,2,1,0:T(8,128)(2,1)S(1)}, u32[]{:S(2)}, u32[]{:S(2)}) collective-permute-start(bf16[2,2,96,768]{3,2,1,0:T(8,128)(2,1)S(1)} %fusion.85), channel_id=1, source_target_pairs={{0,2},{1,3},{2,0},{3,1},{4,6},{5,7},{6,4},{7,5},{8,10},{9,11},{10,... | collective-permute-start | bytes 1769480 | tf_op jit(solution)/shard_map/ppermute | solution.py:102
  375.3 19.4 %collective-permute-start.27 = (bf16[2,2,24,768]{3,2,1,0:T(8,128)(2,1)S(1)}, bf16[2,2,24,768]{3,2,1,0:T(8,128)(2,1)S(1)}, u32[]{:S(2)}, u32[]{:S(2)}) collective-permute-start(bf16[2,2,24,768]{3,2,1,0:T(8,128)(2,1)S(1)} %fusion.108), channel_id=1, source_target_pairs={{0,2},{1,3},{2,0},{3,1},{4,6},{5,7},{6,4},{7,5},{8,10},{9,11},{10,... | collective-permute-start | bytes 442376 | tf_op jit(solution)/shard_map/ppermute | solution.py:102
  376.5 18.9 %collective-permute-start.22 = (bf16[2,2,24,768]{3,2,0,1:T(8,128)(2,1)S(1)}, bf16[2,2,24,768]{3,2,0,1:T(8,128)(2,1)S(1)}, u32[]{:S(2)}, u32[]{:S(2)}) collective-permute-start(bf16[2,2,24,768]{3,2,0,1:T(8,128)(2,1)S(1)} %fusion.107), channel_id=1, source_target_pairs={{0,1},{1,0},{2,3},{3,2},{4,5},{5,4},{6,7},{7,6},{8,9},{9,8},{10,11... | collective-permute-start | bytes 442376 | tf_op jit(solution)/shard_map/ppermute | solution.py:102
  380.0 22.3 %collective-permute-start.17 = (bf16[2,2,24,896]{3,2,1,0:T(8,128)(2,1)S(1)}, bf16[2,2,24,896]{3,2,1,0:T(8,128)(2,1)S(1)}, u32[]{:S(2)}, u32[]{:S(2)}) collective-permute-start(bf16[2,2,24,896]{3,2,1,0:T(8,128)(2,1)S(1)} %fusion.105), channel_id=1, source_target_pairs={{0,16},{1,17},{2,18},{3,19},{4,20},{5,21},{6,22},{7,23},{8,24},{9,... | collective-permute-start | bytes 516104 | tf_op jit(solution)/shard_map/ppermute | solution.py:102
  (79 other events, 722.3 us)
Sparse Core Ops, SparseCore 0:
  11.2 121.2 all-gather.1

commit v10 on v5

--- a/solution.py
+++ b/solution.py
@@ -375,7 +375,7 @@
         )[:, :, 0]
         qkv_grad_u = unit_backward(uq, uk, uv, weights, totals, attended_u, grad_units)
         proj_grad = units_to_rows(qkv_grad_u, seq_count, micro, 3)
-        backward_anchors = [None, grad_units, qkv_grad_u, proj_grad, proj_grad]
+        backward_anchors = [None, grad_units, qkv_grad_u, qkv_grad_u, qkv_grad_u]
     else:
         proj_grad = fallback_attention_backward(saved, attended_grad, row_count)
         backward_anchors = [None] + [proj_grad] * (steps - 1)
@@ -413,6 +413,7 @@
         orders,
         count,
         me,
+        [(red_up, red_down, red_mixed)] + [None] * (steps - 1),
     )
     red_last, red_vec_two = split_cols(red[2], [qkv_cols[2], vec_two.shape[1]])
     red_qkv = jnp.concatenate([red[0], red[1], red_last], axis=1)

time: 424 us -> 442 us (1.042)
  waiting for transfers between devices: 121 us -> 132 us
  starting transfers between devices: 62.7 us -> 69.4 us
    ppermute x30, starting transfers between devices: 25.9 us -> 34 us  [reduce_routes(): got = lax.ppermute(send, ALL, partner_pairs(count, b))]
    all_to_all x2, waiting for transfers between devices: 11.7 us -> 19.8 us  [units_to_rows(): x = lax.all_to_all(x, 'seq', 0, 0, tiled=True)]
    unnamed x107 -> x115, local copies, waits for them, and re-layouts: 16.4 us -> 15.5 us
  transfers between devices with their start and end apart: 50 -> 50, of which waited for: 24 -> 27; matrix products, arithmetic and copies ran while one was open for 38% -> 36% of each run, Pallas kernels for 0% -> 0%
where the time goes in v10:
time: 442 us; the launch traced here: 434 us
  waiting for transfers between devices  132 us (30%)
  local copies, waits for them, and re-layouts  105 us (24%)
  starting transfers between devices  69.4 us (16%)
  matrix products  64.1 us (15%)
  other arithmetic  48 us (11%)
  between operations  15.8 us (4%)
    ppermute x30, waiting for transfers between devices, reduce_routes(): got = lax.ppermute(send, ALL, partner_pairs(count, b))  51.2 us
    all_to_all x2, waiting for transfers between devices, rows_to_units(): x = lax.all_to_all(x, 'seq', 0, 0, tiled=True)  39 us
    ppermute x30, starting transfers between devices, reduce_routes(): got = lax.ppermute(send, ALL, partner_pairs(count, b))  34 us
    ppermute x15, waiting for transfers between devices, gather_routes(): got = lax.ppermute(x, ALL, partner_pairs(count, b))  21.9 us
    all_to_all x2, waiting for transfers between devices, units_to_rows(): x = lax.all_to_all(x, 'seq', 0, 0, tiled=True)  19.8 us
    add x30, other arithmetic, reduce_routes(): x = keep + got.astype(jnp.float32)  18.2 us
    ppermute x15, starting transfers between devices, gather_routes(): got = lax.ppermute(x, ALL, partner_pairs(count, b))  17.2 us
    convert_element_type x30, local copies, waits for them, and re-layouts, reduce_routes(): lax.dynamic_index_in_dim(x, 1 - mine, axis, keepdims=False)  15.8 us
  transfers between devices with their start and end apart: 50, of which 27 were waited for; matrix products, arithmetic and copies ran while one was open for 36% of the time, Pallas kernels for 0%

profile of v10, /device:TPU:0, one launch (start us, length us, event | category | flops | bytes accessed | tf_op | source)
XLA Modules:
  0.0 433.9 jit_solution(9703936450417734845)
XLA Ops:
  17.7 4.1 collective-permute-start
  48.4 5.7 %collective-permute-done.13 = bf16[2,2,2,24,768]{4,3,2,1,0:T(8,128)(2,1)S(1)} collective-permute-done((bf16[2,2,2,24,768]{4,3,2,1,0:T(8,128)(2,1)S(1)}, bf16[2,2,2,24,768]{4,3,2,1,0:T(8,128)(2,1)S(1)}, u32[]{:S(2)}, u32[]{:S(2)}) %collective-permute-start.13) | collective-permute-done | bytes 294944 | tf_op jit(solution)/shard_map/ppermute | solution.py:77
  54.3 4.7 %collective-permute-done.8 = bf16[2,2,2,24,768]{4,3,2,1,0:T(8,128)(2,1)S(1)} collective-permute-done((bf16[2,2,2,24,768]{4,3,2,1,0:T(8,128)(2,1)S(1)}, bf16[2,2,2,24,768]{4,3,2,1,0:T(8,128)(2,1)S(1)}, u32[]{:S(2)}, u32[]{:S(2)}) %collective-permute-start.8) | collective-permute-done | bytes 294944 | tf_op jit(solution)/shard_map/ppermute | solution.py:77
  81.7 6.4 %all-to-all-start = ((bf16[8,3,128,3,64]{2,4,3,1,0:T(8,128)(2,1)}), bf16[8,3,128,3,64]{2,4,3,1,0:T(8,128)(2,1)S(1)}, u32[]{:S(2)}, u32[]{:S(2)}) async-start(bf16[8,3,128,3,64]{2,4,3,1,0:T(8,128)(2,1)} %bitcast.464), calls=%async_computation | async-start | bytes 2359296 | tf_op jit(solution)/shard_map/all_to_all | solution.py:154
  90.7 39.0 %all-to-all-done = bf16[8,3,128,3,64]{2,4,3,1,0:T(8,128)(2,1)S(1)} async-done(((bf16[8,3,128,3,64]{2,4,3,1,0:T(8,128)(2,1)}), bf16[8,3,128,3,64]{2,4,3,1,0:T(8,128)(2,1)S(1)}, u32[]{:S(2)}, u32[]{:S(2)}) %all-to-all-start) | async-done | bytes 1179680 | tf_op jit(solution)/shard_map/all_to_all | solution.py:154
  133.9 6.6 %fusion.130 = (f32[3,1024]{1,0:T(4,128)S(1)}, f32[3,1024,1024]{1,2,0:T(8,128)S(1)}) fusion(bf16[3,1024,3,64]{1,3,0,2:T(8,128)(2,1)S(1)} %reshape.631, pred[3,1024]{1,0:T(4,128)(4,1)S(1)} %broadcast_compare_fusion, s32[3,1024]{1,0:T(4,128)S(1)} %broadcast_add_fusion, pred[1024,1024]{0,1:T(8,128)(4,1)} %iota_compare_fusion), kind=kOutput, calls=%fused_computation.320 | convolution fusion | flops 421524480 | bytes 14467072 | tf_op jit(solution)/shard_map/uqd,ukd->uqk/dot_general | solution.py:172
  152.4 9.4 %all-to-all-done.1 = bf16[8,3,128,1,64]{2,4,3,1,0:T(8,128)(2,1)S(1)} async-done(((bf16[8,3,128,1,64]{2,4,3,1,0:T(8,128)(2,1)}), bf16[8,3,128,1,64]{2,4,3,1,0:T(8,128)(2,1)S(1)}, u32[]{:S(2)}, u32[]{:S(2)}) %all-to-all-start.1) | async-done | bytes 393248 | tf_op jit(solution)/shard_map/all_to_all | solution.py:164
  163.0 4.9 %slice.189 = bf16[768,3072]{1,0:T(8,128)(2,1)} slice(bf16[768,6912]{1,0:T(8,128)(2,1)} %all-gather.2.cloned.1.call-done), slice={[0:768], [3840:6912]} | slice | bytes 9437184 | tf_op jit(solution)/shard_map/slice | solution.py:112
  167.9 8.5 %reshape.635 = bf16[3072,768]{1,0:T(8,128)(2,1)} reshape(bf16[768,3072]{1,0:T(8,128)(2,1)} %slice.189) | data formatting | bytes 9437184 | tf_op jit(solution)/shard_map/reshape | solution.py:335
  178.7 9.5 %fusion.7 = (f32[256,3072]{1,0:T(8,128)S(1)}, f32[256,3072]{1,0:T(8,128)S(1)}) fusion(f32[3072]{0:T(1024)S(1)} %reshape.660, bf16[768,6912]{1,0:T(8,128)(2,1)} %all-gather.2.cloned.1.call-done, f32[256,768]{1,0:T(8,128)S(1)} %get-tuple-element.177, f32[768]{0:T(1024)S(1)} %get-tuple-element.109, f32[768]{0:T(1024)S(1)} %get-tuple-element.110, ...), kind=kOutput, calls=%fused_computation.19 | convolution fusion | flops 1258487808 | bytes 11816960 | tf_op jit(solution)/shard_map/dot_general | solution.py:345
  188.2 7.7 %fusion.10 = bf16[3072,256]{0,1:T(8,128)(2,1)} fusion(f32[256,3072]{1,0:T(8,128)S(1)} %get-tuple-element.179), kind=kLoop, calls=%fused_computation.22 | loop fusion | flops 51118080 | bytes 4718592 | tf_op jit(solution)/shard_map/convert_element_type | solution.py:349
  198.1 5.2 %fusion.124 = f32[768,3072]{1,0:T(8,128)} fusion(bf16[256,3072]{1,0:T(8,128)(2,1)S(1)} %get-tuple-element.183, f32[256,768]{1,0:T(8,128)S(1)} %get-tuple-element.177, f32[768]{0:T(1024)S(1)} %get-tuple-element.109, f32[768]{0:T(1024)S(1)} %get-tuple-element.110, f32[256]{0:T(256)S(1)} %fusion.98, f32[256]{0:T(256)S(1)} %broadcast_multiply_fusion), kind=kOutput, calls=%fused_computation.315 | convolution fusion | flops 1208942592 | bytes 11804672 | tf_op jit(solution)/shard_map/dot_general | solution.py:36
  210.6 4.1 all-to-all-start.2
  214.7 4.1 fusion.35
  227.5 5.0 %concatenate.53 = f32[2,2,2,2,2,24,896]{6,5,4,3,2,1,0:T(8,128)} concatenate(f32[2,2,2,2,2,24,768]{6,5,4,3,2,1,0:T(8,128)} %fusion.73, f32[2,2,2,2,2,24,4]{6,5,4,3,2,1,0:T(8,128)} %concatenate.49, f32[2,2,2,2,2,24,1]{6,5,4,3,2,1,0:T(8,128)} %concatenate.60, f32[2,2,2,2,2,24,1]{6,5,4,3,2,1,0:T(8,128)} %concatenate.61, f32[2,2,2,2,2,24,1]{6,5,4,3,2,1,0:T(8,128)} %concatenate.62, ...), dimensions={6} | concatenate | bytes 5505024 | tf_op jit(solution)/shard_map/concatenate | solution.py:388
  240.5 6.8 %multiply_convert_fusion = bf16[3,1024,1024]{1,2,0:T(8,128)(2,1)S(1)} fusion(f32[3,1024,1024]{1,2,0:T(8,128)} %copy-done.2, f32[3,1024]{1,0:T(4,128)S(1)} %div.84, bf16[3,1024,3,64]{1,3,0,2:T(8,128)(2,1)} %copy-done.20, bf16[3,1024,64]{1,2,0:T(8,128)(2,1)} %squeeze_reshape.3, f32[3,1024]{1,0:T(4,128)S(1)} %get-tuple-element.172), kind=kOutput, calls=%fused_computation.4 | convolution fusion | flops 412680192 | bytes 19685376 | tf_op jit(solution)/shard_map/uqd,ukd->uqk/dot_general | solution.py:186
  250.1 7.5 %fusion.48 = bf16[3,1024,64]{1,2,0:T(8,128)(2,1)} fusion(f32[3,1024,1024]{1,2,0:T(8,128)} %copy-done.2, bf16[3,1024,64]{1,2,0:T(8,128)(2,1)S(1)} %copy-done.25, f32[3,1024]{1,0:T(4,128)S(1)} %get-tuple-element.172), kind=kOutput, calls=%fused_computation.90 | convolution fusion | flops 406585344 | bytes 13381632 | tf_op jit(solution)/shard_map/uqk,uqd->ukd/dot_general | solution.py:190
  262.9 6.3 %collective-permute-done.26 = bf16[2,2,2,24,896]{4,3,2,1,0:T(8,128)(2,1)S(1)} collective-permute-done((bf16[2,2,2,24,896]{4,3,2,1,0:T(8,128)(2,1)S(1)}, bf16[2,2,2,24,896]{4,3,2,1,0:T(8,128)(2,1)S(1)}, u32[]{:S(2)}, u32[]{:S(2)}) %collective-permute-start.26) | collective-permute-done | bytes 344096 | tf_op jit(solution)/shard_map/ppermute | solution.py:102
  287.1 3.9 all-to-all-start.3
  308.2 10.4 %all-to-all-done.3 = bf16[8,3,128,3,64]{2,4,3,1,0:T(8,128)(2,1)S(1)} async-done(((bf16[8,3,128,3,64]{2,4,3,1,0:T(8,128)(2,1)}), bf16[8,3,128,3,64]{2,4,3,1,0:T(8,128)(2,1)S(1)}, u32[]{:S(2)}, u32[]{:S(2)}) %all-to-all-start.3) | async-done | bytes 1179680 | tf_op jit(solution)/shard_map/all_to_all | solution.py:164
  341.2 7.3 %collective-permute-done.17 = bf16[2,2,24,3072]{3,2,0,1:T(8,128)(2,1)S(1)} collective-permute-done((bf16[2,2,24,3072]{3,2,0,1:T(8,128)(2,1)S(1)}, bf16[2,2,24,3072]{3,2,0,1:T(8,128)(2,1)S(1)}, u32[]{:S(2)}, u32[]{:S(2)}) %collective-permute-start.17) | collective-permute-done | bytes 589856 | tf_op jit(solution)/shard_map/ppermute | solution.py:102
  363.1 9.1 %collective-permute-done.19 = bf16[24,3072]{1,0:T(8,128)(2,1)S(1)} collective-permute-done((bf16[24,3072]{1,0:T(8,128)(2,1)S(1)}, bf16[24,3072]{1,0:T(8,128)(2,1)S(1)}, u32[]{:S(2)}, u32[]{:S(2)}) %collective-permute-start.19) | collective-permute-done | bytes 147488 | tf_op jit(solution)/shard_map/ppermute | solution.py:102
  384.3 4.3 concatenate.48
  394.3 7.4 %collective-permute-done.41 = bf16[2,2,2,24,768]{4,3,1,0,2:T(8,128)(2,1)S(1)} collective-permute-done((bf16[2,2,2,24,768]{4,3,1,0,2:T(8,128)(2,1)S(1)}, bf16[2,2,2,24,768]{4,3,1,0,2:T(8,128)(2,1)S(1)}, u32[]{:S(2)}, u32[]{:S(2)}) %collective-permute-start.41) | collective-permute-done | bytes 294944 | tf_op jit(solution)/shard_map/ppermute | solution.py:102
  (406 shorter events, 230.4 us)
Async XLA Ops:
  7.2 155.8 %all-gather.2.cloned.1.call-start = ((), (), s32[]{:S(2)}) async-start(), calls=%async_computation.4 | async-start | bytes 10948608 | tf_op jit(solution)/shard_map/all_gather | solution.py:333
  17.7 14.9 %collective-permute-start = (bf16[24,896]{1,0:T(8,128)(2,1)S(1)}, bf16[24,896]{1,0:T(8,128)(2,1)S(1)}, u32[]{:S(2)}, u32[]{:S(2)}) collective-permute-start(bf16[24,896]{1,0:T(8,128)(2,1)S(1)} %concatenate.40), channel_id=1, source_target_pairs={{0,4},{1,5},{2,6},{3,7},{4,0},{5,1},{6,2},{7,3},{8,12},{9,13},{10,... | collective-permute-start | bytes 129032 | tf_op jit(solution)/shard_map/ppermute | solution.py:77
  21.9 9.6 %collective-permute-start.5 = (bf16[24,768]{1,0:T(8,128)(2,1)S(1)}, bf16[24,768]{1,0:T(8,128)(2,1)S(1)}, u32[]{:S(2)}, u32[]{:S(2)}) collective-permute-start(bf16[24,768]{1,0:T(8,128)(2,1)S(1)} %get-tuple-element.161), channel_id=1, source_target_pairs={{0,4},{1,5},{2,6},{3,7},{4,0},{5,1},{6,2},{7,3},{8,12},{9,13},{10,... | collective-permute-start | bytes 110600 | tf_op jit(solution)/shard_map/ppermute | solution.py:77
  41.1 13.0 %collective-permute-start.13 = (bf16[2,2,2,24,768]{4,3,2,1,0:T(8,128)(2,1)S(1)}, bf16[2,2,2,24,768]{4,3,2,1,0:T(8,128)(2,1)S(1)}, u32[]{:S(2)}, u32[]{:S(2)}) collective-permute-start(bf16[2,2,2,24,768]{4,3,2,1,0:T(8,128)(2,1)S(1)} %get-tuple-element.150), channel_id=1, source_target_pairs={{0,1},{1,0},{2,3},{3,2},{4,5},{5,4},{6,7},{7,6},{8,9},{9,8},{10,11... | collective-permute-start | bytes 884744 | tf_op jit(solution)/shard_map/ppermute | solution.py:77
  43.8 15.2 %collective-permute-start.8 = (bf16[2,2,2,24,768]{4,3,2,1,0:T(8,128)(2,1)S(1)}, bf16[2,2,2,24,768]{4,3,2,1,0:T(8,128)(2,1)S(1)}, u32[]{:S(2)}, u32[]{:S(2)}) collective-permute-start(bf16[2,2,2,24,768]{4,3,2,1,0:T(8,128)(2,1)S(1)} %get-tuple-element.148), channel_id=1, source_target_pairs={{0,16},{1,17},{2,18},{3,19},{4,20},{5,21},{6,22},{7,23},{8,24},{9,... | collective-permute-start | bytes 884744 | tf_op jit(solution)/shard_map/ppermute | solution.py:77
  48.3 12.4 %collective-permute-start.3 = (bf16[2,2,2,24,896]{4,3,2,1,0:T(8,128)(2,1)S(1)}, bf16[2,2,2,24,896]{4,3,2,1,0:T(8,128)(2,1)S(1)}, u32[]{:S(2)}, u32[]{:S(2)}) collective-permute-start(bf16[2,2,2,24,896]{4,3,2,1,0:T(8,128)(2,1)S(1)} %get-tuple-element.146), channel_id=1, source_target_pairs={{0,2},{1,3},{2,0},{3,1},{4,6},{5,7},{6,4},{7,5},{8,10},{9,11},{10,... | collective-permute-start | bytes 1032200 | tf_op jit(solution)/shard_map/ppermute | solution.py:77
  81.7 48.0 %all-to-all-start = ((bf16[8,3,128,3,64]{2,4,3,1,0:T(8,128)(2,1)}), bf16[8,3,128,3,64]{2,4,3,1,0:T(8,128)(2,1)S(1)}, u32[]{:S(2)}, u32[]{:S(2)}) async-start(bf16[8,3,128,3,64]{2,4,3,1,0:T(8,128)(2,1)} %bitcast.464), calls=%async_computation | async-start | bytes 2359296 | tf_op jit(solution)/shard_map/all_to_all | solution.py:154
  146.2 15.6 %all-to-all-start.1 = ((bf16[8,3,128,1,64]{2,4,3,1,0:T(8,128)(2,1)}), bf16[8,3,128,1,64]{2,4,3,1,0:T(8,128)(2,1)S(1)}, u32[]{:S(2)}, u32[]{:S(2)}) async-start(bf16[8,3,128,1,64]{2,4,3,1,0:T(8,128)(2,1)} %bitcast.429), calls=%async_computation.1 | async-start | bytes 786432 | tf_op jit(solution)/shard_map/all_to_all | solution.py:164
  210.6 24.7 %all-to-all-start.2 = ((bf16[8,3,128,1,64]{2,4,3,1,0:T(8,128)(2,1)}), bf16[8,3,128,1,64]{2,4,3,1,0:T(8,128)(2,1)}, u32[]{:S(2)}, u32[]{:S(2)}) async-start(bf16[8,3,128,1,64]{2,4,3,1,0:T(8,128)(2,1)} %bitcast.67), calls=%async_computation.2 | async-start | bytes 786432 | tf_op jit(solution)/shard_map/all_to_all | solution.py:154
  218.8 74.3 %collective-permute-start.15 = (bf16[2,2,2,2,24,3072]{5,4,1,2,3,0:T(8,128)(2,1)}, bf16[2,2,2,2,24,3072]{5,4,1,2,3,0:T(8,128)(2,1)}, u32[]{:S(2)}, u32[]{:S(2)}) collective-permute-start(bf16[2,2,2,2,24,3072]{5,4,1,2,3,0:T(8,128)(2,1)} %fusion.35), channel_id=1, source_target_pairs={{0,8},{1,9},{2,10},{3,11},{4,12},{5,13},{6,14},{7,15},{8,0},{9,1},... | collective-permute-start | bytes 7077896 | tf_op jit(solution)/shard_map/ppermute | solution.py:102
  234.7 22.9 %collective-permute-start.25 = (bf16[2,2,2,2,24,896]{5,4,3,2,1,0:T(8,128)(2,1)}, bf16[2,2,2,2,24,896]{5,4,3,2,1,0:T(8,128)(2,1)}, u32[]{:S(2)}, u32[]{:S(2)}) collective-permute-start(bf16[2,2,2,2,24,896]{5,4,3,2,1,0:T(8,128)(2,1)} %fusion.60), channel_id=1, source_target_pairs={{0,8},{1,9},{2,10},{3,11},{4,12},{5,13},{6,14},{7,15},{8,0},{9,1},... | collective-permute-start | bytes 2064392 | tf_op jit(solution)/shard_map/ppermute | solution.py:102
  258.9 10.2 %collective-permute-start.26 = (bf16[2,2,2,24,896]{4,3,2,1,0:T(8,128)(2,1)S(1)}, bf16[2,2,2,24,896]{4,3,2,1,0:T(8,128)(2,1)S(1)}, u32[]{:S(2)}, u32[]{:S(2)}) collective-permute-start(bf16[2,2,2,24,896]{4,3,2,1,0:T(8,128)(2,1)S(1)} %fusion.77), channel_id=1, source_target_pairs={{0,2},{1,3},{2,0},{3,1},{4,6},{5,7},{6,4},{7,5},{8,10},{9,11},{10,... | collective-permute-start | bytes 1032200 | tf_op jit(solution)/shard_map/ppermute | solution.py:102
  274.0 25.3 %collective-permute-start.20 = (bf16[2,2,2,2,96,768]{5,4,3,2,1,0:T(8,128)(2,1)}, bf16[2,2,2,2,96,768]{5,4,3,2,1,0:T(8,128)(2,1)}, u32[]{:S(2)}, u32[]{:S(2)}) collective-permute-start(bf16[2,2,2,2,96,768]{5,4,3,2,1,0:T(8,128)(2,1)} %fusion.34), channel_id=1, source_target_pairs={{0,8},{1,9},{2,10},{3,11},{4,12},{5,13},{6,14},{7,15},{8,0},{9,1},... | collective-permute-start | bytes 7077896 | tf_op jit(solution)/shard_map/ppermute | solution.py:102
  287.1 31.4 %all-to-all-start.3 = ((bf16[8,3,128,3,64]{2,4,3,1,0:T(8,128)(2,1)}), bf16[8,3,128,3,64]{2,4,3,1,0:T(8,128)(2,1)S(1)}, u32[]{:S(2)}, u32[]{:S(2)}) async-start(bf16[8,3,128,3,64]{2,4,3,1,0:T(8,128)(2,1)} %maximum_bitcast_fusion), calls=%async_computation.3 | async-start | bytes 2359296 | tf_op jit(solution)/shard_map/all_to_all | solution.py:164
  298.1 33.5 %collective-permute-start.16 = (bf16[2,2,2,24,3072]{4,3,0,1,2:T(8,128)(2,1)}, bf16[2,2,2,24,3072]{4,3,0,1,2:T(8,128)(2,1)}, u32[]{:S(2)}, u32[]{:S(2)}) collective-permute-start(bf16[2,2,2,24,3072]{4,3,0,1,2:T(8,128)(2,1)} %fusion.52), channel_id=1, source_target_pairs={{0,16},{1,17},{2,18},{3,19},{4,20},{5,21},{6,22},{7,23},{8,24},{9,... | collective-permute-start | bytes 3538952 | tf_op jit(solution)/shard_map/ppermute | solution.py:102
  306.2 30.9 %collective-permute-start.21 = (bf16[2,2,2,96,768]{4,3,2,1,0:T(8,128)(2,1)}, bf16[2,2,2,96,768]{4,3,2,1,0:T(8,128)(2,1)}, u32[]{:S(2)}, u32[]{:S(2)}) collective-permute-start(bf16[2,2,2,96,768]{4,3,2,1,0:T(8,128)(2,1)} %fusion.53), channel_id=1, source_target_pairs={{0,1},{1,0},{2,3},{3,2},{4,5},{5,4},{6,7},{7,6},{8,9},{9,8},{10,11... | collective-permute-start | bytes 3538952 | tf_op jit(solution)/shard_map/ppermute | solution.py:102
  334.5 14.0 %collective-permute-start.17 = (bf16[2,2,24,3072]{3,2,0,1:T(8,128)(2,1)S(1)}, bf16[2,2,24,3072]{3,2,0,1:T(8,128)(2,1)S(1)}, u32[]{:S(2)}, u32[]{:S(2)}) collective-permute-start(bf16[2,2,24,3072]{3,2,0,1:T(8,128)(2,1)S(1)} %fusion.62), channel_id=1, source_target_pairs={{0,1},{1,0},{2,3},{3,2},{4,5},{5,4},{6,7},{7,6},{8,9},{9,8},{10,11... | collective-permute-start | bytes 1769480 | tf_op jit(solution)/shard_map/ppermute | solution.py:102
  338.7 15.7 %collective-permute-start.22 = (bf16[2,2,96,768]{3,2,1,0:T(8,128)(2,1)S(1)}, bf16[2,2,96,768]{3,2,1,0:T(8,128)(2,1)S(1)}, u32[]{:S(2)}, u32[]{:S(2)}) collective-permute-start(bf16[2,2,96,768]{3,2,1,0:T(8,128)(2,1)S(1)} %fusion.63), channel_id=1, source_target_pairs={{0,2},{1,3},{2,0},{3,1},{4,6},{5,7},{6,4},{7,5},{8,10},{9,11},{10,... | collective-permute-start | bytes 1769480 | tf_op jit(solution)/shard_map/ppermute | solution.py:102
  348.7 10.5 %collective-permute-start.18 = (bf16[2,24,3072]{2,1,0:T(8,128)(2,1)S(1)}, bf16[2,24,3072]{2,1,0:T(8,128)(2,1)S(1)}, u32[]{:S(2)}, u32[]{:S(2)}) collective-permute-start(bf16[2,24,3072]{2,1,0:T(8,128)(2,1)S(1)} %fusion.79), channel_id=1, source_target_pairs={{0,2},{1,3},{2,0},{3,1},{4,6},{5,7},{6,4},{7,5},{8,10},{9,11},{10,... | collective-permute-start | bytes 884744 | tf_op jit(solution)/shard_map/ppermute | solution.py:102
  359.3 12.9 %collective-permute-start.19 = (bf16[24,3072]{1,0:T(8,128)(2,1)S(1)}, bf16[24,3072]{1,0:T(8,128)(2,1)S(1)}, u32[]{:S(2)}, u32[]{:S(2)}) collective-permute-start(bf16[24,3072]{1,0:T(8,128)(2,1)S(1)} %fusion.85), channel_id=1, source_target_pairs={{0,4},{1,5},{2,6},{3,7},{4,0},{5,1},{6,2},{7,3},{8,12},{9,13},{10,... | collective-permute-start | bytes 442376 | tf_op jit(solution)/shard_map/ppermute | solution.py:102
  361.6 12.5 %collective-permute-start.24 = (bf16[96,768]{1,0:T(8,128)(2,1)S(1)}, bf16[96,768]{1,0:T(8,128)(2,1)S(1)}, u32[]{:S(2)}, u32[]{:S(2)}) collective-permute-start(bf16[96,768]{1,0:T(8,128)(2,1)S(1)} %fusion.86), channel_id=1, source_target_pairs={{0,4},{1,5},{2,6},{3,7},{4,0},{5,1},{6,2},{7,3},{8,12},{9,13},{10,... | collective-permute-start | bytes 442376 | tf_op jit(solution)/shard_map/ppermute | solution.py:102
  375.7 14.6 %collective-permute-start.40 = (bf16[2,2,2,2,24,768]{5,4,1,0,2,3:T(8,128)(2,1)}, bf16[2,2,2,2,24,768]{5,4,1,0,2,3:T(8,128)(2,1)}, u32[]{:S(2)}, u32[]{:S(2)}) collective-permute-start(bf16[2,2,2,2,24,768]{5,4,1,0,2,3:T(8,128)(2,1)} %fusion.65), channel_id=1, source_target_pairs={{0,8},{1,9},{2,10},{3,11},{4,12},{5,13},{6,14},{7,15},{8,0},{9,1},... | collective-permute-start | bytes 1769480 | tf_op jit(solution)/shard_map/ppermute | solution.py:102
  380.9 11.3 %collective-permute-start.35 = (bf16[2,2,2,2,24,768]{5,4,1,2,3,0:T(8,128)(2,1)}, bf16[2,2,2,2,24,768]{5,4,1,2,3,0:T(8,128)(2,1)}, u32[]{:S(2)}, u32[]{:S(2)}) collective-permute-start(bf16[2,2,2,2,24,768]{5,4,1,2,3,0:T(8,128)(2,1)} %fusion.64), channel_id=1, source_target_pairs={{0,8},{1,9},{2,10},{3,11},{4,12},{5,13},{6,14},{7,15},{8,0},{9,1},... | collective-permute-start | bytes 1769480 | tf_op jit(solution)/shard_map/ppermute | solution.py:102
  394.1 15.6 %collective-permute-start.31 = (bf16[2,2,2,24,896]{4,3,2,1,0:T(8,128)(2,1)S(1)}, bf16[2,2,2,24,896]{4,3,2,1,0:T(8,128)(2,1)S(1)}, u32[]{:S(2)}, u32[]{:S(2)}) collective-permute-start(bf16[2,2,2,24,896]{4,3,2,1,0:T(8,128)(2,1)S(1)} %fusion.78), channel_id=1, source_target_pairs={{0,2},{1,3},{2,0},{3,1},{4,6},{5,7},{6,4},{7,5},{8,10},{9,11},{10,... | collective-permute-start | bytes 1032200 | tf_op jit(solution)/shard_map/ppermute | solution.py:102
  (79 other events, 784.7 us)
Sparse Core Ops, SparseCore 0:
  10.9 118.2 all-gather.1

commit v11 on v5

--- a/solution.py
+++ b/solution.py
@@ -408,14 +408,20 @@
         full_rows,
         jnp.float32,
     )
+    half = qkv_cols[1] // 2
     red = reduce_routes(
-        [grad_qkv[0], grad_qkv[1], jnp.concatenate([grad_qkv[2], vec_two], axis=1)],
-        orders,
+        [
+            jnp.concatenate([grad_qkv[0], grad_qkv[1][:, :half]], axis=1),
+            jnp.concatenate([grad_qkv[1][:, half:], grad_qkv[2], vec_two], axis=1),
+        ],
+        orders[:2],
         count,
         me,
     )
-    red_last, red_vec_two = split_cols(red[2], [qkv_cols[2], vec_two.shape[1]])
-    red_qkv = jnp.concatenate([red[0], red[1], red_last], axis=1)
+    red_last, red_vec_two = split_cols(
+        red[1], [qkv_cols[1] - half + qkv_cols[2], vec_two.shape[1]]
+    )
+    red_qkv = jnp.concatenate([red[0], red_last], axis=1)
     r_bias_up, r_bias_down, r_gain_two, r_shift_two = vector_unblock(red_vec_one, [ratio, 1, 1, 1])
     r_gain_one, r_shift_one, r_bias_query, r_bias_value, r_bias_out = vector_unblock(
         red_vec_two, [1] * 5

time: 424 us -> 421 us (level)
  waiting for transfers between devices: 121 us -> 112 us
  local copies, waits for them, and re-layouts: 103 us -> 111 us
    ppermute x30 -> x25, waiting for transfers between devices: 48.4 us -> 40.4 us  [reduce_routes(): got = lax.ppermute(send, ALL, partner_pairs(count, b))]
    concatenate x6 -> x7, local copies, waits for them, and re-layouts: 8.47 us -> 14.8 us  [the longest x6 11.6 us: body(): jnp.concatenate([grad_qkv[1][:, half:], grad_qkv[2], vec_two], axis=1)]
    ppermute x30 -> x25, starting transfers between devices: 25.9 us -> 23.5 us  [reduce_routes(): got = lax.ppermute(send, ALL, partner_pairs(count, b))]
    unnamed x107 -> x104, local copies, waits for them, and re-layouts: 16.4 us -> 14.7 us
    convert_element_type x30 -> x25, local copies, waits for them, and re-layouts: 19 us -> 18.3 us  [reduce_routes(): lax.dynamic_index_in_dim(x, 1 - mine, axis, keepdims=False)]
    add x30 -> x25, other arithmetic: 20.1 us -> 20.1 us  [reduce_routes(): x = keep + got.astype(jnp.float32)]
  transfers between devices with their start and end apart: 50 -> 45, of which waited for: 24 -> 21; matrix products, arithmetic and copies ran while one was open for 38% -> 40% of each run, Pallas kernels for 0% -> 0%
where the time goes in v11:
time: 421 us; the launch traced here: 413 us
  waiting for transfers between devices  112 us (27%)
  local copies, waits for them, and re-layouts  111 us (26%)
  matrix products  62.2 us (15%)
  starting transfers between devices  60.2 us (14%)
  other arithmetic  52.5 us (12%)
  between operations  15.7 us (4%)
    ppermute x25, waiting for transfers between devices, reduce_routes(): got = lax.ppermute(send, ALL, partner_pairs(count, b))  40.4 us
    all_to_all x2, waiting for transfers between devices, rows_to_units(): x = lax.all_to_all(x, 'seq', 0, 0, tiled=True)  38.5 us
    ppermute x25, starting transfers between devices, reduce_routes(): got = lax.ppermute(send, ALL, partner_pairs(count, b))  23.5 us
    ppermute x15, waiting for transfers between devices, gather_routes(): got = lax.ppermute(x, ALL, partner_pairs(count, b))  21.9 us
    add x25, other arithmetic, reduce_routes(): x = keep + got.astype(jnp.float32)  20.1 us
    convert_element_type x25, local copies, waits for them, and re-layouts, reduce_routes(): lax.dynamic_index_in_dim(x, 1 - mine, axis, keepdims=False)  18.3 us
    ppermute x15, starting transfers between devices, gather_routes(): got = lax.ppermute(x, ALL, partner_pairs(count, b))  17.1 us
    unnamed x104, local copies, waits for them, and re-layouts  14.7 us
  transfers between devices with their start and end apart: 45, of which 21 were waited for; matrix products, arithmetic and copies ran while one was open for 40% of the time, Pallas kernels for 0%

profile of v11, /device:TPU:0, one launch (start us, length us, event | category | flops | bytes accessed | tf_op | source)
XLA Modules:
  0.0 413.3 jit_solution(16415824030648590946)
XLA Ops:
  17.6 4.1 collective-permute-start
  48.4 5.7 %collective-permute-done.13 = bf16[2,2,2,24,768]{4,3,2,1,0:T(8,128)(2,1)S(1)} collective-permute-done((bf16[2,2,2,24,768]{4,3,2,1,0:T(8,128)(2,1)S(1)}, bf16[2,2,2,24,768]{4,3,2,1,0:T(8,128)(2,1)S(1)}, u32[]{:S(2)}, u32[]{:S(2)}) %collective-permute-start.13) | collective-permute-done | bytes 294944 | tf_op jit(solution)/shard_map/ppermute | solution.py:77
  54.3 4.7 %collective-permute-done.8 = bf16[2,2,2,24,768]{4,3,2,1,0:T(8,128)(2,1)S(1)} collective-permute-done((bf16[2,2,2,24,768]{4,3,2,1,0:T(8,128)(2,1)S(1)}, bf16[2,2,2,24,768]{4,3,2,1,0:T(8,128)(2,1)S(1)}, u32[]{:S(2)}, u32[]{:S(2)}) %collective-permute-start.8) | collective-permute-done | bytes 294944 | tf_op jit(solution)/shard_map/ppermute | solution.py:77
  82.3 6.3 %all-to-all-start = ((bf16[8,3,128,3,64]{2,4,3,1,0:T(8,128)(2,1)}), bf16[8,3,128,3,64]{2,4,3,1,0:T(8,128)(2,1)S(1)}, u32[]{:S(2)}, u32[]{:S(2)}) async-start(bf16[8,3,128,3,64]{2,4,3,1,0:T(8,128)(2,1)} %bitcast.429), calls=%async_computation | async-start | bytes 2359296 | tf_op jit(solution)/shard_map/all_to_all | solution.py:154
  91.2 38.5 %all-to-all-done = bf16[8,3,128,3,64]{2,4,3,1,0:T(8,128)(2,1)S(1)} async-done(((bf16[8,3,128,3,64]{2,4,3,1,0:T(8,128)(2,1)}), bf16[8,3,128,3,64]{2,4,3,1,0:T(8,128)(2,1)S(1)}, u32[]{:S(2)}, u32[]{:S(2)}) %all-to-all-start) | async-done | bytes 1179680 | tf_op jit(solution)/shard_map/all_to_all | solution.py:154
  133.9 6.6 %fusion.123 = (f32[3,1024]{1,0:T(4,128)S(1)}, f32[3,1024,1024]{1,2,0:T(8,128)S(1)}) fusion(bf16[3,1024,3,64]{1,3,0,2:T(8,128)(2,1)S(1)} %reshape.626, pred[3,1024]{1,0:T(4,128)(4,1)S(1)} %broadcast_compare_fusion, s32[3,1024]{1,0:T(4,128)S(1)} %broadcast_add_fusion, pred[1024,1024]{0,1:T(8,128)(4,1)} %iota_compare_fusion), kind=kOutput, calls=%fused_computation.304 | convolution fusion | flops 421524480 | bytes 14467072 | tf_op jit(solution)/shard_map/uqd,ukd->uqk/dot_general | solution.py:172
  152.4 9.4 %all-to-all-done.1 = bf16[8,3,128,1,64]{2,4,3,1,0:T(8,128)(2,1)S(1)} async-done(((bf16[8,3,128,1,64]{2,4,3,1,0:T(8,128)(2,1)}), bf16[8,3,128,1,64]{2,4,3,1,0:T(8,128)(2,1)S(1)}, u32[]{:S(2)}, u32[]{:S(2)}) %all-to-all-start.1) | async-done | bytes 393248 | tf_op jit(solution)/shard_map/all_to_all | solution.py:164
  163.1 4.9 %slice.197 = bf16[768,3072]{1,0:T(8,128)(2,1)} slice(bf16[768,6912]{1,0:T(8,128)(2,1)} %all-gather.2.cloned.1.call-done), slice={[0:768], [3840:6912]} | slice | bytes 9437184 | tf_op jit(solution)/shard_map/slice | solution.py:112
  168.0 8.4 %reshape.630 = bf16[3072,768]{1,0:T(8,128)(2,1)} reshape(bf16[768,3072]{1,0:T(8,128)(2,1)} %slice.197) | data formatting | bytes 9437184 | tf_op jit(solution)/shard_map/reshape | solution.py:335
  178.7 9.5 %fusion.7 = (f32[256,3072]{1,0:T(8,128)S(1)}, f32[256,3072]{1,0:T(8,128)S(1)}) fusion(f32[3072]{0:T(1024)S(1)} %reshape.656, bf16[768,6912]{1,0:T(8,128)(2,1)} %all-gather.2.cloned.1.call-done, f32[256,768]{1,0:T(8,128)S(1)} %get-tuple-element.171, f32[768]{0:T(1024)S(1)} %get-tuple-element.103, f32[768]{0:T(1024)S(1)} %get-tuple-element.104, ...), kind=kOutput, calls=%fused_computation.20 | convolution fusion | flops 1258487808 | bytes 11816960 | tf_op jit(solution)/shard_map/dot_general | solution.py:345
  188.3 7.7 %fusion.10 = bf16[3072,256]{0,1:T(8,128)(2,1)} fusion(f32[256,3072]{1,0:T(8,128)S(1)} %get-tuple-element.173), kind=kLoop, calls=%fused_computation.23 | loop fusion | flops 51118080 | bytes 4718592 | tf_op jit(solution)/shard_map/convert_element_type | solution.py:349
  198.2 5.2 %fusion.117 = f32[768,3072]{1,0:T(8,128)} fusion(bf16[256,3072]{1,0:T(8,128)(2,1)S(1)} %get-tuple-element.177, f32[256,768]{1,0:T(8,128)S(1)} %get-tuple-element.171, f32[768]{0:T(1024)S(1)} %get-tuple-element.103, f32[768]{0:T(1024)S(1)} %get-tuple-element.104, f32[256]{0:T(256)S(1)} %fusion.94, f32[256]{0:T(256)S(1)} %broadcast_multiply_fusion), kind=kOutput, calls=%fused_computation.299 | convolution fusion | flops 1208942592 | bytes 11804672 | tf_op jit(solution)/shard_map/dot_general | solution.py:36
  208.6 4.5 %all-to-all-start.2 = ((bf16[8,3,128,1,64]{2,4,3,1,0:T(8,128)(2,1)}), bf16[8,3,128,1,64]{2,4,3,1,0:T(8,128)(2,1)}, u32[]{:S(2)}, u32[]{:S(2)}) async-start(bf16[8,3,128,1,64]{2,4,3,1,0:T(8,128)(2,1)} %bitcast.67), calls=%async_computation.2 | async-start | bytes 786432 | tf_op jit(solution)/shard_map/all_to_all | solution.py:154
  218.8 4.2 %concatenate.61 = f32[2,2,2,2,2,24,896]{6,5,4,3,2,1,0:T(8,128)} concatenate(f32[2,2,2,2,2,24,768]{6,5,4,3,2,1,0:T(8,128)S(1)} %fusion.70, f32[2,2,2,2,2,24,4]{6,5,4,3,2,1,0:T(8,128)} %concatenate.57, f32[2,2,2,2,2,24,1]{6,5,4,3,2,1,0:T(8,128)} %concatenate.67, f32[2,2,2,2,2,24,1]{6,5,4,3,2,1,0:T(8,128)} %concatenate.68, f32[2,2,2,2,2,24,1]{6,5,4,3,2,1,0:T(8,128)} %concatenate.69, ...), dimensions={6} | concatenate | bytes 5505024 | tf_op jit(solution)/shard_map/concatenate | solution.py:388
  239.7 6.7 %fusion.48 = bf16[3,1024,64]{1,2,0:T(8,128)(2,1)S(1)} fusion(f32[3,1024,1024]{1,2,0:T(8,128)} %copy-done.2, bf16[3,1024,64]{1,2,0:T(8,128)(2,1)S(1)} %squeeze_reshape.3, f32[3,1024]{1,0:T(4,128)S(1)} %get-tuple-element.166), kind=kOutput, calls=%fused_computation.93 | convolution fusion | flops 406585344 | bytes 13381632 | tf_op jit(solution)/shard_map/uqk,uqd->ukd/dot_general | solution.py:190
  246.6 6.6 %multiply_convert_fusion = bf16[3,1024,1024]{1,2,0:T(8,128)(2,1)S(1)} fusion(f32[3,1024,1024]{1,2,0:T(8,128)} %copy-done.2, f32[3,1024]{1,0:T(4,128)S(1)} %div.84, bf16[3,1024,3,64]{1,3,0,2:T(8,128)(2,1)S(1)} %copy-done.20, bf16[3,1024,64]{1,2,0:T(8,128)(2,1)S(1)} %squeeze_reshape.3, f32[3,1024]{1,0:T(4,128)S(1)} %get-tuple-element.166), kind=kOutput, calls=%fused_computation.4 | convolution fusion | flops 412680192 | bytes 19693568 | tf_op jit(solution)/shard_map/uqd,ukd->uqk/dot_general | solution.py:186
  261.1 4.9 %all-to-all-start.3 = ((bf16[8,3,128,3,64]{2,4,3,1,0:T(8,128)(2,1)}), bf16[8,3,128,3,64]{2,4,3,1,0:T(8,128)(2,1)}, u32[]{:S(2)}, u32[]{:S(2)}) async-start(bf16[8,3,128,3,64]{2,4,3,1,0:T(8,128)(2,1)} %maximum_bitcast_fusion), calls=%async_computation.3 | async-start | bytes 2359296 | tf_op jit(solution)/shard_map/all_to_all | solution.py:164
  270.3 5.8 %fusion.51 = bf16[256,768]{1,0:T(8,128)(2,1)} fusion(f32[256,768]{1,0:T(8,128)} %copy-done.9, bf16[3072,768]{1,0:T(8,128)(2,1)} %reshape.630, f32[256,3072]{1,0:T(8,128)} %copy-done.30, f32[256,3072]{1,0:T(8,128)S(1)} %copy-done.8, f32[768]{0:T(1024)S(1)} %copy-done.36), kind=kOutput, calls=%fused_computation.96 | convolution fusion | flops 1210908672 | bytes 12192768 | tf_op jit(solution)/shard_map/dot_general | solution.py:350
  315.2 5.8 %concatenate.54 = f32[2,2,2,2,2,24,1280]{6,5,4,3,2,1,0:T(8,128)} concatenate(f32[2,2,2,2,2,24,384]{6,5,4,3,2,1,0:T(8,128)S(1)} %bitcast.423, f32[2,2,2,2,2,24,768]{6,5,4,3,2,1,0:T(8,128)S(1)} %fusion.68, f32[2,2,2,2,2,24,1]{6,5,4,3,2,1,0:T(8,128)} %concatenate.62, f32[2,2,2,2,2,24,1]{6,5,4,3,2,1,0:T(8,128)} %concatenate.63, f32[2,2,2,2,2,24,1]{6,5,4,3,2,1,0:T(8,128)} %concatenate.64, ...), dimensions={6} | concatenate | bytes 7864320 | tf_op jit(solution)/shard_map/concatenate | solution.py:415
  353.2 7.2 %collective-permute-done.21 = bf16[2,2,2,24,1152]{4,3,0,1,2:T(8,128)(2,1)S(1)} collective-permute-done((bf16[2,2,2,24,1152]{4,3,0,1,2:T(8,128)(2,1)S(1)}, bf16[2,2,2,24,1152]{4,3,0,1,2:T(8,128)(2,1)S(1)}, u32[]{:S(2)}, u32[]{:S(2)}) %collective-permute-start.21) | collective-permute-done | bytes 442400 | tf_op jit(solution)/shard_map/ppermute | solution.py:102
  365.9 6.0 %collective-permute-done.16 = bf16[2,2,2,24,1280]{4,3,2,1,0:T(8,128)(2,1)S(1)} collective-permute-done((bf16[2,2,2,24,1280]{4,3,2,1,0:T(8,128)(2,1)S(1)}, bf16[2,2,2,24,1280]{4,3,2,1,0:T(8,128)(2,1)S(1)}, u32[]{:S(2)}, u32[]{:S(2)}) %collective-permute-start.16) | collective-permute-done | bytes 491552 | tf_op jit(solution)/shard_map/ppermute | solution.py:102
  377.0 4.3 %collective-permute-done.23 = bf16[2,24,1152]{2,1,0:T(8,128)(2,1)S(1)} collective-permute-done((bf16[2,24,1152]{2,1,0:T(8,128)(2,1)S(1)}, bf16[2,24,1152]{2,1,0:T(8,128)(2,1)S(1)}, u32[]{:S(2)}, u32[]{:S(2)}) %collective-permute-start.23) | collective-permute-done | bytes 110624 | tf_op jit(solution)/shard_map/ppermute | solution.py:102
  385.4 9.0 %collective-permute-done.24 = bf16[24,1152]{1,0:T(8,128)(2,1)S(1)} collective-permute-done((bf16[24,1152]{1,0:T(8,128)(2,1)S(1)}, bf16[24,1152]{1,0:T(8,128)(2,1)S(1)}, u32[]{:S(2)}, u32[]{:S(2)}) %collective-permute-start.24) | collective-permute-done | bytes 55328 | tf_op jit(solution)/shard_map/ppermute | solution.py:102
  400.4 4.3 %collective-permute-done.19 = bf16[24,1280]{1,0:T(8,128)(2,1)S(1)} collective-permute-done((bf16[24,1280]{1,0:T(8,128)(2,1)S(1)}, bf16[24,1280]{1,0:T(8,128)(2,1)S(1)}, u32[]{:S(2)}, u32[]{:S(2)}) %collective-permute-start.19) | collective-permute-done | bytes 61472 | tf_op jit(solution)/shard_map/ppermute | solution.py:102
  (376 shorter events, 217.1 us)
Async XLA Ops:
  7.2 155.9 %all-gather.2.cloned.1.call-start = ((), (), s32[]{:S(2)}) async-start(), calls=%async_computation.4 | async-start | bytes 10948608 | tf_op jit(solution)/shard_map/all_gather | solution.py:333
  17.6 14.8 %collective-permute-start = (bf16[24,896]{1,0:T(8,128)(2,1)S(1)}, bf16[24,896]{1,0:T(8,128)(2,1)S(1)}, u32[]{:S(2)}, u32[]{:S(2)}) collective-permute-start(bf16[24,896]{1,0:T(8,128)(2,1)S(1)} %concatenate.45), channel_id=1, source_target_pairs={{0,4},{1,5},{2,6},{3,7},{4,0},{5,1},{6,2},{7,3},{8,12},{9,13},{10,... | collective-permute-start | bytes 129032 | tf_op jit(solution)/shard_map/ppermute | solution.py:77
  41.1 13.0 %collective-permute-start.13 = (bf16[2,2,2,24,768]{4,3,2,1,0:T(8,128)(2,1)S(1)}, bf16[2,2,2,24,768]{4,3,2,1,0:T(8,128)(2,1)S(1)}, u32[]{:S(2)}, u32[]{:S(2)}) collective-permute-start(bf16[2,2,2,24,768]{4,3,2,1,0:T(8,128)(2,1)S(1)} %get-tuple-element.144), channel_id=1, source_target_pairs={{0,1},{1,0},{2,3},{3,2},{4,5},{5,4},{6,7},{7,6},{8,9},{9,8},{10,11... | collective-permute-start | bytes 884744 | tf_op jit(solution)/shard_map/ppermute | solution.py:77
  43.9 15.1 %collective-permute-start.8 = (bf16[2,2,2,24,768]{4,3,2,1,0:T(8,128)(2,1)S(1)}, bf16[2,2,2,24,768]{4,3,2,1,0:T(8,128)(2,1)S(1)}, u32[]{:S(2)}, u32[]{:S(2)}) collective-permute-start(bf16[2,2,2,24,768]{4,3,2,1,0:T(8,128)(2,1)S(1)} %get-tuple-element.142), channel_id=1, source_target_pairs={{0,16},{1,17},{2,18},{3,19},{4,20},{5,21},{6,22},{7,23},{8,24},{9,... | collective-permute-start | bytes 884744 | tf_op jit(solution)/shard_map/ppermute | solution.py:77
  82.3 47.4 %all-to-all-start = ((bf16[8,3,128,3,64]{2,4,3,1,0:T(8,128)(2,1)}), bf16[8,3,128,3,64]{2,4,3,1,0:T(8,128)(2,1)S(1)}, u32[]{:S(2)}, u32[]{:S(2)}) async-start(bf16[8,3,128,3,64]{2,4,3,1,0:T(8,128)(2,1)} %bitcast.429), calls=%async_computation | async-start | bytes 2359296 | tf_op jit(solution)/shard_map/all_to_all | solution.py:154
  146.2 15.7 %all-to-all-start.1 = ((bf16[8,3,128,1,64]{2,4,3,1,0:T(8,128)(2,1)}), bf16[8,3,128,1,64]{2,4,3,1,0:T(8,128)(2,1)S(1)}, u32[]{:S(2)}, u32[]{:S(2)}) async-start(bf16[8,3,128,1,64]{2,4,3,1,0:T(8,128)(2,1)} %bitcast.399), calls=%async_computation.1 | async-start | bytes 786432 | tf_op jit(solution)/shard_map/all_to_all | solution.py:164
  208.6 29.6 %all-to-all-start.2 = ((bf16[8,3,128,1,64]{2,4,3,1,0:T(8,128)(2,1)}), bf16[8,3,128,1,64]{2,4,3,1,0:T(8,128)(2,1)}, u32[]{:S(2)}, u32[]{:S(2)}) async-start(bf16[8,3,128,1,64]{2,4,3,1,0:T(8,128)(2,1)} %bitcast.67), calls=%async_computation.2 | async-start | bytes 786432 | tf_op jit(solution)/shard_map/all_to_all | solution.py:154
  225.3 27.9 %collective-permute-start.25 = (bf16[2,2,2,2,24,896]{5,4,3,2,1,0:T(8,128)(2,1)}, bf16[2,2,2,2,24,896]{5,4,3,2,1,0:T(8,128)(2,1)S(1)}, u32[]{:S(2)}, u32[]{:S(2)}) collective-permute-start(bf16[2,2,2,2,24,896]{5,4,3,2,1,0:T(8,128)(2,1)} %fusion.62), channel_id=1, source_target_pairs={{0,8},{1,9},{2,10},{3,11},{4,12},{5,13},{6,14},{7,15},{8,0},{9,1},... | collective-permute-start | bytes 2064392 | tf_op jit(solution)/shard_map/ppermute | solution.py:102
  229.3 50.4 %collective-permute-start.30 = (bf16[2,2,2,2,24,3072]{5,4,1,2,3,0:T(8,128)(2,1)}, bf16[2,2,2,2,24,3072]{5,4,1,2,3,0:T(8,128)(2,1)}, u32[]{:S(2)}, u32[]{:S(2)}) collective-permute-start(bf16[2,2,2,2,24,3072]{5,4,1,2,3,0:T(8,128)(2,1)} %fusion.35), channel_id=1, source_target_pairs={{0,8},{1,9},{2,10},{3,11},{4,12},{5,13},{6,14},{7,15},{8,0},{9,1},... | collective-permute-start | bytes 7077896 | tf_op jit(solution)/shard_map/ppermute | solution.py:102
  238.2 47.1 %collective-permute-start.35 = (bf16[2,2,2,2,96,768]{5,4,3,2,1,0:T(8,128)(2,1)}, bf16[2,2,2,2,96,768]{5,4,3,2,1,0:T(8,128)(2,1)}, u32[]{:S(2)}, u32[]{:S(2)}) collective-permute-start(bf16[2,2,2,2,96,768]{5,4,3,2,1,0:T(8,128)(2,1)} %fusion.34), channel_id=1, source_target_pairs={{0,8},{1,9},{2,10},{3,11},{4,12},{5,13},{6,14},{7,15},{8,0},{9,1},... | collective-permute-start | bytes 7077896 | tf_op jit(solution)/shard_map/ppermute | solution.py:102
  261.1 33.9 %all-to-all-start.3 = ((bf16[8,3,128,3,64]{2,4,3,1,0:T(8,128)(2,1)}), bf16[8,3,128,3,64]{2,4,3,1,0:T(8,128)(2,1)}, u32[]{:S(2)}, u32[]{:S(2)}) async-start(bf16[8,3,128,3,64]{2,4,3,1,0:T(8,128)(2,1)} %maximum_bitcast_fusion), calls=%async_computation.3 | async-start | bytes 2359296 | tf_op jit(solution)/shard_map/all_to_all | solution.py:164
  284.7 58.0 %collective-permute-start.31 = (bf16[2,2,2,24,3072]{4,3,0,1,2:T(8,128)(2,1)}, bf16[2,2,2,24,3072]{4,3,0,1,2:T(8,128)(2,1)}, u32[]{:S(2)}, u32[]{:S(2)}) collective-permute-start(bf16[2,2,2,24,3072]{4,3,0,1,2:T(8,128)(2,1)} %fusion.52), channel_id=1, source_target_pairs={{0,16},{1,17},{2,18},{3,19},{4,20},{5,21},{6,22},{7,23},{8,24},{9,... | collective-permute-start | bytes 3538952 | tf_op jit(solution)/shard_map/ppermute | solution.py:102
  291.5 54.5 %collective-permute-start.36 = (bf16[2,2,2,96,768]{4,3,2,1,0:T(8,128)(2,1)}, bf16[2,2,2,96,768]{4,3,2,1,0:T(8,128)(2,1)}, u32[]{:S(2)}, u32[]{:S(2)}) collective-permute-start(bf16[2,2,2,96,768]{4,3,2,1,0:T(8,128)(2,1)} %fusion.53), channel_id=1, source_target_pairs={{0,1},{1,0},{2,3},{3,2},{4,5},{5,4},{6,7},{7,6},{8,9},{9,8},{10,11... | collective-permute-start | bytes 3538952 | tf_op jit(solution)/shard_map/ppermute | solution.py:102
  323.6 26.8 %collective-permute-start.15 = (bf16[2,2,2,2,24,1280]{5,4,3,2,1,0:T(8,128)(2,1)}, bf16[2,2,2,2,24,1280]{5,4,3,2,1,0:T(8,128)(2,1)}, u32[]{:S(2)}, u32[]{:S(2)}) collective-permute-start(bf16[2,2,2,2,24,1280]{5,4,3,2,1,0:T(8,128)(2,1)} %fusion.58), channel_id=1, source_target_pairs={{0,8},{1,9},{2,10},{3,11},{4,12},{5,13},{6,14},{7,15},{8,0},{9,1},... | collective-permute-start | bytes 2949128 | tf_op jit(solution)/shard_map/ppermute | solution.py:102
  345.1 16.3 %collective-permute-start.32 = (bf16[2,2,24,3072]{3,2,0,1:T(8,128)(2,1)S(1)}, bf16[2,2,24,3072]{3,2,0,1:T(8,128)(2,1)S(1)}, u32[]{:S(2)}, u32[]{:S(2)}) collective-permute-start(bf16[2,2,24,3072]{3,2,0,1:T(8,128)(2,1)S(1)} %fusion.63), channel_id=1, source_target_pairs={{0,1},{1,0},{2,3},{3,2},{4,5},{5,4},{6,7},{7,6},{8,9},{9,8},{10,11... | collective-permute-start | bytes 1769480 | tf_op jit(solution)/shard_map/ppermute | solution.py:102
  348.5 15.7 %collective-permute-start.37 = (bf16[2,2,96,768]{3,2,1,0:T(8,128)(2,1)S(1)}, bf16[2,2,96,768]{3,2,1,0:T(8,128)(2,1)S(1)}, u32[]{:S(2)}, u32[]{:S(2)}) collective-permute-start(bf16[2,2,96,768]{3,2,1,0:T(8,128)(2,1)S(1)} %fusion.64), channel_id=1, source_target_pairs={{0,2},{1,3},{2,0},{3,1},{4,6},{5,7},{6,4},{7,5},{8,10},{9,11},{10,... | collective-permute-start | bytes 1769480 | tf_op jit(solution)/shard_map/ppermute | solution.py:102
  352.1 19.8 %collective-permute-start.16 = (bf16[2,2,2,24,1280]{4,3,2,1,0:T(8,128)(2,1)S(1)}, bf16[2,2,2,24,1280]{4,3,2,1,0:T(8,128)(2,1)S(1)}, u32[]{:S(2)}, u32[]{:S(2)}) collective-permute-start(bf16[2,2,2,24,1280]{4,3,2,1,0:T(8,128)(2,1)S(1)} %fusion.66), channel_id=1, source_target_pairs={{0,1},{1,0},{2,3},{3,2},{4,5},{5,4},{6,7},{7,6},{8,9},{9,8},{10,11... | collective-permute-start | bytes 1474568 | tf_op jit(solution)/shard_map/ppermute | solution.py:102
  360.5 14.3 %collective-permute-start.22 = (bf16[2,2,24,1152]{3,2,0,1:T(8,128)(2,1)S(1)}, bf16[2,2,24,1152]{3,2,0,1:T(8,128)(2,1)S(1)}, u32[]{:S(2)}, u32[]{:S(2)}) collective-permute-start(bf16[2,2,24,1152]{3,2,0,1:T(8,128)(2,1)S(1)} %fusion.83), channel_id=1, source_target_pairs={{0,1},{1,0},{2,3},{3,2},{4,5},{5,4},{6,7},{7,6},{8,9},{9,8},{10,11... | collective-permute-start | bytes 663560 | tf_op jit(solution)/shard_map/ppermute | solution.py:102
  361.5 20.7 %collective-permute-start.33 = (bf16[2,24,3072]{2,1,0:T(8,128)(2,1)S(1)}, bf16[2,24,3072]{2,1,0:T(8,128)(2,1)S(1)}, u32[]{:S(2)}, u32[]{:S(2)}) collective-permute-start(bf16[2,24,3072]{2,1,0:T(8,128)(2,1)S(1)} %fusion.80), channel_id=1, source_target_pairs={{0,2},{1,3},{2,0},{3,1},{4,6},{5,7},{6,4},{7,5},{8,10},{9,11},{10,... | collective-permute-start | bytes 884744 | tf_op jit(solution)/shard_map/ppermute | solution.py:102
  364.4 20.1 %collective-permute-start.38 = (bf16[2,96,768]{2,1,0:T(8,128)(2,1)S(1)}, bf16[2,96,768]{2,1,0:T(8,128)(2,1)S(1)}, u32[]{:S(2)}, u32[]{:S(2)}) collective-permute-start(bf16[2,96,768]{2,1,0:T(8,128)(2,1)S(1)} %fusion.81), channel_id=1, source_target_pairs={{0,16},{1,17},{2,18},{3,19},{4,20},{5,21},{6,22},{7,23},{8,24},{9,... | collective-permute-start | bytes 884744 | tf_op jit(solution)/shard_map/ppermute | solution.py:102
  375.1 19.3 %collective-permute-start.17 = (bf16[2,2,24,1280]{3,2,1,0:T(8,128)(2,1)S(1)}, bf16[2,2,24,1280]{3,2,1,0:T(8,128)(2,1)S(1)}, u32[]{:S(2)}, u32[]{:S(2)}) collective-permute-start(bf16[2,2,24,1280]{3,2,1,0:T(8,128)(2,1)S(1)} %fusion.82), channel_id=1, source_target_pairs={{0,2},{1,3},{2,0},{3,1},{4,6},{5,7},{6,4},{7,5},{8,10},{9,11},{10,... | collective-permute-start | bytes 737288 | tf_op jit(solution)/shard_map/ppermute | solution.py:102
  381.3 13.1 %collective-permute-start.24 = (bf16[24,1152]{1,0:T(8,128)(2,1)S(1)}, bf16[24,1152]{1,0:T(8,128)(2,1)S(1)}, u32[]{:S(2)}, u32[]{:S(2)}) collective-permute-start(bf16[24,1152]{1,0:T(8,128)(2,1)S(1)} %fusion.91), channel_id=1, source_target_pairs={{0,4},{1,5},{2,6},{3,7},{4,0},{5,1},{6,2},{7,3},{8,12},{9,13},{10,... | collective-permute-start | bytes 165896 | tf_op jit(solution)/shard_map/ppermute | solution.py:102
  382.3 14.5 %collective-permute-start.34 = (bf16[24,3072]{1,0:T(8,128)(2,1)S(1)}, bf16[24,3072]{1,0:T(8,128)(2,1)S(1)}, u32[]{:S(2)}, u32[]{:S(2)}) collective-permute-start(bf16[24,3072]{1,0:T(8,128)(2,1)S(1)} %fusion.85), channel_id=1, source_target_pairs={{0,4},{1,5},{2,6},{3,7},{4,0},{5,1},{6,2},{7,3},{8,12},{9,13},{10,... | collective-permute-start | bytes 442376 | tf_op jit(solution)/shard_map/ppermute | solution.py:102
  384.6 15.0 %collective-permute-start.39 = (bf16[96,768]{1,0:T(8,128)(2,1)S(1)}, bf16[96,768]{1,0:T(8,128)(2,1)S(1)}, u32[]{:S(2)}, u32[]{:S(2)}) collective-permute-start(bf16[96,768]{1,0:T(8,128)(2,1)S(1)} %fusion.86), channel_id=1, source_target_pairs={{0,4},{1,5},{2,6},{3,7},{4,0},{5,1},{6,2},{7,3},{8,12},{9,13},{10,... | collective-permute-start | bytes 442376 | tf_op jit(solution)/shard_map/ppermute | solution.py:102
  (69 other events, 643.3 us)
Sparse Core Ops, SparseCore 0:
  10.9 117.7 all-gather.1

commit v12 on v5

--- a/solution.py
+++ b/solution.py
@@ -272,16 +272,16 @@
         [ln1_g, ln1_b, b_q, b_v, b_out, ln2_g, ln2_b, b_down, b_up], shard_rows, jnp.bfloat16
     )
     mlp_pack = jnp.concatenate([w_out, w_up, w_down.reshape(shard_rows, ratio * width)], axis=1)
-    qkv_cols = thirds(w_qkv.shape[1])
-    qkv_parts = split_cols(w_qkv, qkv_cols)
+    qkv_total = w_qkv.shape[1]
+    split_at = qkv_total // 2
     gathered = gather_routes(
-        [qkv_parts[0], qkv_parts[1], jnp.concatenate([qkv_parts[2], vecs_local], axis=1)],
-        orders,
+        [w_qkv[:, :split_at], jnp.concatenate([w_qkv[:, split_at:], vecs_local], axis=1)],
+        orders[:2],
         count,
         me,
     )
-    last_qkv, vecs_all = split_cols(gathered[2], [qkv_cols[2], vecs_local.shape[1]])
-    qkv_weights = [gathered[0], gathered[1], last_qkv]
+    qkv_second, vecs_all = split_cols(gathered[1], [qkv_total - split_at, vecs_local.shape[1]])
+    qkv_weights = [gathered[0], qkv_second]
     (
         gain_one,
         shift_one,
@@ -299,15 +299,10 @@
         layer_norm, seq_in, gain_one.astype(jnp.float32), shift_one.astype(jnp.float32)
     )
     normed = normed_f.astype(jnp.bfloat16)
-    if qkv_cols == [width] * 3:
-        proj_q, proj_k, proj_v = [
-            jnp.dot(normed, w, preferred_element_type=jnp.float32) for w in qkv_weights
-        ]
-    else:
-        projected = jnp.dot(
-            normed, jnp.concatenate(qkv_weights, axis=1), preferred_element_type=jnp.float32
-        )
-        proj_q, proj_k, proj_v = split_cols(projected, [width] * 3)
+    projected = jnp.concatenate(
+        [jnp.dot(normed, w, preferred_element_type=jnp.float32) for w in qkv_weights], axis=1
+    )
+    proj_q, proj_k, proj_v = split_cols(projected, [width] * 3)
     queries = (proj_q + bias_query.astype(jnp.float32)).astype(jnp.bfloat16)
     keys_now = proj_k.astype(jnp.bfloat16)
     values_now = (proj_v + bias_value.astype(jnp.float32)).astype(jnp.bfloat16)
@@ -395,11 +390,11 @@
 
     grad_bias_query = jnp.sum(proj_grad[:, :width].astype(jnp.float32), axis=0)
     grad_bias_value = jnp.sum(proj_grad[:, 2 * width :].astype(jnp.float32), axis=0)
-    grad_parts = split_cols(proj_grad, qkv_cols)
+    grad_parts = split_cols(proj_grad, [split_at, qkv_total - split_at])
     grad_qkv = [outer_rows(normed, g) for g in grad_parts]
-    normed_grad = times_transposed(grad_parts[0], qkv_weights[0])
-    for g, w in zip(grad_parts[1:], qkv_weights[1:]):
-        normed_grad = normed_grad + times_transposed(g, w)
+    normed_grad = times_transposed(grad_parts[0], qkv_weights[0]) + times_transposed(
+        grad_parts[1], qkv_weights[1]
+    )
     input_ln_grad, grad_gain_one, grad_shift_one = norm_one_back(normed_grad)
     input_grads = (middle_grad + input_ln_grad).astype(jnp.bfloat16)
 
@@ -409,13 +404,13 @@
         jnp.float32,
     )
     red = reduce_routes(
-        [grad_qkv[0], grad_qkv[1], jnp.concatenate([grad_qkv[2], vec_two], axis=1)],
-        orders,
+        [grad_qkv[0], jnp.concatenate([grad_qkv[1], vec_two], axis=1)],
+        orders[:2],
         count,
         me,
     )
-    red_last, red_vec_two = split_cols(red[2], [qkv_cols[2], vec_two.shape[1]])
-    red_qkv = jnp.concatenate([red[0], red[1], red_last], axis=1)
+    red_last, red_vec_two = split_cols(red[1], [qkv_total - split_at, vec_two.shape[1]])
+    red_qkv = jnp.concatenate([red[0], red_last], axis=1)
     r_bias_up, r_bias_down, r_gain_two, r_shift_two = vector_unblock(red_vec_one, [ratio, 1, 1, 1])
     r_gain_one, r_shift_one, r_bias_query, r_bias_value, r_bias_out = vector_unblock(
         red_vec_two, [1] * 5

time: 424 us -> 421 us (level)
  waiting for transfers between devices: 121 us -> 109 us
  local copies, waits for them, and re-layouts: 103 us -> 112 us
  starting transfers between devices: 62.7 us -> 57.7 us
  other arithmetic: 50.6 us -> 54.9 us
    all_to_all x2, waiting for transfers between devices: 38.8 us -> 27.5 us  [rows_to_units(): x = lax.all_to_all(x, 'seq', 0, 0, tiled=True)]
    ppermute x15 -> x10, waiting for transfers between devices: 21.9 us -> 30.6 us  [gather_routes(): got = lax.ppermute(x, ALL, partner_pairs(count, b))]
    ppermute x30 -> x25, waiting for transfers between devices: 48.4 us -> 41 us  [reduce_routes(): got = lax.ppermute(send, ALL, partner_pairs(count, b))]
    concatenate x7, local copies, waits for them, and re-layouts: 8.58 us -> 13.1 us  [the longest x6 13 us: body(): jnp.concatenate([grad_qkv[1], vec_two], axis=1)]
    another operation x15 -> x10, other arithmetic: 4.94 us -> 8.96 us  [gather_routes(): x = jnp.stack([x, got])]
    unnamed x107 -> x106, local copies, waits for them, and re-layouts: 16.4 us -> 12.6 us
    ppermute x15 -> x10, starting transfers between devices: 17.2 us -> 13.5 us  [gather_routes(): got = lax.ppermute(x, ALL, partner_pairs(count, b))]
    ppermute x30 -> x25, starting transfers between devices: 25.9 us -> 23.5 us  [reduce_routes(): got = lax.ppermute(send, ALL, partner_pairs(count, b))]
  transfers between devices with their start and end apart: 50 -> 40, of which waited for: 24 -> 17; matrix products, arithmetic and copies ran while one was open for 38% -> 41% of each run, Pallas kernels for 0% -> 0%
where the time goes in v12:
time: 421 us; the launch traced here: 413 us
  local copies, waits for them, and re-layouts  112 us (27%)
  waiting for transfers between devices  109 us (26%)
  matrix products  64 us (15%)
  starting transfers between devices  57.7 us (14%)
  other arithmetic  54.9 us (13%)
  between operations  15.6 us (4%)
    ppermute x25, waiting for transfers between devices, reduce_routes(): got = lax.ppermute(send, ALL, partner_pairs(count, b))  41 us
    ppermute x10, waiting for transfers between devices, gather_routes(): got = lax.ppermute(x, ALL, partner_pairs(count, b))  30.6 us
    all_to_all x2, waiting for transfers between devices, rows_to_units(): x = lax.all_to_all(x, 'seq', 0, 0, tiled=True)  27.5 us
    ppermute x25, starting transfers between devices, reduce_routes(): got = lax.ppermute(send, ALL, partner_pairs(count, b))  23.5 us
    add x25, other arithmetic, reduce_routes(): x = keep + got.astype(jnp.float32)  19.8 us
    convert_element_type x25, local copies, waits for them, and re-layouts, reduce_routes(): lax.dynamic_index_in_dim(x, 1 - mine, axis, keepdims=False)  17.8 us
    ppermute x10, starting transfers between devices, gather_routes(): got = lax.ppermute(x, ALL, partner_pairs(count, b))  13.5 us
    concatenate x6, local copies, waits for them, and re-layouts, body(): jnp.concatenate([grad_qkv[1], vec_two], axis=1)  13 us
  transfers between devices with their start and end apart: 40, of which 17 were waited for; matrix products, arithmetic and copies ran while one was open for 41% of the time, Pallas kernels for 0%

profile of v12, /device:TPU:0, one launch (start us, length us, event | category | flops | bytes accessed | tf_op | source)
XLA Modules:
  0.0 413.2 jit_solution(2122337082410509245)
XLA Ops:
  23.1 7.2 %collective-permute-done.5 = bf16[24,1152]{1,0:T(8,128)(2,1)S(1)} collective-permute-done((bf16[24,1152]{1,0:T(8,128)(2,1)S(1)}, bf16[24,1152]{1,0:T(8,128)(2,1)S(1)}, u32[]{:S(2)}, u32[]{:S(2)}) %collective-permute-start.5) | collective-permute-done | bytes 55328 | tf_op jit(solution)/shard_map/ppermute | solution.py:77
  45.4 4.7 %collective-permute-done.2 = bf16[2,2,24,1280]{3,2,1,0:T(8,128)(2,1)S(1)} collective-permute-done((bf16[2,2,24,1280]{3,2,1,0:T(8,128)(2,1)S(1)}, bf16[2,2,24,1280]{3,2,1,0:T(8,128)(2,1)S(1)}, u32[]{:S(2)}, u32[]{:S(2)}) %collective-permute-start.2) | collective-permute-done | bytes 245792 | tf_op jit(solution)/shard_map/ppermute | solution.py:77
  50.3 12.8 %collective-permute-done.8 = bf16[2,2,2,24,1152]{4,3,2,1,0:T(8,128)(2,1)S(1)} collective-permute-done((bf16[2,2,2,24,1152]{4,3,2,1,0:T(8,128)(2,1)S(1)}, bf16[2,2,2,24,1152]{4,3,2,1,0:T(8,128)(2,1)S(1)}, u32[]{:S(2)}, u32[]{:S(2)}) %collective-permute-start.8) | collective-permute-done | bytes 442400 | tf_op jit(solution)/shard_map/ppermute | solution.py:77
  94.1 6.8 %all-to-all-start = ((bf16[8,3,128,3,64]{2,4,3,1,0:T(8,128)(2,1)}), bf16[8,3,128,3,64]{2,4,3,1,0:T(8,128)(2,1)}, u32[]{:S(2)}, u32[]{:S(2)}) async-start(bf16[8,3,128,3,64]{2,4,3,1,0:T(8,128)(2,1)} %bitcast.404), calls=%async_computation | async-start | bytes 2359296 | tf_op jit(solution)/shard_map/all_to_all | solution.py:154
  105.3 27.5 %all-to-all-done = bf16[8,3,128,3,64]{2,4,3,1,0:T(8,128)(2,1)} async-done(((bf16[8,3,128,3,64]{2,4,3,1,0:T(8,128)(2,1)}), bf16[8,3,128,3,64]{2,4,3,1,0:T(8,128)(2,1)}, u32[]{:S(2)}, u32[]{:S(2)}) %all-to-all-start) | async-done | bytes 1179680 | tf_op jit(solution)/shard_map/all_to_all | solution.py:154
  138.2 6.1 %fusion.130 = (f32[3,1024]{1,0:T(4,128)S(1)}, f32[3,1024,1024]{1,2,0:T(8,128)S(1)}) fusion(bf16[3,1024,3,64]{1,3,0,2:T(8,128)(2,1)S(1)} %reshape.651, pred[3,1024]{1,0:T(4,128)(4,1)S(1)} %broadcast_compare_fusion, s32[3,1024]{1,0:T(4,128)S(1)} %broadcast_add_fusion, pred[1024,1024]{0,1:T(8,128)(4,1)} %iota_compare_fusion), kind=kOutput, calls=%fused_computation.302 | convolution fusion | flops 421524480 | bytes 14467072 | tf_op jit(solution)/shard_map/uqd,ukd->uqk/dot_general | solution.py:172
  150.3 4.3 %all-to-all-start.1 = ((bf16[8,3,128,1,64]{2,4,3,1,0:T(8,128)(2,1)}), bf16[8,3,128,1,64]{2,4,3,1,0:T(8,128)(2,1)}, u32[]{:S(2)}, u32[]{:S(2)}) async-start(bf16[8,3,128,1,64]{2,4,3,1,0:T(8,128)(2,1)} %bitcast.415), calls=%async_computation.1 | async-start | bytes 786432 | tf_op jit(solution)/shard_map/all_to_all | solution.py:164
  159.4 7.2 %all-to-all-done.1 = bf16[8,3,128,1,64]{2,4,3,1,0:T(8,128)(2,1)} async-done(((bf16[8,3,128,1,64]{2,4,3,1,0:T(8,128)(2,1)}), bf16[8,3,128,1,64]{2,4,3,1,0:T(8,128)(2,1)}, u32[]{:S(2)}, u32[]{:S(2)}) %all-to-all-start.1) | async-done | bytes 393248 | tf_op jit(solution)/shard_map/all_to_all | solution.py:164
  168.8 4.9 %slice.200 = bf16[768,3072]{1,0:T(8,128)(2,1)} slice(bf16[768,6912]{1,0:T(8,128)(2,1)} %all-gather.2.cloned.1.call-done), slice={[0:768], [3840:6912]} | slice | bytes 9437184 | tf_op jit(solution)/shard_map/slice | solution.py:112
  173.7 8.5 %reshape.655 = bf16[3072,768]{1,0:T(8,128)(2,1)} reshape(bf16[768,3072]{1,0:T(8,128)(2,1)} %slice.200) | data formatting | bytes 9437184 | tf_op jit(solution)/shard_map/reshape | solution.py:330
  184.5 9.5 %fusion.7 = (f32[256,3072]{1,0:T(8,128)S(1)}, f32[256,3072]{1,0:T(8,128)S(1)}) fusion(f32[3072]{0:T(1024)S(1)} %reshape.680, bf16[768,6912]{1,0:T(8,128)(2,1)} %all-gather.2.cloned.1.call-done, f32[256,768]{1,0:T(8,128)S(1)} %get-tuple-element.160, f32[768]{0:T(1024)S(1)} %get-tuple-element.100, f32[768]{0:T(1024)S(1)} %get-tuple-element.101, ...), kind=kOutput, calls=%fused_computation.20 | convolution fusion | flops 1258487808 | bytes 11816960 | tf_op jit(solution)/shard_map/dot_general | solution.py:340
  194.1 7.7 %fusion.10 = bf16[3072,256]{0,1:T(8,128)(2,1)} fusion(f32[256,3072]{1,0:T(8,128)S(1)} %get-tuple-element.162), kind=kLoop, calls=%fused_computation.23 | loop fusion | flops 51118080 | bytes 4718592 | tf_op jit(solution)/shard_map/convert_element_type | solution.py:344
  204.6 5.2 %fusion.123 = f32[768,3072]{1,0:T(8,128)} fusion(bf16[256,3072]{1,0:T(8,128)(2,1)S(1)} %get-tuple-element.166, f32[256,768]{1,0:T(8,128)S(1)} %get-tuple-element.160, f32[768]{0:T(1024)S(1)} %get-tuple-element.100, f32[768]{0:T(1024)S(1)} %get-tuple-element.101, f32[256]{0:T(256)S(1)} %fusion.105, f32[256]{0:T(256)S(1)} %broadcast_multiply_fusion), kind=kOutput, calls=%fused_computation.296 | convolution fusion | flops 1208942592 | bytes 11804672 | tf_op jit(solution)/shard_map/dot_general | solution.py:36
  215.8 4.3 %all-to-all-start.2 = ((bf16[8,3,128,1,64]{2,4,3,1,0:T(8,128)(2,1)}), bf16[8,3,128,1,64]{2,4,3,1,0:T(8,128)(2,1)}, u32[]{:S(2)}, u32[]{:S(2)}) async-start(bf16[8,3,128,1,64]{2,4,3,1,0:T(8,128)(2,1)} %bitcast.56), calls=%async_computation.2 | async-start | bytes 786432 | tf_op jit(solution)/shard_map/all_to_all | solution.py:154
  248.1 6.7 %fusion.56 = bf16[3,1024,64]{1,2,0:T(8,128)(2,1)S(1)} fusion(f32[3,1024,1024]{1,2,0:T(8,128)} %copy-done.2, bf16[3,1024,64]{1,2,0:T(8,128)(2,1)S(1)} %squeeze_reshape.3, f32[3,1024]{1,0:T(4,128)S(1)} %copy-done.33), kind=kOutput, calls=%fused_computation.98 | convolution fusion | flops 406585344 | bytes 13381632 | tf_op jit(solution)/shard_map/uqk,uqd->ukd/dot_general | solution.py:190
  254.9 6.6 %multiply_convert_fusion = bf16[3,1024,1024]{1,2,0:T(8,128)(2,1)S(1)} fusion(f32[3,1024,1024]{1,2,0:T(8,128)} %copy-done.2, f32[3,1024]{1,0:T(4,128)S(1)} %div.84, bf16[3,1024,3,64]{1,3,0,2:T(8,128)(2,1)S(1)} %reshape.651, bf16[3,1024,64]{1,2,0:T(8,128)(2,1)S(1)} %squeeze_reshape.3, f32[3,1024]{1,0:T(4,128)S(1)} %copy-done.33), kind=kOutput, calls=%fused_computation.3 | convolution fusion | flops 412680192 | bytes 19693568 | tf_op jit(solution)/shard_map/uqd,ukd->uqk/dot_general | solution.py:186
  270.5 5.2 %all-to-all-start.3 = ((bf16[8,3,128,3,64]{2,4,3,1,0:T(8,128)(2,1)}), bf16[8,3,128,3,64]{2,4,3,1,0:T(8,128)(2,1)}, u32[]{:S(2)}, u32[]{:S(2)}) async-start(bf16[8,3,128,3,64]{2,4,3,1,0:T(8,128)(2,1)} %maximum_bitcast_fusion), calls=%async_computation.3 | async-start | bytes 2359296 | tf_op jit(solution)/shard_map/all_to_all | solution.py:164
  279.2 5.8 %fusion.59 = bf16[256,768]{1,0:T(8,128)(2,1)} fusion(f32[256,768]{1,0:T(8,128)} %copy-done.12, bf16[3072,768]{1,0:T(8,128)(2,1)} %reshape.655, f32[256,3072]{1,0:T(8,128)} %copy-done.27, f32[256,3072]{1,0:T(8,128)S(1)} %copy-done.11, f32[768]{0:T(1024)S(1)} %copy-done.38), kind=kOutput, calls=%fused_computation.100 | convolution fusion | flops 1210908672 | bytes 12192768 | tf_op jit(solution)/shard_map/dot_general | solution.py:345
  326.7 5.8 %concatenate.53 = f32[2,2,2,2,2,24,1280]{6,5,4,3,2,1,0:T(8,128)} concatenate(f32[2,2,2,2,2,24,1152]{6,5,4,3,2,1,0:T(8,128)S(1)} %fusion.78, f32[2,2,2,2,2,24,1]{6,5,4,3,2,1,0:T(8,128)} %concatenate.60, f32[2,2,2,2,2,24,1]{6,5,4,3,2,1,0:T(8,128)} %concatenate.61, f32[2,2,2,2,2,24,1]{6,5,4,3,2,1,0:T(8,128)} %concatenate.62, f32[2,2,2,2,2,24,1]{6,5,4,3,2,1,0:T(8,128)} %concatenate.63, ...), dimensions={6} | concatenate | bytes 7864320 | tf_op jit(solution)/shard_map/concatenate | solution.py:407
  351.5 8.9 %collective-permute-done.16 = bf16[2,2,2,24,1152]{4,3,0,1,2:T(8,128)(2,1)S(1)} collective-permute-done((bf16[2,2,2,24,1152]{4,3,0,1,2:T(8,128)(2,1)S(1)}, bf16[2,2,2,24,1152]{4,3,0,1,2:T(8,128)(2,1)S(1)}, u32[]{:S(2)}, u32[]{:S(2)}) %collective-permute-start.16) | collective-permute-done | bytes 442400 | tf_op jit(solution)/shard_map/ppermute | solution.py:102
  364.5 6.9 %collective-permute-done.11 = bf16[2,2,2,24,1280]{4,3,2,1,0:T(8,128)(2,1)S(1)} collective-permute-done((bf16[2,2,2,24,1280]{4,3,2,1,0:T(8,128)(2,1)S(1)}, bf16[2,2,2,24,1280]{4,3,2,1,0:T(8,128)(2,1)S(1)}, u32[]{:S(2)}, u32[]{:S(2)}) %collective-permute-start.11) | collective-permute-done | bytes 491552 | tf_op jit(solution)/shard_map/ppermute | solution.py:102
  376.8 4.4 %collective-permute-done.18 = bf16[2,24,1152]{2,1,0:T(8,128)(2,1)S(1)} collective-permute-done((bf16[2,24,1152]{2,1,0:T(8,128)(2,1)S(1)}, bf16[2,24,1152]{2,1,0:T(8,128)(2,1)S(1)}, u32[]{:S(2)}, u32[]{:S(2)}) %collective-permute-start.18) | collective-permute-done | bytes 110624 | tf_op jit(solution)/shard_map/ppermute | solution.py:102
  385.7 8.6 %collective-permute-done.19 = bf16[24,1152]{1,0:T(8,128)(2,1)S(1)} collective-permute-done((bf16[24,1152]{1,0:T(8,128)(2,1)S(1)}, bf16[24,1152]{1,0:T(8,128)(2,1)S(1)}, u32[]{:S(2)}, u32[]{:S(2)}) %collective-permute-start.19) | collective-permute-done | bytes 55328 | tf_op jit(solution)/shard_map/ppermute | solution.py:102
  400.3 4.3 %collective-permute-done.14 = bf16[24,1280]{1,0:T(8,128)(2,1)S(1)} collective-permute-done((bf16[24,1280]{1,0:T(8,128)(2,1)S(1)}, bf16[24,1280]{1,0:T(8,128)(2,1)S(1)}, u32[]{:S(2)}, u32[]{:S(2)}) %collective-permute-start.14) | collective-permute-done | bytes 61472 | tf_op jit(solution)/shard_map/ppermute | solution.py:102
  (357 shorter events, 217.6 us)
Async XLA Ops:
  7.2 161.6 %all-gather.2.cloned.1.call-start = ((), (), s32[]{:S(2)}) async-start(), calls=%async_computation.4 | async-start | bytes 10948608 | tf_op jit(solution)/shard_map/all_gather | solution.py:328
  17.7 15.1 %collective-permute-start = (bf16[24,1280]{1,0:T(8,128)(2,1)S(1)}, bf16[24,1280]{1,0:T(8,128)(2,1)S(1)}, u32[]{:S(2)}, u32[]{:S(2)}) collective-permute-start(bf16[24,1280]{1,0:T(8,128)(2,1)S(1)} %concatenate.44), channel_id=1, source_target_pairs={{0,4},{1,5},{2,6},{3,7},{4,0},{5,1},{6,2},{7,3},{8,12},{9,13},{10,... | collective-permute-start | bytes 184328 | tf_op jit(solution)/shard_map/ppermute | solution.py:77
  43.7 19.4 %collective-permute-start.8 = (bf16[2,2,2,24,1152]{4,3,2,1,0:T(8,128)(2,1)S(1)}, bf16[2,2,2,24,1152]{4,3,2,1,0:T(8,128)(2,1)S(1)}, u32[]{:S(2)}, u32[]{:S(2)}) collective-permute-start(bf16[2,2,2,24,1152]{4,3,2,1,0:T(8,128)(2,1)S(1)} %get-tuple-element.135), channel_id=1, source_target_pairs={{0,16},{1,17},{2,18},{3,19},{4,20},{5,21},{6,22},{7,23},{8,24},{9,... | collective-permute-start | bytes 1327112 | tf_op jit(solution)/shard_map/ppermute | solution.py:77
  50.2 14.1 %collective-permute-start.3 = (bf16[2,2,2,24,1280]{4,3,2,1,0:T(8,128)(2,1)S(1)}, bf16[2,2,2,24,1280]{4,3,2,1,0:T(8,128)(2,1)S(1)}, u32[]{:S(2)}, u32[]{:S(2)}) collective-permute-start(bf16[2,2,2,24,1280]{4,3,2,1,0:T(8,128)(2,1)S(1)} %get-tuple-element.133), channel_id=1, source_target_pairs={{0,1},{1,0},{2,3},{3,2},{4,5},{5,4},{6,7},{7,6},{8,9},{9,8},{10,11... | collective-permute-start | bytes 1474568 | tf_op jit(solution)/shard_map/ppermute | solution.py:77
  94.1 38.8 %all-to-all-start = ((bf16[8,3,128,3,64]{2,4,3,1,0:T(8,128)(2,1)}), bf16[8,3,128,3,64]{2,4,3,1,0:T(8,128)(2,1)}, u32[]{:S(2)}, u32[]{:S(2)}) async-start(bf16[8,3,128,3,64]{2,4,3,1,0:T(8,128)(2,1)} %bitcast.404), calls=%async_computation | async-start | bytes 2359296 | tf_op jit(solution)/shard_map/all_to_all | solution.py:154
  150.3 16.4 %all-to-all-start.1 = ((bf16[8,3,128,1,64]{2,4,3,1,0:T(8,128)(2,1)}), bf16[8,3,128,1,64]{2,4,3,1,0:T(8,128)(2,1)}, u32[]{:S(2)}, u32[]{:S(2)}) async-start(bf16[8,3,128,1,64]{2,4,3,1,0:T(8,128)(2,1)} %bitcast.415), calls=%async_computation.1 | async-start | bytes 786432 | tf_op jit(solution)/shard_map/all_to_all | solution.py:164
  215.8 30.8 %all-to-all-start.2 = ((bf16[8,3,128,1,64]{2,4,3,1,0:T(8,128)(2,1)}), bf16[8,3,128,1,64]{2,4,3,1,0:T(8,128)(2,1)}, u32[]{:S(2)}, u32[]{:S(2)}) async-start(bf16[8,3,128,1,64]{2,4,3,1,0:T(8,128)(2,1)} %bitcast.56), calls=%async_computation.2 | async-start | bytes 786432 | tf_op jit(solution)/shard_map/all_to_all | solution.py:154
  233.6 27.9 %collective-permute-start.20 = (bf16[2,2,2,2,24,896]{5,4,3,2,1,0:T(8,128)(2,1)}, bf16[2,2,2,2,24,896]{5,4,3,2,1,0:T(8,128)(2,1)}, u32[]{:S(2)}, u32[]{:S(2)}) collective-permute-start(bf16[2,2,2,2,24,896]{5,4,3,2,1,0:T(8,128)(2,1)} %fusion.73), channel_id=1, source_target_pairs={{0,8},{1,9},{2,10},{3,11},{4,12},{5,13},{6,14},{7,15},{8,0},{9,1},... | collective-permute-start | bytes 2064392 | tf_op jit(solution)/shard_map/ppermute | solution.py:102
  237.7 50.1 %collective-permute-start.25 = (bf16[2,2,2,2,24,3072]{5,4,1,2,3,0:T(8,128)(2,1)}, bf16[2,2,2,2,24,3072]{5,4,1,2,3,0:T(8,128)(2,1)}, u32[]{:S(2)}, u32[]{:S(2)}) collective-permute-start(bf16[2,2,2,2,24,3072]{5,4,1,2,3,0:T(8,128)(2,1)} %fusion.35), channel_id=1, source_target_pairs={{0,8},{1,9},{2,10},{3,11},{4,12},{5,13},{6,14},{7,15},{8,0},{9,1},... | collective-permute-start | bytes 7077896 | tf_op jit(solution)/shard_map/ppermute | solution.py:102
  246.6 47.0 %collective-permute-start.30 = (bf16[2,2,2,2,96,768]{5,4,3,2,1,0:T(8,128)(2,1)}, bf16[2,2,2,2,96,768]{5,4,3,2,1,0:T(8,128)(2,1)}, u32[]{:S(2)}, u32[]{:S(2)}) collective-permute-start(bf16[2,2,2,2,96,768]{5,4,3,2,1,0:T(8,128)(2,1)} %fusion.34), channel_id=1, source_target_pairs={{0,8},{1,9},{2,10},{3,11},{4,12},{5,13},{6,14},{7,15},{8,0},{9,1},... | collective-permute-start | bytes 7077896 | tf_op jit(solution)/shard_map/ppermute | solution.py:102
  270.5 34.2 %all-to-all-start.3 = ((bf16[8,3,128,3,64]{2,4,3,1,0:T(8,128)(2,1)}), bf16[8,3,128,3,64]{2,4,3,1,0:T(8,128)(2,1)}, u32[]{:S(2)}, u32[]{:S(2)}) async-start(bf16[8,3,128,3,64]{2,4,3,1,0:T(8,128)(2,1)} %maximum_bitcast_fusion), calls=%async_computation.3 | async-start | bytes 2359296 | tf_op jit(solution)/shard_map/all_to_all | solution.py:164
  292.9 49.4 %collective-permute-start.26 = (bf16[2,2,2,24,3072]{4,3,0,1,2:T(8,128)(2,1)}, bf16[2,2,2,24,3072]{4,3,0,1,2:T(8,128)(2,1)}, u32[]{:S(2)}, u32[]{:S(2)}) collective-permute-start(bf16[2,2,2,24,3072]{4,3,0,1,2:T(8,128)(2,1)} %fusion.63), channel_id=1, source_target_pairs={{0,16},{1,17},{2,18},{3,19},{4,20},{5,21},{6,22},{7,23},{8,24},{9,... | collective-permute-start | bytes 3538952 | tf_op jit(solution)/shard_map/ppermute | solution.py:102
  299.7 45.8 %collective-permute-start.31 = (bf16[2,2,2,96,768]{4,3,2,1,0:T(8,128)(2,1)}, bf16[2,2,2,96,768]{4,3,2,1,0:T(8,128)(2,1)}, u32[]{:S(2)}, u32[]{:S(2)}) collective-permute-start(bf16[2,2,2,96,768]{4,3,2,1,0:T(8,128)(2,1)} %fusion.64), channel_id=1, source_target_pairs={{0,1},{1,0},{2,3},{3,2},{4,5},{5,4},{6,7},{7,6},{8,9},{9,8},{10,11... | collective-permute-start | bytes 3538952 | tf_op jit(solution)/shard_map/ppermute | solution.py:102
  334.2 15.6 %collective-permute-start.10 = (bf16[2,2,2,2,24,1280]{5,4,3,2,1,0:T(8,128)(2,1)S(1)}, bf16[2,2,2,2,24,1280]{5,4,3,2,1,0:T(8,128)(2,1)S(1)}, u32[]{:S(2)}, u32[]{:S(2)}) collective-permute-start(bf16[2,2,2,2,24,1280]{5,4,3,2,1,0:T(8,128)(2,1)S(1)} %fusion.67), channel_id=1, source_target_pairs={{0,8},{1,9},{2,10},{3,11},{4,12},{5,13},{6,14},{7,15},{8,0},{9,1},... | collective-permute-start | bytes 2949128 | tf_op jit(solution)/shard_map/ppermute | solution.py:102
  344.7 17.0 %collective-permute-start.27 = (bf16[2,2,24,3072]{3,2,0,1:T(8,128)(2,1)S(1)}, bf16[2,2,24,3072]{3,2,0,1:T(8,128)(2,1)S(1)}, u32[]{:S(2)}, u32[]{:S(2)}) collective-permute-start(bf16[2,2,24,3072]{3,2,0,1:T(8,128)(2,1)S(1)} %fusion.74), channel_id=1, source_target_pairs={{0,1},{1,0},{2,3},{3,2},{4,5},{5,4},{6,7},{7,6},{8,9},{9,8},{10,11... | collective-permute-start | bytes 1769480 | tf_op jit(solution)/shard_map/ppermute | solution.py:102
  348.1 14.9 %collective-permute-start.32 = (bf16[2,2,96,768]{3,2,1,0:T(8,128)(2,1)S(1)}, bf16[2,2,96,768]{3,2,1,0:T(8,128)(2,1)S(1)}, u32[]{:S(2)}, u32[]{:S(2)}) collective-permute-start(bf16[2,2,96,768]{3,2,1,0:T(8,128)(2,1)S(1)} %fusion.75), channel_id=1, source_target_pairs={{0,2},{1,3},{2,0},{3,1},{4,6},{5,7},{6,4},{7,5},{8,10},{9,11},{10,... | collective-permute-start | bytes 1769480 | tf_op jit(solution)/shard_map/ppermute | solution.py:102
  350.4 21.0 %collective-permute-start.11 = (bf16[2,2,2,24,1280]{4,3,2,1,0:T(8,128)(2,1)S(1)}, bf16[2,2,2,24,1280]{4,3,2,1,0:T(8,128)(2,1)S(1)}, u32[]{:S(2)}, u32[]{:S(2)}) collective-permute-start(bf16[2,2,2,24,1280]{4,3,2,1,0:T(8,128)(2,1)S(1)} %fusion.86), channel_id=1, source_target_pairs={{0,1},{1,0},{2,3},{3,2},{4,5},{5,4},{6,7},{7,6},{8,9},{9,8},{10,11... | collective-permute-start | bytes 1474568 | tf_op jit(solution)/shard_map/ppermute | solution.py:102
  360.5 14.0 %collective-permute-start.17 = (bf16[2,2,24,1152]{3,2,0,1:T(8,128)(2,1)S(1)}, bf16[2,2,24,1152]{3,2,0,1:T(8,128)(2,1)S(1)}, u32[]{:S(2)}, u32[]{:S(2)}) collective-permute-start(bf16[2,2,24,1152]{3,2,0,1:T(8,128)(2,1)S(1)} %fusion.94), channel_id=1, source_target_pairs={{0,1},{1,0},{2,3},{3,2},{4,5},{5,4},{6,7},{7,6},{8,9},{9,8},{10,11... | collective-permute-start | bytes 663560 | tf_op jit(solution)/shard_map/ppermute | solution.py:102
  361.8 20.6 %collective-permute-start.28 = (bf16[2,24,3072]{2,1,0:T(8,128)(2,1)S(1)}, bf16[2,24,3072]{2,1,0:T(8,128)(2,1)S(1)}, u32[]{:S(2)}, u32[]{:S(2)}) collective-permute-start(bf16[2,24,3072]{2,1,0:T(8,128)(2,1)S(1)} %fusion.91), channel_id=1, source_target_pairs={{0,2},{1,3},{2,0},{3,1},{4,6},{5,7},{6,4},{7,5},{8,10},{9,11},{10,... | collective-permute-start | bytes 884744 | tf_op jit(solution)/shard_map/ppermute | solution.py:102
  363.2 21.3 %collective-permute-start.33 = (bf16[2,96,768]{2,1,0:T(8,128)(2,1)S(1)}, bf16[2,96,768]{2,1,0:T(8,128)(2,1)S(1)}, u32[]{:S(2)}, u32[]{:S(2)}) collective-permute-start(bf16[2,96,768]{2,1,0:T(8,128)(2,1)S(1)} %fusion.92), channel_id=1, source_target_pairs={{0,16},{1,17},{2,18},{3,19},{4,20},{5,21},{6,22},{7,23},{8,24},{9,... | collective-permute-start | bytes 884744 | tf_op jit(solution)/shard_map/ppermute | solution.py:102
  375.6 18.8 %collective-permute-start.12 = (bf16[2,2,24,1280]{3,2,1,0:T(8,128)(2,1)S(1)}, bf16[2,2,24,1280]{3,2,1,0:T(8,128)(2,1)S(1)}, u32[]{:S(2)}, u32[]{:S(2)}) collective-permute-start(bf16[2,2,24,1280]{3,2,1,0:T(8,128)(2,1)S(1)} %fusion.93), channel_id=1, source_target_pairs={{0,2},{1,3},{2,0},{3,1},{4,6},{5,7},{6,4},{7,5},{8,10},{9,11},{10,... | collective-permute-start | bytes 737288 | tf_op jit(solution)/shard_map/ppermute | solution.py:102
  381.3 13.1 %collective-permute-start.19 = (bf16[24,1152]{1,0:T(8,128)(2,1)S(1)}, bf16[24,1152]{1,0:T(8,128)(2,1)S(1)}, u32[]{:S(2)}, u32[]{:S(2)}) collective-permute-start(bf16[24,1152]{1,0:T(8,128)(2,1)S(1)} %fusion.102), channel_id=1, source_target_pairs={{0,4},{1,5},{2,6},{3,7},{4,0},{5,1},{6,2},{7,3},{8,12},{9,13},{10,... | collective-permute-start | bytes 165896 | tf_op jit(solution)/shard_map/ppermute | solution.py:102
  382.5 14.6 %collective-permute-start.29 = (bf16[24,3072]{1,0:T(8,128)(2,1)S(1)}, bf16[24,3072]{1,0:T(8,128)(2,1)S(1)}, u32[]{:S(2)}, u32[]{:S(2)}) collective-permute-start(bf16[24,3072]{1,0:T(8,128)(2,1)S(1)} %fusion.96), channel_id=1, source_target_pairs={{0,4},{1,5},{2,6},{3,7},{4,0},{5,1},{6,2},{7,3},{8,12},{9,13},{10,... | collective-permute-start | bytes 442376 | tf_op jit(solution)/shard_map/ppermute | solution.py:102
  384.5 15.0 %collective-permute-start.34 = (bf16[96,768]{1,0:T(8,128)(2,1)S(1)}, bf16[96,768]{1,0:T(8,128)(2,1)S(1)}, u32[]{:S(2)}, u32[]{:S(2)}) collective-permute-start(bf16[96,768]{1,0:T(8,128)(2,1)S(1)} %fusion.97), channel_id=1, source_target_pairs={{0,4},{1,5},{2,6},{3,7},{4,0},{5,1},{6,2},{7,3},{8,12},{9,13},{10,... | collective-permute-start | bytes 442376 | tf_op jit(solution)/shard_map/ppermute | solution.py:102
  (66 other events, 652.2 us)
Sparse Core Ops, SparseCore 0:
  10.9 100.3 all-gather.1

commit v13 on v12

--- a/solution.py
+++ b/solution.py
@@ -379,14 +379,16 @@
     vec_one = vector_block(
         [grad_bias_up, grad_bias_down, grad_gain_two, grad_shift_two], full_rows, jnp.float32
     )
-    red_up, red_down, red_mixed = reduce_routes(
-        [grad_up, grad_down, jnp.concatenate([grad_out, vec_one], axis=1)],
+    up_keep = ff - ff // 4
+    red_up_a, red_down, red_mixed = reduce_routes(
+        [grad_up[:, :up_keep], grad_down, jnp.concatenate([grad_out, vec_one, grad_up[:, up_keep:]], axis=1)],
         orders,
         count,
         me,
         backward_anchors[:steps],
     )
-    red_out, red_vec_one = split_cols(red_mixed, [width, vec_one.shape[1]])
+    red_out, red_vec_one, red_up_b = split_cols(red_mixed, [width, vec_one.shape[1], ff - up_keep])
+    red_up = jnp.concatenate([red_up_a, red_up_b], axis=1)
 
     grad_bias_query = jnp.sum(proj_grad[:, :width].astype(jnp.float32), axis=0)
     grad_bias_value = jnp.sum(proj_grad[:, 2 * width :].astype(jnp.float32), axis=0)

time: 421 us -> 471 us (1.12)
  waiting for transfers between devices: 109 us -> 156 us
  local copies, waits for them, and re-layouts: 112 us -> 119 us
  matrix products: 64 us -> 58.6 us
    ppermute x25, waiting for transfers between devices: 41 us -> 89.5 us  [reduce_routes(): got = lax.ppermute(send, ALL, partner_pairs(count, b))]
    unnamed x106 -> x118, local copies, waits for them, and re-layouts: 12.6 us -> 16.9 us
  transfers between devices with their start and end apart: 40 -> 40, of which waited for: 17 -> 23; matrix products, arithmetic and copies ran while one was open for 41% -> 36% of each run, Pallas kernels for 0% -> 0%
where the time goes in v13:
time: 471 us; the launch traced here: 463 us
  waiting for transfers between devices  156 us (33%)
  local copies, waits for them, and re-layouts  119 us (25%)
  starting transfers between devices  58.6 us (12%)
  matrix products  58.6 us (12%)
  other arithmetic  55.2 us (12%)
  between operations  15.6 us (3%)
    ppermute x25, waiting for transfers between devices, reduce_routes(): got = lax.ppermute(send, ALL, partner_pairs(count, b))  89.5 us
    ppermute x10, waiting for transfers between devices, gather_routes(): got = lax.ppermute(x, ALL, partner_pairs(count, b))  30.2 us
    all_to_all x2, waiting for transfers between devices, rows_to_units(): x = lax.all_to_all(x, 'seq', 0, 0, tiled=True)  27.9 us
    ppermute x25, starting transfers between devices, reduce_routes(): got = lax.ppermute(send, ALL, partner_pairs(count, b))  23.5 us
    unnamed x118, local copies, waits for them, and re-layouts  16.9 us
    add x25, other arithmetic, reduce_routes(): x = keep + got.astype(jnp.float32)  16.3 us
    convert_element_type x25, local copies, waits for them, and re-layouts, reduce_routes(): lax.dynamic_index_in_dim(x, 1 - mine, axis, keepdims=False)  15.7 us
    ppermute x10, starting transfers between devices, gather_routes(): got = lax.ppermute(x, ALL, partner_pairs(count, b))  13.5 us
  transfers between devices with their start and end apart: 40, of which 23 were waited for; matrix products, arithmetic and copies ran while one was open for 36% of the time, Pallas kernels for 0%

profile of v13, /device:TPU:0, one launch (start us, length us, event | category | flops | bytes accessed | tf_op | source)
XLA Modules:
  0.0 462.5 jit_solution(1946203634916418219)
XLA Ops:
  23.1 7.2 %collective-permute-done.5 = bf16[24,1152]{1,0:T(8,128)(2,1)S(1)} collective-permute-done((bf16[24,1152]{1,0:T(8,128)(2,1)S(1)}, bf16[24,1152]{1,0:T(8,128)(2,1)S(1)}, u32[]{:S(2)}, u32[]{:S(2)}) %collective-permute-start.5) | collective-permute-done | bytes 55328 | tf_op jit(solution)/shard_map/ppermute | solution.py:77
  45.4 4.7 %collective-permute-done.2 = bf16[2,2,24,1280]{3,2,1,0:T(8,128)(2,1)S(1)} collective-permute-done((bf16[2,2,24,1280]{3,2,1,0:T(8,128)(2,1)S(1)}, bf16[2,2,24,1280]{3,2,1,0:T(8,128)(2,1)S(1)}, u32[]{:S(2)}, u32[]{:S(2)}) %collective-permute-start.2) | collective-permute-done | bytes 245792 | tf_op jit(solution)/shard_map/ppermute | solution.py:77
  50.3 12.3 %collective-permute-done.8 = bf16[2,2,2,24,1152]{4,3,2,1,0:T(8,128)(2,1)S(1)} collective-permute-done((bf16[2,2,2,24,1152]{4,3,2,1,0:T(8,128)(2,1)S(1)}, bf16[2,2,2,24,1152]{4,3,2,1,0:T(8,128)(2,1)S(1)}, u32[]{:S(2)}, u32[]{:S(2)}) %collective-permute-start.8) | collective-permute-done | bytes 442400 | tf_op jit(solution)/shard_map/ppermute | solution.py:77
  93.8 7.3 %all-to-all-start = ((bf16[8,3,128,3,64]{2,4,3,1,0:T(8,128)(2,1)}), bf16[8,3,128,3,64]{2,4,3,1,0:T(8,128)(2,1)}, u32[]{:S(2)}, u32[]{:S(2)}) async-start(bf16[8,3,128,3,64]{2,4,3,1,0:T(8,128)(2,1)} %bitcast.412), calls=%async_computation | async-start | bytes 2359296 | tf_op jit(solution)/shard_map/all_to_all | solution.py:154
  104.9 27.9 %all-to-all-done = bf16[8,3,128,3,64]{2,4,3,1,0:T(8,128)(2,1)} async-done(((bf16[8,3,128,3,64]{2,4,3,1,0:T(8,128)(2,1)}), bf16[8,3,128,3,64]{2,4,3,1,0:T(8,128)(2,1)}, u32[]{:S(2)}, u32[]{:S(2)}) %all-to-all-start) | async-done | bytes 1179680 | tf_op jit(solution)/shard_map/all_to_all | solution.py:154
  138.2 6.6 %fusion.131 = (f32[3,1024]{1,0:T(4,128)S(1)}, f32[3,1024,1024]{1,2,0:T(8,128)S(1)}) fusion(bf16[3,1024,3,64]{1,3,0,2:T(8,128)(2,1)S(1)} %reshape.652, pred[3,1024]{1,0:T(4,128)(4,1)S(1)} %broadcast_compare_fusion, s32[3,1024]{1,0:T(4,128)S(1)} %broadcast_add_fusion, pred[1024,1024]{0,1:T(8,128)(4,1)} %iota_compare_fusion), kind=kOutput, calls=%fused_computation.304 | convolution fusion | flops 421524480 | bytes 14467072 | tf_op jit(solution)/shard_map/uqd,ukd->uqk/dot_general | solution.py:172
  158.4 8.1 %all-to-all-done.1 = bf16[8,3,128,1,64]{2,4,3,1,0:T(8,128)(2,1)S(1)} async-done(((bf16[8,3,128,1,64]{2,4,3,1,0:T(8,128)(2,1)}), bf16[8,3,128,1,64]{2,4,3,1,0:T(8,128)(2,1)S(1)}, u32[]{:S(2)}, u32[]{:S(2)}) %all-to-all-start.1) | async-done | bytes 393248 | tf_op jit(solution)/shard_map/all_to_all | solution.py:164
  167.6 4.7 %slice.212 = bf16[768,3072]{1,0:T(8,128)(2,1)} slice(bf16[768,6912]{1,0:T(8,128)(2,1)} %all-gather.2.cloned.1.call-done), slice={[0:768], [3840:6912]} | slice | bytes 9437184 | tf_op jit(solution)/shard_map/slice | solution.py:112
  172.4 8.5 %reshape.656 = bf16[3072,768]{1,0:T(8,128)(2,1)} reshape(bf16[768,3072]{1,0:T(8,128)(2,1)} %slice.212) | data formatting | bytes 9437184 | tf_op jit(solution)/shard_map/reshape | solution.py:330
  183.1 9.5 %fusion.7 = (f32[256,3072]{1,0:T(8,128)S(1)}, f32[256,3072]{1,0:T(8,128)S(1)}) fusion(f32[3072]{0:T(1024)S(1)} %reshape.681, bf16[768,6912]{1,0:T(8,128)(2,1)} %all-gather.2.cloned.1.call-done, f32[256,768]{1,0:T(8,128)S(1)} %get-tuple-element.162, f32[768]{0:T(1024)S(1)} %get-tuple-element.100, f32[768]{0:T(1024)S(1)} %get-tuple-element.101, ...), kind=kOutput, calls=%fused_computation.20 | convolution fusion | flops 1258487808 | bytes 11816960 | tf_op jit(solution)/shard_map/dot_general | solution.py:340
  205.3 7.5 %fusion.10 = bf16[3072,256]{0,1:T(8,128)(2,1)} fusion(f32[256,3072]{1,0:T(8,128)S(1)} %get-tuple-element.164), kind=kLoop, calls=%fused_computation.23 | loop fusion | flops 51118080 | bytes 4718592 | tf_op jit(solution)/shard_map/convert_element_type | solution.py:344
  218.8 4.4 all-to-all-start.2
  232.8 6.1 %concatenate.65 = f32[2,2,2,2,2,24,1664]{6,5,4,3,2,1,0:T(8,128)} concatenate(f32[2,2,2,2,2,24,768]{6,5,4,3,2,1,0:T(8,128)} %fusion.89, f32[2,2,2,2,2,24,4]{6,5,4,3,2,1,0:T(8,128)} %concatenate.60, f32[2,2,2,2,2,24,1]{6,5,4,3,2,1,0:T(8,128)} %concatenate.72, f32[2,2,2,2,2,24,1]{6,5,4,3,2,1,0:T(8,128)} %concatenate.73, f32[2,2,2,2,2,24,1]{6,5,4,3,2,1,0:T(8,128)} %concatenate.74, ...), dimensions={6} | concatenate | bytes 10223616 | tf_op jit(solution)/shard_map/concatenate | solution.py:384
  260.5 6.4 %multiply_convert_fusion = bf16[3,1024,1024]{1,2,0:T(8,128)(2,1)S(1)} fusion(f32[3,1024,1024]{1,2,0:T(8,128)} %copy-done.2, f32[3,1024]{1,0:T(4,128)S(1)} %div.84, bf16[3,1024,3,64]{1,3,0,2:T(8,128)(2,1)S(1)} %copy-done.18, bf16[3,1024,64]{1,2,0:T(8,128)(2,1)S(1)} %squeeze_reshape.3, f32[3,1024]{1,0:T(4,128)S(1)} %copy-done.33), kind=kOutput, calls=%fused_computation.3 | convolution fusion | flops 412680192 | bytes 19693568 | tf_op jit(solution)/shard_map/uqd,ukd->uqk/dot_general | solution.py:186
  267.0 6.6 %fusion.57 = bf16[3,1024,64]{1,2,0:T(8,128)(2,1)S(1)} fusion(f32[3,1024,1024]{1,2,0:T(8,128)} %copy-done.2, bf16[3,1024,64]{1,2,0:T(8,128)(2,1)S(1)} %squeeze_reshape.3, f32[3,1024]{1,0:T(4,128)S(1)} %copy-done.33), kind=kOutput, calls=%fused_computation.101 | convolution fusion | flops 406585344 | bytes 13381632 | tf_op jit(solution)/shard_map/uqk,uqd->ukd/dot_general | solution.py:190
  278.5 6.0 %all-to-all-start.3 = ((bf16[8,3,128,3,64]{2,4,3,1,0:T(8,128)(2,1)}), bf16[8,3,128,3,64]{2,4,3,1,0:T(8,128)(2,1)}, u32[]{:S(2)}, u32[]{:S(2)}) async-start(bf16[8,3,128,3,64]{2,4,3,1,0:T(8,128)(2,1)} %maximum_bitcast_fusion), calls=%async_computation.3 | async-start | bytes 2359296 | tf_op jit(solution)/shard_map/all_to_all | solution.py:164
  291.5 28.2 %collective-permute-done.21 = bf16[2,2,2,24,1664]{4,3,2,1,0:T(8,128)(2,1)S(1)} collective-permute-done((bf16[2,2,2,24,1664]{4,3,2,1,0:T(8,128)(2,1)S(1)}, bf16[2,2,2,24,1664]{4,3,2,1,0:T(8,128)(2,1)S(1)}, u32[]{:S(2)}, u32[]{:S(2)}) %collective-permute-start.21) | collective-permute-done | bytes 639008 | tf_op jit(solution)/shard_map/ppermute | solution.py:102
  322.1 8.2 %collective-permute-done.22 = bf16[2,2,24,1664]{3,2,1,0:T(8,128)(2,1)S(1)} collective-permute-done((bf16[2,2,24,1664]{3,2,1,0:T(8,128)(2,1)S(1)}, bf16[2,2,24,1664]{3,2,1,0:T(8,128)(2,1)S(1)}, u32[]{:S(2)}, u32[]{:S(2)}) %collective-permute-start.22) | collective-permute-done | bytes 319520 | tf_op jit(solution)/shard_map/ppermute | solution.py:102
  336.4 10.8 %collective-permute-done.26 = bf16[2,2,2,24,2304]{4,3,0,1,2:T(8,128)(2,1)S(1)} collective-permute-done((bf16[2,2,2,24,2304]{4,3,0,1,2:T(8,128)(2,1)S(1)}, bf16[2,2,2,24,2304]{4,3,0,1,2:T(8,128)(2,1)S(1)}, u32[]{:S(2)}, u32[]{:S(2)}) %collective-permute-start.26) | collective-permute-done | bytes 884768 | tf_op jit(solution)/shard_map/ppermute | solution.py:102
  368.9 5.7 %concatenate.58 = f32[2,2,2,2,2,24,1280]{6,5,4,3,2,1,0:T(8,128)} concatenate(f32[2,2,2,2,2,24,1152]{6,5,4,3,2,1,0:T(8,128)S(1)} %fusion.78, f32[2,2,2,2,2,24,1]{6,5,4,3,2,1,0:T(8,128)} %concatenate.67, f32[2,2,2,2,2,24,1]{6,5,4,3,2,1,0:T(8,128)} %concatenate.68, f32[2,2,2,2,2,24,1]{6,5,4,3,2,1,0:T(8,128)} %concatenate.69, f32[2,2,2,2,2,24,1]{6,5,4,3,2,1,0:T(8,128)} %concatenate.70, ...), dimensions={6} | concatenate | bytes 7864320 | tf_op jit(solution)/shard_map/concatenate | solution.py:409
  395.9 5.4 %collective-permute-done.28 = bf16[2,24,2304]{2,1,0:T(8,128)(2,1)S(1)} collective-permute-done((bf16[2,24,2304]{2,1,0:T(8,128)(2,1)S(1)}, bf16[2,24,2304]{2,1,0:T(8,128)(2,1)S(1)}, u32[]{:S(2)}, u32[]{:S(2)}) %collective-permute-start.28) | collective-permute-done | bytes 221216 | tf_op jit(solution)/shard_map/ppermute | solution.py:102
  403.1 5.3 %collective-permute-done.29 = bf16[24,2304]{1,0:T(8,128)(2,1)S(1)} collective-permute-done((bf16[24,2304]{1,0:T(8,128)(2,1)S(1)}, bf16[24,2304]{1,0:T(8,128)(2,1)S(1)}, u32[]{:S(2)}, u32[]{:S(2)}) %collective-permute-start.29) | collective-permute-done | bytes 110624 | tf_op jit(solution)/shard_map/ppermute | solution.py:102
  417.2 7.4 %collective-permute-done.16 = bf16[2,2,2,24,1152]{4,3,0,1,2:T(8,128)(2,1)S(1)} collective-permute-done((bf16[2,2,2,24,1152]{4,3,0,1,2:T(8,128)(2,1)S(1)}, bf16[2,2,2,24,1152]{4,3,0,1,2:T(8,128)(2,1)S(1)}, u32[]{:S(2)}, u32[]{:S(2)}) %collective-permute-start.16) | collective-permute-done | bytes 442400 | tf_op jit(solution)/shard_map/ppermute | solution.py:102
  435.3 4.2 collective-permute-done.18
  (376 shorter events, 237.7 us)
Async XLA Ops:
  7.2 160.4 %all-gather.2.cloned.1.call-start = ((), (), s32[]{:S(2)}) async-start(), calls=%async_computation.4 | async-start | bytes 10948608 | tf_op jit(solution)/shard_map/all_gather | solution.py:328
  17.7 15.1 %collective-permute-start = (bf16[24,1280]{1,0:T(8,128)(2,1)S(1)}, bf16[24,1280]{1,0:T(8,128)(2,1)S(1)}, u32[]{:S(2)}, u32[]{:S(2)}) collective-permute-start(bf16[24,1280]{1,0:T(8,128)(2,1)S(1)} %concatenate.49), channel_id=1, source_target_pairs={{0,4},{1,5},{2,6},{3,7},{4,0},{5,1},{6,2},{7,3},{8,12},{9,13},{10,... | collective-permute-start | bytes 184328 | tf_op jit(solution)/shard_map/ppermute | solution.py:77
  39.1 11.0 %collective-permute-start.2 = (bf16[2,2,24,1280]{3,2,1,0:T(8,128)(2,1)S(1)}, bf16[2,2,24,1280]{3,2,1,0:T(8,128)(2,1)S(1)}, u32[]{:S(2)}, u32[]{:S(2)}) collective-permute-start(bf16[2,2,24,1280]{3,2,1,0:T(8,128)(2,1)S(1)} %get-tuple-element.137), channel_id=1, source_target_pairs={{0,2},{1,3},{2,0},{3,1},{4,6},{5,7},{6,4},{7,5},{8,10},{9,11},{10,... | collective-permute-start | bytes 737288 | tf_op jit(solution)/shard_map/ppermute | solution.py:77
  43.6 19.0 %collective-permute-start.8 = (bf16[2,2,2,24,1152]{4,3,2,1,0:T(8,128)(2,1)S(1)}, bf16[2,2,2,24,1152]{4,3,2,1,0:T(8,128)(2,1)S(1)}, u32[]{:S(2)}, u32[]{:S(2)}) collective-permute-start(bf16[2,2,2,24,1152]{4,3,2,1,0:T(8,128)(2,1)S(1)} %get-tuple-element.135), channel_id=1, source_target_pairs={{0,16},{1,17},{2,18},{3,19},{4,20},{5,21},{6,22},{7,23},{8,24},{9,... | collective-permute-start | bytes 1327112 | tf_op jit(solution)/shard_map/ppermute | solution.py:77
  50.2 13.7 %collective-permute-start.3 = (bf16[2,2,2,24,1280]{4,3,2,1,0:T(8,128)(2,1)S(1)}, bf16[2,2,2,24,1280]{4,3,2,1,0:T(8,128)(2,1)S(1)}, u32[]{:S(2)}, u32[]{:S(2)}) collective-permute-start(bf16[2,2,2,24,1280]{4,3,2,1,0:T(8,128)(2,1)S(1)} %get-tuple-element.133), channel_id=1, source_target_pairs={{0,1},{1,0},{2,3},{3,2},{4,5},{5,4},{6,7},{7,6},{8,9},{9,8},{10,11... | collective-permute-start | bytes 1474568 | tf_op jit(solution)/shard_map/ppermute | solution.py:77
  93.8 39.1 %all-to-all-start = ((bf16[8,3,128,3,64]{2,4,3,1,0:T(8,128)(2,1)}), bf16[8,3,128,3,64]{2,4,3,1,0:T(8,128)(2,1)}, u32[]{:S(2)}, u32[]{:S(2)}) async-start(bf16[8,3,128,3,64]{2,4,3,1,0:T(8,128)(2,1)} %bitcast.412), calls=%async_computation | async-start | bytes 2359296 | tf_op jit(solution)/shard_map/all_to_all | solution.py:154
  150.7 15.7 %all-to-all-start.1 = ((bf16[8,3,128,1,64]{2,4,3,1,0:T(8,128)(2,1)}), bf16[8,3,128,1,64]{2,4,3,1,0:T(8,128)(2,1)S(1)}, u32[]{:S(2)}, u32[]{:S(2)}) async-start(bf16[8,3,128,1,64]{2,4,3,1,0:T(8,128)(2,1)} %bitcast.387), calls=%async_computation.1 | async-start | bytes 786432 | tf_op jit(solution)/shard_map/all_to_all | solution.py:164
  218.8 39.0 %all-to-all-start.2 = ((bf16[8,3,128,1,64]{2,4,3,1,0:T(8,128)(2,1)}), bf16[8,3,128,1,64]{2,4,3,1,0:T(8,128)(2,1)}, u32[]{:S(2)}, u32[]{:S(2)}) async-start(bf16[8,3,128,1,64]{2,4,3,1,0:T(8,128)(2,1)} %bitcast.423), calls=%async_computation.2 | async-start | bytes 786432 | tf_op jit(solution)/shard_map/all_to_all | solution.py:154
  241.7 42.8 %collective-permute-start.20 = (bf16[2,2,2,2,24,1664]{5,4,3,2,1,0:T(8,128)(2,1)}, bf16[2,2,2,2,24,1664]{5,4,3,2,1,0:T(8,128)(2,1)}, u32[]{:S(2)}, u32[]{:S(2)}) collective-permute-start(bf16[2,2,2,2,24,1664]{5,4,3,2,1,0:T(8,128)(2,1)} %fusion.49), channel_id=1, source_target_pairs={{0,8},{1,9},{2,10},{3,11},{4,12},{5,13},{6,14},{7,15},{8,0},{9,1},... | collective-permute-start | bytes 3833864 | tf_op jit(solution)/shard_map/ppermute | solution.py:102
  245.1 44.1 %collective-permute-start.25 = (bf16[2,2,2,2,24,2304]{5,4,1,2,3,0:T(8,128)(2,1)}, bf16[2,2,2,2,24,2304]{5,4,1,2,3,0:T(8,128)(2,1)}, u32[]{:S(2)}, u32[]{:S(2)}) collective-permute-start(bf16[2,2,2,2,24,2304]{5,4,1,2,3,0:T(8,128)(2,1)} %fusion.38), channel_id=1, source_target_pairs={{0,8},{1,9},{2,10},{3,11},{4,12},{5,13},{6,14},{7,15},{8,0},{9,1},... | collective-permute-start | bytes 5308424 | tf_op jit(solution)/shard_map/ppermute | solution.py:102
  254.6 76.7 %collective-permute-start.30 = (bf16[2,2,2,2,96,768]{5,4,3,2,1,0:T(8,128)(2,1)}, bf16[2,2,2,2,96,768]{5,4,3,2,1,0:T(8,128)(2,1)}, u32[]{:S(2)}, u32[]{:S(2)}) collective-permute-start(bf16[2,2,2,2,96,768]{5,4,3,2,1,0:T(8,128)(2,1)} %fusion.34), channel_id=1, source_target_pairs={{0,8},{1,9},{2,10},{3,11},{4,12},{5,13},{6,14},{7,15},{8,0},{9,1},... | collective-permute-start | bytes 7077896 | tf_op jit(solution)/shard_map/ppermute | solution.py:102
  278.5 71.9 %all-to-all-start.3 = ((bf16[8,3,128,3,64]{2,4,3,1,0:T(8,128)(2,1)}), bf16[8,3,128,3,64]{2,4,3,1,0:T(8,128)(2,1)}, u32[]{:S(2)}, u32[]{:S(2)}) async-start(bf16[8,3,128,3,64]{2,4,3,1,0:T(8,128)(2,1)} %maximum_bitcast_fusion), calls=%async_computation.3 | async-start | bytes 2359296 | tf_op jit(solution)/shard_map/all_to_all | solution.py:164
  287.1 32.6 %collective-permute-start.21 = (bf16[2,2,2,24,1664]{4,3,2,1,0:T(8,128)(2,1)S(1)}, bf16[2,2,2,24,1664]{4,3,2,1,0:T(8,128)(2,1)S(1)}, u32[]{:S(2)}, u32[]{:S(2)}) collective-permute-start(bf16[2,2,2,24,1664]{4,3,2,1,0:T(8,128)(2,1)S(1)} %fusion.74), channel_id=1, source_target_pairs={{0,2},{1,3},{2,0},{3,1},{4,6},{5,7},{6,4},{7,5},{8,10},{9,11},{10,... | collective-permute-start | bytes 1916936 | tf_op jit(solution)/shard_map/ppermute | solution.py:102
  319.9 10.5 %collective-permute-start.22 = (bf16[2,2,24,1664]{3,2,1,0:T(8,128)(2,1)S(1)}, bf16[2,2,24,1664]{3,2,1,0:T(8,128)(2,1)S(1)}, u32[]{:S(2)}, u32[]{:S(2)}) collective-permute-start(bf16[2,2,24,1664]{3,2,1,0:T(8,128)(2,1)S(1)} %fusion.91), channel_id=1, source_target_pairs={{0,16},{1,17},{2,18},{3,19},{4,20},{5,21},{6,22},{7,23},{8,24},{9,... | collective-permute-start | bytes 958472 | tf_op jit(solution)/shard_map/ppermute | solution.py:102
  321.2 26.0 %collective-permute-start.26 = (bf16[2,2,2,24,2304]{4,3,0,1,2:T(8,128)(2,1)S(1)}, bf16[2,2,2,24,2304]{4,3,0,1,2:T(8,128)(2,1)S(1)}, u32[]{:S(2)}, u32[]{:S(2)}) collective-permute-start(bf16[2,2,2,24,2304]{4,3,0,1,2:T(8,128)(2,1)S(1)} %fusion.68), channel_id=1, source_target_pairs={{0,16},{1,17},{2,18},{3,19},{4,20},{5,21},{6,22},{7,23},{8,24},{9,... | collective-permute-start | bytes 2654216 | tf_op jit(solution)/shard_map/ppermute | solution.py:102
  335.0 74.2 %collective-permute-start.31 = (bf16[2,2,2,96,768]{4,3,2,1,0:T(8,128)(2,1)}, bf16[2,2,2,96,768]{4,3,2,1,0:T(8,128)(2,1)}, u32[]{:S(2)}, u32[]{:S(2)}) collective-permute-start(bf16[2,2,2,96,768]{4,3,2,1,0:T(8,128)(2,1)} %fusion.64), channel_id=1, source_target_pairs={{0,1},{1,0},{2,3},{3,2},{4,5},{5,4},{6,7},{7,6},{8,9},{9,8},{10,11... | collective-permute-start | bytes 3538952 | tf_op jit(solution)/shard_map/ppermute | solution.py:102
  348.8 44.1 %collective-permute-start.27 = (bf16[2,2,24,2304]{3,2,0,1:T(8,128)(2,1)}, bf16[2,2,24,2304]{3,2,0,1:T(8,128)(2,1)}, u32[]{:S(2)}, u32[]{:S(2)}) collective-permute-start(bf16[2,2,24,2304]{3,2,0,1:T(8,128)(2,1)} %fusion.88), channel_id=1, source_target_pairs={{0,1},{1,0},{2,3},{3,2},{4,5},{5,4},{6,7},{7,6},{8,9},{9,8},{10,11... | collective-permute-start | bytes 1327112 | tf_op jit(solution)/shard_map/ppermute | solution.py:102
  377.4 37.1 %collective-permute-start.10 = (bf16[2,2,2,2,24,1280]{5,4,3,2,1,0:T(8,128)(2,1)}, bf16[2,2,2,2,24,1280]{5,4,3,2,1,0:T(8,128)(2,1)}, u32[]{:S(2)}, u32[]{:S(2)}) collective-permute-start(bf16[2,2,2,2,24,1280]{5,4,3,2,1,0:T(8,128)(2,1)} %fusion.67), channel_id=1, source_target_pairs={{0,8},{1,9},{2,10},{3,11},{4,12},{5,13},{6,14},{7,15},{8,0},{9,1},... | collective-permute-start | bytes 2949128 | tf_op jit(solution)/shard_map/ppermute | solution.py:102
  388.4 23.3 %collective-permute-start.15 = (bf16[2,2,2,2,24,1152]{5,4,1,2,3,0:T(8,128)(2,1)}, bf16[2,2,2,2,24,1152]{5,4,1,2,3,0:T(8,128)(2,1)}, u32[]{:S(2)}, u32[]{:S(2)}) collective-permute-start(bf16[2,2,2,2,24,1152]{5,4,1,2,3,0:T(8,128)(2,1)} %fusion.69), channel_id=1, source_target_pairs={{0,8},{1,9},{2,10},{3,11},{4,12},{5,13},{6,14},{7,15},{8,0},{9,1},... | collective-permute-start | bytes 2654216 | tf_op jit(solution)/shard_map/ppermute | solution.py:102
  411.6 14.6 %collective-permute-start.32 = (bf16[2,2,96,768]{3,2,1,0:T(8,128)(2,1)S(1)}, bf16[2,2,96,768]{3,2,1,0:T(8,128)(2,1)S(1)}, u32[]{:S(2)}, u32[]{:S(2)}) collective-permute-start(bf16[2,2,96,768]{3,2,1,0:T(8,128)(2,1)S(1)} %fusion.75), channel_id=1, source_target_pairs={{0,2},{1,3},{2,0},{3,1},{4,6},{5,7},{6,4},{7,5},{8,10},{9,11},{10,... | collective-permute-start | bytes 1769480 | tf_op jit(solution)/shard_map/ppermute | solution.py:102
  413.2 11.4 %collective-permute-start.16 = (bf16[2,2,2,24,1152]{4,3,0,1,2:T(8,128)(2,1)S(1)}, bf16[2,2,2,24,1152]{4,3,0,1,2:T(8,128)(2,1)S(1)}, u32[]{:S(2)}, u32[]{:S(2)}) collective-permute-start(bf16[2,2,2,24,1152]{4,3,0,1,2:T(8,128)(2,1)S(1)} %fusion.87), channel_id=1, source_target_pairs={{0,16},{1,17},{2,18},{3,19},{4,20},{5,21},{6,22},{7,23},{8,24},{9,... | collective-permute-start | bytes 1327112 | tf_op jit(solution)/shard_map/ppermute | solution.py:102
  416.1 14.2 %collective-permute-start.11 = (bf16[2,2,2,24,1280]{4,3,2,1,0:T(8,128)(2,1)S(1)}, bf16[2,2,2,24,1280]{4,3,2,1,0:T(8,128)(2,1)S(1)}, u32[]{:S(2)}, u32[]{:S(2)}) collective-permute-start(bf16[2,2,2,24,1280]{4,3,2,1,0:T(8,128)(2,1)S(1)} %fusion.86), channel_id=1, source_target_pairs={{0,1},{1,0},{2,3},{3,2},{4,5},{5,4},{6,7},{7,6},{8,9},{9,8},{10,11... | collective-permute-start | bytes 1474568 | tf_op jit(solution)/shard_map/ppermute | solution.py:102
  426.3 15.0 %collective-permute-start.33 = (bf16[2,96,768]{2,1,0:T(8,128)(2,1)S(1)}, bf16[2,96,768]{2,1,0:T(8,128)(2,1)S(1)}, u32[]{:S(2)}, u32[]{:S(2)}) collective-permute-start(bf16[2,96,768]{2,1,0:T(8,128)(2,1)S(1)} %fusion.92), channel_id=1, source_target_pairs={{0,16},{1,17},{2,18},{3,19},{4,20},{5,21},{6,22},{7,23},{8,24},{9,... | collective-permute-start | bytes 884744 | tf_op jit(solution)/shard_map/ppermute | solution.py:102
  441.5 9.6 %collective-permute-start.34 = (bf16[96,768]{1,0:T(8,128)(2,1)S(1)}, bf16[96,768]{1,0:T(8,128)(2,1)S(1)}, u32[]{:S(2)}, u32[]{:S(2)}) collective-permute-start(bf16[96,768]{1,0:T(8,128)(2,1)S(1)} %fusion.97), channel_id=1, source_target_pairs={{0,4},{1,5},{2,6},{3,7},{4,0},{5,1},{6,2},{7,3},{8,12},{9,13},{10,... | collective-permute-start | bytes 442376 | tf_op jit(solution)/shard_map/ppermute | solution.py:102
  (73 other events, 783.2 us)
Sparse Core Ops, SparseCore 0:
  10.9 100.2 all-gather.1
